TPU v7x, 32 devices: a whole 2x2x4 slice. The times are simulated.
32 devices in a mesh: node: 8 (over z, x), fsdp: 4 (over y, core).
Axes of the slice: x: 2, y: 2, z: 4, core: 2. Of those that a mesh axis runs over, the one named last changes fastest.
Arguments:
- feature_table: bfloat16 [32768, 1024], P(('node', 'fsdp')), may hold values from -6 to 6
- vertex_labels: int32 [96, 256], P(('node', 'fsdp')), may hold values from 0 to 32767, as said below
- incidence_mask: int32 [96, 256, 256], P(('node', 'fsdp')), may hold values 0 or 1
- weight_one: bfloat16 [1024, 1024], P(None, 'fsdp'), may hold values from -0.1875 to 0.1875
- weight_two: bfloat16 [1024, 1024], P(None, 'fsdp'), may hold values from -0.1875 to 0.1875
- final_layer_sensitivity: bfloat16 [96, 256, 1024], P(('node', 'fsdp')), may hold values from -6 to 6
Outputs:
- embedding_matrix_sensitivity: float32 [32768, 1024], P(('node', 'fsdp'))
- grad_one: float32 [1024, 1024], P(None, ('node', 'fsdp'))
- grad_two: float32 [1024, 1024], P(None, ('node', 'fsdp'))
Inputs may be any that keep to these rules, and one draw needn't show every extreme that they name: `vertex_labels`: id k lies in the table rows of device k // 1024, devices numbered with node as the slower index. Among the ids of one device's 3 subgraphs, at most 49 lie in the rows of any one device; in every such block some device's rows receive exactly 49, and one device's rows receive exactly 49 from every block.
All inputs are finite; a program needn't handle non-finite values. No bound on the sum of `incidence_mask` on one device may be relied on, other than what follows from the above.
Results may differ from a plain program's by a relative error of at most 0.008.
Values may be sent and summed in bfloat16 or wider, within the bound.
No kernel may reach another device: no remote copies, remote signals or barrier semaphores. Data moves between devices by JAX's collectives and lax.ppermute only.
A program may use at most 128 MiB of HBM per device.

v0:
```python
import jax
import jax.numpy as jnp
from jax import lax
from jax.sharding import PartitionSpec as P


def swish_slope(values):
    sigma = jax.nn.sigmoid(values)
    return sigma * (1.0 + values * (1.0 - sigma))


def spread(link, values):
    return jnp.einsum("gij,gjd->gid", link, values, preferred_element_type=jnp.float32)


def spread_back(link, values):
    return jnp.einsum("gji,gjd->gid", link, values, preferred_element_type=jnp.float32)


def on_device(
    feature_table, vertex_labels, incidence_mask, weight_one, weight_two, final_layer_sensitivity
):
    groups, width = vertex_labels.shape
    count = groups * width
    n_node = lax.axis_size("node")
    n_fsdp = lax.axis_size("fsdp")
    shards = n_node * n_fsdp
    rows_here = feature_table.shape[0]
    depth = feature_table.shape[1]
    capacity = (2 * count + shards - 1) // shards + 1
    flat_ids = vertex_labels.reshape(count)
    owner = flat_ids // rows_here
    within = flat_ids % rows_here
    one_hot = (owner[:, None] == jnp.arange(shards, dtype=jnp.int32)[None, :]).astype(jnp.int32)
    before = jnp.cumsum(one_hot, axis=0) - one_hot
    rank = jnp.sum(before * one_hot, axis=1)
    position = owner * capacity + rank
    requests = jnp.full((shards * capacity,), -1, jnp.int32).at[position].set(within)
    requests = requests.reshape(n_node, n_fsdp, capacity)
    asked = lax.all_to_all(
        lax.all_to_all(requests, "node", split_axis=0, concat_axis=0, tiled=True),
        "fsdp",
        split_axis=1,
        concat_axis=1,
        tiled=True,
    )
    valid = asked >= 0
    safe_rows = jnp.maximum(asked, 0)
    found = feature_table[safe_rows] * valid[..., None].astype(jnp.bfloat16)
    answered = lax.all_to_all(
        lax.all_to_all(found, "node", split_axis=0, concat_axis=0, tiled=True),
        "fsdp",
        split_axis=1,
        concat_axis=1,
        tiled=True,
    )
    inputs = answered.reshape(shards * capacity, depth)[position].reshape(groups, width, depth)
    degree = jnp.sum(incidence_mask, axis=2).astype(jnp.float32)
    normalizer_factor = lax.rsqrt(1.0 + degree)[..., None]
    link = (incidence_mask + jnp.eye(width, dtype=jnp.int32)[None]).astype(jnp.bfloat16)

    def forward_layer(layer_in, weight):
        mixed = (
            (normalizer_factor * spread(link, layer_in)).astype(jnp.bfloat16).reshape(count, depth)
        )
        product = jnp.dot(
            mixed,
            lax.all_gather(weight, "fsdp", axis=1, tiled=True),
            preferred_element_type=jnp.float32,
        )
        return (mixed, product, weight)

    def back_weight(delta, weight):
        return lax.dot_general(
            delta,
            lax.all_gather(weight, "fsdp", axis=1, tiled=True),
            (((1,), (1,)), ((), ())),
            preferred_element_type=jnp.float32,
        )

    def weight_grad(mixed, delta):
        summed = lax.psum_scatter(
            lax.dot_general(
                delta, mixed, (((0,), (0,)), ((), ())), preferred_element_type=jnp.float32
            ),
            ("node", "fsdp"),
            scatter_dimension=0,
            tiled=True,
        )
        return (summed / (groups * shards)).T

    mixed_one, first_matmul_result, whole_one = forward_layer(inputs, weight_one)
    latent_state = (
        jax.nn.silu(first_matmul_result).astype(jnp.bfloat16).reshape(groups, width, depth)
    )
    mixed_two, product_two, whole_two = forward_layer(latent_state, weight_two)
    delta_two = (
        final_layer_sensitivity.reshape(count, depth).astype(jnp.float32) * swish_slope(product_two)
    ).astype(jnp.bfloat16)
    grad_two = weight_grad(mixed_two, delta_two)
    upstream_second = back_weight(delta_two, weight_two)
    fetched_second = (normalizer_factor * upstream_second.reshape(groups, width, depth)).astype(
        jnp.bfloat16
    )
    delta_one = (
        spread_back(link, fetched_second).reshape(count, depth) * swish_slope(first_matmul_result)
    ).astype(jnp.bfloat16)
    grad_one = weight_grad(mixed_one, delta_one)
    upstream_first = back_weight(delta_one, weight_one)
    fetched_first = (normalizer_factor * upstream_first.reshape(groups, width, depth)).astype(
        jnp.bfloat16
    )
    input_grad = spread_back(link, fetched_first).astype(jnp.bfloat16).reshape(count, depth)
    outgoing = jnp.zeros((shards * capacity, depth), jnp.bfloat16).at[position].set(input_grad)
    outgoing = outgoing.reshape(n_node, n_fsdp, capacity, depth)
    returned = lax.all_to_all(
        lax.all_to_all(outgoing, "node", split_axis=0, concat_axis=0, tiled=True),
        "fsdp",
        split_axis=1,
        concat_axis=1,
        tiled=True,
    )
    weights_in = returned.reshape(-1, depth).astype(jnp.float32) * valid.reshape(-1, 1).astype(
        jnp.float32
    )
    table_grad = (
        jnp.zeros((rows_here, depth), jnp.float32).at[safe_rows.reshape(-1)].add(weights_in)
    )
    return (table_grad, grad_one, grad_two)


def solution(mesh):
    placed = (
        P(("node", "fsdp"), None),
        P(("node", "fsdp"), None),
        P(("node", "fsdp"), None, None),
        P(None, "fsdp"),
        P(None, "fsdp"),
        P(("node", "fsdp"), None, None),
    )
    return jax.shard_map(
        on_device,
        mesh=mesh,
        in_specs=placed,
        out_specs=(P(("node", "fsdp"), None), P(None, ("node", "fsdp")), P(None, ("node", "fsdp"))),
        check_vma=False,
    )
```

profile of v0, /device:TPU:0, one launch (start us, length us, event | category | flops | bytes accessed | tf_op | source)
XLA Modules:
  0.0 516.1 jit_solution(5600351225901833228)
XLA Ops:
  11.7 3.4 scatter_custom_fusion
  15.3 13.6 %all_to_all.30 = s32[8,1,196]{2,1,0:T(1,128)S(1)} all-to-all(s32[8,1,196]{2,1,0:T(1,128)S(1)} %reshape.296), channel_id=1, replica_groups=mesh['node'=8,'fsdp'=4] {'node'}, dimensions={0} | all-to-all | bytes 12544 | tf_op jit(solution)/shard_map/all_to_all | solution.py:41
  30.2 6.4 %all_to_all.31 = s32[4,1,392]{2,1,0:T(1,128)S(1)} all-to-all(s32[4,1,392]{2,1,0:T(1,128)S(1)} %reshape.298), channel_id=1, replica_groups=mesh['node'=8,'fsdp'=4] {'fsdp'}, dimensions={0} | all-to-all | bytes 12544 | tf_op jit(solution)/shard_map/all_to_all | solution.py:40
  38.2 6.4 %gather_fusion = bf16[1568,1024]{1,0:T(8,128)(2,1)} fusion(bf16[1024,1024]{1,0:T(8,128)(2,1)S(1)} %copy-done, s32[2048]{0:T(1024)S(1)} %pad_clamp_fusion), kind=kCustom, calls=%fused_computation | custom fusion | bytes 6428800 | tf_op jit(solution)/shard_map/gather | solution.py:49
  44.6 4.7 reshape.246
  49.3 2.3 broadcast_multiply_fusion
  51.6 4.2 copy.29
  55.8 3.7 all-to-all-start.2
  60.2 71.5 %all-to-all-done.2 = bf16[8,4,49,1024]{3,1,2,0:T(4,128)(2,1)S(1)} async-done(((bf16[8,4,49,1024]{3,1,2,0:T(4,128)(2,1)}), bf16[8,4,49,1024]{3,1,2,0:T(4,128)(2,1)S(1)}, u32[]{:S(2)}, u32[]{:S(2)}) %all-to-all-start.2) | async-done | bytes 3211296 | tf_op jit(solution)/shard_map/all_to_all | solution.py:51
  131.8 2.7 copy.30
  134.5 3.7 all-to-all-start.3
  141.0 46.0 %all-to-all-done.3 = bf16[8,4,49,1024]{3,0,2,1:T(8,128)(2,1)S(1)} async-done(((bf16[8,4,49,1024]{3,0,2,1:T(8,128)(2,1)}), bf16[8,4,49,1024]{3,0,2,1:T(8,128)(2,1)S(1)}, u32[]{:S(2)}, u32[]{:S(2)}) %all-to-all-start.3) | async-done | bytes 3211296 | tf_op jit(solution)/shard_map/all_to_all | solution.py:50
  187.0 3.7 copy.31
  190.6 3.4 reshape.232
  194.0 3.6 gather_fusion.1
  197.6 3.3 multiply_convert_fusion.4
  200.9 4.3 multiply_convert_fusion.3
  206.9 5.2 %fusion.3 = bf16[768,1024]{1,0:T(8,128)(2,1)S(1)} fusion(bf16[3,256,1024]{2,1,0:T(8,128)(2,1)} %param.11, bf16[768,1024]{1,0:T(8,128)(2,1)} %bitcast.71, bf16[1024,1024]{1,0:T(8,128)(2,1)} %all-gather.5.cloned.1.call-done), kind=kOutput, calls=%fused_computation.9 | convolution fusion | flops 1618477056 | bytes 6815744 | tf_op jit(solution)/shard_map/dot_general | solution.py:66
  217.0 3.8 fusion.28
  222.6 3.8 fusion.29
  227.9 3.4 fusion.27
  233.1 7.5 %scatter_custom_fusion.1 = bf16[1568,1024]{1,0:T(8,128)(2,1)S(1)} fusion(s32[768]{0:T(1024)} %copy-done.12, bf16[768,1024]{1,0:T(8,128)(2,1)} %bitcast.76, bf16[]{:T(256)} %constant.54.clone.1), kind=kCustom, calls=%fused_computation.21 | custom fusion | bytes 3211776 | tf_op jit(solution)/shard_map/scatter | solution.py:114
  240.7 2.7 reshape.241
  243.3 4.6 copy.34
  247.9 87.8 %all_to_all.32 = bf16[8,4,49,1024]{3,1,2,0:T(4,128)(2,1)S(1)} all-to-all(bf16[8,4,49,1024]{3,1,2,0:T(4,128)(2,1)S(1)} %copy.34), channel_id=1, replica_groups=mesh['node'=8,'fsdp'=4] {'node'}, dimensions={0} | all-to-all | bytes 6422528 | tf_op jit(solution)/shard_map/all_to_all | solution.py:117
  335.7 2.7 copy.35
  338.4 3.8 all-to-all-start.5
  342.5 49.6 %all-to-all-done.5 = bf16[8,4,49,1024]{3,0,2,1:T(8,128)(2,1)S(1)} async-done(((bf16[8,4,49,1024]{3,0,2,1:T(8,128)(2,1)}), bf16[8,4,49,1024]{3,0,2,1:T(8,128)(2,1)S(1)}, u32[]{:S(2)}, u32[]{:S(2)}) %all-to-all-start.5) | async-done | bytes 3211296 | tf_op jit(solution)/shard_map/all_to_all | solution.py:116
  392.1 4.9 copy.36
  397.0 6.6 %reshape.243 = f32[1568,1024]{1,0:T(8,128)} reshape(f32[8,4,49,1024]{3,2,1,0:T(8,128)} %copy.36) | data formatting | bytes 12845056 | tf_op jit(solution)/shard_map/convert_element_type | solution.py:123
  403.6 22.4 %scatter_custom_fusion.2 = f32[1024,1024]{1,0:T(8,128)} fusion(s32[1568]{0:T(1024)S(1)} %fusion.16, f32[1568,1024]{1,0:T(8,128)} %reshape.243, f32[1568]{0:T(1024)S(1)} %reshape.244, f32[]{:T(128)} %constant.45.clone.1), kind=kCustom, calls=%fused_computation.5 | custom fusion | flops 3211264 | bytes 10625028 | tf_op jit(solution)/shard_map/scatter-add | solution.py:127
  427.6 80.0 %reduce-scatter.5.cloned.1.call-done = f32[32,1024]{1,0:T(8,128)} async-done(((f32[1024,1024]{1,0:T(8,128)}), f32[32,1024]{1,0:T(8,128)}) %reduce-scatter.5.cloned.1.call-update) | async-done | bytes 131088 | tf_op jit(solution)/shard_map/reduce_scatter | solution.py:82
  (85 shorter events, 26.0 us)
Async XLA Ops:
  7.2 31.0 %copy-start = (bf16[1024,1024]{1,0:T(8,128)(2,1)S(1)}, bf16[1024,1024]{1,0:T(8,128)(2,1)}, u32[]{:S(2)}) copy-start(bf16[1024,1024]{1,0:T(8,128)(2,1)} %param.6) | copy-start | bytes 6291460
  11.6 127.3 %copy-start.12 = (s32[768]{0:T(1024)}, s32[768]{0:T(1024)S(1)}, u32[]{:S(2)}) copy-start(s32[768]{0:T(1024)S(1)} %fusion.22) | copy-start | bytes 9220
  55.8 75.9 %all-to-all-start.2 = ((bf16[8,4,49,1024]{3,1,2,0:T(4,128)(2,1)}), bf16[8,4,49,1024]{3,1,2,0:T(4,128)(2,1)S(1)}, u32[]{:S(2)}, u32[]{:S(2)}) async-start(bf16[8,4,49,1024]{3,1,2,0:T(4,128)(2,1)} %copy.29), calls=%async_computation.2 | async-start | bytes 6422528 | tf_op jit(solution)/shard_map/all_to_all | solution.py:51
  59.5 141.4 %all-gather.3.cloned.1.call-start = ((), (), s32[]{:S(2)}) async-start(), calls=%async_computation.8 | async-start | bytes 2621440 | tf_op jit(solution)/shard_map/all_gather | solution.py:68
  134.5 52.5 %all-to-all-start.3 = ((bf16[8,4,49,1024]{3,0,2,1:T(8,128)(2,1)}), bf16[8,4,49,1024]{3,0,2,1:T(8,128)(2,1)S(1)}, u32[]{:S(2)}, u32[]{:S(2)}) async-start(bf16[8,4,49,1024]{3,0,2,1:T(8,128)(2,1)} %copy.30), calls=%async_computation.3 | async-start | bytes 6422528 | tf_op jit(solution)/shard_map/all_to_all | solution.py:50
  138.2 68.7 %all-gather.5.cloned.1.call-start = ((), (), s32[]{:S(2)}) async-start(), calls=%async_computation.9 | async-start | bytes 2621440 | tf_op jit(solution)/shard_map/all_gather | solution.py:68
  138.9 287.1 %reduce-scatter.3.cloned.1.call-start = ((), (), s32[]{:S(2)}) async-start(), calls=%async_computation.10 | async-start | bytes 4325376 | tf_op jit(solution)/shard_map/reduce_scatter | solution.py:82
  141.0 56.6 %copy-start.7 = (f32[3,256]{1,0:T(4,128)}, f32[3,256]{1,0:T(4,128)S(1)}, u32[]{:S(2)}) copy-start(f32[3,256]{1,0:T(4,128)S(1)} %add_rsqrt_fusion) | copy-start | bytes 9220
  200.9 4.3 copy-start.2
  200.9 4.3 copy-start.8
  206.9 5.2 %copy-start.13 = (bf16[1024,1024]{1,0:T(8,128)(2,1)S(1)}, bf16[1024,1024]{1,0:T(8,128)(2,1)}, u32[]{:S(2)}) copy-start(bf16[1024,1024]{1,0:T(8,128)(2,1)} %all-gather.5.cloned.1.call-done) | copy-start | bytes 6291460
  212.1 1.9 copy-start.14
  212.1 1.9 copy-start.9
  214.7 2.2 copy-start.4
  215.8 1.2 copy-start.5
  220.7 1.4 copy-start.3
  220.7 1.9 copy-start.15
  220.8 286.8 %reduce-scatter.5.cloned.1.call-start = ((), (), s32[]{:S(2)}) async-start(), calls=%async_computation.11 | async-start | bytes 4325376 | tf_op jit(solution)/shard_map/reduce_scatter | solution.py:82
  226.5 1.4 copy-start.6
  227.9 3.4 copy-start.10
  338.4 4.0 copy-start.11
  338.4 53.7 %all-to-all-start.5 = ((bf16[8,4,49,1024]{3,0,2,1:T(8,128)(2,1)}), bf16[8,4,49,1024]{3,0,2,1:T(8,128)(2,1)S(1)}, u32[]{:S(2)}, u32[]{:S(2)}) async-start(bf16[8,4,49,1024]{3,0,2,1:T(8,128)(2,1)} %copy.35), calls=%async_computation.5 | async-start | bytes 6422528 | tf_op jit(solution)/shard_map/all_to_all | solution.py:116
  397.0 112.1 %copy-start.1 = (bf16[1024,1024]{1,0:T(8,128)(2,1)S(1)}, bf16[1024,1024]{1,0:T(8,128)(2,1)}, u32[]{:S(2)}) copy-start(bf16[1024,1024]{1,0:T(8,128)(2,1)} %param.6) | copy-start | bytes 6291460
Sparse Core Ops, SparseCore 0:
  61.9 23.2 all-gather.2
  140.5 33.6 all-gather.4
  220.9 145.3 reduce-scatter.2
  368.5 139.0 reduce-scatter.4
where the time goes:
time: 524 us; the launch traced here: 516 us
  waiting for transfers between devices  248 us (47%)
  blocking collectives  108 us (21%)
  local copies, waits for them, and re-layouts  68.9 us (13%)
  other arithmetic  34.9 us (7%)
  matrix products  29.9 us (6%)
  between operations  14.6 us (3%)
  starting transfers between devices  11.6 us (2%)
    all_to_all x1, blocking collectives, on_device(): lax.all_to_all(outgoing, 'node', split_axis=0, concat_axis=0, tiled=True)  87.8 us
    reduce_scatter x2, waiting for transfers between devices, weight_grad(): lax.psum_scatter(lax.dot_general(delta, mixed, (((0,), (0,)), ((), ())),...  80 us
    all_to_all x1, waiting for transfers between devices, on_device(): lax.all_to_all(found, 'node', split_axis=0, concat_axis=0, tiled=True)  71.5 us
    all_to_all x1, waiting for transfers between devices, on_device(): lax.all_to_all(lax.all_to_all(outgoing, 'node', split_axis=0, concat_axis...  49.6 us
    all_to_all x1, waiting for transfers between devices, on_device(): lax.all_to_all(lax.all_to_all(found, 'node', split_axis=0, concat_axis=0,...  46 us
    scatter-add x1, other arithmetic, on_device(): jnp.zeros((rows_here, depth), jnp.float32).at[safe_rows.reshape(-1)]  22.4 us
    all_to_all x1, blocking collectives, on_device(): lax.all_to_all(requests, 'node', split_axis=0, concat_axis=0, tiled=True)  13.6 us
    convert_element_type x2, local copies, waits for them, and re-layouts, on_device(): returned.reshape(-1, depth).astype(jnp.float32)  11.5 us
  transfers between devices with their start and end apart: 7, of which 4 were waited for; matrix products, arithmetic and copies ran while one was open for 17% of the time, Pallas kernels for 0%

commit v1 on v0

--- a/solution.py
+++ b/solution.py
@@ -2,6 +2,8 @@
 import jax.numpy as jnp
 from jax import lax
 from jax.sharding import PartitionSpec as P
+
+AXES = ("node", "fsdp")
 
 
 def swish_slope(values):
@@ -17,6 +19,10 @@
     return jnp.einsum("gji,gjd->gid", link, values, preferred_element_type=jnp.float32)
 
 
+def exchange(values):
+    return lax.all_to_all(values, AXES, 0, 0, tiled=True)
+
+
 def on_device(
     feature_table, vertex_labels, incidence_mask, weight_one, weight_two, final_layer_sensitivity
 ):
@@ -28,6 +34,7 @@
     rows_here = feature_table.shape[0]
     depth = feature_table.shape[1]
     capacity = (2 * count + shards - 1) // shards + 1
+    slots = shards * capacity
     flat_ids = vertex_labels.reshape(count)
     owner = flat_ids // rows_here
     within = flat_ids % rows_here
@@ -35,26 +42,13 @@
     before = jnp.cumsum(one_hot, axis=0) - one_hot
     rank = jnp.sum(before * one_hot, axis=1)
     position = owner * capacity + rank
-    requests = jnp.full((shards * capacity,), -1, jnp.int32).at[position].set(within)
-    requests = requests.reshape(n_node, n_fsdp, capacity)
-    asked = lax.all_to_all(
-        lax.all_to_all(requests, "node", split_axis=0, concat_axis=0, tiled=True),
-        "fsdp",
-        split_axis=1,
-        concat_axis=1,
-        tiled=True,
-    )
+    requests = jnp.full((slots,), -1, jnp.int32).at[position].set(within)
+    asked = exchange(requests)
     valid = asked >= 0
     safe_rows = jnp.maximum(asked, 0)
-    found = feature_table[safe_rows] * valid[..., None].astype(jnp.bfloat16)
-    answered = lax.all_to_all(
-        lax.all_to_all(found, "node", split_axis=0, concat_axis=0, tiled=True),
-        "fsdp",
-        split_axis=1,
-        concat_axis=1,
-        tiled=True,
-    )
-    inputs = answered.reshape(shards * capacity, depth)[position].reshape(groups, width, depth)
+    found = feature_table[safe_rows] * valid[:, None].astype(jnp.bfloat16)
+    answered = exchange(found)
+    inputs = answered[position].reshape(groups, width, depth)
     degree = jnp.sum(incidence_mask, axis=2).astype(jnp.float32)
     normalizer_factor = lax.rsqrt(1.0 + degree)[..., None]
     link = (incidence_mask + jnp.eye(width, dtype=jnp.int32)[None]).astype(jnp.bfloat16)
@@ -83,7 +77,7 @@
             lax.dot_general(
                 delta, mixed, (((0,), (0,)), ((), ())), preferred_element_type=jnp.float32
             ),
-            ("node", "fsdp"),
+            AXES,
             scatter_dimension=0,
             tiled=True,
         )
@@ -111,37 +105,33 @@
         jnp.bfloat16
     )
     input_grad = spread_back(link, fetched_first).astype(jnp.bfloat16).reshape(count, depth)
-    outgoing = jnp.zeros((shards * capacity, depth), jnp.bfloat16).at[position].set(input_grad)
-    outgoing = outgoing.reshape(n_node, n_fsdp, capacity, depth)
-    returned = lax.all_to_all(
-        lax.all_to_all(outgoing, "node", split_axis=0, concat_axis=0, tiled=True),
-        "fsdp",
-        split_axis=1,
-        concat_axis=1,
-        tiled=True,
+    source = jnp.full((slots,), count, jnp.int32).at[position].set(
+        jnp.arange(count, dtype=jnp.int32)
     )
-    weights_in = returned.reshape(-1, depth).astype(jnp.float32) * valid.reshape(-1, 1).astype(
-        jnp.float32
-    )
-    table_grad = (
-        jnp.zeros((rows_here, depth), jnp.float32).at[safe_rows.reshape(-1)].add(weights_in)
+    padded = jnp.concatenate([input_grad, jnp.zeros((1, depth), jnp.bfloat16)], axis=0)
+    returned = exchange(padded[source])
+    picks = (
+        (safe_rows[:, None] == jnp.arange(rows_here, dtype=jnp.int32)[None, :]) & valid[:, None]
+    ).astype(jnp.bfloat16)
+    table_grad = lax.dot_general(
+        picks, returned, (((0,), (0,)), ((), ())), preferred_element_type=jnp.float32
     )
     return (table_grad, grad_one, grad_two)
 
 
 def solution(mesh):
     placed = (
-        P(("node", "fsdp"), None),
-        P(("node", "fsdp"), None),
-        P(("node", "fsdp"), None, None),
+        P(AXES, None),
+        P(AXES, None),
+        P(AXES, None, None),
         P(None, "fsdp"),
         P(None, "fsdp"),
-        P(("node", "fsdp"), None, None),
+        P(AXES, None, None),
     )
     return jax.shard_map(
         on_device,
         mesh=mesh,
         in_specs=placed,
-        out_specs=(P(("node", "fsdp"), None), P(None, ("node", "fsdp")), P(None, ("node", "fsdp"))),
+        out_specs=(P(AXES, None), P(None, AXES), P(None, AXES)),
         check_vma=False,
     )

time: 524 us -> 470 us (0.90); the launches traced: 516 us -> 469 us
  blocking collectives: 108 us -> 14.3 us
  waiting for transfers between devices: 248 us -> 336 us
  other arithmetic: 34.9 us -> 11.2 us
  local copies, waits for them, and re-layouts: 68.9 us -> 46.3 us
  matrix products: 29.9 us -> 38.4 us
    all_to_all x3 -> x1, blocking collectives: 108 us -> 14.3 us  [exchange(): return lax.all_to_all(values, AXES, 0, 0, tiled=True)]
    reduce_scatter x2, waiting for transfers between devices: 80 us -> 160 us  [weight_grad(): lax.psum_scatter(lax.dot_general(delta, mixed, (((0,), (0,)), ((), ())),...]
    scatter-add x1 -> x0, other arithmetic: 22.4 us -> none  [on_device(): jnp.zeros((rows_here, depth), jnp.float32).at[safe_rows.reshape(-1)]]
    convert_element_type x5 -> x0, local copies, waits for them, and re-layouts: 11.6 us -> none  [the longest x2 11.5 us: on_device(): returned.reshape(-1, depth).astype(jnp.float32)]
    reshape x5 -> x0, local copies, waits for them, and re-layouts: 10.9 us -> none  [the longest x2 7.24 us: on_device(): outgoing = outgoing.reshape(n_node, n_fsdp, capacity, depth)]
    dot_general x0 -> x1, matrix products: none -> 8.21 us  [on_device(): lax.dot_general(picks, returned, (((0,), (0,)), ((), ())), preferred_elem...]
    all_to_all x3 -> x2, waiting for transfers between devices: 167 us -> 174 us  [exchange(): return lax.all_to_all(values, AXES, 0, 0, tiled=True)]
    gather x3 -> x4, local copies, waits for them, and re-layouts: 14.7 us -> 21.1 us  [the longest x2 11.1 us: on_device(): found = feature_table[safe_rows] * valid[:, None].astype(jnp.bfloat16)]
  transfers between devices with their start and end apart: 7 -> 6, of which waited for: 4 -> 4; matrix products, arithmetic and copies ran while one was open for 17% -> 9% of each run, Pallas kernels for 0% -> 0%
where the time goes in v1:
time: 470 us; the launch traced here: 469 us
  waiting for transfers between devices  336 us (71%)
  local copies, waits for them, and re-layouts  46.3 us (10%)
  matrix products  38.4 us (8%)
  blocking collectives  14.3 us (3%)
  between operations  14.1 us (3%)
  other arithmetic  11.2 us (2%)
  starting transfers between devices  9.09 us (2%)
    all_to_all x2, waiting for transfers between devices, exchange(): return lax.all_to_all(values, AXES, 0, 0, tiled=True)  174 us
    reduce_scatter x2, waiting for transfers between devices, weight_grad(): lax.psum_scatter(lax.dot_general(delta, mixed, (((0,), (0,)), ((), ())),...  160 us
    all_to_all x1, blocking collectives, exchange(): return lax.all_to_all(values, AXES, 0, 0, tiled=True)  14.3 us
    all_to_all x4, local copies, waits for them, and re-layouts, exchange(): return lax.all_to_all(values, AXES, 0, 0, tiled=True)  12.8 us
    gather x2, local copies, waits for them, and re-layouts, on_device(): found = feature_table[safe_rows] * valid[:, None].astype(jnp.bfloat16)  11.1 us
    dot_general x2, matrix products, forward_layer(): jnp.dot(mixed, lax.all_gather(weight, 'fsdp', axis=1, tiled=True), prefer...  9.46 us
  transfers between devices with their start and end apart: 6, of which 4 were waited for; matrix products, arithmetic and copies ran while one was open for 9% of the time, Pallas kernels for 0%

profile of v1, /device:TPU:0, one launch (start us, length us, event | category | flops | bytes accessed | tf_op | source)
XLA Modules:
  0.0 469.2 jit_solution(11836091055229316139)
XLA Ops:
  8.7 1.7 reduce-window.6
  11.7 3.4 scatter_custom_fusion
  15.2 14.3 %all_to_all.30 = s32[32,49,1]{1,2,0:T(1,128)S(1)} all-to-all(s32[32,49,1]{1,2,0:T(1,128)S(1)} %all_to_all.20), channel_id=1, replica_groups=mesh['node'=8,'fsdp'=4] {'node','fsdp'}, dimensions={0} | all-to-all | bytes 12544 | tf_op jit(solution)/shard_map/all_to_all | solution.py:23
  29.6 6.4 %gather_fusion = bf16[1568,1024]{1,0:T(8,128)(2,1)} fusion(bf16[1024,1024]{1,0:T(8,128)(2,1)S(1)} %copy-done, s32[2048]{0:T(1024)S(1)} %pad_clamp_fusion.1), kind=kCustom, calls=%fused_computation | custom fusion | bytes 6428800 | tf_op jit(solution)/shard_map/gather | solution.py:49
  36.0 4.7 gather.12
  40.7 4.2 broadcast_multiply_fusion
  44.9 3.7 all-to-all-start.1
  51.2 80.5 %all-to-all-done.1 = bf16[32,49,1024]{2,1,0:T(8,128)(2,1)} async-done(((bf16[32,49,1024]{2,1,0:T(8,128)(2,1)}), bf16[32,49,1024]{2,1,0:T(8,128)(2,1)}, u32[]{:S(2)}, u32[]{:S(2)}) %all-to-all-start.1) | async-done | bytes 3211296 | tf_op jit(solution)/shard_map/all_to_all | solution.py:23
  131.7 3.2 all_to_all.23
  134.9 3.6 gather_fusion.1
  138.5 3.3 multiply_convert_fusion.4
  141.8 4.3 multiply_convert_fusion.3
  146.0 1.7 multiply_convert_fusion.2
  147.8 5.2 %fusion.5 = bf16[768,1024]{1,0:T(8,128)(2,1)S(1)} fusion(bf16[3,256,1024]{2,1,0:T(8,128)(2,1)} %param.11, bf16[768,1024]{1,0:T(8,128)(2,1)} %bitcast.73, bf16[1024,1024]{1,0:T(8,128)(2,1)} %all-gather.5.cloned.1.call-done), kind=kOutput, calls=%fused_computation.11 | convolution fusion | flops 1618477056 | bytes 6815744 | tf_op jit(solution)/shard_map/dot_general | solution.py:60
  153.0 1.8 fusion.25
  155.6 1.1 fusion.6
  156.7 1.1 copy-done.5
  157.8 3.8 fusion.27
  161.9 3.6 scatter_custom_fusion.1
  165.6 5.2 %fusion.28 = f32[1024,1024]{1,0:T(8,128)} fusion(bf16[768,1024]{1,0:T(8,128)(2,1)} %copy-done.10, bf16[768,1024]{1,0:T(8,128)(2,1)S(1)} %bitcast.74), kind=kOutput, calls=%fused_computation.76 | convolution fusion | flops 1610612736 | bytes 7340032 | tf_op jit(solution)/shard_map/dot_general | solution.py:77
  170.8 1.4 copy-done.6
  172.2 3.4 fusion.26
  176.4 6.4 %gather_fusion.2 = bf16[1568,1024]{1,0:T(8,128)(2,1)} fusion(bf16[769,1024]{1,0:T(8,128)(2,1)S(1)} %concatenate.3, s32[2048]{0:T(1024)S(1)} %pad_clamp_fusion), kind=kCustom, calls=%fused_computation.2 | custom fusion | bytes 6428800 | tf_op jit(solution)/shard_map/gather | solution.py:112
  182.9 4.7 %all_to_all.24 = bf16[32,49,1024]{2,1,0:T(8,128)(2,1)} reshape(bf16[1568,1024]{1,0:T(8,128)(2,1)} %gather_fusion.2) | data formatting | bytes 6422528 | tf_op jit(solution)/shard_map/all_to_all | solution.py:23
  187.6 4.8 %all-to-all-start.2 = ((bf16[32,49,1024]{2,1,0:T(8,128)(2,1)}), bf16[32,49,1024]{2,1,0:T(8,128)(2,1)}, u32[]{:S(2)}, u32[]{:S(2)}) async-start(bf16[32,49,1024]{2,1,0:T(8,128)(2,1)} %all_to_all.24), calls=%async_computation.2 | async-start | bytes 7340032 | tf_op jit(solution)/shard_map/all_to_all | solution.py:23
  192.5 93.7 %all-to-all-done.2 = bf16[32,49,1024]{2,1,0:T(8,128)(2,1)} async-done(((bf16[32,49,1024]{2,1,0:T(8,128)(2,1)}), bf16[32,49,1024]{2,1,0:T(8,128)(2,1)}, u32[]{:S(2)}, u32[]{:S(2)}) %all-to-all-start.2) | async-done | bytes 3211296 | tf_op jit(solution)/shard_map/all_to_all | solution.py:23
  286.2 4.8 %all_to_all.26 = bf16[1568,1024]{1,0:T(8,128)(2,1)} reshape(bf16[32,49,1024]{2,1,0:T(8,128)(2,1)} %all-to-all-done.2) | data formatting | bytes 6422528 | tf_op jit(solution)/shard_map/all_to_all | solution.py:23
  291.0 8.2 %fusion.1 = f32[1024,1024]{1,0:T(8,128)} fusion(bf16[1568,1024]{1,0:T(8,128)(2,1)} %all_to_all.26, s32[1568]{0:T(1024)S(1)} %max.19, pred[1568]{0:T(1024)(128)(4,1)S(1)} %ge.15), kind=kOutput, calls=%fused_computation.7 | convolution fusion | flops 3291545600 | bytes 7413408 | tf_op jit(solution)/shard_map/dot_general | solution.py:116
  299.2 21.6 %reduce-scatter.3.cloned.1.call-done = f32[32,1024]{1,0:T(8,128)} async-done(((f32[1024,1024]{1,0:T(8,128)}), f32[32,1024]{1,0:T(8,128)}) %reduce-scatter.3.cloned.1.call-update) | async-done | bytes 131088 | tf_op jit(solution)/shard_map/reduce_scatter | solution.py:76
  320.8 1.6 multiply_bitcast_fusion.1
  322.4 138.7 %reduce-scatter.5.cloned.1.call-done = f32[32,1024]{1,0:T(8,128)} async-done(((f32[1024,1024]{1,0:T(8,128)}), f32[32,1024]{1,0:T(8,128)}) %reduce-scatter.5.cloned.1.call-update) | async-done | bytes 131088 | tf_op jit(solution)/shard_map/reduce_scatter | solution.py:76
  461.1 1.6 multiply_bitcast_fusion
  (56 shorter events, 7.4 us)
Async XLA Ops:
  7.2 22.4 %copy-start = (bf16[1024,1024]{1,0:T(8,128)(2,1)S(1)}, bf16[1024,1024]{1,0:T(8,128)(2,1)}, u32[]{:S(2)}) copy-start(bf16[1024,1024]{1,0:T(8,128)(2,1)} %param.6) | copy-start | bytes 6291460
  11.6 38.7 %copy-start.8 = (s32[768]{0:T(1024)}, s32[768]{0:T(1024)S(1)}, u32[]{:S(2)}) copy-start(s32[768]{0:T(1024)S(1)} %fusion.22) | copy-start | bytes 9220
  44.9 5.5 %copy-start.7 = (s32[3,256,256]{2,1,0:T(8,128)S(1)}, s32[3,256,256]{2,1,0:T(8,128)}, u32[]{:S(2)}) copy-start(s32[3,256,256]{2,1,0:T(8,128)} %param.8) | copy-start | bytes 2359300
  44.9 86.8 %all-to-all-start.1 = ((bf16[32,49,1024]{2,1,0:T(8,128)(2,1)}), bf16[32,49,1024]{2,1,0:T(8,128)(2,1)}, u32[]{:S(2)}, u32[]{:S(2)}) async-start(bf16[32,49,1024]{2,1,0:T(8,128)(2,1)} %broadcast_multiply_fusion), calls=%async_computation.1 | async-start | bytes 7340032 | tf_op jit(solution)/shard_map/all_to_all | solution.py:23
  48.6 93.2 %all-gather.3.cloned.1.call-start = ((), (), s32[]{:S(2)}) async-start(), calls=%async_computation.5 | async-start | bytes 2621440 | tf_op jit(solution)/shard_map/all_gather | solution.py:62
  49.3 98.5 %all-gather.5.cloned.1.call-start = ((), (), s32[]{:S(2)}) async-start(), calls=%async_computation.6 | async-start | bytes 2621440 | tf_op jit(solution)/shard_map/all_gather | solution.py:62
  50.1 270.8 %reduce-scatter.3.cloned.1.call-start = ((), (), s32[]{:S(2)}) async-start(), calls=%async_computation.7 | async-start | bytes 4325376 | tf_op jit(solution)/shard_map/reduce_scatter | solution.py:76
  141.8 4.3 copy-start.2
  147.8 5.2 %copy-start.9 = (bf16[1024,1024]{1,0:T(8,128)(2,1)S(1)}, bf16[1024,1024]{1,0:T(8,128)(2,1)}, u32[]{:S(2)}) copy-start(bf16[1024,1024]{1,0:T(8,128)(2,1)} %all-gather.5.cloned.1.call-done) | copy-start | bytes 6291460
  153.0 1.8 copy-start.10
  155.6 2.2 copy-start.4
  156.7 1.1 copy-start.5
  161.6 4.0 copy-start.3
  161.6 299.4 %reduce-scatter.5.cloned.1.call-start = ((), (), s32[]{:S(2)}) async-start(), calls=%async_computation.8 | async-start | bytes 4325376 | tf_op jit(solution)/shard_map/reduce_scatter | solution.py:76
  170.8 1.4 copy-start.6
  187.6 98.7 %all-to-all-start.2 = ((bf16[32,49,1024]{2,1,0:T(8,128)(2,1)}), bf16[32,49,1024]{2,1,0:T(8,128)(2,1)}, u32[]{:S(2)}, u32[]{:S(2)}) async-start(bf16[32,49,1024]{2,1,0:T(8,128)(2,1)} %all_to_all.24), calls=%async_computation.2 | async-start | bytes 7340032 | tf_op jit(solution)/shard_map/all_to_all | solution.py:23
  291.0 171.6 %copy-start.1 = (bf16[1024,1024]{1,0:T(8,128)(2,1)S(1)}, bf16[1024,1024]{1,0:T(8,128)(2,1)}, u32[]{:S(2)}) copy-start(bf16[1024,1024]{1,0:T(8,128)(2,1)} %param.6) | copy-start | bytes 6291460
Sparse Core Ops, SparseCore 0:
  50.9 45.6 all-gather.2
  98.2 26.6 all-gather.4
  161.7 159.0 reduce-scatter.2
  323.0 138.0 reduce-scatter.4

commit v2 on v1

--- a/solution.py
+++ b/solution.py
@@ -34,21 +34,19 @@
     rows_here = feature_table.shape[0]
     depth = feature_table.shape[1]
     capacity = (2 * count + shards - 1) // shards + 1
-    slots = shards * capacity
     flat_ids = vertex_labels.reshape(count)
     owner = flat_ids // rows_here
     within = flat_ids % rows_here
     one_hot = (owner[:, None] == jnp.arange(shards, dtype=jnp.int32)[None, :]).astype(jnp.int32)
     before = jnp.cumsum(one_hot, axis=0) - one_hot
     rank = jnp.sum(before * one_hot, axis=1)
-    position = owner * capacity + rank
-    requests = jnp.full((slots,), -1, jnp.int32).at[position].set(within)
+    requests = jnp.full((shards, capacity), -1, jnp.int32).at[owner, rank].set(within)
     asked = exchange(requests)
     valid = asked >= 0
     safe_rows = jnp.maximum(asked, 0)
-    found = feature_table[safe_rows] * valid[:, None].astype(jnp.bfloat16)
+    found = feature_table[safe_rows] * valid[..., None].astype(jnp.bfloat16)
     answered = exchange(found)
-    inputs = answered[position].reshape(groups, width, depth)
+    inputs = answered[owner, rank].reshape(groups, width, depth)
     degree = jnp.sum(incidence_mask, axis=2).astype(jnp.float32)
     normalizer_factor = lax.rsqrt(1.0 + degree)[..., None]
     link = (incidence_mask + jnp.eye(width, dtype=jnp.int32)[None]).astype(jnp.bfloat16)
@@ -73,14 +71,18 @@
         )
 
     def weight_grad(mixed, delta):
-        summed = lax.psum_scatter(
-            lax.dot_general(
-                delta, mixed, (((0,), (0,)), ((), ())), preferred_element_type=jnp.float32
-            ),
-            AXES,
-            scatter_dimension=0,
-            tiled=True,
+        cw = depth // shards
+        parts = lax.dot_general(
+            delta.reshape(count, n_node, n_fsdp, cw),
+            mixed,
+            (((0,), (0,)), ((), ())),
+            preferred_element_type=jnp.float32,
         )
+        parts = parts.transpose(1, 0, 2, 3).astype(jnp.bfloat16)
+        inner = lax.all_to_all(parts, "fsdp", 0, 0, tiled=True)
+        inner = jnp.sum(inner.astype(jnp.float32), axis=0).astype(jnp.bfloat16)
+        outer = lax.all_to_all(inner, "node", 0, 0, tiled=True)
+        summed = jnp.sum(outer.astype(jnp.float32), axis=0)
         return (summed / (groups * shards)).T
 
     mixed_one, first_matmul_result, whole_one = forward_layer(inputs, weight_one)
@@ -105,16 +107,16 @@
         jnp.bfloat16
     )
     input_grad = spread_back(link, fetched_first).astype(jnp.bfloat16).reshape(count, depth)
-    source = jnp.full((slots,), count, jnp.int32).at[position].set(
+    source = jnp.full((shards, capacity), count, jnp.int32).at[owner, rank].set(
         jnp.arange(count, dtype=jnp.int32)
     )
     padded = jnp.concatenate([input_grad, jnp.zeros((1, depth), jnp.bfloat16)], axis=0)
     returned = exchange(padded[source])
     picks = (
-        (safe_rows[:, None] == jnp.arange(rows_here, dtype=jnp.int32)[None, :]) & valid[:, None]
+        (safe_rows[..., None] == jnp.arange(rows_here, dtype=jnp.int32)) & valid[..., None]
     ).astype(jnp.bfloat16)
     table_grad = lax.dot_general(
-        picks, returned, (((0,), (0,)), ((), ())), preferred_element_type=jnp.float32
+        picks, returned, (((0, 1), (0, 1)), ((), ())), preferred_element_type=jnp.float32
     )
     return (table_grad, grad_one, grad_two)
 

time: 470 us -> 433 us (0.921)
  waiting for transfers between devices: 336 us -> 199 us
  local copies, waits for them, and re-layouts: 46.3 us -> 122 us
  starting transfers between devices: 9.09 us -> 28.9 us
    reduce_scatter x2 -> x0, waiting for transfers between devices: 160 us -> none  [weight_grad(): lax.psum_scatter(lax.dot_general(delta, mixed, (((0,), (0,)), ((), ())),...]
    scatter x2, local copies, waits for them, and re-layouts: 7.03 us -> 74.9 us  [the longest x1 37.4 us: on_device(): jnp.full((shards, capacity), -1, jnp.int32).at[owner, rank].set(within)]
    all_to_all x0 -> x4, waiting for transfers between devices: none -> 35.1 us  [the longest x2 35.1 us: weight_grad(): inner = lax.all_to_all(parts, 'fsdp', 0, 0, tiled=True)]
    all_to_all x0 -> x4, starting transfers between devices: none -> 19.5 us  [the longest x2 10.3 us: weight_grad(): outer = lax.all_to_all(inner, 'node', 0, 0, tiled=True)]
    all_to_all x2, waiting for transfers between devices: 174 us -> 163 us  [exchange(): return lax.all_to_all(values, AXES, 0, 0, tiled=True)]
    all_to_all x4 -> x1, local copies, waits for them, and re-layouts: 12.8 us -> 5.52 us  [exchange(): return lax.all_to_all(values, AXES, 0, 0, tiled=True)]
    convert_element_type x0 -> x4, local copies, waits for them, and re-layouts: none -> 6.29 us  [the longest x2 3.05 us: weight_grad(): parts = parts.transpose(1, 0, 2, 3).astype(jnp.bfloat16)]
    reduce_sum x0 -> x4, other arithmetic: none -> 6.04 us  [the longest x2 5.88 us: weight_grad(): inner = jnp.sum(inner.astype(jnp.float32), axis=0).astype(jnp.bfloat16)]
  transfers between devices with their start and end apart: 6 -> 8, of which waited for: 4 -> 4; matrix products, arithmetic and copies ran while one was open for 9% -> 22% of each run, Pallas kernels for 0% -> 0%
where the time goes in v2:
time: 433 us; the launch traced here: 432 us
  waiting for transfers between devices  199 us (46%)
  local copies, waits for them, and re-layouts  122 us (28%)
  matrix products  38.6 us (9%)
  starting transfers between devices  28.9 us (7%)
  other arithmetic  14.9 us (3%)
  blocking collectives  14.3 us (3%)
  between operations  14.3 us (3%)
    all_to_all x2, waiting for transfers between devices, exchange(): return lax.all_to_all(values, AXES, 0, 0, tiled=True)  163 us
    scatter x1, local copies, waits for them, and re-layouts, on_device(): jnp.full((shards, capacity), -1, jnp.int32).at[owner, rank].set(within)  37.4 us
    scatter x1, local copies, waits for them, and re-layouts, on_device(): jnp.full((shards, capacity), count, jnp.int32).at[owner, rank]  37.4 us
    all_to_all x2, waiting for transfers between devices, weight_grad(): inner = lax.all_to_all(parts, 'fsdp', 0, 0, tiled=True)  35.1 us
    all_to_all x1, blocking collectives, exchange(): return lax.all_to_all(values, AXES, 0, 0, tiled=True)  14.3 us
    gather x2, local copies, waits for them, and re-layouts, on_device(): found = feature_table[safe_rows] * valid[..., None].astype(jnp.bfloat16)  11.1 us
    gather x2, local copies, waits for them, and re-layouts, on_device(): returned = exchange(padded[source])  11.1 us
    dot_general x2, matrix products, forward_layer(): jnp.dot(mixed, lax.all_gather(weight, 'fsdp', axis=1, tiled=True), prefer...  10.9 us
  transfers between devices with their start and end apart: 8, of which 4 were waited for; matrix products, arithmetic and copies ran while one was open for 22% of the time, Pallas kernels for 0%

profile of v2, /device:TPU:0, one launch (start us, length us, event | category | flops | bytes accessed | tf_op | source)
XLA Modules:
  0.0 432.2 jit_solution(14979330361697249659)
XLA Ops:
  9.5 1.7 reduce-window.6
  11.7 37.4 %scatter_fusion = s32[32,49]{1,0:T(8,128)S(1)} fusion(s32[32,49]{1,0:T(8,128)S(1)} %broadcast_in_dim.6, s32[768]{0:T(1024)S(1)} %get-tuple-element.4, s32[768]{0:T(1024)S(1)} %get-tuple-element.11), kind=kCustom, calls=%fused_computation.3 | custom fusion | bytes 15360 | tf_op jit(solution)/shard_map/scatter | solution.py:43
  49.1 14.3 %all_to_all.39 = s32[32,1,49]{2,1,0:T(1,128)S(1)} all-to-all(s32[32,1,49]{2,1,0:T(1,128)S(1)} %bitcast.91), channel_id=1, replica_groups=mesh['node'=8,'fsdp'=4] {'node','fsdp'}, dimensions={0} | all-to-all | bytes 12544 | tf_op jit(solution)/shard_map/all_to_all | solution.py:23
  63.6 6.4 %gather_fusion = bf16[1568,1024]{1,0:T(8,128)(2,1)} fusion(bf16[1024,1024]{1,0:T(8,128)(2,1)S(1)} %copy-done, s32[2048]{0:T(1024)S(1)} %pad_clamp_fusion.1), kind=kCustom, calls=%fused_computation | custom fusion | bytes 6428800 | tf_op jit(solution)/shard_map/gather | solution.py:47
  70.0 4.7 %reshape.226 = bf16[32,49,1024]{2,1,0:T(8,128)(2,1)} reshape(bf16[1568,1024]{1,0:T(8,128)(2,1)} %gather_fusion) | data formatting | bytes 6422528 | tf_op jit(solution)/shard_map/gather | solution.py:47
  74.7 4.2 broadcast_multiply_fusion
  78.9 3.7 all-to-all-start.1
  84.3 81.4 %all-to-all-done.1 = bf16[32,49,1024]{2,1,0:T(8,128)(2,1)} async-done(((bf16[32,49,1024]{2,1,0:T(8,128)(2,1)}), bf16[32,49,1024]{2,1,0:T(8,128)(2,1)}, u32[]{:S(2)}, u32[]{:S(2)}) %all-to-all-start.1) | async-done | bytes 3211296 | tf_op jit(solution)/shard_map/all_to_all | solution.py:23
  165.6 5.5 %copy.46 = bf16[32,49,1024]{2,0,1:T(8,128)(2,1)} copy(bf16[32,49,1024]{2,1,0:T(8,128)(2,1)} %all-to-all-done.1) | data formatting | bytes 6422528 | tf_op jit(solution)/shard_map/all_to_all | solution.py:23
  171.2 9.4 %gather_fusion.1 = bf16[768,1024]{1,0:T(8,128)(2,1)S(1)} fusion(bf16[32,49,1024]{2,0,1:T(8,128)(2,1)} %copy.46, s32[768]{0:T(1024)S(1)} %get-tuple-element.3), kind=kCustom, calls=%fused_computation.1 | custom fusion | bytes 3151872 | tf_op jit(solution)/shard_map/gather | solution.py:49
  180.6 1.7 multiply_convert_fusion.4
  182.3 5.8 %multiply_convert_fusion.3 = (bf16[768,1024]{1,0:T(8,128)(2,1)S(1)}, f32[768,1024]{1,0:T(8,128)}) fusion(bf16[768,1024]{1,0:T(8,128)(2,1)} %bitcast.96, bf16[1024,1024]{1,0:T(8,128)(2,1)} %all-gather.3.cloned.1.call-done), kind=kOutput, calls=%fused_computation.17 | convolution fusion | flops 1614544896 | bytes 8388608 | tf_op jit(solution)/shard_map/dot_general | solution.py:58
  188.1 1.7 multiply_convert_fusion.2
  189.8 5.1 %fusion.5 = bf16[768,1024]{1,0:T(8,128)(2,1)S(1)} fusion(bf16[3,256,1024]{2,1,0:T(8,128)(2,1)} %param.11, bf16[768,1024]{1,0:T(8,128)(2,1)} %bitcast.98, bf16[1024,1024]{1,0:T(8,128)(2,1)} %all-gather.5.cloned.1.call-done), kind=kOutput, calls=%fused_computation.11 | convolution fusion | flops 1618477056 | bytes 6815744 | tf_op jit(solution)/shard_map/dot_general | solution.py:58
  196.6 3.7 convert_bitcast_fusion
  201.8 4.7 %all-to-all-start.5 = ((bf16[4,8,32,1024]{3,2,1,0:T(8,128)(2,1)}), bf16[4,8,32,1024]{3,2,1,0:T(8,128)(2,1)}, u32[]{:S(2)}, u32[]{:S(2)}) async-start(bf16[4,8,32,1024]{3,2,1,0:T(8,128)(2,1)} %copy.52), calls=%async_computation.5 | async-start | bytes 4194304 | tf_op jit(solution)/shard_map/all_to_all | solution.py:82
  206.5 3.4 fusion.28
  214.5 3.7 convert_bitcast_fusion.1
  219.6 12.3 %all-to-all-done.5 = bf16[4,8,32,1024]{3,2,1,0:T(8,128)(2,1)} async-done(((bf16[4,8,32,1024]{3,2,1,0:T(8,128)(2,1)}), bf16[4,8,32,1024]{3,2,1,0:T(8,128)(2,1)}, u32[]{:S(2)}, u32[]{:S(2)}) %all-to-all-start.5) | async-done | bytes 2097184 | tf_op jit(solution)/shard_map/all_to_all | solution.py:82
  232.0 4.5 %all-to-all-start.3 = ((bf16[4,8,32,1024]{3,2,1,0:T(8,128)(2,1)}), bf16[4,8,32,1024]{3,2,1,0:T(8,128)(2,1)}, u32[]{:S(2)}, u32[]{:S(2)}) async-start(bf16[4,8,32,1024]{3,2,1,0:T(8,128)(2,1)} %copy.50), calls=%async_computation.3 | async-start | bytes 4194304 | tf_op jit(solution)/shard_map/all_to_all | solution.py:82
  236.5 2.9 reduce_sum.67
  239.4 22.8 %all-to-all-done.3 = bf16[4,8,32,1024]{3,2,1,0:T(8,128)(2,1)} async-done(((bf16[4,8,32,1024]{3,2,1,0:T(8,128)(2,1)}), bf16[4,8,32,1024]{3,2,1,0:T(8,128)(2,1)}, u32[]{:S(2)}, u32[]{:S(2)}) %all-to-all-start.3) | async-done | bytes 2097184 | tf_op jit(solution)/shard_map/all_to_all | solution.py:82
  262.2 4.4 %all-to-all-start.6 = ((bf16[8,32,1024]{2,1,0:T(8,128)(2,1)}), bf16[8,32,1024]{2,1,0:T(8,128)(2,1)S(1)}, u32[]{:S(2)}, u32[]{:S(2)}) async-start(bf16[8,32,1024]{2,1,0:T(8,128)(2,1)} %reduce_sum.67), calls=%async_computation.6 | async-start | bytes 1048576 | tf_op jit(solution)/shard_map/all_to_all | solution.py:84
  266.6 37.4 %scatter_fusion.1 = s32[32,49]{1,0:T(8,128)S(1)} fusion(s32[32,49]{1,0:T(8,128)S(1)} %broadcast_in_dim.7, s32[768]{0:T(1024)S(1)} %get-tuple-element.4, s32[768]{0:T(1024)S(1)} %iota.31), kind=kCustom, calls=%fused_computation.4 | custom fusion | bytes 15360 | tf_op jit(solution)/shard_map/scatter | solution.py:110
  304.1 2.9 reduce_sum.65
  307.1 6.0 %all-to-all-start.4 = ((bf16[8,32,1024]{2,1,0:T(8,128)(2,1)}), bf16[8,32,1024]{2,1,0:T(8,128)(2,1)S(1)}, u32[]{:S(2)}, u32[]{:S(2)}) async-start(bf16[8,32,1024]{2,1,0:T(8,128)(2,1)} %reduce_sum.65), calls=%async_computation.4 | async-start | bytes 1048576 | tf_op jit(solution)/shard_map/all_to_all | solution.py:84
  313.1 3.4 fusion.29
  317.3 6.4 %gather_fusion.2 = bf16[1568,1024]{1,0:T(8,128)(2,1)} fusion(bf16[769,1024]{1,0:T(8,128)(2,1)S(1)} %concatenate.9, s32[2048]{0:T(1024)S(1)} %pad_clamp_fusion), kind=kCustom, calls=%fused_computation.2 | custom fusion | bytes 6428800 | tf_op jit(solution)/shard_map/gather | solution.py:114
  323.7 4.7 %reshape.240 = bf16[32,49,1024]{2,1,0:T(8,128)(2,1)} reshape(bf16[1568,1024]{1,0:T(8,128)(2,1)} %gather_fusion.2) | data formatting | bytes 6422528 | tf_op jit(solution)/shard_map/gather | solution.py:114
  328.4 5.5 %all-to-all-start.2 = ((bf16[32,49,1024]{2,1,0:T(8,128)(2,1)}), bf16[32,49,1024]{2,1,0:T(8,128)(2,1)}, u32[]{:S(2)}, u32[]{:S(2)}) async-start(bf16[32,49,1024]{2,1,0:T(8,128)(2,1)} %reshape.240), calls=%async_computation.2 | async-start | bytes 7340032 | tf_op jit(solution)/shard_map/all_to_all | solution.py:23
  335.4 81.2 %all-to-all-done.2 = bf16[32,49,1024]{2,1,0:T(8,128)(2,1)} async-done(((bf16[32,49,1024]{2,1,0:T(8,128)(2,1)}), bf16[32,49,1024]{2,1,0:T(8,128)(2,1)}, u32[]{:S(2)}, u32[]{:S(2)}) %all-to-all-start.2) | async-done | bytes 3211296 | tf_op jit(solution)/shard_map/all_to_all | solution.py:23
  416.6 8.7 %fusion.7 = f32[1024,1024]{1,0:T(8,128)} fusion(bf16[32,49,1024]{2,1,0:T(8,128)(2,1)} %all-to-all-done.2, s32[32,49]{1,0:T(8,128)S(1)} %get-tuple-element.9, pred[32,49]{1,0:T(8,128)(4,1)S(1)} %get-tuple-element.6), kind=kOutput, calls=%fused_computation.20 | convolution fusion | flops 3291545600 | bytes 7413408 | tf_op jit(solution)/shard_map/dot_general | solution.py:118
  (51 shorter events, 16.2 us)
Async XLA Ops:
  7.2 56.4 %copy-start = (bf16[1024,1024]{1,0:T(8,128)(2,1)S(1)}, bf16[1024,1024]{1,0:T(8,128)(2,1)}, u32[]{:S(2)}) copy-start(bf16[1024,1024]{1,0:T(8,128)(2,1)} %param.6) | copy-start | bytes 6291460
  78.9 5.2 %copy-start.3 = (s32[3,256,256]{2,1,0:T(8,128)S(1)}, s32[3,256,256]{2,1,0:T(8,128)}, u32[]{:S(2)}) copy-start(s32[3,256,256]{2,1,0:T(8,128)} %param.8) | copy-start | bytes 2359300
  78.9 86.8 %all-to-all-start.1 = ((bf16[32,49,1024]{2,1,0:T(8,128)(2,1)}), bf16[32,49,1024]{2,1,0:T(8,128)(2,1)}, u32[]{:S(2)}, u32[]{:S(2)}) async-start(bf16[32,49,1024]{2,1,0:T(8,128)(2,1)} %broadcast_multiply_fusion), calls=%async_computation.1 | async-start | bytes 7340032 | tf_op jit(solution)/shard_map/all_to_all | solution.py:23
  82.6 99.8 %all-gather.3.cloned.1.call-start = ((), (), s32[]{:S(2)}) async-start(), calls=%async_computation.7 | async-start | bytes 2621440 | tf_op jit(solution)/shard_map/all_gather | solution.py:60
  83.3 106.5 %all-gather.5.cloned.1.call-start = ((), (), s32[]{:S(2)}) async-start(), calls=%async_computation.8 | async-start | bytes 2621440 | tf_op jit(solution)/shard_map/all_gather | solution.py:60
  201.8 30.2 %all-to-all-start.5 = ((bf16[4,8,32,1024]{3,2,1,0:T(8,128)(2,1)}), bf16[4,8,32,1024]{3,2,1,0:T(8,128)(2,1)}, u32[]{:S(2)}, u32[]{:S(2)}) async-start(bf16[4,8,32,1024]{3,2,1,0:T(8,128)(2,1)} %copy.52), calls=%async_computation.5 | async-start | bytes 4194304 | tf_op jit(solution)/shard_map/all_to_all | solution.py:82
  209.9 1.9 copy-start.2
  232.0 30.2 %all-to-all-start.3 = ((bf16[4,8,32,1024]{3,2,1,0:T(8,128)(2,1)}), bf16[4,8,32,1024]{3,2,1,0:T(8,128)(2,1)}, u32[]{:S(2)}, u32[]{:S(2)}) async-start(bf16[4,8,32,1024]{3,2,1,0:T(8,128)(2,1)} %copy.50), calls=%async_computation.3 | async-start | bytes 4194304 | tf_op jit(solution)/shard_map/all_to_all | solution.py:82
  262.2 44.9 %all-to-all-start.6 = ((bf16[8,32,1024]{2,1,0:T(8,128)(2,1)}), bf16[8,32,1024]{2,1,0:T(8,128)(2,1)S(1)}, u32[]{:S(2)}, u32[]{:S(2)}) async-start(bf16[8,32,1024]{2,1,0:T(8,128)(2,1)} %reduce_sum.67), calls=%async_computation.6 | async-start | bytes 1048576 | tf_op jit(solution)/shard_map/all_to_all | solution.py:84
  307.1 21.4 %all-to-all-start.4 = ((bf16[8,32,1024]{2,1,0:T(8,128)(2,1)}), bf16[8,32,1024]{2,1,0:T(8,128)(2,1)S(1)}, u32[]{:S(2)}, u32[]{:S(2)}) async-start(bf16[8,32,1024]{2,1,0:T(8,128)(2,1)} %reduce_sum.65), calls=%async_computation.4 | async-start | bytes 1048576 | tf_op jit(solution)/shard_map/all_to_all | solution.py:84
  328.4 88.2 %all-to-all-start.2 = ((bf16[32,49,1024]{2,1,0:T(8,128)(2,1)}), bf16[32,49,1024]{2,1,0:T(8,128)(2,1)}, u32[]{:S(2)}, u32[]{:S(2)}) async-start(bf16[32,49,1024]{2,1,0:T(8,128)(2,1)} %reshape.240), calls=%async_computation.2 | async-start | bytes 7340032 | tf_op jit(solution)/shard_map/all_to_all | solution.py:23
  416.6 8.7 %copy-start.1 = (bf16[1024,1024]{1,0:T(8,128)(2,1)S(1)}, bf16[1024,1024]{1,0:T(8,128)(2,1)}, u32[]{:S(2)}) copy-start(bf16[1024,1024]{1,0:T(8,128)(2,1)} %param.6) | copy-start | bytes 6291460
Sparse Core Ops, SparseCore 0:
  84.9 45.6 all-gather.2
  132.2 26.6 all-gather.4

commit v3 on v2

--- a/solution.py
+++ b/solution.py
@@ -40,13 +40,27 @@
     one_hot = (owner[:, None] == jnp.arange(shards, dtype=jnp.int32)[None, :]).astype(jnp.int32)
     before = jnp.cumsum(one_hot, axis=0) - one_hot
     rank = jnp.sum(before * one_hot, axis=1)
-    requests = jnp.full((shards, capacity), -1, jnp.int32).at[owner, rank].set(within)
-    asked = exchange(requests)
+    position = owner * capacity + rank
+    requests = jnp.full((shards * capacity,), -1, jnp.int32).at[position].set(within)
+    asked = exchange(requests.reshape(shards, capacity))
     valid = asked >= 0
     safe_rows = jnp.maximum(asked, 0)
-    found = feature_table[safe_rows] * valid[..., None].astype(jnp.bfloat16)
+    picks = (
+        (safe_rows[..., None] == jnp.arange(rows_here, dtype=jnp.int32)) & valid[..., None]
+    ).astype(jnp.bfloat16)
+    found = jnp.dot(picks, feature_table, preferred_element_type=jnp.float32).astype(jnp.bfloat16)
     answered = exchange(found)
-    inputs = answered[owner, rank].reshape(groups, width, depth)
+    slot_of = (
+        (owner[:, None, None] == jnp.arange(shards, dtype=jnp.int32)[:, None])
+        & (rank[:, None, None] == jnp.arange(capacity, dtype=jnp.int32))
+    ).astype(jnp.bfloat16)
+    inputs = (
+        lax.dot_general(
+            slot_of, answered, (((1, 2), (0, 1)), ((), ())), preferred_element_type=jnp.float32
+        )
+        .astype(jnp.bfloat16)
+        .reshape(groups, width, depth)
+    )
     degree = jnp.sum(incidence_mask, axis=2).astype(jnp.float32)
     normalizer_factor = lax.rsqrt(1.0 + degree)[..., None]
     link = (incidence_mask + jnp.eye(width, dtype=jnp.int32)[None]).astype(jnp.bfloat16)
@@ -107,14 +121,10 @@
         jnp.bfloat16
     )
     input_grad = spread_back(link, fetched_first).astype(jnp.bfloat16).reshape(count, depth)
-    source = jnp.full((shards, capacity), count, jnp.int32).at[owner, rank].set(
-        jnp.arange(count, dtype=jnp.int32)
-    )
-    padded = jnp.concatenate([input_grad, jnp.zeros((1, depth), jnp.bfloat16)], axis=0)
-    returned = exchange(padded[source])
-    picks = (
-        (safe_rows[..., None] == jnp.arange(rows_here, dtype=jnp.int32)) & valid[..., None]
+    outgoing = lax.dot_general(
+        slot_of, input_grad, (((0,), (0,)), ((), ())), preferred_element_type=jnp.float32
     ).astype(jnp.bfloat16)
+    returned = exchange(outgoing)
     table_grad = lax.dot_general(
         picks, returned, (((0, 1), (0, 1)), ((), ())), preferred_element_type=jnp.float32
     )

time: 433 us -> 345 us (0.80)
  local copies, waits for them, and re-layouts: 122 us -> 14.5 us
  waiting for transfers between devices: 199 us -> 212 us
  matrix products: 38.6 us -> 51.5 us
  starting transfers between devices: 28.9 us -> 24.5 us
    scatter x2 -> x1, local copies, waits for them, and re-layouts: 74.9 us -> 3.38 us  [on_device(): jnp.full((shards * capacity,), -1, jnp.int32).at[position].set(within)]
    gather x5 -> x0, local copies, waits for them, and re-layouts: 31.6 us -> none  [the longest x2 11.1 us: on_device(): found = feature_table[safe_rows] * valid[..., None].astype(jnp.bfloat16)]
    all_to_all x2, waiting for transfers between devices: 0.01 us -> 16.3 us  [weight_grad(): outer = lax.all_to_all(inner, 'node', 0, 0, tiled=True)]
    dot_general x0 -> x3, matrix products: none -> 15.1 us  [the longest x1 5.48 us: on_device(): jnp.dot(picks, feature_table, preferred_element_type=jnp.float32)]
    all_to_all x1, local copies, waits for them, and re-layouts: 5.52 us -> 0.11 us  [exchange(): return lax.all_to_all(values, AXES, 0, 0, tiled=True)]
  transfers between devices with their start and end apart: 8 -> 8, of which waited for: 4 -> 6; matrix products, arithmetic and copies ran while one was open for 22% -> 13% of each run, Pallas kernels for 0% -> 0%
where the time goes in v3:
time: 345 us; the launch traced here: 344 us
  waiting for transfers between devices  212 us (61%)
  matrix products  51.5 us (15%)
  starting transfers between devices  24.5 us (7%)
  local copies, waits for them, and re-layouts  14.5 us (4%)
  between operations  14.4 us (4%)
  blocking collectives  14.3 us (4%)
  other arithmetic  12.3 us (4%)
    all_to_all x2, waiting for transfers between devices, exchange(): return lax.all_to_all(values, AXES, 0, 0, tiled=True)  161 us
    all_to_all x2, waiting for transfers between devices, weight_grad(): inner = lax.all_to_all(parts, 'fsdp', 0, 0, tiled=True)  34.1 us
    all_to_all x2, waiting for transfers between devices, weight_grad(): outer = lax.all_to_all(inner, 'node', 0, 0, tiled=True)  16.3 us
    all_to_all x1, blocking collectives, exchange(): return lax.all_to_all(values, AXES, 0, 0, tiled=True)  14.3 us
    dot_general x2, matrix products, forward_layer(): jnp.dot(mixed, lax.all_gather(weight, 'fsdp', axis=1, tiled=True), prefer...  10.5 us
    dot_general x1, matrix products, on_device(): lax.dot_general(picks, returned, (((0, 1), (0, 1)), ((), ())), preferred_...  8.74 us
    all_to_all x2, starting transfers between devices, weight_grad(): outer = lax.all_to_all(inner, 'node', 0, 0, tiled=True)  8.48 us
    all_to_all x2, starting transfers between devices, weight_grad(): inner = lax.all_to_all(parts, 'fsdp', 0, 0, tiled=True)  8.26 us
  transfers between devices with their start and end apart: 8, of which 6 were waited for; matrix products, arithmetic and copies ran while one was open for 13% of the time, Pallas kernels for 0%

profile of v3, /device:TPU:0, one launch (start us, length us, event | category | flops | bytes accessed | tf_op | source)
XLA Modules:
  0.0 343.7 jit_solution(10682770953859275037)
XLA Ops:
  9.5 1.7 reduce-window.6
  11.6 3.4 scatter_custom_fusion
  15.2 14.3 %all_to_all.39 = s32[32,1,49]{2,1,0:T(1,128)S(1)} all-to-all(s32[32,1,49]{2,1,0:T(1,128)S(1)} %all_to_all.24), channel_id=1, replica_groups=mesh['node'=8,'fsdp'=4] {'node','fsdp'}, dimensions={0} | all-to-all | bytes 12544 | tf_op jit(solution)/shard_map/all_to_all | solution.py:23
  29.5 5.5 %fusion.22 = bf16[32,49,1024]{2,1,0:T(8,128)(2,1)} fusion(s32[32,49]{1,0:T(8,128)S(1)} %maximum_bitcast_fusion, pred[32,49]{1,0:T(8,128)(4,1)S(1)} %compare_bitcast_fusion, bf16[1024,1024]{1,0:T(8,128)(2,1)S(1)} %copy-done), kind=kOutput, calls=%fused_computation.29 | convolution fusion | flops 3293151232 | bytes 5316256 | tf_op jit(solution)/shard_map/dot_general | solution.py:51
  35.0 3.7 %all-to-all-start.1 = ((bf16[32,49,1024]{2,1,0:T(8,128)(2,1)}), bf16[32,49,1024]{2,1,0:T(8,128)(2,1)}, u32[]{:S(2)}, u32[]{:S(2)}) async-start(bf16[32,49,1024]{2,1,0:T(8,128)(2,1)} %fusion.22), calls=%async_computation.1 | async-start | bytes 7340032 | tf_op jit(solution)/shard_map/all_to_all | solution.py:23
  40.5 81.3 %all-to-all-done.1 = bf16[32,49,1024]{2,1,0:T(8,128)(2,1)} async-done(((bf16[32,49,1024]{2,1,0:T(8,128)(2,1)}), bf16[32,49,1024]{2,1,0:T(8,128)(2,1)}, u32[]{:S(2)}, u32[]{:S(2)}) %all-to-all-start.1) | async-done | bytes 3211296 | tf_op jit(solution)/shard_map/all_to_all | solution.py:23
  121.8 5.2 %bitcast_convert_fusion = bf16[768,1024]{1,0:T(8,128)(2,1)S(1)} fusion(bf16[32,49,1024]{2,1,0:T(8,128)(2,1)} %all-to-all-done.1, pred[768,49]{0,1:T(8,128)(4,1)S(1)} %iota_compare_fusion.2, pred[768,32]{0,1:T(8,128)(4,1)S(1)} %iota_compare_fusion.4), kind=kOutput, calls=%fused_computation.17 | convolution fusion | flops 2468241408 | bytes 4846336 | tf_op jit(solution)/shard_map/dot_general | solution.py:58
  127.6 5.9 %multiply_convert_fusion.3 = (bf16[768,1024]{1,0:T(8,128)(2,1)S(1)}, f32[768,1024]{1,0:T(8,128)}) fusion(bf16[768,1024]{1,0:T(8,128)(2,1)S(1)} %bitcast.95, bf16[1024,1024]{1,0:T(8,128)(2,1)} %all-gather.3.cloned.1.call-done), kind=kOutput, calls=%fused_computation.21 | convolution fusion | flops 1614544896 | bytes 8388608 | tf_op jit(solution)/shard_map/dot_general | solution.py:72
  134.1 4.6 %fusion.13 = bf16[768,1024]{1,0:T(8,128)(2,1)S(1)} fusion(bf16[3,256,1024]{2,1,0:T(8,128)(2,1)} %param.11, bf16[768,1024]{1,0:T(8,128)(2,1)S(1)} %bitcast.97, bf16[1024,1024]{1,0:T(8,128)(2,1)} %all-gather.5.cloned.1.call-done), kind=kOutput, calls=%fused_computation.14 | convolution fusion | flops 1618477056 | bytes 6815744 | tf_op jit(solution)/shard_map/dot_general | solution.py:72
  138.7 1.7 copy.41
  140.4 3.2 convert_bitcast_fusion
  143.6 1.5 copy.42
  145.1 3.8 %all-to-all-start.5 = ((bf16[4,8,32,1024]{3,2,1,0:T(8,128)(2,1)}), bf16[4,8,32,1024]{3,2,1,0:T(8,128)(2,1)S(1)}, u32[]{:S(2)}, u32[]{:S(2)}) async-start(bf16[4,8,32,1024]{3,2,1,0:T(8,128)(2,1)} %copy.42), calls=%async_computation.5 | async-start | bytes 4194304 | tf_op jit(solution)/shard_map/all_to_all | solution.py:96
  149.0 3.9 %fusion.47 = f32[768,1024]{1,0:T(8,128)S(1)} fusion(bf16[768,1024]{1,0:T(8,128)(2,1)} %copy-done.4, bf16[1024,1024]{1,0:T(8,128)(2,1)} %all-gather.5.cloned.1.call-done), kind=kOutput, calls=%fused_computation.82 | convolution fusion | flops 1610612736 | bytes 6815744 | tf_op jit(solution)/shard_map/dot_general | solution.py:80
  154.7 2.2 fusion.14
  157.0 2.6 copy.39
  159.6 3.7 %convert_bitcast_fusion.1 = bf16[4,8,32,1024]{3,2,0,1:T(8,128)(2,1)S(1)} fusion(bf16[768,8,4,32]{0,3,2,1:T(8,128)(2,1)} %bitcast.102, bf16[768,1024,1,1]{1,0,3,2:T(8,128)(2,1)} %bitcast.96), kind=kOutput, calls=%fused_computation.33 | convolution fusion | flops 1611661312 | bytes 5242880 | tf_op jit(solution)/shard_map/dot_general | solution.py:89
  163.2 1.5 copy.40
  164.7 9.6 %all-to-all-done.5 = bf16[4,8,32,1024]{3,2,1,0:T(8,128)(2,1)S(1)} async-done(((bf16[4,8,32,1024]{3,2,1,0:T(8,128)(2,1)}), bf16[4,8,32,1024]{3,2,1,0:T(8,128)(2,1)S(1)}, u32[]{:S(2)}, u32[]{:S(2)}) %all-to-all-start.5) | async-done | bytes 2097184 | tf_op jit(solution)/shard_map/all_to_all | solution.py:96
  174.4 4.4 %all-to-all-start.3 = ((bf16[4,8,32,1024]{3,2,1,0:T(8,128)(2,1)}), bf16[4,8,32,1024]{3,2,1,0:T(8,128)(2,1)}, u32[]{:S(2)}, u32[]{:S(2)}) async-start(bf16[4,8,32,1024]{3,2,1,0:T(8,128)(2,1)} %copy.40), calls=%async_computation.3 | async-start | bytes 4194304 | tf_op jit(solution)/shard_map/all_to_all | solution.py:96
  178.8 1.3 reduce_sum.67
  180.1 24.4 %all-to-all-done.3 = bf16[4,8,32,1024]{3,2,1,0:T(8,128)(2,1)} async-done(((bf16[4,8,32,1024]{3,2,1,0:T(8,128)(2,1)}), bf16[4,8,32,1024]{3,2,1,0:T(8,128)(2,1)}, u32[]{:S(2)}, u32[]{:S(2)}) %all-to-all-start.3) | async-done | bytes 2097184 | tf_op jit(solution)/shard_map/all_to_all | solution.py:96
  204.5 4.3 %all-to-all-start.6 = ((bf16[8,32,1024]{2,1,0:T(8,128)(2,1)}), bf16[8,32,1024]{2,1,0:T(8,128)(2,1)}, u32[]{:S(2)}, u32[]{:S(2)}) async-start(bf16[8,32,1024]{2,1,0:T(8,128)(2,1)} %reduce_sum.67), calls=%async_computation.6 | async-start | bytes 1048576 | tf_op jit(solution)/shard_map/all_to_all | solution.py:98
  208.9 3.9 %fusion.48 = f32[768,1024]{1,0:T(8,128)S(1)} fusion(bf16[768,1024]{1,0:T(8,128)(2,1)} %fusion.14, bf16[1024,1024]{1,0:T(8,128)(2,1)} %all-gather.3.cloned.1.call-done), kind=kOutput, calls=%fused_computation.83 | convolution fusion | flops 1610612736 | bytes 6815744 | tf_op jit(solution)/shard_map/dot_general | solution.py:80
  212.8 2.9 reduce_sum.65
  215.7 7.5 %all-to-all-done.6 = bf16[8,32,1024]{2,1,0:T(8,128)(2,1)} async-done(((bf16[8,32,1024]{2,1,0:T(8,128)(2,1)}), bf16[8,32,1024]{2,1,0:T(8,128)(2,1)}, u32[]{:S(2)}, u32[]{:S(2)}) %all-to-all-start.6) | async-done | bytes 524320 | tf_op jit(solution)/shard_map/all_to_all | solution.py:98
  223.2 4.1 %all-to-all-start.4 = ((bf16[8,32,1024]{2,1,0:T(8,128)(2,1)}), bf16[8,32,1024]{2,1,0:T(8,128)(2,1)}, u32[]{:S(2)}, u32[]{:S(2)}) async-start(bf16[8,32,1024]{2,1,0:T(8,128)(2,1)} %reduce_sum.65), calls=%async_computation.4 | async-start | bytes 1048576 | tf_op jit(solution)/shard_map/all_to_all | solution.py:98
  228.2 4.4 %fusion.19 = bf16[32,49,1024]{2,1,0:T(8,128)(2,1)} fusion(bf16[768,1024,1]{1,0,2:T(8,128)(2,1)S(1)} %bitcast.103, pred[768,49]{0,1:T(8,128)(4,1)S(1)} %copy-done.7, pred[768,32]{0,1:T(8,128)(4,1)S(1)} %copy-done.9), kind=kOutput, calls=%fused_computation.28 | convolution fusion | flops 2469060608 | bytes 4846336 | tf_op jit(solution)/shard_map/dot_general | solution.py:124
  232.6 8.8 %all-to-all-done.4 = bf16[8,32,1024]{2,1,0:T(8,128)(2,1)} async-done(((bf16[8,32,1024]{2,1,0:T(8,128)(2,1)}), bf16[8,32,1024]{2,1,0:T(8,128)(2,1)}, u32[]{:S(2)}, u32[]{:S(2)}) %all-to-all-start.4) | async-done | bytes 524320 | tf_op jit(solution)/shard_map/all_to_all | solution.py:98
  241.4 3.8 %all-to-all-start.2 = ((bf16[32,49,1024]{2,1,0:T(8,128)(2,1)}), bf16[32,49,1024]{2,1,0:T(8,128)(2,1)}, u32[]{:S(2)}, u32[]{:S(2)}) async-start(bf16[32,49,1024]{2,1,0:T(8,128)(2,1)} %fusion.19), calls=%async_computation.2 | async-start | bytes 7340032 | tf_op jit(solution)/shard_map/all_to_all | solution.py:23
  248.8 79.2 %all-to-all-done.2 = bf16[32,49,1024]{2,1,0:T(8,128)(2,1)} async-done(((bf16[32,49,1024]{2,1,0:T(8,128)(2,1)}), bf16[32,49,1024]{2,1,0:T(8,128)(2,1)}, u32[]{:S(2)}, u32[]{:S(2)}) %all-to-all-start.2) | async-done | bytes 3211296 | tf_op jit(solution)/shard_map/all_to_all | solution.py:23
  328.1 8.7 %fusion.25 = f32[1024,1024]{1,0:T(8,128)} fusion(bf16[32,49,1024]{2,1,0:T(8,128)(2,1)} %all-to-all-done.2, s32[32,49]{1,0:T(8,128)S(1)} %copy-done.11, pred[32,49]{1,0:T(8,128)(4,1)S(1)} %compare_bitcast_fusion), kind=kOutput, calls=%fused_computation.30 | convolution fusion | flops 3291545600 | bytes 7413408 | tf_op jit(solution)/shard_map/dot_general | solution.py:128
  (56 shorter events, 12.0 us)
Async XLA Ops:
  7.2 22.3 %copy-start = (bf16[1024,1024]{1,0:T(8,128)(2,1)S(1)}, bf16[1024,1024]{1,0:T(8,128)(2,1)}, u32[]{:S(2)}) copy-start(bf16[1024,1024]{1,0:T(8,128)(2,1)} %param.6) | copy-start | bytes 6291460
  29.5 5.5 %copy-start.10 = (s32[32,49]{1,0:T(8,128)}, s32[32,49]{1,0:T(8,128)S(1)}, u32[]{:S(2)}) copy-start(s32[32,49]{1,0:T(8,128)S(1)} %maximum_bitcast_fusion) | copy-start | bytes 18820
  35.0 5.2 %copy-start.5 = (s32[3,256,256]{2,1,0:T(8,128)S(1)}, s32[3,256,256]{2,1,0:T(8,128)}, u32[]{:S(2)}) copy-start(s32[3,256,256]{2,1,0:T(8,128)} %param.8) | copy-start | bytes 2359300
  35.0 86.8 %all-to-all-start.1 = ((bf16[32,49,1024]{2,1,0:T(8,128)(2,1)}), bf16[32,49,1024]{2,1,0:T(8,128)(2,1)}, u32[]{:S(2)}, u32[]{:S(2)}) async-start(bf16[32,49,1024]{2,1,0:T(8,128)(2,1)} %fusion.22), calls=%async_computation.1 | async-start | bytes 7340032 | tf_op jit(solution)/shard_map/all_to_all | solution.py:23
  38.7 89.0 %all-gather.3.cloned.1.call-start = ((), (), s32[]{:S(2)}) async-start(), calls=%async_computation.7 | async-start | bytes 2621440 | tf_op jit(solution)/shard_map/all_gather | solution.py:74
  39.4 94.7 %all-gather.5.cloned.1.call-start = ((), (), s32[]{:S(2)}) async-start(), calls=%async_computation.8 | async-start | bytes 2621440 | tf_op jit(solution)/shard_map/all_gather | solution.py:74
  40.2 86.8 %copy-start.8 = (pred[768,32]{0,1:T(8,128)(4,1)}, pred[768,32]{0,1:T(8,128)(4,1)S(1)}, u32[]{:S(2)}) copy-start(pred[768,32]{0,1:T(8,128)(4,1)S(1)} %iota_compare_fusion.4) | copy-start | bytes 73732
  40.5 86.5 %copy-start.6 = (pred[768,49]{0,1:T(8,128)(4,1)}, pred[768,49]{0,1:T(8,128)(4,1)S(1)}, u32[]{:S(2)}) copy-start(pred[768,49]{0,1:T(8,128)(4,1)S(1)} %iota_compare_fusion.2) | copy-start | bytes 112900
  127.6 5.9 %copy-start.3 = (bf16[3,256,1024]{2,1,0:T(8,128)(2,1)}, bf16[3,256,1024]{2,1,0:T(8,128)(2,1)S(1)}, u32[]{:S(2)}) copy-start(bf16[3,256,1024]{2,1,0:T(8,128)(2,1)S(1)} %multiply_convert_fusion.4) | copy-start | bytes 4718596
  138.7 4.9 %copy-start.4 = (bf16[768,1024]{1,0:T(8,128)(2,1)}, bf16[768,1024]{1,0:T(8,128)(2,1)S(1)}, u32[]{:S(2)}) copy-start(bf16[768,1024]{1,0:T(8,128)(2,1)S(1)} %fusion.13) | copy-start | bytes 4718596
  145.1 29.2 %all-to-all-start.5 = ((bf16[4,8,32,1024]{3,2,1,0:T(8,128)(2,1)}), bf16[4,8,32,1024]{3,2,1,0:T(8,128)(2,1)S(1)}, u32[]{:S(2)}, u32[]{:S(2)}) async-start(bf16[4,8,32,1024]{3,2,1,0:T(8,128)(2,1)} %copy.42), calls=%async_computation.5 | async-start | bytes 4194304 | tf_op jit(solution)/shard_map/all_to_all | solution.py:96
  152.9 1.9 copy-start.2
  174.4 30.2 %all-to-all-start.3 = ((bf16[4,8,32,1024]{3,2,1,0:T(8,128)(2,1)}), bf16[4,8,32,1024]{3,2,1,0:T(8,128)(2,1)}, u32[]{:S(2)}, u32[]{:S(2)}) async-start(bf16[4,8,32,1024]{3,2,1,0:T(8,128)(2,1)} %copy.40), calls=%async_computation.3 | async-start | bytes 4194304 | tf_op jit(solution)/shard_map/all_to_all | solution.py:96
  204.5 18.7 %all-to-all-start.6 = ((bf16[8,32,1024]{2,1,0:T(8,128)(2,1)}), bf16[8,32,1024]{2,1,0:T(8,128)(2,1)}, u32[]{:S(2)}, u32[]{:S(2)}) async-start(bf16[8,32,1024]{2,1,0:T(8,128)(2,1)} %reduce_sum.67), calls=%async_computation.6 | async-start | bytes 1048576 | tf_op jit(solution)/shard_map/all_to_all | solution.py:98
  223.2 18.2 %all-to-all-start.4 = ((bf16[8,32,1024]{2,1,0:T(8,128)(2,1)}), bf16[8,32,1024]{2,1,0:T(8,128)(2,1)}, u32[]{:S(2)}, u32[]{:S(2)}) async-start(bf16[8,32,1024]{2,1,0:T(8,128)(2,1)} %reduce_sum.65), calls=%async_computation.4 | async-start | bytes 1048576 | tf_op jit(solution)/shard_map/all_to_all | solution.py:98
  227.4 0.8 copy-start.7
  227.4 0.8 copy-start.9
  232.6 95.5 %copy-start.11 = (s32[32,49]{1,0:T(8,128)S(1)}, s32[32,49]{1,0:T(8,128)}, u32[]{:S(2)}) copy-start(s32[32,49]{1,0:T(8,128)} %copy-done.10) | copy-start | bytes 18820
  241.4 86.6 %all-to-all-start.2 = ((bf16[32,49,1024]{2,1,0:T(8,128)(2,1)}), bf16[32,49,1024]{2,1,0:T(8,128)(2,1)}, u32[]{:S(2)}, u32[]{:S(2)}) async-start(bf16[32,49,1024]{2,1,0:T(8,128)(2,1)} %fusion.19), calls=%async_computation.2 | async-start | bytes 7340032 | tf_op jit(solution)/shard_map/all_to_all | solution.py:23
  328.1 8.7 %copy-start.1 = (bf16[1024,1024]{1,0:T(8,128)(2,1)S(1)}, bf16[1024,1024]{1,0:T(8,128)(2,1)}, u32[]{:S(2)}) copy-start(bf16[1024,1024]{1,0:T(8,128)(2,1)} %param.6) | copy-start | bytes 6291460
Sparse Core Ops, SparseCore 0:
  41.0 45.6 all-gather.2
  88.3 26.6 all-gather.4

commit v4 on v3

--- a/solution.py
+++ b/solution.py
@@ -94,10 +94,9 @@
         )
         parts = parts.transpose(1, 0, 2, 3).astype(jnp.bfloat16)
         inner = lax.all_to_all(parts, "fsdp", 0, 0, tiled=True)
-        inner = jnp.sum(inner.astype(jnp.float32), axis=0).astype(jnp.bfloat16)
-        outer = lax.all_to_all(inner, "node", 0, 0, tiled=True)
-        summed = jnp.sum(outer.astype(jnp.float32), axis=0)
-        return (summed / (groups * shards)).T
+        inner = jnp.sum(inner.astype(jnp.float32), axis=0)
+        summed = lax.psum_scatter(inner, "node", scatter_dimension=0, tiled=True)
+        return (summed.reshape(cw, depth) / (groups * shards)).T
 
     mixed_one, first_matmul_result, whole_one = forward_layer(inputs, weight_one)
     latent_state = (

time: 345 us -> 377 us (1.093)
  waiting for transfers between devices: 212 us -> 253 us
  starting transfers between devices: 24.5 us -> 16.1 us
    reduce_scatter x0 -> x2, waiting for transfers between devices: none -> 145 us  [weight_grad(): summed = lax.psum_scatter(inner, 'node', scatter_dimension=0, tiled=True)]
    all_to_all x2, waiting for transfers between devices: 161 us -> 81.3 us  [exchange(): return lax.all_to_all(values, AXES, 0, 0, tiled=True)]
    all_to_all x2 -> x0, waiting for transfers between devices: 16.3 us -> none  [weight_grad(): outer = lax.all_to_all(inner, 'node', 0, 0, tiled=True)]
    all_to_all x2 -> x0, starting transfers between devices: 8.48 us -> none  [weight_grad(): outer = lax.all_to_all(inner, 'node', 0, 0, tiled=True)]
    all_to_all x2, waiting for transfers between devices: 34.1 us -> 26.1 us  [weight_grad(): inner = lax.all_to_all(parts, 'fsdp', 0, 0, tiled=True)]
  transfers between devices with their start and end apart: 8 -> 8, of which waited for: 6 -> 5; matrix products, arithmetic and copies ran while one was open for 13% -> 12% of each run, Pallas kernels for 0% -> 0%
where the time goes in v4:
time: 377 us; the launch traced here: 376 us
  waiting for transfers between devices  253 us (67%)
  matrix products  51.6 us (14%)
  starting transfers between devices  16.1 us (4%)
  local copies, waits for them, and re-layouts  14.7 us (4%)
  blocking collectives  14.3 us (4%)
  between operations  14.1 us (4%)
  other arithmetic  12 us (3%)
    reduce_scatter x2, waiting for transfers between devices, weight_grad(): summed = lax.psum_scatter(inner, 'node', scatter_dimension=0, tiled=True)  145 us
    all_to_all x2, waiting for transfers between devices, exchange(): return lax.all_to_all(values, AXES, 0, 0, tiled=True)  81.3 us
    all_to_all x2, waiting for transfers between devices, weight_grad(): inner = lax.all_to_all(parts, 'fsdp', 0, 0, tiled=True)  26.1 us
    all_to_all x1, blocking collectives, exchange(): return lax.all_to_all(values, AXES, 0, 0, tiled=True)  14.3 us
    dot_general x2, matrix products, forward_layer(): jnp.dot(mixed, lax.all_gather(weight, 'fsdp', axis=1, tiled=True), prefer...  10.5 us
    dot_general x1, matrix products, on_device(): lax.dot_general(picks, returned, (((0, 1), (0, 1)), ((), ())), preferred_...  8.74 us
    all_to_all x2, starting transfers between devices, weight_grad(): inner = lax.all_to_all(parts, 'fsdp', 0, 0, tiled=True)  8.26 us
    dot_general x2, matrix products, back_weight(): lax.dot_general(delta, lax.all_gather(weight, 'fsdp', axis=1, tiled=True)...  7.79 us
  transfers between devices with their start and end apart: 8, of which 5 were waited for; matrix products, arithmetic and copies ran while one was open for 12% of the time, Pallas kernels for 0%

profile of v4, /device:TPU:0, one launch (start us, length us, event | category | flops | bytes accessed | tf_op | source)
XLA Modules:
  0.0 376.1 jit_solution(8341084922480489139)
XLA Ops:
  9.5 1.7 reduce-window.6
  11.6 3.4 scatter_custom_fusion
  15.2 14.3 %all_to_all.29 = s32[32,1,49]{2,1,0:T(1,128)S(1)} all-to-all(s32[32,1,49]{2,1,0:T(1,128)S(1)} %all_to_all.18), channel_id=1, replica_groups=mesh['node'=8,'fsdp'=4] {'node','fsdp'}, dimensions={0} | all-to-all | bytes 12544 | tf_op jit(solution)/shard_map/all_to_all | solution.py:23
  29.5 5.5 %fusion.22 = bf16[32,49,1024]{2,1,0:T(8,128)(2,1)} fusion(s32[32,49]{1,0:T(8,128)S(1)} %maximum_bitcast_fusion, pred[32,49]{1,0:T(8,128)(4,1)S(1)} %compare_bitcast_fusion, bf16[1024,1024]{1,0:T(8,128)(2,1)S(1)} %copy-done), kind=kOutput, calls=%fused_computation.31 | convolution fusion | flops 3293151232 | bytes 5316256 | tf_op jit(solution)/shard_map/dot_general | solution.py:51
  35.0 3.7 all-to-all-start.1
  40.5 81.3 %all-to-all-done.1 = bf16[32,49,1024]{2,1,0:T(8,128)(2,1)} async-done(((bf16[32,49,1024]{2,1,0:T(8,128)(2,1)}), bf16[32,49,1024]{2,1,0:T(8,128)(2,1)}, u32[]{:S(2)}, u32[]{:S(2)}) %all-to-all-start.1) | async-done | bytes 3211296 | tf_op jit(solution)/shard_map/all_to_all | solution.py:23
  121.8 5.2 %bitcast_convert_fusion = bf16[768,1024]{1,0:T(8,128)(2,1)S(1)} fusion(bf16[32,49,1024]{2,1,0:T(8,128)(2,1)} %all-to-all-done.1, pred[768,49]{0,1:T(8,128)(4,1)S(1)} %iota_compare_fusion.2, pred[768,32]{0,1:T(8,128)(4,1)S(1)} %iota_compare_fusion.4), kind=kOutput, calls=%fused_computation.19 | convolution fusion | flops 2468241408 | bytes 4846336 | tf_op jit(solution)/shard_map/dot_general | solution.py:58
  127.6 5.9 %multiply_convert_fusion.3 = (bf16[768,1024]{1,0:T(8,128)(2,1)S(1)}, f32[768,1024]{1,0:T(8,128)}) fusion(bf16[768,1024]{1,0:T(8,128)(2,1)S(1)} %bitcast.99, bf16[1024,1024]{1,0:T(8,128)(2,1)} %all-gather.3.cloned.1.call-done), kind=kOutput, calls=%fused_computation.23 | convolution fusion | flops 1614544896 | bytes 8388608 | tf_op jit(solution)/shard_map/dot_general | solution.py:72
  134.1 4.6 %fusion.13 = bf16[768,1024]{1,0:T(8,128)(2,1)S(1)} fusion(bf16[3,256,1024]{2,1,0:T(8,128)(2,1)} %param.11, bf16[768,1024]{1,0:T(8,128)(2,1)S(1)} %bitcast.101, bf16[1024,1024]{1,0:T(8,128)(2,1)} %all-gather.5.cloned.1.call-done), kind=kOutput, calls=%fused_computation.16 | convolution fusion | flops 1618477056 | bytes 6815744 | tf_op jit(solution)/shard_map/dot_general | solution.py:72
  138.7 1.7 copy.32
  140.4 3.2 convert_bitcast_fusion
  143.6 1.5 copy.33
  145.1 3.8 %all-to-all-start.4 = ((bf16[4,8,32,1024]{3,2,1,0:T(8,128)(2,1)}), bf16[4,8,32,1024]{3,2,1,0:T(8,128)(2,1)S(1)}, u32[]{:S(2)}, u32[]{:S(2)}) async-start(bf16[4,8,32,1024]{3,2,1,0:T(8,128)(2,1)} %copy.33), calls=%async_computation.5 | async-start | bytes 4194304 | tf_op jit(solution)/shard_map/all_to_all | solution.py:96
  149.0 3.9 %fusion.47 = f32[768,1024]{1,0:T(8,128)S(1)} fusion(bf16[768,1024]{1,0:T(8,128)(2,1)} %copy-done.4, bf16[1024,1024]{1,0:T(8,128)(2,1)} %all-gather.5.cloned.1.call-done), kind=kOutput, calls=%fused_computation.82 | convolution fusion | flops 1610612736 | bytes 6815744 | tf_op jit(solution)/shard_map/dot_general | solution.py:80
  153.6 1.2 copy-done.2
  154.8 2.2 fusion.14
  157.0 2.6 copy.30
  159.6 3.7 convert_bitcast_fusion.1
  163.3 1.6 copy.31
  164.8 9.5 %all-to-all-done.4 = bf16[4,8,32,1024]{3,2,1,0:T(8,128)(2,1)S(1)} async-done(((bf16[4,8,32,1024]{3,2,1,0:T(8,128)(2,1)}), bf16[4,8,32,1024]{3,2,1,0:T(8,128)(2,1)S(1)}, u32[]{:S(2)}, u32[]{:S(2)}) %all-to-all-start.4) | async-done | bytes 2097184 | tf_op jit(solution)/shard_map/all_to_all | solution.py:96
  174.4 4.4 %all-to-all-start.3 = ((bf16[4,8,32,1024]{3,2,1,0:T(8,128)(2,1)}), bf16[4,8,32,1024]{3,2,1,0:T(8,128)(2,1)}, u32[]{:S(2)}, u32[]{:S(2)}) async-start(bf16[4,8,32,1024]{3,2,1,0:T(8,128)(2,1)} %copy.31), calls=%async_computation.3 | async-start | bytes 4194304 | tf_op jit(solution)/shard_map/all_to_all | solution.py:96
  178.8 3.9 %fusion.48 = f32[768,1024]{1,0:T(8,128)S(1)} fusion(bf16[768,1024]{1,0:T(8,128)(2,1)} %fusion.14, bf16[1024,1024]{1,0:T(8,128)(2,1)} %all-gather.3.cloned.1.call-done), kind=kOutput, calls=%fused_computation.83 | convolution fusion | flops 1610612736 | bytes 6815744 | tf_op jit(solution)/shard_map/dot_general | solution.py:80
  183.5 4.4 %fusion.19 = bf16[32,49,1024]{2,1,0:T(8,128)(2,1)} fusion(bf16[768,1024,1]{1,0,2:T(8,128)(2,1)S(1)} %bitcast.107, pred[768,49]{0,1:T(8,128)(4,1)S(1)} %copy-done.7, pred[768,32]{0,1:T(8,128)(4,1)S(1)} %copy-done.9), kind=kOutput, calls=%fused_computation.30 | convolution fusion | flops 2469060608 | bytes 4846336 | tf_op jit(solution)/shard_map/dot_general | solution.py:123
  188.0 16.6 %all-to-all-done.3 = bf16[4,8,32,1024]{3,2,1,0:T(8,128)(2,1)} async-done(((bf16[4,8,32,1024]{3,2,1,0:T(8,128)(2,1)}), bf16[4,8,32,1024]{3,2,1,0:T(8,128)(2,1)}, u32[]{:S(2)}, u32[]{:S(2)}) %all-to-all-start.3) | async-done | bytes 2097184 | tf_op jit(solution)/shard_map/all_to_all | solution.py:96
  204.6 3.6 all-to-all-start.2
  208.2 1.4 convert_reduce_fusion
  209.9 3.1 convert_reduce_fusion.1
  213.0 77.6 %reduce-scatter.5.cloned.1.call-done = f32[1,32,1024]{2,1,0:T(8,128)} async-done(((f32[8,32,1024]{2,1,0:T(8,128)}), f32[1,32,1024]{2,1,0:T(8,128)}) %reduce-scatter.5.cloned.1.call-update) | async-done | bytes 131088 | tf_op jit(solution)/shard_map/reduce_scatter | solution.py:98
  290.6 1.6 multiply_bitcast_fusion
  292.2 67.0 %reduce-scatter.3.cloned.1.call-done = f32[1,32,1024]{2,1,0:T(8,128)} async-done(((f32[8,32,1024]{2,1,0:T(8,128)}), f32[1,32,1024]{2,1,0:T(8,128)}) %reduce-scatter.3.cloned.1.call-update) | async-done | bytes 131088 | tf_op jit(solution)/shard_map/reduce_scatter | solution.py:98
  359.2 1.6 multiply_bitcast_fusion.1
  360.8 8.7 %fusion.25 = f32[1024,1024]{1,0:T(8,128)} fusion(bf16[32,49,1024]{2,1,0:T(8,128)(2,1)} %all-to-all-done.2, s32[32,49]{1,0:T(8,128)S(1)} %copy-done.11, pred[32,49]{1,0:T(8,128)(4,1)S(1)} %compare_bitcast_fusion), kind=kOutput, calls=%fused_computation.32 | convolution fusion | flops 3291545600 | bytes 7413408 | tf_op jit(solution)/shard_map/dot_general | solution.py:127
  (56 shorter events, 7.6 us)
Async XLA Ops:
  7.2 22.3 %copy-start = (bf16[1024,1024]{1,0:T(8,128)(2,1)S(1)}, bf16[1024,1024]{1,0:T(8,128)(2,1)}, u32[]{:S(2)}) copy-start(bf16[1024,1024]{1,0:T(8,128)(2,1)} %param.6) | copy-start | bytes 6291460
  29.5 5.5 %copy-start.10 = (s32[32,49]{1,0:T(8,128)}, s32[32,49]{1,0:T(8,128)S(1)}, u32[]{:S(2)}) copy-start(s32[32,49]{1,0:T(8,128)S(1)} %maximum_bitcast_fusion) | copy-start | bytes 18820
  35.0 5.2 %copy-start.5 = (s32[3,256,256]{2,1,0:T(8,128)S(1)}, s32[3,256,256]{2,1,0:T(8,128)}, u32[]{:S(2)}) copy-start(s32[3,256,256]{2,1,0:T(8,128)} %param.8) | copy-start | bytes 2359300
  35.0 86.8 %all-to-all-start.1 = ((bf16[32,49,1024]{2,1,0:T(8,128)(2,1)}), bf16[32,49,1024]{2,1,0:T(8,128)(2,1)}, u32[]{:S(2)}, u32[]{:S(2)}) async-start(bf16[32,49,1024]{2,1,0:T(8,128)(2,1)} %fusion.22), calls=%async_computation.1 | async-start | bytes 7340032 | tf_op jit(solution)/shard_map/all_to_all | solution.py:23
  38.7 89.0 %all-gather.3.cloned.1.call-start = ((), (), s32[]{:S(2)}) async-start(), calls=%async_computation.7 | async-start | bytes 2621440 | tf_op jit(solution)/shard_map/all_gather | solution.py:74
  39.4 94.7 %all-gather.5.cloned.1.call-start = ((), (), s32[]{:S(2)}) async-start(), calls=%async_computation.8 | async-start | bytes 2621440 | tf_op jit(solution)/shard_map/all_gather | solution.py:74
  40.2 86.8 %copy-start.8 = (pred[768,32]{0,1:T(8,128)(4,1)}, pred[768,32]{0,1:T(8,128)(4,1)S(1)}, u32[]{:S(2)}) copy-start(pred[768,32]{0,1:T(8,128)(4,1)S(1)} %iota_compare_fusion.4) | copy-start | bytes 73732
  40.5 86.5 %copy-start.6 = (pred[768,49]{0,1:T(8,128)(4,1)}, pred[768,49]{0,1:T(8,128)(4,1)S(1)}, u32[]{:S(2)}) copy-start(pred[768,49]{0,1:T(8,128)(4,1)S(1)} %iota_compare_fusion.2) | copy-start | bytes 112900
  127.6 5.9 %copy-start.3 = (bf16[3,256,1024]{2,1,0:T(8,128)(2,1)}, bf16[3,256,1024]{2,1,0:T(8,128)(2,1)S(1)}, u32[]{:S(2)}) copy-start(bf16[3,256,1024]{2,1,0:T(8,128)(2,1)S(1)} %multiply_convert_fusion.4) | copy-start | bytes 4718596
  138.7 4.9 %copy-start.4 = (bf16[768,1024]{1,0:T(8,128)(2,1)}, bf16[768,1024]{1,0:T(8,128)(2,1)S(1)}, u32[]{:S(2)}) copy-start(bf16[768,1024]{1,0:T(8,128)(2,1)S(1)} %fusion.13) | copy-start | bytes 4718596
  145.1 29.2 %all-to-all-start.4 = ((bf16[4,8,32,1024]{3,2,1,0:T(8,128)(2,1)}), bf16[4,8,32,1024]{3,2,1,0:T(8,128)(2,1)S(1)}, u32[]{:S(2)}, u32[]{:S(2)}) async-start(bf16[4,8,32,1024]{3,2,1,0:T(8,128)(2,1)} %copy.33), calls=%async_computation.5 | async-start | bytes 4194304 | tf_op jit(solution)/shard_map/all_to_all | solution.py:96
  152.9 1.9 copy-start.2
  174.4 30.2 %all-to-all-start.3 = ((bf16[4,8,32,1024]{3,2,1,0:T(8,128)(2,1)}), bf16[4,8,32,1024]{3,2,1,0:T(8,128)(2,1)}, u32[]{:S(2)}, u32[]{:S(2)}) async-start(bf16[4,8,32,1024]{3,2,1,0:T(8,128)(2,1)} %copy.31), calls=%async_computation.3 | async-start | bytes 4194304 | tf_op jit(solution)/shard_map/all_to_all | solution.py:96
  182.7 0.8 copy-start.7
  182.7 0.8 copy-start.9
  204.6 156.2 %all-to-all-start.2 = ((bf16[32,49,1024]{2,1,0:T(8,128)(2,1)}), bf16[32,49,1024]{2,1,0:T(8,128)(2,1)}, u32[]{:S(2)}, u32[]{:S(2)}) async-start(bf16[32,49,1024]{2,1,0:T(8,128)(2,1)} %fusion.19), calls=%async_computation.2 | async-start | bytes 7340032 | tf_op jit(solution)/shard_map/all_to_all | solution.py:23
  208.1 82.5 %reduce-scatter.5.cloned.1.call-start = ((), (), s32[]{:S(2)}) async-start(), calls=%async_computation.10 | async-start | bytes 1179648 | tf_op jit(solution)/shard_map/reduce_scatter | solution.py:98
  209.6 151.2 %copy-start.11 = (s32[32,49]{1,0:T(8,128)S(1)}, s32[32,49]{1,0:T(8,128)}, u32[]{:S(2)}) copy-start(s32[32,49]{1,0:T(8,128)} %copy-done.10) | copy-start | bytes 18820
  209.6 149.6 %reduce-scatter.3.cloned.1.call-start = ((), (), s32[]{:S(2)}) async-start(), calls=%async_computation.9 | async-start | bytes 1179648 | tf_op jit(solution)/shard_map/reduce_scatter | solution.py:98
  360.8 8.7 %copy-start.1 = (bf16[1024,1024]{1,0:T(8,128)(2,1)S(1)}, bf16[1024,1024]{1,0:T(8,128)(2,1)}, u32[]{:S(2)}) copy-start(bf16[1024,1024]{1,0:T(8,128)(2,1)} %param.6) | copy-start | bytes 6291460
Sparse Core Ops, SparseCore 0:
  41.0 45.6 all-gather.2
  88.3 26.6 all-gather.4
  212.3 78.2 reduce-scatter.4
  293.9 65.2 reduce-scatter.2

commit v5 on v4

--- a/solution.py
+++ b/solution.py
@@ -84,19 +84,29 @@
             preferred_element_type=jnp.float32,
         )
 
-    def weight_grad(mixed, delta):
-        cw = depth // shards
-        parts = lax.dot_general(
-            delta.reshape(count, n_node, n_fsdp, cw),
+    def grad_parts(mixed, delta):
+        return lax.dot_general(
+            delta.reshape(count, shards, depth // shards),
             mixed,
             (((0,), (0,)), ((), ())),
             preferred_element_type=jnp.float32,
         )
-        parts = parts.transpose(1, 0, 2, 3).astype(jnp.bfloat16)
-        inner = lax.all_to_all(parts, "fsdp", 0, 0, tiled=True)
-        inner = jnp.sum(inner.astype(jnp.float32), axis=0)
-        summed = lax.psum_scatter(inner, "node", scatter_dimension=0, tiled=True)
-        return (summed.reshape(cw, depth) / (groups * shards)).T
+
+    def reduce_blocks(parts):
+        me = lax.axis_index(AXES)
+        step = 1
+        while step < shards:
+            held = parts.shape[1]
+            pair = parts.reshape(parts.shape[0], held // 2, 2, *parts.shape[2:])
+            upper = (me // step) % 2 == 1
+            keep = jnp.where(upper, pair[:, :, 1], pair[:, :, 0])
+            send = jnp.where(upper, pair[:, :, 0], pair[:, :, 1])
+            if step > 1:
+                send = send.astype(jnp.bfloat16)
+            moved = lax.ppermute(send, AXES, [(i, i ^ step) for i in range(shards)])
+            parts = keep + moved.astype(jnp.float32)
+            step *= 2
+        return parts[:, 0] / (groups * shards)
 
     mixed_one, first_matmul_result, whole_one = forward_layer(inputs, weight_one)
     latent_state = (
@@ -106,7 +116,7 @@
     delta_two = (
         final_layer_sensitivity.reshape(count, depth).astype(jnp.float32) * swish_slope(product_two)
     ).astype(jnp.bfloat16)
-    grad_two = weight_grad(mixed_two, delta_two)
+    parts_two = grad_parts(mixed_two, delta_two)
     upstream_second = back_weight(delta_two, weight_two)
     fetched_second = (normalizer_factor * upstream_second.reshape(groups, width, depth)).astype(
         jnp.bfloat16
@@ -114,7 +124,7 @@
     delta_one = (
         spread_back(link, fetched_second).reshape(count, depth) * swish_slope(first_matmul_result)
     ).astype(jnp.bfloat16)
-    grad_one = weight_grad(mixed_one, delta_one)
+    parts_one = grad_parts(mixed_one, delta_one)
     upstream_first = back_weight(delta_one, weight_one)
     fetched_first = (normalizer_factor * upstream_first.reshape(groups, width, depth)).astype(
         jnp.bfloat16
@@ -127,7 +137,8 @@
     table_grad = lax.dot_general(
         picks, returned, (((0, 1), (0, 1)), ((), ())), preferred_element_type=jnp.float32
     )
-    return (table_grad, grad_one, grad_two)
+    grads = reduce_blocks(jnp.stack([parts_one, parts_two]))
+    return (table_grad, grads[0].T, grads[1].T)
 
 
 def solution(mesh):

time: 377 us -> 287 us (0.76)
  waiting for transfers between devices: 253 us -> 161 us
    reduce_scatter x2 -> x0, waiting for transfers between devices: 145 us -> none  [weight_grad(): summed = lax.psum_scatter(inner, 'node', scatter_dimension=0, tiled=True)]
    ppermute x0 -> x5, waiting for transfers between devices: none -> 78.8 us  [reduce_blocks(): moved = lax.ppermute(send, AXES, [(i, i ^ step) for i in range(shards)])]
    all_to_all x2 -> x0, waiting for transfers between devices: 26.1 us -> none  [weight_grad(): inner = lax.all_to_all(parts, 'fsdp', 0, 0, tiled=True)]
    add x0 -> x3, other arithmetic: none -> 9.59 us  [reduce_blocks(): parts = keep + moved.astype(jnp.float32)]
    all_to_all x2 -> x0, starting transfers between devices: 8.26 us -> none  [weight_grad(): inner = lax.all_to_all(parts, 'fsdp', 0, 0, tiled=True)]
    ppermute x0 -> x5, starting transfers between devices: none -> 6.66 us  [reduce_blocks(): moved = lax.ppermute(send, AXES, [(i, i ^ step) for i in range(shards)])]
    reduce_sum x2 -> x0, other arithmetic: 4.48 us -> none  [weight_grad(): inner = jnp.sum(inner.astype(jnp.float32), axis=0)]
  transfers between devices with their start and end apart: 8 -> 9, of which waited for: 5 -> 5; matrix products, arithmetic and copies ran while one was open for 12% -> 11% of each run, Pallas kernels for 0% -> 0%
where the time goes in v5:
time: 287 us
  waiting for transfers between devices  161 us (56%)
  matrix products  50 us (17%)
  starting transfers between devices  15.8 us (6%)
  other arithmetic  15.7 us (5%)
  local copies, waits for them, and re-layouts  15.3 us (5%)
  between operations  14.5 us (5%)
  blocking collectives  14.3 us (5%)
    all_to_all x2, waiting for transfers between devices, exchange(): return lax.all_to_all(values, AXES, 0, 0, tiled=True)  81.3 us
    ppermute x5, waiting for transfers between devices, reduce_blocks(): moved = lax.ppermute(send, AXES, [(i, i ^ step) for i in range(shards)])  78.8 us
    all_to_all x1, blocking collectives, exchange(): return lax.all_to_all(values, AXES, 0, 0, tiled=True)  14.3 us
    dot_general x2, matrix products, forward_layer(): jnp.dot(mixed, lax.all_gather(weight, 'fsdp', axis=1, tiled=True), prefer...  12.2 us
    add x3, other arithmetic, reduce_blocks(): parts = keep + moved.astype(jnp.float32)  9.59 us
    all_to_all x2, starting transfers between devices, exchange(): return lax.all_to_all(values, AXES, 0, 0, tiled=True)  8.87 us
    dot_general x1, matrix products, on_device(): lax.dot_general(picks, returned, (((0, 1), (0, 1)), ((), ())), preferred_...  8.74 us
    ppermute x5, starting transfers between devices, reduce_blocks(): moved = lax.ppermute(send, AXES, [(i, i ^ step) for i in range(shards)])  6.66 us
  transfers between devices with their start and end apart: 9, of which 5 were waited for; matrix products, arithmetic and copies ran while one was open for 11% of the time, Pallas kernels for 0%

profile of v5, /device:TPU:0, one launch (start us, length us, event | category | flops | bytes accessed | tf_op | source)
XLA Modules:
  0.0 286.9 jit_solution(7263398923272778913)
XLA Ops:
  8.8 1.7 reduce-window.6
  11.6 3.4 %scatter_custom_fusion = s32[1568]{0:T(1024)S(1)} fusion(s32[768]{0:T(1024)S(1)} %fusion.59, s32[768]{0:T(1024)S(1)} %get-tuple-element.7, s32[]{:T(128)} %constant.116.clone.1), kind=kCustom, calls=%fused_computation.103 | custom fusion | bytes 6276 | tf_op jit(solution)/shard_map/scatter | solution.py:44
  15.1 14.3 %all_to_all.19 = s32[32,1,49]{2,1,0:T(1,128)S(1)} all-to-all(s32[32,1,49]{2,1,0:T(1,128)S(1)} %all_to_all.12), channel_id=1, replica_groups=mesh['node'=8,'fsdp'=4] {'node','fsdp'}, dimensions={0} | all-to-all | bytes 12544 | tf_op jit(solution)/shard_map/all_to_all | solution.py:23
  29.5 5.5 %fusion.25 = bf16[32,49,1024]{2,1,0:T(8,128)(2,1)} fusion(s32[32,49]{1,0:T(8,128)S(1)} %maximum_bitcast_fusion, pred[32,49]{1,0:T(8,128)(4,1)S(1)} %compare_bitcast_fusion, bf16[1024,1024]{1,0:T(8,128)(2,1)S(1)} %copy-done), kind=kOutput, calls=%fused_computation.37 | convolution fusion | flops 3293151232 | bytes 5316256 | tf_op jit(solution)/shard_map/dot_general | solution.py:51
  35.0 3.7 %all-to-all-start.1 = ((bf16[32,49,1024]{2,1,0:T(8,128)(2,1)}), bf16[32,49,1024]{2,1,0:T(8,128)(2,1)}, u32[]{:S(2)}, u32[]{:S(2)}) async-start(bf16[32,49,1024]{2,1,0:T(8,128)(2,1)} %fusion.25), calls=%async_computation.1 | async-start | bytes 7340032 | tf_op jit(solution)/shard_map/all_to_all | solution.py:23
  40.4 81.3 %all-to-all-done.1 = bf16[32,49,1024]{2,1,0:T(8,128)(2,1)} async-done(((bf16[32,49,1024]{2,1,0:T(8,128)(2,1)}), bf16[32,49,1024]{2,1,0:T(8,128)(2,1)}, u32[]{:S(2)}, u32[]{:S(2)}) %all-to-all-start.1) | async-done | bytes 3211296 | tf_op jit(solution)/shard_map/all_to_all | solution.py:23
  121.7 5.2 %bitcast_convert_fusion = bf16[768,1024]{1,0:T(8,128)(2,1)S(1)} fusion(bf16[32,49,1024]{2,1,0:T(8,128)(2,1)} %all-to-all-done.1, pred[768,49]{0,1:T(8,128)(4,1)S(1)} %iota_compare_fusion.2, pred[768,32]{0,1:T(8,128)(4,1)S(1)} %iota_compare_fusion.4), kind=kOutput, calls=%fused_computation.25 | convolution fusion | flops 2468241408 | bytes 4846336 | tf_op jit(solution)/shard_map/dot_general | solution.py:58
  127.6 5.9 %multiply_convert_fusion.3 = (bf16[768,1024]{1,0:T(8,128)(2,1)S(1)}, f32[768,1024]{1,0:T(8,128)}) fusion(bf16[768,1024]{1,0:T(8,128)(2,1)S(1)} %bitcast.223, bf16[1024,1024]{1,0:T(8,128)(2,1)} %all-gather.3.cloned.1.call-done), kind=kOutput, calls=%fused_computation.29 | convolution fusion | flops 1614544896 | bytes 8388608 | tf_op jit(solution)/shard_map/dot_general | solution.py:72
  134.1 6.3 %fusion.16 = bf16[768,1024]{1,0:T(8,128)(2,1)} fusion(bf16[3,256,1024]{2,1,0:T(8,128)(2,1)} %param.11, bf16[768,1024]{1,0:T(8,128)(2,1)S(1)} %bitcast.225, bf16[1024,1024]{1,0:T(8,128)(2,1)} %all-gather.5.cloned.1.call-done), kind=kOutput, calls=%fused_computation.22 | convolution fusion | flops 1618477056 | bytes 6815744 | tf_op jit(solution)/shard_map/dot_general | solution.py:72
  140.4 2.7 copy.99
  143.1 3.9 %fusion.62 = f32[768,1024]{1,0:T(8,128)S(1)} fusion(bf16[768,1024]{1,0:T(8,128)(2,1)} %fusion.16, bf16[1024,1024]{1,0:T(8,128)(2,1)} %all-gather.5.cloned.1.call-done), kind=kOutput, calls=%fused_computation.110 | convolution fusion | flops 1610612736 | bytes 6815744 | tf_op jit(solution)/shard_map/dot_general | solution.py:80
  147.7 1.2 copy-done.5
  149.9 1.6 copy.98
  151.5 3.8 %convolution_bitcast_fusion.1 = f32[1,16,2,32,1024]{4,3,2,1,0:T(8,128)S(1)} fusion(bf16[16,2,32,768]{3,2,1,0:T(8,128)(2,1)} %bitcast.230, bf16[768,1024,1,1]{1,0,3,2:T(8,128)(2,1)} %bitcast.224), kind=kOutput, calls=%fused_computation.39 | convolution fusion | flops 1610612736 | bytes 7340032 | tf_op jit(solution)/shard_map/dot_general | solution.py:88
  155.4 1.8 convolution_bitcast_fusion
  157.3 2.4 select_bitcast_fusion
  159.6 1.1 copy-done.4
  160.7 1.8 fusion.63
  163.3 4.5 %fusion.22 = bf16[32,49,1024]{2,1,0:T(8,128)(2,1)} fusion(bf16[768,1024,1]{1,0,2:T(8,128)(2,1)S(1)} %bitcast.231, pred[768,49]{0,1:T(8,128)(4,1)S(1)} %iota_compare_fusion.2, pred[768,32]{0,1:T(8,128)(4,1)S(1)} %iota_compare_fusion.4), kind=kOutput, calls=%fused_computation.36 | convolution fusion | flops 2469060608 | bytes 4846336 | tf_op jit(solution)/shard_map/dot_general | solution.py:133
  167.7 5.2 %all-to-all-start.2 = ((bf16[32,49,1024]{2,1,0:T(8,128)(2,1)}), bf16[32,49,1024]{2,1,0:T(8,128)(2,1)}, u32[]{:S(2)}, u32[]{:S(2)}) async-start(bf16[32,49,1024]{2,1,0:T(8,128)(2,1)} %fusion.22), calls=%async_computation.2 | async-start | bytes 7340032 | tf_op jit(solution)/shard_map/all_to_all | solution.py:23
  173.0 5.3 %fusion.11 = f32[2,16,32,1024]{3,2,1,0:T(8,128)S(1)} fusion(f32[2,16,32,1024]{3,2,1,0:T(8,128)} %collective-permute-done, pred[]{:T(512)S(6)} %eq.111, f32[1,16,2,32,1024]{4,3,2,1,0:T(8,128)} %copy-done.4, f32[1,16,2,32,1024]{4,3,2,1,0:T(8,128)} %copy-done.3), kind=kLoop, calls=%fused_computation.15 | loop fusion | flops 4194304 | bytes 16777216 | tf_op jit(solution)/shard_map/add | solution.py:107
  178.3 2.0 copy-done.2
  180.5 1.5 collective-permute-start.1
  182.0 49.5 %collective-permute-done.1 = bf16[2,8,32,1024]{3,2,1,0:T(8,128)(2,1)S(1)} collective-permute-done((bf16[2,8,32,1024]{3,2,1,0:T(8,128)(2,1)S(1)}, bf16[2,8,32,1024]{3,2,1,0:T(8,128)(2,1)S(1)}, u32[]{:S(2)}, u32[]{:S(2)}) %collective-permute-start.1) | collective-permute-done | bytes 1048608 | tf_op jit(solution)/shard_map/ppermute | solution.py:106
  231.5 3.0 %bitcast_add_fusion = f32[2,8,32,1024]{3,2,1,0:T(8,128)S(1)} fusion(bf16[2,8,32,1024]{3,2,1,0:T(8,128)(2,1)S(1)} %collective-permute-done.1, f32[2,8,2,32,1024]{4,3,2,1,0:T(8,128)} %bitcast.216, pred[]{:T(512)S(6)} %eq.110), kind=kLoop, calls=%fused_computation.43 | loop fusion | flops 1572864 | bytes 7340033 | tf_op jit(solution)/shard_map/add | solution.py:107
  234.6 2.7 collective-permute-start.2
  237.3 16.0 %collective-permute-done.2 = bf16[2,4,32,1024]{3,2,1,0:T(8,128)(2,1)} collective-permute-done((bf16[2,4,32,1024]{3,2,1,0:T(8,128)(2,1)S(1)}, bf16[2,4,32,1024]{3,2,1,0:T(8,128)(2,1)}, u32[]{:S(2)}, u32[]{:S(2)}) %collective-permute-start.2) | collective-permute-done | bytes 524320 | tf_op jit(solution)/shard_map/ppermute | solution.py:106
  253.3 1.3 fusion.39
  254.8 7.7 %collective-permute-done.3 = bf16[2,2,32,1024]{3,2,1,0:T(8,128)(2,1)S(1)} collective-permute-done((bf16[2,2,32,1024]{3,2,1,0:T(8,128)(2,1)S(1)}, bf16[2,2,32,1024]{3,2,1,0:T(8,128)(2,1)S(1)}, u32[]{:S(2)}, u32[]{:S(2)}) %collective-permute-start.3) | collective-permute-done | bytes 262176 | tf_op jit(solution)/shard_map/ppermute | solution.py:106
  262.6 2.4 collective-permute-start.4
  265.0 5.5 %collective-permute-done.4 = bf16[2,1,32,1024]{3,2,0,1:T(8,128)(2,1)S(1)} collective-permute-done((bf16[2,1,32,1024]{3,2,0,1:T(8,128)(2,1)S(1)}, bf16[2,1,32,1024]{3,2,0,1:T(8,128)(2,1)S(1)}, u32[]{:S(2)}, u32[]{:S(2)}) %collective-permute-start.4) | collective-permute-done | bytes 131104 | tf_op jit(solution)/shard_map/ppermute | solution.py:106
  271.3 8.7 %fusion.28 = f32[1024,1024]{1,0:T(8,128)} fusion(bf16[32,49,1024]{2,1,0:T(8,128)(2,1)} %all-to-all-done.2, s32[32,49]{1,0:T(8,128)S(1)} %maximum_bitcast_fusion, pred[32,49]{1,0:T(8,128)(4,1)S(1)} %compare_bitcast_fusion), kind=kOutput, calls=%fused_computation.40 | convolution fusion | flops 3291545600 | bytes 7413408 | tf_op jit(solution)/shard_map/dot_general | solution.py:137
  (61 shorter events, 9.6 us)
Async XLA Ops:
  7.2 22.3 %copy-start = (bf16[1024,1024]{1,0:T(8,128)(2,1)S(1)}, bf16[1024,1024]{1,0:T(8,128)(2,1)}, u32[]{:S(2)}) copy-start(bf16[1024,1024]{1,0:T(8,128)(2,1)} %param.6) | copy-start | bytes 6291460
  35.0 5.2 %copy-start.10 = (s32[3,256,256]{2,1,0:T(8,128)S(1)}, s32[3,256,256]{2,1,0:T(8,128)}, u32[]{:S(2)}) copy-start(s32[3,256,256]{2,1,0:T(8,128)} %param.8) | copy-start | bytes 2359300
  35.0 86.8 %all-to-all-start.1 = ((bf16[32,49,1024]{2,1,0:T(8,128)(2,1)}), bf16[32,49,1024]{2,1,0:T(8,128)(2,1)}, u32[]{:S(2)}, u32[]{:S(2)}) async-start(bf16[32,49,1024]{2,1,0:T(8,128)(2,1)} %fusion.25), calls=%async_computation.1 | async-start | bytes 7340032 | tf_op jit(solution)/shard_map/all_to_all | solution.py:23
  38.6 88.9 %all-gather.3.cloned.1.call-start = ((), (), s32[]{:S(2)}) async-start(), calls=%async_computation.3 | async-start | bytes 2621440 | tf_op jit(solution)/shard_map/all_gather | solution.py:74
  39.4 94.7 %all-gather.5.cloned.1.call-start = ((), (), s32[]{:S(2)}) async-start(), calls=%async_computation.4 | async-start | bytes 2621440 | tf_op jit(solution)/shard_map/all_gather | solution.py:74
  127.5 5.9 %copy-start.6 = (bf16[3,256,1024]{2,1,0:T(8,128)(2,1)}, bf16[3,256,1024]{2,1,0:T(8,128)(2,1)S(1)}, u32[]{:S(2)}) copy-start(bf16[3,256,1024]{2,1,0:T(8,128)(2,1)S(1)} %multiply_convert_fusion.4) | copy-start | bytes 4718596
  134.1 6.3 %copy-start.7 = (bf16[3,256,1024]{2,1,0:T(8,128)(2,1)}, bf16[3,256,1024]{2,1,0:T(8,128)(2,1)S(1)}, u32[]{:S(2)}) copy-start(bf16[3,256,1024]{2,1,0:T(8,128)(2,1)S(1)} %multiply_convert_fusion.2) | copy-start | bytes 4718596
  147.0 1.9 copy-start.5
  151.5 3.8 %copy-start.8 = (bf16[3,256,1024]{2,1,0:T(8,128)(2,1)S(1)}, bf16[3,256,1024]{2,1,0:T(8,128)(2,1)}, u32[]{:S(2)}) copy-start(bf16[3,256,1024]{2,1,0:T(8,128)(2,1)} %copy-done.7) | copy-start | bytes 4718596
  151.5 3.8 %copy-start.9 = (bf16[768,1024]{0,1:T(8,128)(2,1)S(1)}, bf16[768,1024]{0,1:T(8,128)(2,1)}, u32[]{:S(2)}) copy-start(bf16[768,1024]{0,1:T(8,128)(2,1)} %copy.99) | copy-start | bytes 4718596
  155.3 2.0 copy-start.3
  157.3 3.4 %copy-start.4 = (f32[1,16,2,32,1024]{4,3,2,1,0:T(8,128)}, f32[1,16,2,32,1024]{4,3,2,1,0:T(8,128)S(1)}, u32[]{:S(2)}) copy-start(f32[1,16,2,32,1024]{4,3,2,1,0:T(8,128)S(1)} %convolution_bitcast_fusion) | copy-start | bytes 12582916
  157.3 3.4 %copy-start.11 = (bf16[1024,1024]{1,0:T(8,128)(2,1)S(1)}, bf16[1024,1024]{1,0:T(8,128)(2,1)}, u32[]{:S(2)}) copy-start(bf16[1024,1024]{1,0:T(8,128)(2,1)} %all-gather.3.cloned.1.call-done) | copy-start | bytes 6291460
  160.7 12.3 %collective-permute-start = (f32[2,16,32,1024]{3,2,1,0:T(8,128)}, f32[2,16,32,1024]{3,2,1,0:T(8,128)}, u32[]{:S(2)}, u32[]{:S(2)}) collective-permute-start(f32[2,16,32,1024]{3,2,1,0:T(8,128)} %select_bitcast_fusion), channel_id=1, source_target_pairs={{0,1},{1,0},{2,3},{3,2},{4,5},{5,4},{6,7},{7,6},{8,9},{9,8},{10,11... | collective-permute-start | bytes 12582920 | tf_op jit(solution)/shard_map/ppermute | solution.py:106
  167.7 103.6 %all-to-all-start.2 = ((bf16[32,49,1024]{2,1,0:T(8,128)(2,1)}), bf16[32,49,1024]{2,1,0:T(8,128)(2,1)}, u32[]{:S(2)}, u32[]{:S(2)}) async-start(bf16[32,49,1024]{2,1,0:T(8,128)(2,1)} %fusion.22), calls=%async_computation.2 | async-start | bytes 7340032 | tf_op jit(solution)/shard_map/all_to_all | solution.py:23
  178.3 2.0 copy-start.2
  180.5 51.0 %collective-permute-start.1 = (bf16[2,8,32,1024]{3,2,1,0:T(8,128)(2,1)S(1)}, bf16[2,8,32,1024]{3,2,1,0:T(8,128)(2,1)S(1)}, u32[]{:S(2)}, u32[]{:S(2)}) collective-permute-start(bf16[2,8,32,1024]{3,2,1,0:T(8,128)(2,1)S(1)} %fusion.37), channel_id=1, source_target_pairs={{0,2},{1,3},{2,0},{3,1},{4,6},{5,7},{6,4},{7,5},{8,10},{9,11},{10,... | collective-permute-start | bytes 3145736 | tf_op jit(solution)/shard_map/ppermute | solution.py:106
  234.6 18.7 %collective-permute-start.2 = (bf16[2,4,32,1024]{3,2,1,0:T(8,128)(2,1)S(1)}, bf16[2,4,32,1024]{3,2,1,0:T(8,128)(2,1)}, u32[]{:S(2)}, u32[]{:S(2)}) collective-permute-start(bf16[2,4,32,1024]{3,2,1,0:T(8,128)(2,1)S(1)} %fusion.40), channel_id=1, source_target_pairs={{0,4},{1,5},{2,6},{3,7},{4,0},{5,1},{6,2},{7,3},{8,12},{9,13},{10,... | collective-permute-start | bytes 1572872 | tf_op jit(solution)/shard_map/ppermute | solution.py:106
  254.7 7.8 %collective-permute-start.3 = (bf16[2,2,32,1024]{3,2,1,0:T(8,128)(2,1)S(1)}, bf16[2,2,32,1024]{3,2,1,0:T(8,128)(2,1)S(1)}, u32[]{:S(2)}, u32[]{:S(2)}) collective-permute-start(bf16[2,2,32,1024]{3,2,1,0:T(8,128)(2,1)S(1)} %fusion.44), channel_id=1, source_target_pairs={{0,8},{1,9},{2,10},{3,11},{4,12},{5,13},{6,14},{7,15},{8,0},{9,1},... | collective-permute-start | bytes 786440 | tf_op jit(solution)/shard_map/ppermute | solution.py:106
  262.6 7.9 %collective-permute-start.4 = (bf16[2,1,32,1024]{3,2,0,1:T(8,128)(2,1)S(1)}, bf16[2,1,32,1024]{3,2,0,1:T(8,128)(2,1)S(1)}, u32[]{:S(2)}, u32[]{:S(2)}) collective-permute-start(bf16[2,1,32,1024]{3,2,0,1:T(8,128)(2,1)S(1)} %fusion.49), channel_id=1, source_target_pairs={{0,16},{1,17},{2,18},{3,19},{4,20},{5,21},{6,22},{7,23},{8,24},{9,... | collective-permute-start | bytes 393224 | tf_op jit(solution)/shard_map/ppermute | solution.py:106
  271.3 8.7 %copy-start.1 = (bf16[1024,1024]{1,0:T(8,128)(2,1)S(1)}, bf16[1024,1024]{1,0:T(8,128)(2,1)}, u32[]{:S(2)}) copy-start(bf16[1024,1024]{1,0:T(8,128)(2,1)} %param.6) | copy-start | bytes 6291460
Sparse Core Ops, SparseCore 0:
  41.0 45.6 all-gather.2
  88.3 26.6 all-gather.4

commit v6 on v5

--- a/solution.py
+++ b/solution.py
@@ -137,8 +137,9 @@
     table_grad = lax.dot_general(
         picks, returned, (((0, 1), (0, 1)), ((), ())), preferred_element_type=jnp.float32
     )
-    grads = reduce_blocks(jnp.stack([parts_one, parts_two]))
-    return (table_grad, grads[0].T, grads[1].T)
+    grad_one = reduce_blocks(parts_one[None])[0].T
+    grad_two = reduce_blocks(parts_two[None])[0].T
+    return (table_grad, grad_one, grad_two)
 
 
 def solution(mesh):

time: 287 us -> 270 us (0.941)
  waiting for transfers between devices: 161 us -> 136 us
  starting transfers between devices: 15.8 us -> 25.1 us
    ppermute x5 -> x10, waiting for transfers between devices: 78.8 us -> 53.3 us  [reduce_blocks(): moved = lax.ppermute(send, AXES, [(i, i ^ step) for i in range(shards)])]
    ppermute x5 -> x10, starting transfers between devices: 6.66 us -> 16.1 us  [reduce_blocks(): moved = lax.ppermute(send, AXES, [(i, i ^ step) for i in range(shards)])]
    add x3 -> x6, other arithmetic: 9.59 us -> 6.64 us  [reduce_blocks(): parts = keep + moved.astype(jnp.float32)]
  transfers between devices with their start and end apart: 9 -> 14, of which waited for: 5 -> 7; matrix products, arithmetic and copies ran while one was open for 11% -> 10% of each run, Pallas kernels for 0% -> 0%
where the time goes in v6:
time: 270 us
  waiting for transfers between devices  136 us (50%)
  matrix products  51 us (19%)
  starting transfers between devices  25.1 us (9%)
  local copies, waits for them, and re-layouts  15.1 us (6%)
  between operations  14.5 us (5%)
  blocking collectives  14.3 us (5%)
  other arithmetic  14 us (5%)
    all_to_all x2, waiting for transfers between devices, exchange(): return lax.all_to_all(values, AXES, 0, 0, tiled=True)  81.3 us
    ppermute x10, waiting for transfers between devices, reduce_blocks(): moved = lax.ppermute(send, AXES, [(i, i ^ step) for i in range(shards)])  53.3 us
    ppermute x10, starting transfers between devices, reduce_blocks(): moved = lax.ppermute(send, AXES, [(i, i ^ step) for i in range(shards)])  16.1 us
    all_to_all x1, blocking collectives, exchange(): return lax.all_to_all(values, AXES, 0, 0, tiled=True)  14.3 us
    dot_general x2, matrix products, forward_layer(): jnp.dot(mixed, lax.all_gather(weight, 'fsdp', axis=1, tiled=True), prefer...  12.3 us
    all_to_all x2, starting transfers between devices, exchange(): return lax.all_to_all(values, AXES, 0, 0, tiled=True)  8.76 us
    dot_general x1, matrix products, on_device(): lax.dot_general(picks, returned, (((0, 1), (0, 1)), ((), ())), preferred_...  8.74 us
    dot_general x2, matrix products, back_weight(): lax.dot_general(delta, lax.all_gather(weight, 'fsdp', axis=1, tiled=True)...  7.3 us
  transfers between devices with their start and end apart: 14, of which 7 were waited for; matrix products, arithmetic and copies ran while one was open for 10% of the time, Pallas kernels for 0%

profile of v6, /device:TPU:0, one launch (start us, length us, event | category | flops | bytes accessed | tf_op | source)
XLA Modules:
  0.0 269.8 jit_solution(14278715062193327661)
XLA Ops:
  8.8 1.7 reduce-window.6
  11.6 3.4 %scatter_custom_fusion = s32[1568]{0:T(1024)S(1)} fusion(s32[768]{0:T(1024)S(1)} %fusion.65, s32[768]{0:T(1024)S(1)} %get-tuple-element.5, s32[]{:T(128)} %constant.137.clone.1), kind=kCustom, calls=%fused_computation.120 | custom fusion | bytes 6276 | tf_op jit(solution)/shard_map/scatter | solution.py:44
  15.1 14.3 %all_to_all.19 = s32[32,1,49]{2,1,0:T(1,128)S(1)} all-to-all(s32[32,1,49]{2,1,0:T(1,128)S(1)} %all_to_all.12), channel_id=1, replica_groups=mesh['node'=8,'fsdp'=4] {'node','fsdp'}, dimensions={0} | all-to-all | bytes 12544 | tf_op jit(solution)/shard_map/all_to_all | solution.py:23
  29.5 5.5 %fusion.22 = bf16[32,49,1024]{2,1,0:T(8,128)(2,1)} fusion(s32[32,49]{1,0:T(8,128)S(1)} %maximum_bitcast_fusion, pred[32,49]{1,0:T(8,128)(4,1)S(1)} %compare_bitcast_fusion, bf16[1024,1024]{1,0:T(8,128)(2,1)S(1)} %copy-done), kind=kOutput, calls=%fused_computation.29 | convolution fusion | flops 3293151232 | bytes 5316256 | tf_op jit(solution)/shard_map/dot_general | solution.py:51
  35.0 3.7 %all-to-all-start.1 = ((bf16[32,49,1024]{2,1,0:T(8,128)(2,1)}), bf16[32,49,1024]{2,1,0:T(8,128)(2,1)}, u32[]{:S(2)}, u32[]{:S(2)}) async-start(bf16[32,49,1024]{2,1,0:T(8,128)(2,1)} %fusion.22), calls=%async_computation.1 | async-start | bytes 7340032 | tf_op jit(solution)/shard_map/all_to_all | solution.py:23
  40.5 81.3 %all-to-all-done.1 = bf16[32,49,1024]{2,1,0:T(8,128)(2,1)} async-done(((bf16[32,49,1024]{2,1,0:T(8,128)(2,1)}), bf16[32,49,1024]{2,1,0:T(8,128)(2,1)}, u32[]{:S(2)}, u32[]{:S(2)}) %all-to-all-start.1) | async-done | bytes 3211296 | tf_op jit(solution)/shard_map/all_to_all | solution.py:23
  121.7 5.2 %bitcast_convert_fusion = bf16[768,1024]{1,0:T(8,128)(2,1)S(1)} fusion(bf16[32,49,1024]{2,1,0:T(8,128)(2,1)} %all-to-all-done.1, pred[768,49]{0,1:T(8,128)(4,1)S(1)} %iota_compare_fusion.2, pred[768,32]{0,1:T(8,128)(4,1)S(1)} %iota_compare_fusion.4), kind=kOutput, calls=%fused_computation.17 | convolution fusion | flops 2468241408 | bytes 4846336 | tf_op jit(solution)/shard_map/dot_general | solution.py:58
  127.6 5.9 %multiply_convert_fusion.3 = (bf16[768,1024]{1,0:T(8,128)(2,1)S(1)}, f32[768,1024]{1,0:T(8,128)}) fusion(bf16[768,1024]{1,0:T(8,128)(2,1)S(1)} %bitcast.289, bf16[1024,1024]{1,0:T(8,128)(2,1)} %all-gather.3.cloned.1.call-done), kind=kOutput, calls=%fused_computation.21 | convolution fusion | flops 1614544896 | bytes 8388608 | tf_op jit(solution)/shard_map/dot_general | solution.py:72
  134.1 6.4 %fusion.13 = bf16[768,1024]{1,0:T(8,128)(2,1)} fusion(bf16[3,256,1024]{2,1,0:T(8,128)(2,1)} %param.11, bf16[768,1024]{1,0:T(8,128)(2,1)S(1)} %bitcast.291, bf16[1024,1024]{1,0:T(8,128)(2,1)} %all-gather.5.cloned.1.call-done), kind=kOutput, calls=%fused_computation.14 | convolution fusion | flops 1618477056 | bytes 6815744 | tf_op jit(solution)/shard_map/dot_general | solution.py:72
  140.5 2.6 copy.124
  143.1 3.9 %fusion.68 = f32[768,1024]{1,0:T(8,128)S(1)} fusion(bf16[768,1024]{1,0:T(8,128)(2,1)} %fusion.13, bf16[1024,1024]{1,0:T(8,128)(2,1)} %all-gather.5.cloned.1.call-done), kind=kOutput, calls=%fused_computation.127 | convolution fusion | flops 1610612736 | bytes 6815744 | tf_op jit(solution)/shard_map/dot_general | solution.py:80
  149.9 1.6 copy.109
  151.5 3.4 %fusion.69 = f32[768,1024]{1,0:T(8,128)S(1)} fusion(bf16[768,1024]{1,0:T(8,128)(2,1)S(1)} %fusion.14, bf16[1024,1024]{1,0:T(8,128)(2,1)} %all-gather.3.cloned.1.call-done), kind=kOutput, calls=%fused_computation.128 | convolution fusion | flops 1610612736 | bytes 6815744 | tf_op jit(solution)/shard_map/dot_general | solution.py:80
  155.6 4.5 %fusion.19 = bf16[32,49,1024]{2,1,0:T(8,128)(2,1)} fusion(bf16[768,1024,1]{1,0,2:T(8,128)(2,1)S(1)} %bitcast.297, pred[768,49]{0,1:T(8,128)(4,1)S(1)} %iota_compare_fusion.2, pred[768,32]{0,1:T(8,128)(4,1)S(1)} %iota_compare_fusion.4), kind=kOutput, calls=%fused_computation.28 | convolution fusion | flops 2469060608 | bytes 4846336 | tf_op jit(solution)/shard_map/dot_general | solution.py:133
  160.1 5.1 %all-to-all-start.2 = ((bf16[32,49,1024]{2,1,0:T(8,128)(2,1)}), bf16[32,49,1024]{2,1,0:T(8,128)(2,1)}, u32[]{:S(2)}, u32[]{:S(2)}) async-start(bf16[32,49,1024]{2,1,0:T(8,128)(2,1)} %fusion.19), calls=%async_computation.2 | async-start | bytes 7340032 | tf_op jit(solution)/shard_map/all_to_all | solution.py:23
  165.2 3.2 %convolution_bitcast_fusion.1 = f32[1,16,2,32,1024]{4,3,2,1,0:T(8,128)S(1)} fusion(bf16[16,2,32,768]{3,2,1,0:T(8,128)(2,1)} %bitcast.294, bf16[768,1024,1,1]{1,0,3,2:T(8,128)(2,1)S(1)} %bitcast.290), kind=kOutput, calls=%fused_computation.31 | convolution fusion | flops 1610612736 | bytes 7340032 | tf_op jit(solution)/shard_map/dot_general | solution.py:88
  168.4 1.9 select_bitcast_fusion.1
  172.5 1.8 convolution_bitcast_fusion
  176.3 3.7 %fusion.29 = f32[1,16,32,1024]{3,2,1,0:T(8,128)S(1)} fusion(f32[1,16,32,1024]{3,2,1,0:T(8,128)} %collective-permute-done, f32[1,16,2,32,1024]{4,3,2,1,0:T(8,128)} %copy-done.4, pred[]{:T(512)S(6)} %eq.121), kind=kLoop, calls=%fused_computation.35 | loop fusion | flops 1048576 | bytes 8388609 | tf_op jit(solution)/shard_map/add | solution.py:107
  180.1 1.6 collective-permute-start.1
  181.7 2.3 bitcast_add_fusion
  184.6 26.9 %collective-permute-done.1 = bf16[1,8,32,1024]{3,2,1,0:T(8,128)(2,1)S(1)} collective-permute-done((bf16[1,8,32,1024]{3,2,1,0:T(8,128)(2,1)S(1)}, bf16[1,8,32,1024]{3,2,1,0:T(8,128)(2,1)S(1)}, u32[]{:S(2)}, u32[]{:S(2)}) %collective-permute-start.1) | collective-permute-done | bytes 524320 | tf_op jit(solution)/shard_map/ppermute | solution.py:106
  211.9 2.0 collective-permute-start.2
  213.9 9.9 %collective-permute-done.6 = bf16[1,8,32,1024]{3,2,1,0:T(8,128)(2,1)S(1)} collective-permute-done((bf16[1,8,32,1024]{3,2,1,0:T(8,128)(2,1)S(1)}, bf16[1,8,32,1024]{3,2,1,0:T(8,128)(2,1)S(1)}, u32[]{:S(2)}, u32[]{:S(2)}) %collective-permute-start.6) | collective-permute-done | bytes 524320 | tf_op jit(solution)/shard_map/ppermute | solution.py:106
  224.1 2.7 %collective-permute-start.7 = (bf16[1,4,32,1024]{3,2,1,0:T(8,128)(2,1)S(1)}, bf16[1,4,32,1024]{3,2,1,0:T(8,128)(2,1)S(1)}, u32[]{:S(2)}, u32[]{:S(2)}) collective-permute-start(bf16[1,4,32,1024]{3,2,1,0:T(8,128)(2,1)S(1)} %fusion.42), channel_id=1, source_target_pairs={{0,4},{1,5},{2,6},{3,7},{4,0},{5,1},{6,2},{7,3},{8,12},{9,13},{10,... | collective-permute-start | bytes 786440 | tf_op jit(solution)/shard_map/ppermute | solution.py:106
  228.1 7.5 %collective-permute-done.7 = bf16[1,4,32,1024]{3,2,1,0:T(8,128)(2,1)S(1)} collective-permute-done((bf16[1,4,32,1024]{3,2,1,0:T(8,128)(2,1)S(1)}, bf16[1,4,32,1024]{3,2,1,0:T(8,128)(2,1)S(1)}, u32[]{:S(2)}, u32[]{:S(2)}) %collective-permute-start.7) | collective-permute-done | bytes 262176 | tf_op jit(solution)/shard_map/ppermute | solution.py:106
  235.8 1.9 collective-permute-start.8
  237.7 2.7 %collective-permute-start.4 = (bf16[1,1,32,1024]{3,2,1,0:T(8,128)(2,1)S(1)}, bf16[1,1,32,1024]{3,2,1,0:T(8,128)(2,1)S(1)}, u32[]{:S(2)}, u32[]{:S(2)}) collective-permute-start(bf16[1,1,32,1024]{3,2,1,0:T(8,128)(2,1)S(1)} %fusion.58), channel_id=1, source_target_pairs={{0,16},{1,17},{2,18},{3,19},{4,20},{5,21},{6,22},{7,23},{8,24},{9,... | collective-permute-start | bytes 196616 | tf_op jit(solution)/shard_map/ppermute | solution.py:106
  240.4 1.7 collective-permute-done.8
  242.2 3.4 %collective-permute-start.9 = (bf16[1,1,32,1024]{3,2,1,0:T(8,128)(2,1)S(1)}, bf16[1,1,32,1024]{3,2,1,0:T(8,128)(2,1)S(1)}, u32[]{:S(2)}, u32[]{:S(2)}) collective-permute-start(bf16[1,1,32,1024]{3,2,1,0:T(8,128)(2,1)S(1)} %fusion.59), channel_id=1, source_target_pairs={{0,16},{1,17},{2,18},{3,19},{4,20},{5,21},{6,22},{7,23},{8,24},{9,... | collective-permute-start | bytes 196616 | tf_op jit(solution)/shard_map/ppermute | solution.py:106
  245.6 7.1 %collective-permute-done.4 = bf16[1,1,32,1024]{3,2,1,0:T(8,128)(2,1)S(1)} collective-permute-done((bf16[1,1,32,1024]{3,2,1,0:T(8,128)(2,1)S(1)}, bf16[1,1,32,1024]{3,2,1,0:T(8,128)(2,1)S(1)}, u32[]{:S(2)}, u32[]{:S(2)}) %collective-permute-start.4) | collective-permute-done | bytes 65568 | tf_op jit(solution)/shard_map/ppermute | solution.py:106
  254.3 8.7 %fusion.25 = f32[1024,1024]{1,0:T(8,128)} fusion(bf16[32,49,1024]{2,1,0:T(8,128)(2,1)} %all-to-all-done.2, s32[32,49]{1,0:T(8,128)S(1)} %maximum_bitcast_fusion, pred[32,49]{1,0:T(8,128)(4,1)S(1)} %compare_bitcast_fusion), kind=kOutput, calls=%fused_computation.32 | convolution fusion | flops 3291545600 | bytes 7413408 | tf_op jit(solution)/shard_map/dot_general | solution.py:137
  (80 shorter events, 17.9 us)
Async XLA Ops:
  7.2 22.3 %copy-start = (bf16[1024,1024]{1,0:T(8,128)(2,1)S(1)}, bf16[1024,1024]{1,0:T(8,128)(2,1)}, u32[]{:S(2)}) copy-start(bf16[1024,1024]{1,0:T(8,128)(2,1)} %param.6) | copy-start | bytes 6291460
  35.0 5.3 %copy-start.11 = (s32[3,256,256]{2,1,0:T(8,128)S(1)}, s32[3,256,256]{2,1,0:T(8,128)}, u32[]{:S(2)}) copy-start(s32[3,256,256]{2,1,0:T(8,128)} %param.8) | copy-start | bytes 2359300
  35.0 86.8 %all-to-all-start.1 = ((bf16[32,49,1024]{2,1,0:T(8,128)(2,1)}), bf16[32,49,1024]{2,1,0:T(8,128)(2,1)}, u32[]{:S(2)}, u32[]{:S(2)}) async-start(bf16[32,49,1024]{2,1,0:T(8,128)(2,1)} %fusion.22), calls=%async_computation.1 | async-start | bytes 7340032 | tf_op jit(solution)/shard_map/all_to_all | solution.py:23
  38.7 88.9 %all-gather.3.cloned.1.call-start = ((), (), s32[]{:S(2)}) async-start(), calls=%async_computation.3 | async-start | bytes 2621440 | tf_op jit(solution)/shard_map/all_gather | solution.py:74
  39.4 94.7 %all-gather.5.cloned.1.call-start = ((), (), s32[]{:S(2)}) async-start(), calls=%async_computation.4 | async-start | bytes 2621440 | tf_op jit(solution)/shard_map/all_gather | solution.py:74
  127.6 5.9 %copy-start.6 = (bf16[3,256,1024]{2,1,0:T(8,128)(2,1)}, bf16[3,256,1024]{2,1,0:T(8,128)(2,1)S(1)}, u32[]{:S(2)}) copy-start(bf16[3,256,1024]{2,1,0:T(8,128)(2,1)S(1)} %multiply_convert_fusion.4) | copy-start | bytes 4718596
  134.0 6.5 %copy-start.8 = (bf16[3,256,1024]{2,1,0:T(8,128)(2,1)}, bf16[3,256,1024]{2,1,0:T(8,128)(2,1)S(1)}, u32[]{:S(2)}) copy-start(bf16[3,256,1024]{2,1,0:T(8,128)(2,1)S(1)} %multiply_convert_fusion.2) | copy-start | bytes 4718596
  147.0 1.9 copy-start.5
  160.1 5.1 %copy-start.7 = (bf16[3,256,1024]{2,1,0:T(8,128)(2,1)S(1)}, bf16[3,256,1024]{2,1,0:T(8,128)(2,1)}, u32[]{:S(2)}) copy-start(bf16[3,256,1024]{2,1,0:T(8,128)(2,1)} %copy-done.6) | copy-start | bytes 4718596
  160.1 94.2 %all-to-all-start.2 = ((bf16[32,49,1024]{2,1,0:T(8,128)(2,1)}), bf16[32,49,1024]{2,1,0:T(8,128)(2,1)}, u32[]{:S(2)}, u32[]{:S(2)}) async-start(bf16[32,49,1024]{2,1,0:T(8,128)(2,1)} %fusion.19), calls=%async_computation.2 | async-start | bytes 7340032 | tf_op jit(solution)/shard_map/all_to_all | solution.py:23
  168.4 3.1 %copy-start.4 = (f32[1,16,2,32,1024]{4,3,2,1,0:T(8,128)}, f32[1,16,2,32,1024]{4,3,2,1,0:T(8,128)S(1)}, u32[]{:S(2)}) copy-start(f32[1,16,2,32,1024]{4,3,2,1,0:T(8,128)S(1)} %convolution_bitcast_fusion.1) | copy-start | bytes 12582916
  168.4 3.1 %copy-start.9 = (bf16[3,256,1024]{2,1,0:T(8,128)(2,1)S(1)}, bf16[3,256,1024]{2,1,0:T(8,128)(2,1)}, u32[]{:S(2)}) copy-start(bf16[3,256,1024]{2,1,0:T(8,128)(2,1)} %copy-done.8) | copy-start | bytes 4718596
  168.4 4.1 %copy-start.10 = (bf16[768,1024]{0,1:T(8,128)(2,1)S(1)}, bf16[768,1024]{0,1:T(8,128)(2,1)}, u32[]{:S(2)}) copy-start(bf16[768,1024]{0,1:T(8,128)(2,1)} %copy.124) | copy-start | bytes 4718596
  171.5 4.7 %collective-permute-start = (f32[1,16,32,1024]{3,2,1,0:T(8,128)}, f32[1,16,32,1024]{3,2,1,0:T(8,128)}, u32[]{:S(2)}, u32[]{:S(2)}) collective-permute-start(f32[1,16,32,1024]{3,2,1,0:T(8,128)} %select_bitcast_fusion.1), channel_id=1, source_target_pairs={{0,1},{1,0},{2,3},{3,2},{4,5},{5,4},{6,7},{7,6},{8,9},{9,8},{10,11... | collective-permute-start | bytes 6291464 | tf_op jit(solution)/shard_map/ppermute | solution.py:106
  174.3 2.0 copy-start.2
  176.3 5.5 %collective-permute-start.5 = (f32[1,16,32,1024]{3,2,1,0:T(8,128)S(1)}, f32[1,16,32,1024]{3,2,1,0:T(8,128)}, u32[]{:S(2)}, u32[]{:S(2)}) collective-permute-start(f32[1,16,32,1024]{3,2,1,0:T(8,128)S(1)} %select_bitcast_fusion), channel_id=1, source_target_pairs={{0,1},{1,0},{2,3},{3,2},{4,5},{5,4},{6,7},{7,6},{8,9},{9,8},{10,11... | collective-permute-start | bytes 6291464 | tf_op jit(solution)/shard_map/ppermute | solution.py:106
  176.3 5.4 %copy-start.3 = (f32[1,16,2,32,1024]{4,3,1,2,0:T(8,128)S(1)}, f32[1,16,2,32,1024]{4,3,1,2,0:T(8,128)}, u32[]{:S(2)}) copy-start(f32[1,16,2,32,1024]{4,3,1,2,0:T(8,128)} %copy-done.2) | copy-start | bytes 12582916
  180.1 31.5 %collective-permute-start.1 = (bf16[1,8,32,1024]{3,2,1,0:T(8,128)(2,1)S(1)}, bf16[1,8,32,1024]{3,2,1,0:T(8,128)(2,1)S(1)}, u32[]{:S(2)}, u32[]{:S(2)}) collective-permute-start(bf16[1,8,32,1024]{3,2,1,0:T(8,128)(2,1)S(1)} %fusion.37), channel_id=1, source_target_pairs={{0,2},{1,3},{2,0},{3,1},{4,6},{5,7},{6,4},{7,5},{8,10},{9,11},{10,... | collective-permute-start | bytes 1572872 | tf_op jit(solution)/shard_map/ppermute | solution.py:106
  184.1 39.7 %collective-permute-start.6 = (bf16[1,8,32,1024]{3,2,1,0:T(8,128)(2,1)S(1)}, bf16[1,8,32,1024]{3,2,1,0:T(8,128)(2,1)S(1)}, u32[]{:S(2)}, u32[]{:S(2)}) collective-permute-start(bf16[1,8,32,1024]{3,2,1,0:T(8,128)(2,1)S(1)} %fusion.38), channel_id=1, source_target_pairs={{0,2},{1,3},{2,0},{3,1},{4,6},{5,7},{6,4},{7,5},{8,10},{9,11},{10,... | collective-permute-start | bytes 1572872 | tf_op jit(solution)/shard_map/ppermute | solution.py:106
  211.9 14.9 %collective-permute-start.2 = (bf16[1,4,32,1024]{3,2,1,0:T(8,128)(2,1)S(1)}, bf16[1,4,32,1024]{3,2,1,0:T(8,128)(2,1)S(1)}, u32[]{:S(2)}, u32[]{:S(2)}) collective-permute-start(bf16[1,4,32,1024]{3,2,1,0:T(8,128)(2,1)S(1)} %fusion.41), channel_id=1, source_target_pairs={{0,4},{1,5},{2,6},{3,7},{4,0},{5,1},{6,2},{7,3},{8,12},{9,13},{10,... | collective-permute-start | bytes 786440 | tf_op jit(solution)/shard_map/ppermute | solution.py:106
  224.1 11.6 %collective-permute-start.7 = (bf16[1,4,32,1024]{3,2,1,0:T(8,128)(2,1)S(1)}, bf16[1,4,32,1024]{3,2,1,0:T(8,128)(2,1)S(1)}, u32[]{:S(2)}, u32[]{:S(2)}) collective-permute-start(bf16[1,4,32,1024]{3,2,1,0:T(8,128)(2,1)S(1)} %fusion.42), channel_id=1, source_target_pairs={{0,4},{1,5},{2,6},{3,7},{4,0},{5,1},{6,2},{7,3},{8,12},{9,13},{10,... | collective-permute-start | bytes 786440 | tf_op jit(solution)/shard_map/ppermute | solution.py:106
  226.9 10.7 %collective-permute-start.3 = (bf16[1,2,32,1024]{3,2,1,0:T(8,128)(2,1)S(1)}, bf16[1,2,32,1024]{3,2,1,0:T(8,128)(2,1)S(1)}, u32[]{:S(2)}, u32[]{:S(2)}) collective-permute-start(bf16[1,2,32,1024]{3,2,1,0:T(8,128)(2,1)S(1)} %fusion.48), channel_id=1, source_target_pairs={{0,8},{1,9},{2,10},{3,11},{4,12},{5,13},{6,14},{7,15},{8,0},{9,1},... | collective-permute-start | bytes 393224 | tf_op jit(solution)/shard_map/ppermute | solution.py:106
  235.8 6.4 %collective-permute-start.8 = (bf16[1,2,32,1024]{3,2,1,0:T(8,128)(2,1)S(1)}, bf16[1,2,32,1024]{3,2,1,0:T(8,128)(2,1)S(1)}, u32[]{:S(2)}, u32[]{:S(2)}) collective-permute-start(bf16[1,2,32,1024]{3,2,1,0:T(8,128)(2,1)S(1)} %fusion.49), channel_id=1, source_target_pairs={{0,8},{1,9},{2,10},{3,11},{4,12},{5,13},{6,14},{7,15},{8,0},{9,1},... | collective-permute-start | bytes 393224 | tf_op jit(solution)/shard_map/ppermute | solution.py:106
  237.7 15.0 %collective-permute-start.4 = (bf16[1,1,32,1024]{3,2,1,0:T(8,128)(2,1)S(1)}, bf16[1,1,32,1024]{3,2,1,0:T(8,128)(2,1)S(1)}, u32[]{:S(2)}, u32[]{:S(2)}) collective-permute-start(bf16[1,1,32,1024]{3,2,1,0:T(8,128)(2,1)S(1)} %fusion.58), channel_id=1, source_target_pairs={{0,16},{1,17},{2,18},{3,19},{4,20},{5,21},{6,22},{7,23},{8,24},{9,... | collective-permute-start | bytes 196616 | tf_op jit(solution)/shard_map/ppermute | solution.py:106
  242.2 11.3 %collective-permute-start.9 = (bf16[1,1,32,1024]{3,2,1,0:T(8,128)(2,1)S(1)}, bf16[1,1,32,1024]{3,2,1,0:T(8,128)(2,1)S(1)}, u32[]{:S(2)}, u32[]{:S(2)}) collective-permute-start(bf16[1,1,32,1024]{3,2,1,0:T(8,128)(2,1)S(1)} %fusion.59), channel_id=1, source_target_pairs={{0,16},{1,17},{2,18},{3,19},{4,20},{5,21},{6,22},{7,23},{8,24},{9,... | collective-permute-start | bytes 196616 | tf_op jit(solution)/shard_map/ppermute | solution.py:106
  254.3 8.7 %copy-start.1 = (bf16[1024,1024]{1,0:T(8,128)(2,1)S(1)}, bf16[1024,1024]{1,0:T(8,128)(2,1)}, u32[]{:S(2)}) copy-start(bf16[1024,1024]{1,0:T(8,128)(2,1)} %param.6) | copy-start | bytes 6291460
Sparse Core Ops, SparseCore 0:
  41.0 45.6 all-gather.2
  88.3 26.6 all-gather.4

commit v7 on v6

--- a/solution.py
+++ b/solution.py
@@ -92,10 +92,9 @@
             preferred_element_type=jnp.float32,
         )
 
-    def reduce_blocks(parts):
+    def reduce_blocks(parts, step, stop):
         me = lax.axis_index(AXES)
-        step = 1
-        while step < shards:
+        while step < stop:
             held = parts.shape[1]
             pair = parts.reshape(parts.shape[0], held // 2, 2, *parts.shape[2:])
             upper = (me // step) % 2 == 1
@@ -106,7 +105,10 @@
             moved = lax.ppermute(send, AXES, [(i, i ^ step) for i in range(shards)])
             parts = keep + moved.astype(jnp.float32)
             step *= 2
-        return parts[:, 0] / (groups * shards)
+        return parts
+
+    def finish(parts):
+        return (parts[0, 0] / (groups * shards)).T
 
     mixed_one, first_matmul_result, whole_one = forward_layer(inputs, weight_one)
     latent_state = (
@@ -133,12 +135,15 @@
     outgoing = lax.dot_general(
         slot_of, input_grad, (((0,), (0,)), ((), ())), preferred_element_type=jnp.float32
     ).astype(jnp.bfloat16)
+    early = min(4, shards)
+    parts_two = reduce_blocks(parts_two[None], 1, early)
+    outgoing, parts_two = lax.optimization_barrier((outgoing, parts_two))
     returned = exchange(outgoing)
     table_grad = lax.dot_general(
         picks, returned, (((0, 1), (0, 1)), ((), ())), preferred_element_type=jnp.float32
     )
-    grad_one = reduce_blocks(parts_one[None])[0].T
-    grad_two = reduce_blocks(parts_two[None])[0].T
+    grad_one = finish(reduce_blocks(parts_one[None], 1, shards))
+    grad_two = finish(reduce_blocks(parts_two, early, shards))
     return (table_grad, grad_one, grad_two)
 
 

time: 270 us -> 294 us (1.089)
  waiting for transfers between devices: 136 us -> 164 us
  starting transfers between devices: 25.1 us -> 14.6 us
  other arithmetic: 14 us -> 20.5 us
    ppermute x10, waiting for transfers between devices: 53.3 us -> 81.8 us  [reduce_blocks(): moved = lax.ppermute(send, AXES, [(i, i ^ step) for i in range(shards)])]
    ppermute x10, starting transfers between devices: 16.1 us -> 5.8 us  [reduce_blocks(): moved = lax.ppermute(send, AXES, [(i, i ^ step) for i in range(shards)])]
    add x6, other arithmetic: 6.64 us -> 9.96 us  [reduce_blocks(): parts = keep + moved.astype(jnp.float32)]
    unnamed x25 -> x21, local copies, waits for them, and re-layouts: 5.66 us -> 6.55 us
  transfers between devices with their start and end apart: 14 -> 14, of which waited for: 7 -> 9; matrix products, arithmetic and copies ran while one was open for 10% -> 14% of each run, Pallas kernels for 0% -> 0%
where the time goes in v7:
time: 294 us; the launch traced here: 293 us
  waiting for transfers between devices  164 us (56%)
  matrix products  49.3 us (17%)
  other arithmetic  20.5 us (7%)
  local copies, waits for them, and re-layouts  16 us (5%)
  starting transfers between devices  14.6 us (5%)
  between operations  14.5 us (5%)
  blocking collectives  14.3 us (5%)
    ppermute x10, waiting for transfers between devices, reduce_blocks(): moved = lax.ppermute(send, AXES, [(i, i ^ step) for i in range(shards)])  81.8 us
    all_to_all x2, waiting for transfers between devices, exchange(): return lax.all_to_all(values, AXES, 0, 0, tiled=True)  81.3 us
    all_to_all x1, blocking collectives, exchange(): return lax.all_to_all(values, AXES, 0, 0, tiled=True)  14.3 us
    dot_general x2, matrix products, forward_layer(): jnp.dot(mixed, lax.all_gather(weight, 'fsdp', axis=1, tiled=True), prefer...  11.6 us
    add x6, other arithmetic, reduce_blocks(): parts = keep + moved.astype(jnp.float32)  9.96 us
    dot_general x1, matrix products, on_device(): lax.dot_general(picks, returned, (((0, 1), (0, 1)), ((), ())), preferred_...  8.74 us
    all_to_all x2, starting transfers between devices, exchange(): return lax.all_to_all(values, AXES, 0, 0, tiled=True)  8.52 us
    unnamed x21, local copies, waits for them, and re-layouts  6.55 us
  transfers between devices with their start and end apart: 14, of which 9 were waited for; matrix products, arithmetic and copies ran while one was open for 14% of the time, Pallas kernels for 0%

profile of v7, /device:TPU:0, one launch (start us, length us, event | category | flops | bytes accessed | tf_op | source)
XLA Modules:
  0.0 293.4 jit_solution(269480597170146668)
XLA Ops:
  8.8 1.7 reduce-window.6
  11.6 3.4 %scatter_custom_fusion = s32[1568]{0:T(1024)S(1)} fusion(s32[768]{0:T(1024)S(1)} %fusion.65, s32[768]{0:T(1024)S(1)} %get-tuple-element.9, s32[]{:T(128)} %constant.137.clone.1), kind=kCustom, calls=%fused_computation.120 | custom fusion | bytes 6276 | tf_op jit(solution)/shard_map/scatter | solution.py:44
  15.1 14.3 %all_to_all.19 = s32[32,1,49]{2,1,0:T(1,128)S(1)} all-to-all(s32[32,1,49]{2,1,0:T(1,128)S(1)} %all_to_all.12), channel_id=1, replica_groups=mesh['node'=8,'fsdp'=4] {'node','fsdp'}, dimensions={0} | all-to-all | bytes 12544 | tf_op jit(solution)/shard_map/all_to_all | solution.py:23
  29.5 5.5 %fusion.22 = bf16[32,49,1024]{2,1,0:T(8,128)(2,1)} fusion(s32[32,49]{1,0:T(8,128)S(1)} %maximum_bitcast_fusion, pred[32,49]{1,0:T(8,128)(4,1)S(1)} %compare_bitcast_fusion, bf16[1024,1024]{1,0:T(8,128)(2,1)S(1)} %copy-done), kind=kOutput, calls=%fused_computation.29 | convolution fusion | flops 3293151232 | bytes 5316256 | tf_op jit(solution)/shard_map/dot_general | solution.py:51
  35.0 3.7 %all-to-all-start.1 = ((bf16[32,49,1024]{2,1,0:T(8,128)(2,1)}), bf16[32,49,1024]{2,1,0:T(8,128)(2,1)}, u32[]{:S(2)}, u32[]{:S(2)}) async-start(bf16[32,49,1024]{2,1,0:T(8,128)(2,1)} %fusion.22), calls=%async_computation.1 | async-start | bytes 7340032 | tf_op jit(solution)/shard_map/all_to_all | solution.py:23
  40.5 81.3 %all-to-all-done.1 = bf16[32,49,1024]{2,1,0:T(8,128)(2,1)} async-done(((bf16[32,49,1024]{2,1,0:T(8,128)(2,1)}), bf16[32,49,1024]{2,1,0:T(8,128)(2,1)}, u32[]{:S(2)}, u32[]{:S(2)}) %all-to-all-start.1) | async-done | bytes 3211296 | tf_op jit(solution)/shard_map/all_to_all | solution.py:23
  121.7 5.2 %bitcast_convert_fusion = bf16[768,1024]{1,0:T(8,128)(2,1)S(1)} fusion(bf16[32,49,1024]{2,1,0:T(8,128)(2,1)} %all-to-all-done.1, pred[768,49]{0,1:T(8,128)(4,1)S(1)} %iota_compare_fusion.2, pred[768,32]{0,1:T(8,128)(4,1)S(1)} %iota_compare_fusion.4), kind=kOutput, calls=%fused_computation.17 | convolution fusion | flops 2468241408 | bytes 4846336 | tf_op jit(solution)/shard_map/dot_general | solution.py:58
  127.6 5.9 %multiply_convert_fusion.3 = (bf16[768,1024]{1,0:T(8,128)(2,1)S(1)}, f32[768,1024]{1,0:T(8,128)}) fusion(bf16[768,1024]{1,0:T(8,128)(2,1)S(1)} %bitcast.287, bf16[1024,1024]{1,0:T(8,128)(2,1)} %all-gather.3.cloned.1.call-done), kind=kOutput, calls=%fused_computation.21 | convolution fusion | flops 1614544896 | bytes 8388608 | tf_op jit(solution)/shard_map/dot_general | solution.py:72
  134.1 5.8 %fusion.13 = bf16[768,1024]{1,0:T(8,128)(2,1)} fusion(bf16[3,256,1024]{2,1,0:T(8,128)(2,1)} %param.11, bf16[768,1024]{1,0:T(8,128)(2,1)S(1)} %bitcast.289, bf16[1024,1024]{1,0:T(8,128)(2,1)} %all-gather.5.cloned.1.call-done), kind=kOutput, calls=%fused_computation.14 | convolution fusion | flops 1618477056 | bytes 6815744 | tf_op jit(solution)/shard_map/dot_general | solution.py:72
  139.8 2.6 copy.109
  142.4 3.9 %fusion.68 = f32[768,1024]{1,0:T(8,128)S(1)} fusion(bf16[768,1024]{1,0:T(8,128)(2,1)} %fusion.13, bf16[1024,1024]{1,0:T(8,128)(2,1)} %all-gather.5.cloned.1.call-done), kind=kOutput, calls=%fused_computation.127 | convolution fusion | flops 1610612736 | bytes 6815744 | tf_op jit(solution)/shard_map/dot_general | solution.py:80
  147.7 1.8 convolution_bitcast_fusion.1
  149.6 1.7 select_bitcast_fusion.1
  154.7 1.6 copy.116
  156.3 3.7 %convolution_bitcast_fusion = f32[1,16,2,32,1024]{4,3,1,2,0:T(8,128)S(1)} fusion(bf16[768,1024,1,1]{1,0,2,3:T(8,128)(2,1)} %bitcast.288, bf16[16,2,32,768]{3,2,1,0:T(8,128)(2,1)} %bitcast.294), kind=kOutput, calls=%fused_computation.30 | convolution fusion | flops 1610612736 | bytes 7340032 | tf_op jit(solution)/shard_map/dot_general | solution.py:88
  160.0 1.8 select_bitcast_fusion
  163.1 1.8 fusion.69
  167.1 2.3 fusion.29
  170.4 4.4 %fusion.19 = bf16[32,49,1024]{2,1,0:T(8,128)(2,1)} fusion(bf16[768,1024,1]{1,0,2:T(8,128)(2,1)S(1)} %bitcast.295, pred[768,49]{0,1:T(8,128)(4,1)S(1)} %iota_compare_fusion.2, pred[768,32]{0,1:T(8,128)(4,1)S(1)} %iota_compare_fusion.4), kind=kOutput, calls=%fused_computation.28 | convolution fusion | flops 2469060608 | bytes 4846336 | tf_op jit(solution)/shard_map/dot_general | solution.py:135
  174.8 8.8 %collective-permute-done.1 = bf16[1,8,32,1024]{3,2,1,0:T(8,128)(2,1)S(1)} collective-permute-done((bf16[1,8,32,1024]{3,2,1,0:T(8,128)(2,1)S(1)}, bf16[1,8,32,1024]{3,2,1,0:T(8,128)(2,1)S(1)}, u32[]{:S(2)}, u32[]{:S(2)}) %collective-permute-start.1) | collective-permute-done | bytes 524320 | tf_op jit(solution)/shard_map/ppermute | solution.py:105
  183.8 4.8 %all-to-all-start.2 = ((bf16[32,49,1024]{2,1,0:T(8,128)(2,1)}), bf16[32,49,1024]{2,1,0:T(8,128)(2,1)}, u32[]{:S(2)}, u32[]{:S(2)}) async-start(bf16[32,49,1024]{2,1,0:T(8,128)(2,1)} %fusion.19), calls=%async_computation.2 | async-start | bytes 7340032 | tf_op jit(solution)/shard_map/all_to_all | solution.py:23
  188.7 3.7 %bitcast_add_fusion = f32[1,16,32,1024]{3,2,1,0:T(8,128)S(1)} fusion(f32[1,16,32,1024]{3,2,1,0:T(8,128)} %collective-permute-done.2, f32[1,16,2,32,1024]{4,3,1,2,0:T(8,128)} %copy-done.2, pred[]{:T(512)S(6)} %eq.118), kind=kLoop, calls=%fused_computation.36 | loop fusion | flops 1048576 | bytes 8388609 | tf_op jit(solution)/shard_map/add | solution.py:106
  193.3 1.7 collective-permute-start.3
  195.0 40.1 %collective-permute-done.3 = bf16[1,8,32,1024]{3,2,1,0:T(8,128)(2,1)} collective-permute-done((bf16[1,8,32,1024]{3,2,1,0:T(8,128)(2,1)}, bf16[1,8,32,1024]{3,2,1,0:T(8,128)(2,1)}, u32[]{:S(2)}, u32[]{:S(2)}) %collective-permute-start.3) | collective-permute-done | bytes 524320 | tf_op jit(solution)/shard_map/ppermute | solution.py:105
  235.1 2.3 bitcast_add_fusion.1
  238.7 1.5 collective-permute-start.4
  240.9 8.7 %collective-permute-done.4 = bf16[1,4,32,1024]{3,2,1,0:T(8,128)(2,1)S(1)} collective-permute-done((bf16[1,4,32,1024]{3,2,1,0:T(8,128)(2,1)S(1)}, bf16[1,4,32,1024]{3,2,1,0:T(8,128)(2,1)S(1)}, u32[]{:S(2)}, u32[]{:S(2)}) %collective-permute-start.4) | collective-permute-done | bytes 262176 | tf_op jit(solution)/shard_map/ppermute | solution.py:105
  251.0 4.4 %collective-permute-done.7 = bf16[1,4,32,1024]{3,2,1,0:T(8,128)(2,1)S(1)} collective-permute-done((bf16[1,4,32,1024]{3,2,1,0:T(8,128)(2,1)S(1)}, bf16[1,4,32,1024]{3,2,1,0:T(8,128)(2,1)S(1)}, u32[]{:S(2)}, u32[]{:S(2)}) %collective-permute-start.7) | collective-permute-done | bytes 262176 | tf_op jit(solution)/shard_map/ppermute | solution.py:105
  255.6 2.6 collective-permute-done.5
  258.4 4.1 %collective-permute-done.8 = bf16[1,2,32,1024]{3,2,1,0:T(8,128)(2,1)S(1)} collective-permute-done((bf16[1,2,32,1024]{3,2,1,0:T(8,128)(2,1)S(1)}, bf16[1,2,32,1024]{3,2,1,0:T(8,128)(2,1)S(1)}, u32[]{:S(2)}, u32[]{:S(2)}) %collective-permute-start.8) | collective-permute-done | bytes 131104 | tf_op jit(solution)/shard_map/ppermute | solution.py:105
  263.3 13.0 %collective-permute-done.6 = bf16[1,1,32,1024]{3,2,1,0:T(8,128)(2,1)S(1)} collective-permute-done((bf16[1,1,32,1024]{3,2,1,0:T(8,128)(2,1)S(1)}, bf16[1,1,32,1024]{3,2,1,0:T(8,128)(2,1)S(1)}, u32[]{:S(2)}, u32[]{:S(2)}) %collective-permute-start.6) | collective-permute-done | bytes 65568 | tf_op jit(solution)/shard_map/ppermute | solution.py:105
  277.9 8.7 %fusion.25 = f32[1024,1024]{1,0:T(8,128)} fusion(bf16[32,49,1024]{2,1,0:T(8,128)(2,1)} %all-to-all-done.2, s32[32,49]{1,0:T(8,128)S(1)} %maximum_bitcast_fusion, pred[32,49]{1,0:T(8,128)(4,1)S(1)} %compare_bitcast_fusion), kind=kOutput, calls=%fused_computation.32 | convolution fusion | flops 3291545600 | bytes 7413408 | tf_op jit(solution)/shard_map/dot_general | solution.py:142
  (76 shorter events, 22.2 us)
Async XLA Ops:
  7.2 22.3 %copy-start = (bf16[1024,1024]{1,0:T(8,128)(2,1)S(1)}, bf16[1024,1024]{1,0:T(8,128)(2,1)}, u32[]{:S(2)}) copy-start(bf16[1024,1024]{1,0:T(8,128)(2,1)} %param.6) | copy-start | bytes 6291460
  35.0 5.3 %copy-start.8 = (s32[3,256,256]{2,1,0:T(8,128)S(1)}, s32[3,256,256]{2,1,0:T(8,128)}, u32[]{:S(2)}) copy-start(s32[3,256,256]{2,1,0:T(8,128)} %param.8) | copy-start | bytes 2359300
  35.0 86.8 %all-to-all-start.1 = ((bf16[32,49,1024]{2,1,0:T(8,128)(2,1)}), bf16[32,49,1024]{2,1,0:T(8,128)(2,1)}, u32[]{:S(2)}, u32[]{:S(2)}) async-start(bf16[32,49,1024]{2,1,0:T(8,128)(2,1)} %fusion.22), calls=%async_computation.1 | async-start | bytes 7340032 | tf_op jit(solution)/shard_map/all_to_all | solution.py:23
  38.7 88.9 %all-gather.3.cloned.1.call-start = ((), (), s32[]{:S(2)}) async-start(), calls=%async_computation.3 | async-start | bytes 2621440 | tf_op jit(solution)/shard_map/all_gather | solution.py:74
  39.4 94.7 %all-gather.5.cloned.1.call-start = ((), (), s32[]{:S(2)}) async-start(), calls=%async_computation.4 | async-start | bytes 2621440 | tf_op jit(solution)/shard_map/all_gather | solution.py:74
  127.6 5.9 %copy-start.6 = (bf16[3,256,1024]{2,1,0:T(8,128)(2,1)}, bf16[3,256,1024]{2,1,0:T(8,128)(2,1)S(1)}, u32[]{:S(2)}) copy-start(bf16[3,256,1024]{2,1,0:T(8,128)(2,1)S(1)} %multiply_convert_fusion.4) | copy-start | bytes 4718596
  146.3 1.4 copy-start.7
  149.5 3.1 %copy-start.3 = (f32[1,16,2,32,1024]{4,3,2,1,0:T(8,128)}, f32[1,16,2,32,1024]{4,3,2,1,0:T(8,128)S(1)}, u32[]{:S(2)}) copy-start(f32[1,16,2,32,1024]{4,3,2,1,0:T(8,128)S(1)} %convolution_bitcast_fusion.1) | copy-start | bytes 12582916
  149.5 4.1 %copy-start.5 = (f32[768,1024]{1,0:T(8,128)S(1)}, f32[768,1024]{1,0:T(8,128)}, u32[]{:S(2)}) copy-start(f32[768,1024]{1,0:T(8,128)} %get-tuple-element.12) | copy-start | bytes 9437188
  152.7 13.0 %collective-permute-start = (f32[1,16,32,1024]{3,2,1,0:T(8,128)}, f32[1,16,32,1024]{3,2,1,0:T(8,128)}, u32[]{:S(2)}, u32[]{:S(2)}) collective-permute-start(f32[1,16,32,1024]{3,2,1,0:T(8,128)} %select_bitcast_fusion.1), channel_id=1, source_target_pairs={{0,1},{1,0},{2,3},{3,2},{4,5},{5,4},{6,7},{7,6},{8,9},{9,8},{10,11... | collective-permute-start | bytes 6291464 | tf_op jit(solution)/shard_map/ppermute | solution.py:105
  160.0 2.8 copy-start.2
  160.0 3.1 %copy-start.9 = (bf16[1024,1024]{1,0:T(8,128)(2,1)S(1)}, bf16[1024,1024]{1,0:T(8,128)(2,1)}, u32[]{:S(2)}) copy-start(bf16[1024,1024]{1,0:T(8,128)(2,1)} %all-gather.3.cloned.1.call-done) | copy-start | bytes 6291460
  162.8 25.9 %collective-permute-start.2 = (f32[1,16,32,1024]{3,2,1,0:T(8,128)}, f32[1,16,32,1024]{3,2,1,0:T(8,128)}, u32[]{:S(2)}, u32[]{:S(2)}) collective-permute-start(f32[1,16,32,1024]{3,2,1,0:T(8,128)} %select_bitcast_fusion), channel_id=1, source_target_pairs={{0,1},{1,0},{2,3},{3,2},{4,5},{5,4},{6,7},{7,6},{8,9},{9,8},{10,11... | collective-permute-start | bytes 6291464 | tf_op jit(solution)/shard_map/ppermute | solution.py:105
  164.9 2.2 copy-start.4
  169.5 14.1 %collective-permute-start.1 = (bf16[1,8,32,1024]{3,2,1,0:T(8,128)(2,1)S(1)}, bf16[1,8,32,1024]{3,2,1,0:T(8,128)(2,1)S(1)}, u32[]{:S(2)}, u32[]{:S(2)}) collective-permute-start(bf16[1,8,32,1024]{3,2,1,0:T(8,128)(2,1)S(1)} %fusion.37), channel_id=1, source_target_pairs={{0,2},{1,3},{2,0},{3,1},{4,6},{5,7},{6,4},{7,5},{8,10},{9,11},{10,... | collective-permute-start | bytes 1572872 | tf_op jit(solution)/shard_map/ppermute | solution.py:105
  183.8 94.0 %all-to-all-start.2 = ((bf16[32,49,1024]{2,1,0:T(8,128)(2,1)}), bf16[32,49,1024]{2,1,0:T(8,128)(2,1)}, u32[]{:S(2)}, u32[]{:S(2)}) async-start(bf16[32,49,1024]{2,1,0:T(8,128)(2,1)} %fusion.19), calls=%async_computation.2 | async-start | bytes 7340032 | tf_op jit(solution)/shard_map/all_to_all | solution.py:23
  193.3 41.8 %collective-permute-start.3 = (bf16[1,8,32,1024]{3,2,1,0:T(8,128)(2,1)}, bf16[1,8,32,1024]{3,2,1,0:T(8,128)(2,1)}, u32[]{:S(2)}, u32[]{:S(2)}) collective-permute-start(bf16[1,8,32,1024]{3,2,1,0:T(8,128)(2,1)} %fusion.38), channel_id=1, source_target_pairs={{0,2},{1,3},{2,0},{3,1},{4,6},{5,7},{6,4},{7,5},{8,10},{9,11},{10,... | collective-permute-start | bytes 1572872 | tf_op jit(solution)/shard_map/ppermute | solution.py:105
  238.7 10.9 %collective-permute-start.4 = (bf16[1,4,32,1024]{3,2,1,0:T(8,128)(2,1)S(1)}, bf16[1,4,32,1024]{3,2,1,0:T(8,128)(2,1)S(1)}, u32[]{:S(2)}, u32[]{:S(2)}) collective-permute-start(bf16[1,4,32,1024]{3,2,1,0:T(8,128)(2,1)S(1)} %fusion.41), channel_id=1, source_target_pairs={{0,4},{1,5},{2,6},{3,7},{4,0},{5,1},{6,2},{7,3},{8,12},{9,13},{10,... | collective-permute-start | bytes 786440 | tf_op jit(solution)/shard_map/ppermute | solution.py:105
  240.2 15.2 %collective-permute-start.7 = (bf16[1,4,32,1024]{3,2,1,0:T(8,128)(2,1)S(1)}, bf16[1,4,32,1024]{3,2,1,0:T(8,128)(2,1)S(1)}, u32[]{:S(2)}, u32[]{:S(2)}) collective-permute-start(bf16[1,4,32,1024]{3,2,1,0:T(8,128)(2,1)S(1)} %fusion.42), channel_id=1, source_target_pairs={{0,4},{1,5},{2,6},{3,7},{4,0},{5,1},{6,2},{7,3},{8,12},{9,13},{10,... | collective-permute-start | bytes 786440 | tf_op jit(solution)/shard_map/ppermute | solution.py:105
  250.9 7.3 %collective-permute-start.5 = (bf16[1,2,32,1024]{3,2,1,0:T(8,128)(2,1)S(1)}, bf16[1,2,32,1024]{3,2,1,0:T(8,128)(2,1)S(1)}, u32[]{:S(2)}, u32[]{:S(2)}) collective-permute-start(bf16[1,2,32,1024]{3,2,1,0:T(8,128)(2,1)S(1)} %fusion.48), channel_id=1, source_target_pairs={{0,8},{1,9},{2,10},{3,11},{4,12},{5,13},{6,14},{7,15},{8,0},{9,1},... | collective-permute-start | bytes 393224 | tf_op jit(solution)/shard_map/ppermute | solution.py:105
  255.6 6.9 %collective-permute-start.8 = (bf16[1,2,32,1024]{3,2,1,0:T(8,128)(2,1)S(1)}, bf16[1,2,32,1024]{3,2,1,0:T(8,128)(2,1)S(1)}, u32[]{:S(2)}, u32[]{:S(2)}) collective-permute-start(bf16[1,2,32,1024]{3,2,1,0:T(8,128)(2,1)S(1)} %fusion.49), channel_id=1, source_target_pairs={{0,8},{1,9},{2,10},{3,11},{4,12},{5,13},{6,14},{7,15},{8,0},{9,1},... | collective-permute-start | bytes 393224 | tf_op jit(solution)/shard_map/ppermute | solution.py:105
  258.3 18.1 %collective-permute-start.6 = (bf16[1,1,32,1024]{3,2,1,0:T(8,128)(2,1)S(1)}, bf16[1,1,32,1024]{3,2,1,0:T(8,128)(2,1)S(1)}, u32[]{:S(2)}, u32[]{:S(2)}) collective-permute-start(bf16[1,1,32,1024]{3,2,1,0:T(8,128)(2,1)S(1)} %fusion.58), channel_id=1, source_target_pairs={{0,16},{1,17},{2,18},{3,19},{4,20},{5,21},{6,22},{7,23},{8,24},{9,... | collective-permute-start | bytes 196616 | tf_op jit(solution)/shard_map/ppermute | solution.py:105
  262.5 14.7 %collective-permute-start.9 = (bf16[1,1,32,1024]{3,2,1,0:T(8,128)(2,1)S(1)}, bf16[1,1,32,1024]{3,2,1,0:T(8,128)(2,1)S(1)}, u32[]{:S(2)}, u32[]{:S(2)}) collective-permute-start(bf16[1,1,32,1024]{3,2,1,0:T(8,128)(2,1)S(1)} %fusion.59), channel_id=1, source_target_pairs={{0,16},{1,17},{2,18},{3,19},{4,20},{5,21},{6,22},{7,23},{8,24},{9,... | collective-permute-start | bytes 196616 | tf_op jit(solution)/shard_map/ppermute | solution.py:105
  277.9 8.7 %copy-start.1 = (bf16[1024,1024]{1,0:T(8,128)(2,1)S(1)}, bf16[1024,1024]{1,0:T(8,128)(2,1)}, u32[]{:S(2)}) copy-start(bf16[1024,1024]{1,0:T(8,128)(2,1)} %param.6) | copy-start | bytes 6291460
Sparse Core Ops, SparseCore 0:
  41.0 45.6 all-gather.2
  88.3 26.6 all-gather.4

commit v8 on v6

--- a/solution.py
+++ b/solution.py
@@ -54,20 +54,30 @@
         (owner[:, None, None] == jnp.arange(shards, dtype=jnp.int32)[:, None])
         & (rank[:, None, None] == jnp.arange(capacity, dtype=jnp.int32))
     ).astype(jnp.bfloat16)
-    inputs = (
-        lax.dot_general(
-            slot_of, answered, (((1, 2), (0, 1)), ((), ())), preferred_element_type=jnp.float32
-        )
-        .astype(jnp.bfloat16)
-        .reshape(groups, width, depth)
-    )
     degree = jnp.sum(incidence_mask, axis=2).astype(jnp.float32)
     normalizer_factor = lax.rsqrt(1.0 + degree)[..., None]
     link = (incidence_mask + jnp.eye(width, dtype=jnp.int32)[None]).astype(jnp.bfloat16)
+    linked_slots = (
+        jnp.einsum(
+            "gij,gjsc->gisc",
+            link,
+            slot_of.reshape(groups, width, shards, capacity),
+            preferred_element_type=jnp.float32,
+        )
+        .astype(jnp.bfloat16)
+        .reshape(count, shards, capacity)
+    )
+    spread_in = lax.dot_general(
+        linked_slots, answered, (((1, 2), (0, 1)), ((), ())), preferred_element_type=jnp.float32
+    )
 
-    def forward_layer(layer_in, weight):
+    def forward_layer(layer_in, weight, spread_done=None):
+        if spread_done is None:
+            spread_done = spread(link, layer_in)
         mixed = (
-            (normalizer_factor * spread(link, layer_in)).astype(jnp.bfloat16).reshape(count, depth)
+            (normalizer_factor * spread_done.reshape(groups, width, depth))
+            .astype(jnp.bfloat16)
+            .reshape(count, depth)
         )
         product = jnp.dot(
             mixed,
@@ -108,7 +118,7 @@
             step *= 2
         return parts[:, 0] / (groups * shards)
 
-    mixed_one, first_matmul_result, whole_one = forward_layer(inputs, weight_one)
+    mixed_one, first_matmul_result, whole_one = forward_layer(None, weight_one, spread_in)
     latent_state = (
         jax.nn.silu(first_matmul_result).astype(jnp.bfloat16).reshape(groups, width, depth)
     )
@@ -129,9 +139,11 @@
     fetched_first = (normalizer_factor * upstream_first.reshape(groups, width, depth)).astype(
         jnp.bfloat16
     )
-    input_grad = spread_back(link, fetched_first).astype(jnp.bfloat16).reshape(count, depth)
     outgoing = lax.dot_general(
-        slot_of, input_grad, (((0,), (0,)), ((), ())), preferred_element_type=jnp.float32
+        linked_slots,
+        fetched_first.reshape(count, depth),
+        (((0,), (0,)), ((), ())),
+        preferred_element_type=jnp.float32,
     ).astype(jnp.bfloat16)
     returned = exchange(outgoing)
     table_grad = lax.dot_general(

time: 270 us -> 270 us (level)
  waiting for transfers between devices: 136 us -> 133 us
    dot_general x2 -> x3, matrix products: 9.66 us -> 13.1 us  [the longest x1 5.93 us: on_device(): lax.dot_general(linked_slots, answered, (((1, 2), (0, 1)), ((), ())), pre...]
    unnamed x25 -> x29, local copies, waits for them, and re-layouts: 5.66 us -> 5.69 us
  transfers between devices with their start and end apart: 14 -> 14, of which waited for: 7 -> 7; matrix products, arithmetic and copies ran while one was open for 10% -> 11% of each run, Pallas kernels for 0% -> 0%
where the time goes in v8:
time: 270 us
  waiting for transfers between devices  133 us (49%)
  matrix products  53.3 us (20%)
  starting transfers between devices  25.2 us (9%)
  local copies, waits for them, and re-layouts  15.1 us (6%)
  between operations  14.5 us (5%)
  blocking collectives  14.3 us (5%)
  other arithmetic  14 us (5%)
    all_to_all x2, waiting for transfers between devices, exchange(): return lax.all_to_all(values, AXES, 0, 0, tiled=True)  78.8 us
    ppermute x10, waiting for transfers between devices, reduce_blocks(): moved = lax.ppermute(send, AXES, [(i, i ^ step) for i in range(shards)])  53.3 us
    ppermute x10, starting transfers between devices, reduce_blocks(): moved = lax.ppermute(send, AXES, [(i, i ^ step) for i in range(shards)])  16.1 us
    all_to_all x1, blocking collectives, exchange(): return lax.all_to_all(values, AXES, 0, 0, tiled=True)  14.3 us
    dot_general x2, matrix products, forward_layer(): jnp.dot(mixed, lax.all_gather(weight, 'fsdp', axis=1, tiled=True), prefer...  12.2 us
    all_to_all x2, starting transfers between devices, exchange(): return lax.all_to_all(values, AXES, 0, 0, tiled=True)  8.79 us
    dot_general x1, matrix products, on_device(): lax.dot_general(picks, returned, (((0, 1), (0, 1)), ((), ())), preferred_...  8.74 us
    dot_general x2, matrix products, back_weight(): lax.dot_general(delta, lax.all_gather(weight, 'fsdp', axis=1, tiled=True)...  7.45 us
  transfers between devices with their start and end apart: 14, of which 7 were waited for; matrix products, arithmetic and copies ran while one was open for 11% of the time, Pallas kernels for 0%

profile of v8, /device:TPU:0, one launch (start us, length us, event | category | flops | bytes accessed | tf_op | source)
XLA Modules:
  0.0 269.6 jit_solution(10243952735749050121)
XLA Ops:
  8.8 1.7 reduce-window.6
  11.6 3.4 %scatter_custom_fusion = s32[1568]{0:T(1024)S(1)} fusion(s32[768]{0:T(1024)S(1)} %fusion.69, s32[768]{0:T(1024)S(1)} %get-tuple-element.5, s32[]{:T(128)} %constant.137.clone.1), kind=kCustom, calls=%fused_computation.127 | custom fusion | bytes 6276 | tf_op jit(solution)/shard_map/scatter | solution.py:44
  15.1 14.3 %all_to_all.19 = s32[32,1,49]{2,1,0:T(1,128)S(1)} all-to-all(s32[32,1,49]{2,1,0:T(1,128)S(1)} %all_to_all.12), channel_id=1, replica_groups=mesh['node'=8,'fsdp'=4] {'node','fsdp'}, dimensions={0} | all-to-all | bytes 12544 | tf_op jit(solution)/shard_map/all_to_all | solution.py:23
  29.5 5.5 %fusion.18 = bf16[32,49,1024]{2,1,0:T(8,128)(2,1)} fusion(s32[32,49]{1,0:T(8,128)S(1)} %maximum_bitcast_fusion, pred[32,49]{1,0:T(8,128)(4,1)S(1)} %compare_bitcast_fusion, bf16[1024,1024]{1,0:T(8,128)(2,1)S(1)} %copy-done), kind=kOutput, calls=%fused_computation.27 | convolution fusion | flops 3293151232 | bytes 5316256 | tf_op jit(solution)/shard_map/dot_general | solution.py:51
  35.0 3.7 %all-to-all-start.1 = ((bf16[32,49,1024]{2,1,0:T(8,128)(2,1)}), bf16[32,49,1024]{2,1,0:T(8,128)(2,1)}, u32[]{:S(2)}, u32[]{:S(2)}) async-start(bf16[32,49,1024]{2,1,0:T(8,128)(2,1)} %fusion.18), calls=%async_computation.1 | async-start | bytes 7340032 | tf_op jit(solution)/shard_map/all_to_all | solution.py:23
  40.5 2.5 fusion.24
  43.0 78.8 %all-to-all-done.1 = bf16[32,49,1024]{2,1,0:T(8,128)(2,1)} async-done(((bf16[32,49,1024]{2,1,0:T(8,128)(2,1)}), bf16[32,49,1024]{2,1,0:T(8,128)(2,1)}, u32[]{:S(2)}, u32[]{:S(2)}) %all-to-all-start.1) | async-done | bytes 3211296 | tf_op jit(solution)/shard_map/all_to_all | solution.py:23
  121.8 5.9 %fusion.15 = bf16[3,256,1024]{2,1,0:T(8,128)(2,1)S(1)} fusion(bf16[3,256,32,49]{1,3,2,0:T(8,128)(2,1)} %fusion.24, bf16[32,49,1024]{2,1,0:T(8,128)(2,1)} %all-to-all-done.1, f32[3,256]{1,0:T(4,128)S(1)} %add_rsqrt_fusion), kind=kOutput, calls=%fused_computation.19 | convolution fusion | flops 2467823616 | bytes 7195648 | tf_op jit(solution)/shard_map/dot_general | solution.py:70
  127.7 5.9 %multiply_convert_fusion.3 = (bf16[768,1024]{1,0:T(8,128)(2,1)S(1)}, f32[768,1024]{1,0:T(8,128)}) fusion(bf16[768,1024]{1,0:T(8,128)(2,1)S(1)} %bitcast.312, bf16[1024,1024]{1,0:T(8,128)(2,1)} %all-gather.3.cloned.1.call-done), kind=kOutput, calls=%fused_computation.23 | convolution fusion | flops 1614544896 | bytes 8388608 | tf_op jit(solution)/shard_map/dot_general | solution.py:82
  134.2 6.3 %fusion.13 = bf16[768,1024]{1,0:T(8,128)(2,1)} fusion(bf16[3,256,1024]{2,1,0:T(8,128)(2,1)} %param.11, bf16[768,1024]{1,0:T(8,128)(2,1)S(1)} %bitcast.301, bf16[1024,1024]{1,0:T(8,128)(2,1)} %all-gather.5.cloned.1.call-done), kind=kOutput, calls=%fused_computation.15 | convolution fusion | flops 1618477056 | bytes 6815744 | tf_op jit(solution)/shard_map/dot_general | solution.py:82
  140.5 2.6 copy.119
  143.1 3.9 %fusion.72 = f32[768,1024]{1,0:T(8,128)S(1)} fusion(bf16[768,1024]{1,0:T(8,128)(2,1)} %fusion.13, bf16[1024,1024]{1,0:T(8,128)(2,1)} %all-gather.5.cloned.1.call-done), kind=kOutput, calls=%fused_computation.135 | convolution fusion | flops 1610612736 | bytes 6815744 | tf_op jit(solution)/shard_map/dot_general | solution.py:90
  151.5 3.6 %fusion.73 = f32[768,1024]{1,0:T(8,128)S(1)} fusion(bf16[768,1024]{1,0:T(8,128)(2,1)S(1)} %fusion.14, bf16[1024,1024]{1,0:T(8,128)(2,1)} %all-gather.3.cloned.1.call-done), kind=kOutput, calls=%fused_computation.136 | convolution fusion | flops 1610612736 | bytes 6815744 | tf_op jit(solution)/shard_map/dot_general | solution.py:90
  155.1 4.7 %bitcast_convert_fusion = bf16[32,49,1024]{2,1,0:T(8,128)(2,1)} fusion(bf16[3,256,32,49]{1,3,2,0:T(8,128)(2,1)S(1)} %copy-done.13, f32[3,256,1024]{2,1,0:T(8,128)S(1)} %bitcast.311, f32[3,256]{1,0:T(4,128)S(1)} %add_rsqrt_fusion), kind=kOutput, calls=%fused_computation.1 | convolution fusion | flops 2469429248 | bytes 8768512 | tf_op jit(solution)/shard_map/dot_general | solution.py:142
  159.8 5.1 %all-to-all-start.2 = ((bf16[32,49,1024]{2,1,0:T(8,128)(2,1)}), bf16[32,49,1024]{2,1,0:T(8,128)(2,1)}, u32[]{:S(2)}, u32[]{:S(2)}) async-start(bf16[32,49,1024]{2,1,0:T(8,128)(2,1)} %bitcast_convert_fusion), calls=%async_computation.2 | async-start | bytes 7340032 | tf_op jit(solution)/shard_map/all_to_all | solution.py:23
  165.0 3.2 %convolution_bitcast_fusion.1 = f32[1,16,2,32,1024]{4,3,2,1,0:T(8,128)S(1)} fusion(bf16[16,2,32,768]{3,2,1,0:T(8,128)(2,1)S(1)} %bitcast.304, bf16[768,1024,1,1]{1,0,3,2:T(8,128)(2,1)} %bitcast.313), kind=kOutput, calls=%fused_computation.29 | convolution fusion | flops 1610612736 | bytes 7340032 | tf_op jit(solution)/shard_map/dot_general | solution.py:98
  168.2 1.8 select_bitcast_fusion.1
  172.3 1.8 convolution_bitcast_fusion
  176.1 3.7 %fusion.28 = f32[1,16,32,1024]{3,2,1,0:T(8,128)S(1)} fusion(f32[1,16,32,1024]{3,2,1,0:T(8,128)} %collective-permute-done, f32[1,16,2,32,1024]{4,3,2,1,0:T(8,128)} %copy-done.4, pred[]{:T(512)S(6)} %eq.133), kind=kLoop, calls=%fused_computation.34 | loop fusion | flops 1048576 | bytes 8388609 | tf_op jit(solution)/shard_map/add | solution.py:117
  179.9 1.6 collective-permute-start.1
  181.5 2.3 bitcast_add_fusion
  184.4 26.9 %collective-permute-done.1 = bf16[1,8,32,1024]{3,2,1,0:T(8,128)(2,1)S(1)} collective-permute-done((bf16[1,8,32,1024]{3,2,1,0:T(8,128)(2,1)S(1)}, bf16[1,8,32,1024]{3,2,1,0:T(8,128)(2,1)S(1)}, u32[]{:S(2)}, u32[]{:S(2)}) %collective-permute-start.1) | collective-permute-done | bytes 524320 | tf_op jit(solution)/shard_map/ppermute | solution.py:116
  211.6 2.0 collective-permute-start.2
  213.7 9.9 %collective-permute-done.6 = bf16[1,8,32,1024]{3,2,1,0:T(8,128)(2,1)S(1)} collective-permute-done((bf16[1,8,32,1024]{3,2,1,0:T(8,128)(2,1)S(1)}, bf16[1,8,32,1024]{3,2,1,0:T(8,128)(2,1)S(1)}, u32[]{:S(2)}, u32[]{:S(2)}) %collective-permute-start.6) | collective-permute-done | bytes 524320 | tf_op jit(solution)/shard_map/ppermute | solution.py:116
  223.8 2.7 %collective-permute-start.7 = (bf16[1,4,32,1024]{3,2,1,0:T(8,128)(2,1)S(1)}, bf16[1,4,32,1024]{3,2,1,0:T(8,128)(2,1)S(1)}, u32[]{:S(2)}, u32[]{:S(2)}) collective-permute-start(bf16[1,4,32,1024]{3,2,1,0:T(8,128)(2,1)S(1)} %fusion.44), channel_id=1, source_target_pairs={{0,4},{1,5},{2,6},{3,7},{4,0},{5,1},{6,2},{7,3},{8,12},{9,13},{10,... | collective-permute-start | bytes 786440 | tf_op jit(solution)/shard_map/ppermute | solution.py:116
  227.9 7.5 %collective-permute-done.7 = bf16[1,4,32,1024]{3,2,1,0:T(8,128)(2,1)S(1)} collective-permute-done((bf16[1,4,32,1024]{3,2,1,0:T(8,128)(2,1)S(1)}, bf16[1,4,32,1024]{3,2,1,0:T(8,128)(2,1)S(1)}, u32[]{:S(2)}, u32[]{:S(2)}) %collective-permute-start.7) | collective-permute-done | bytes 262176 | tf_op jit(solution)/shard_map/ppermute | solution.py:116
  235.5 1.9 collective-permute-start.8
  237.5 2.7 %collective-permute-start.4 = (bf16[1,1,32,1024]{3,2,1,0:T(8,128)(2,1)S(1)}, bf16[1,1,32,1024]{3,2,1,0:T(8,128)(2,1)S(1)}, u32[]{:S(2)}, u32[]{:S(2)}) collective-permute-start(bf16[1,1,32,1024]{3,2,1,0:T(8,128)(2,1)S(1)} %fusion.60), channel_id=1, source_target_pairs={{0,16},{1,17},{2,18},{3,19},{4,20},{5,21},{6,22},{7,23},{8,24},{9,... | collective-permute-start | bytes 196616 | tf_op jit(solution)/shard_map/ppermute | solution.py:116
  240.2 1.7 collective-permute-done.8
  242.0 3.4 %collective-permute-start.9 = (bf16[1,1,32,1024]{3,2,1,0:T(8,128)(2,1)S(1)}, bf16[1,1,32,1024]{3,2,1,0:T(8,128)(2,1)S(1)}, u32[]{:S(2)}, u32[]{:S(2)}) collective-permute-start(bf16[1,1,32,1024]{3,2,1,0:T(8,128)(2,1)S(1)} %fusion.61), channel_id=1, source_target_pairs={{0,16},{1,17},{2,18},{3,19},{4,20},{5,21},{6,22},{7,23},{8,24},{9,... | collective-permute-start | bytes 196616 | tf_op jit(solution)/shard_map/ppermute | solution.py:116
  245.4 7.1 %collective-permute-done.4 = bf16[1,1,32,1024]{3,2,1,0:T(8,128)(2,1)S(1)} collective-permute-done((bf16[1,1,32,1024]{3,2,1,0:T(8,128)(2,1)S(1)}, bf16[1,1,32,1024]{3,2,1,0:T(8,128)(2,1)S(1)}, u32[]{:S(2)}, u32[]{:S(2)}) %collective-permute-start.4) | collective-permute-done | bytes 65568 | tf_op jit(solution)/shard_map/ppermute | solution.py:116
  254.0 8.7 %fusion.21 = f32[1024,1024]{1,0:T(8,128)} fusion(bf16[32,49,1024]{2,1,0:T(8,128)(2,1)} %all-to-all-done.2, s32[32,49]{1,0:T(8,128)S(1)} %maximum_bitcast_fusion, pred[32,49]{1,0:T(8,128)(4,1)S(1)} %compare_bitcast_fusion), kind=kOutput, calls=%fused_computation.30 | convolution fusion | flops 3291545600 | bytes 7413408 | tf_op jit(solution)/shard_map/dot_general | solution.py:149
  (85 shorter events, 18.3 us)
Async XLA Ops:
  7.2 22.3 %copy-start = (bf16[1024,1024]{1,0:T(8,128)(2,1)S(1)}, bf16[1024,1024]{1,0:T(8,128)(2,1)}, u32[]{:S(2)}) copy-start(bf16[1024,1024]{1,0:T(8,128)(2,1)} %param.6) | copy-start | bytes 6291460
  35.0 5.2 %copy-start.11 = (s32[3,256]{1,0:T(4,128)S(1)}, s32[3,256]{1,0:T(4,128)}, u32[]{:S(2)}) copy-start(s32[3,256]{1,0:T(4,128)} %param.7) | copy-start | bytes 9220
  35.0 5.3 %copy-start.10 = (s32[3,256,256]{2,1,0:T(8,128)S(1)}, s32[3,256,256]{2,1,0:T(8,128)}, u32[]{:S(2)}) copy-start(s32[3,256,256]{2,1,0:T(8,128)} %param.8) | copy-start | bytes 2359300
  35.0 86.8 %all-to-all-start.1 = ((bf16[32,49,1024]{2,1,0:T(8,128)(2,1)}), bf16[32,49,1024]{2,1,0:T(8,128)(2,1)}, u32[]{:S(2)}, u32[]{:S(2)}) async-start(bf16[32,49,1024]{2,1,0:T(8,128)(2,1)} %fusion.18), calls=%async_computation.1 | async-start | bytes 7340032 | tf_op jit(solution)/shard_map/all_to_all | solution.py:23
  38.7 89.1 %all-gather.3.cloned.1.call-start = ((), (), s32[]{:S(2)}) async-start(), calls=%async_computation.3 | async-start | bytes 2621440 | tf_op jit(solution)/shard_map/all_gather | solution.py:84
  39.4 94.8 %all-gather.5.cloned.1.call-start = ((), (), s32[]{:S(2)}) async-start(), calls=%async_computation.4 | async-start | bytes 2621440 | tf_op jit(solution)/shard_map/all_gather | solution.py:84
  127.7 5.9 %copy-start.12 = (bf16[3,256,1024]{2,1,0:T(8,128)(2,1)}, bf16[3,256,1024]{2,1,0:T(8,128)(2,1)S(1)}, u32[]{:S(2)}) copy-start(bf16[3,256,1024]{2,1,0:T(8,128)(2,1)S(1)} %fusion.15) | copy-start | bytes 4718596
  134.2 6.3 %copy-start.6 = (bf16[3,256,1024]{2,1,0:T(8,128)(2,1)}, bf16[3,256,1024]{2,1,0:T(8,128)(2,1)S(1)}, u32[]{:S(2)}) copy-start(bf16[3,256,1024]{2,1,0:T(8,128)(2,1)S(1)} %multiply_convert_fusion.2) | copy-start | bytes 4718596
  147.0 1.9 copy-start.5
  151.5 3.6 %copy-start.13 = (bf16[3,256,32,49]{1,3,2,0:T(8,128)(2,1)S(1)}, bf16[3,256,32,49]{1,3,2,0:T(8,128)(2,1)}, u32[]{:S(2)}) copy-start(bf16[3,256,32,49]{1,3,2,0:T(8,128)(2,1)} %fusion.24) | copy-start | bytes 7225348
  159.8 5.1 %copy-start.9 = (bf16[768,1024]{0,1:T(8,128)(2,1)S(1)}, bf16[768,1024]{0,1:T(8,128)(2,1)}, u32[]{:S(2)}) copy-start(bf16[768,1024]{0,1:T(8,128)(2,1)} %copy.104) | copy-start | bytes 4718596
  159.8 94.2 %all-to-all-start.2 = ((bf16[32,49,1024]{2,1,0:T(8,128)(2,1)}), bf16[32,49,1024]{2,1,0:T(8,128)(2,1)}, u32[]{:S(2)}, u32[]{:S(2)}) async-start(bf16[32,49,1024]{2,1,0:T(8,128)(2,1)} %bitcast_convert_fusion), calls=%async_computation.2 | async-start | bytes 7340032 | tf_op jit(solution)/shard_map/all_to_all | solution.py:23
  168.2 3.1 %copy-start.4 = (f32[1,16,2,32,1024]{4,3,2,1,0:T(8,128)}, f32[1,16,2,32,1024]{4,3,2,1,0:T(8,128)S(1)}, u32[]{:S(2)}) copy-start(f32[1,16,2,32,1024]{4,3,2,1,0:T(8,128)S(1)} %convolution_bitcast_fusion.1) | copy-start | bytes 12582916
  168.2 3.1 %copy-start.7 = (bf16[3,256,1024]{2,1,0:T(8,128)(2,1)S(1)}, bf16[3,256,1024]{2,1,0:T(8,128)(2,1)}, u32[]{:S(2)}) copy-start(bf16[3,256,1024]{2,1,0:T(8,128)(2,1)} %copy-done.6) | copy-start | bytes 4718596
  168.2 4.1 %copy-start.8 = (bf16[768,1024]{0,1:T(8,128)(2,1)S(1)}, bf16[768,1024]{0,1:T(8,128)(2,1)}, u32[]{:S(2)}) copy-start(bf16[768,1024]{0,1:T(8,128)(2,1)} %copy.119) | copy-start | bytes 4718596
  171.3 4.7 %collective-permute-start = (f32[1,16,32,1024]{3,2,1,0:T(8,128)}, f32[1,16,32,1024]{3,2,1,0:T(8,128)}, u32[]{:S(2)}, u32[]{:S(2)}) collective-permute-start(f32[1,16,32,1024]{3,2,1,0:T(8,128)} %select_bitcast_fusion.1), channel_id=1, source_target_pairs={{0,1},{1,0},{2,3},{3,2},{4,5},{5,4},{6,7},{7,6},{8,9},{9,8},{10,11... | collective-permute-start | bytes 6291464 | tf_op jit(solution)/shard_map/ppermute | solution.py:116
  174.1 2.0 copy-start.2
  176.0 5.4 %collective-permute-start.5 = (f32[1,16,32,1024]{3,2,1,0:T(8,128)S(1)}, f32[1,16,32,1024]{3,2,1,0:T(8,128)}, u32[]{:S(2)}, u32[]{:S(2)}) collective-permute-start(f32[1,16,32,1024]{3,2,1,0:T(8,128)S(1)} %select_bitcast_fusion), channel_id=1, source_target_pairs={{0,1},{1,0},{2,3},{3,2},{4,5},{5,4},{6,7},{7,6},{8,9},{9,8},{10,11... | collective-permute-start | bytes 6291464 | tf_op jit(solution)/shard_map/ppermute | solution.py:116
  176.1 5.4 %copy-start.3 = (f32[1,16,2,32,1024]{4,3,1,2,0:T(8,128)S(1)}, f32[1,16,2,32,1024]{4,3,1,2,0:T(8,128)}, u32[]{:S(2)}) copy-start(f32[1,16,2,32,1024]{4,3,1,2,0:T(8,128)} %copy-done.2) | copy-start | bytes 12582916
  179.9 31.5 %collective-permute-start.1 = (bf16[1,8,32,1024]{3,2,1,0:T(8,128)(2,1)S(1)}, bf16[1,8,32,1024]{3,2,1,0:T(8,128)(2,1)S(1)}, u32[]{:S(2)}, u32[]{:S(2)}) collective-permute-start(bf16[1,8,32,1024]{3,2,1,0:T(8,128)(2,1)S(1)} %fusion.38), channel_id=1, source_target_pairs={{0,2},{1,3},{2,0},{3,1},{4,6},{5,7},{6,4},{7,5},{8,10},{9,11},{10,... | collective-permute-start | bytes 1572872 | tf_op jit(solution)/shard_map/ppermute | solution.py:116
  183.9 39.7 %collective-permute-start.6 = (bf16[1,8,32,1024]{3,2,1,0:T(8,128)(2,1)S(1)}, bf16[1,8,32,1024]{3,2,1,0:T(8,128)(2,1)S(1)}, u32[]{:S(2)}, u32[]{:S(2)}) collective-permute-start(bf16[1,8,32,1024]{3,2,1,0:T(8,128)(2,1)S(1)} %fusion.39), channel_id=1, source_target_pairs={{0,2},{1,3},{2,0},{3,1},{4,6},{5,7},{6,4},{7,5},{8,10},{9,11},{10,... | collective-permute-start | bytes 1572872 | tf_op jit(solution)/shard_map/ppermute | solution.py:116
  211.6 14.9 %collective-permute-start.2 = (bf16[1,4,32,1024]{3,2,1,0:T(8,128)(2,1)S(1)}, bf16[1,4,32,1024]{3,2,1,0:T(8,128)(2,1)S(1)}, u32[]{:S(2)}, u32[]{:S(2)}) collective-permute-start(bf16[1,4,32,1024]{3,2,1,0:T(8,128)(2,1)S(1)} %fusion.43), channel_id=1, source_target_pairs={{0,4},{1,5},{2,6},{3,7},{4,0},{5,1},{6,2},{7,3},{8,12},{9,13},{10,... | collective-permute-start | bytes 786440 | tf_op jit(solution)/shard_map/ppermute | solution.py:116
  223.8 11.6 %collective-permute-start.7 = (bf16[1,4,32,1024]{3,2,1,0:T(8,128)(2,1)S(1)}, bf16[1,4,32,1024]{3,2,1,0:T(8,128)(2,1)S(1)}, u32[]{:S(2)}, u32[]{:S(2)}) collective-permute-start(bf16[1,4,32,1024]{3,2,1,0:T(8,128)(2,1)S(1)} %fusion.44), channel_id=1, source_target_pairs={{0,4},{1,5},{2,6},{3,7},{4,0},{5,1},{6,2},{7,3},{8,12},{9,13},{10,... | collective-permute-start | bytes 786440 | tf_op jit(solution)/shard_map/ppermute | solution.py:116
  226.7 10.7 %collective-permute-start.3 = (bf16[1,2,32,1024]{3,2,1,0:T(8,128)(2,1)S(1)}, bf16[1,2,32,1024]{3,2,1,0:T(8,128)(2,1)S(1)}, u32[]{:S(2)}, u32[]{:S(2)}) collective-permute-start(bf16[1,2,32,1024]{3,2,1,0:T(8,128)(2,1)S(1)} %fusion.50), channel_id=1, source_target_pairs={{0,8},{1,9},{2,10},{3,11},{4,12},{5,13},{6,14},{7,15},{8,0},{9,1},... | collective-permute-start | bytes 393224 | tf_op jit(solution)/shard_map/ppermute | solution.py:116
  235.5 6.4 %collective-permute-start.8 = (bf16[1,2,32,1024]{3,2,1,0:T(8,128)(2,1)S(1)}, bf16[1,2,32,1024]{3,2,1,0:T(8,128)(2,1)S(1)}, u32[]{:S(2)}, u32[]{:S(2)}) collective-permute-start(bf16[1,2,32,1024]{3,2,1,0:T(8,128)(2,1)S(1)} %fusion.51), channel_id=1, source_target_pairs={{0,8},{1,9},{2,10},{3,11},{4,12},{5,13},{6,14},{7,15},{8,0},{9,1},... | collective-permute-start | bytes 393224 | tf_op jit(solution)/shard_map/ppermute | solution.py:116
  237.5 15.0 %collective-permute-start.4 = (bf16[1,1,32,1024]{3,2,1,0:T(8,128)(2,1)S(1)}, bf16[1,1,32,1024]{3,2,1,0:T(8,128)(2,1)S(1)}, u32[]{:S(2)}, u32[]{:S(2)}) collective-permute-start(bf16[1,1,32,1024]{3,2,1,0:T(8,128)(2,1)S(1)} %fusion.60), channel_id=1, source_target_pairs={{0,16},{1,17},{2,18},{3,19},{4,20},{5,21},{6,22},{7,23},{8,24},{9,... | collective-permute-start | bytes 196616 | tf_op jit(solution)/shard_map/ppermute | solution.py:116
  242.0 11.3 %collective-permute-start.9 = (bf16[1,1,32,1024]{3,2,1,0:T(8,128)(2,1)S(1)}, bf16[1,1,32,1024]{3,2,1,0:T(8,128)(2,1)S(1)}, u32[]{:S(2)}, u32[]{:S(2)}) collective-permute-start(bf16[1,1,32,1024]{3,2,1,0:T(8,128)(2,1)S(1)} %fusion.61), channel_id=1, source_target_pairs={{0,16},{1,17},{2,18},{3,19},{4,20},{5,21},{6,22},{7,23},{8,24},{9,... | collective-permute-start | bytes 196616 | tf_op jit(solution)/shard_map/ppermute | solution.py:116
  254.0 8.7 %copy-start.1 = (bf16[1024,1024]{1,0:T(8,128)(2,1)S(1)}, bf16[1024,1024]{1,0:T(8,128)(2,1)}, u32[]{:S(2)}) copy-start(bf16[1024,1024]{1,0:T(8,128)(2,1)} %param.6) | copy-start | bytes 6291460
Sparse Core Ops, SparseCore 0:
  41.0 45.6 all-gather.2
  88.3 26.6 all-gather.4

commit v9 on v8

--- a/solution.py
+++ b/solution.py
@@ -40,9 +40,11 @@
     one_hot = (owner[:, None] == jnp.arange(shards, dtype=jnp.int32)[None, :]).astype(jnp.int32)
     before = jnp.cumsum(one_hot, axis=0) - one_hot
     rank = jnp.sum(before * one_hot, axis=1)
-    position = owner * capacity + rank
-    requests = jnp.full((shards * capacity,), -1, jnp.int32).at[position].set(within)
-    asked = exchange(requests.reshape(shards, capacity))
+    every_id = lax.all_gather(flat_ids, AXES)
+    mine = (every_id // rows_here == lax.axis_index(AXES)).astype(jnp.int32)
+    order = jnp.cumsum(mine, axis=1) - mine
+    hit = (mine[..., None] > 0) & (order[..., None] == jnp.arange(capacity, dtype=jnp.int32))
+    asked = jnp.sum(jnp.where(hit, (every_id % rows_here + 1)[..., None], 0), axis=1) - 1
     valid = asked >= 0
     safe_rows = jnp.maximum(asked, 0)
     picks = (

time: 270 us -> 296 us (1.096)
  blocking collectives: 14.3 us -> 43.5 us
  local copies, waits for them, and re-layouts: 15.1 us -> 10.7 us
  other arithmetic: 14 us -> 17 us
    all_gather x0 -> x1, blocking collectives: none -> 43.5 us  [on_device(): every_id = lax.all_gather(flat_ids, AXES)]
    all_to_all x1 -> x0, blocking collectives: 14.3 us -> none  [exchange(): return lax.all_to_all(values, AXES, 0, 0, tiled=True)]
    scatter x1 -> x0, local copies, waits for them, and re-layouts: 3.38 us -> none  [on_device(): jnp.full((shards * capacity,), -1, jnp.int32).at[position].set(within)]
where the time goes in v9:
time: 296 us; the launch traced here: 295 us
  waiting for transfers between devices  131 us (44%)
  matrix products  53.3 us (18%)
  blocking collectives  43.5 us (15%)
  starting transfers between devices  25.7 us (9%)
  other arithmetic  17 us (6%)
  between operations  14.5 us (5%)
  local copies, waits for them, and re-layouts  10.7 us (4%)
    all_to_all x2, waiting for transfers between devices, exchange(): return lax.all_to_all(values, AXES, 0, 0, tiled=True)  76.5 us
    ppermute x10, waiting for transfers between devices, reduce_blocks(): moved = lax.ppermute(send, AXES, [(i, i ^ step) for i in range(shards)])  52.9 us
    all_gather x1, blocking collectives, on_device(): every_id = lax.all_gather(flat_ids, AXES)  43.5 us
    ppermute x10, starting transfers between devices, reduce_blocks(): moved = lax.ppermute(send, AXES, [(i, i ^ step) for i in range(shards)])  16.9 us
    dot_general x2, matrix products, forward_layer(): jnp.dot(mixed, lax.all_gather(weight, 'fsdp', axis=1, tiled=True), prefer...  12.2 us
    dot_general x1, matrix products, on_device(): lax.dot_general(picks, returned, (((0, 1), (0, 1)), ((), ())), preferred_...  8.74 us
    all_to_all x2, starting transfers between devices, exchange(): return lax.all_to_all(values, AXES, 0, 0, tiled=True)  8.53 us
    dot_general x2, matrix products, back_weight(): lax.dot_general(delta, lax.all_gather(weight, 'fsdp', axis=1, tiled=True)...  7.45 us
  transfers between devices with their start and end apart: 14, of which 7 were waited for; matrix products, arithmetic and copies ran while one was open for 11% of the time, Pallas kernels for 0%

profile of v9, /device:TPU:0, one launch (start us, length us, event | category | flops | bytes accessed | tf_op | source)
XLA Modules:
  0.0 295.3 jit_solution(11694057658334982064)
XLA Ops:
  8.0 43.5 %all-gather = s32[32,1,768]{2,1,0:T(1,128)S(1)} all-gather(s32[1,1,768]{2,1,0:T(1,128)S(1)} %reshape.754), channel_id=1, replica_groups=mesh['node'=8,'fsdp'=4] {'node','fsdp'}, dimensions={0}, use_global_device_ids=true | all-gather | bytes 101376 | tf_op jit(solution)/shard_map/all_gather | solution.py:43
  51.6 1.7 reduce-window.14
  55.0 5.5 %fusion.19 = bf16[32,49,1024]{2,1,0:T(8,128)(2,1)} fusion(s32[32,49]{1,0:T(8,128)S(1)} %add_maximum_fusion, pred[32,49]{1,0:T(8,128)(4,1)S(1)} %add_compare_fusion, bf16[1024,1024]{1,0:T(8,128)(2,1)S(1)} %copy-done), kind=kOutput, calls=%fused_computation.29 | convolution fusion | flops 3293151232 | bytes 5316256 | tf_op jit(solution)/shard_map/dot_general | solution.py:53
  60.5 3.7 %all-to-all-start = ((bf16[32,49,1024]{2,1,0:T(8,128)(2,1)}), bf16[32,49,1024]{2,1,0:T(8,128)(2,1)}, u32[]{:S(2)}, u32[]{:S(2)}) async-start(bf16[32,49,1024]{2,1,0:T(8,128)(2,1)} %fusion.19), calls=%async_computation | async-start | bytes 7340032 | tf_op jit(solution)/shard_map/all_to_all | solution.py:23
  65.8 1.7 reduce-window.16
  68.3 2.5 fusion.25
  70.8 76.5 %all-to-all-done = bf16[32,49,1024]{2,1,0:T(8,128)(2,1)} async-done(((bf16[32,49,1024]{2,1,0:T(8,128)(2,1)}), bf16[32,49,1024]{2,1,0:T(8,128)(2,1)}, u32[]{:S(2)}, u32[]{:S(2)}) %all-to-all-start) | async-done | bytes 3211296 | tf_op jit(solution)/shard_map/all_to_all | solution.py:23
  147.3 5.9 %fusion.16 = bf16[3,256,1024]{2,1,0:T(8,128)(2,1)S(1)} fusion(bf16[3,256,32,49]{1,3,2,0:T(8,128)(2,1)} %fusion.25, bf16[32,49,1024]{2,1,0:T(8,128)(2,1)} %all-to-all-done, f32[3,256]{1,0:T(4,128)S(1)} %add_rsqrt_fusion), kind=kOutput, calls=%fused_computation.21 | convolution fusion | flops 2467823616 | bytes 7195648 | tf_op jit(solution)/shard_map/dot_general | solution.py:72
  153.3 5.9 %multiply_convert_fusion.3 = (bf16[768,1024]{1,0:T(8,128)(2,1)S(1)}, f32[768,1024]{1,0:T(8,128)}) fusion(bf16[768,1024]{1,0:T(8,128)(2,1)S(1)} %bitcast.337, bf16[1024,1024]{1,0:T(8,128)(2,1)} %all-gather.4.cloned.1.call-done), kind=kOutput, calls=%fused_computation.25 | convolution fusion | flops 1614544896 | bytes 8388608 | tf_op jit(solution)/shard_map/dot_general | solution.py:84
  159.8 6.3 %fusion.14 = bf16[768,1024]{1,0:T(8,128)(2,1)} fusion(bf16[3,256,1024]{2,1,0:T(8,128)(2,1)} %param.11, bf16[768,1024]{1,0:T(8,128)(2,1)S(1)} %bitcast.329, bf16[1024,1024]{1,0:T(8,128)(2,1)} %all-gather.6.cloned.1.call-done), kind=kOutput, calls=%fused_computation.17 | convolution fusion | flops 1618477056 | bytes 6815744 | tf_op jit(solution)/shard_map/dot_general | solution.py:84
  166.1 2.6 copy.155
  168.7 3.9 %fusion.76 = f32[768,1024]{1,0:T(8,128)S(1)} fusion(bf16[768,1024]{1,0:T(8,128)(2,1)} %fusion.14, bf16[1024,1024]{1,0:T(8,128)(2,1)} %all-gather.6.cloned.1.call-done), kind=kOutput, calls=%fused_computation.146 | convolution fusion | flops 1610612736 | bytes 6815744 | tf_op jit(solution)/shard_map/dot_general | solution.py:92
  175.5 1.8 copy.140
  177.3 3.6 %fusion.77 = f32[768,1024]{1,0:T(8,128)S(1)} fusion(bf16[768,1024]{1,0:T(8,128)(2,1)S(1)} %fusion.15, bf16[1024,1024]{1,0:T(8,128)(2,1)} %all-gather.4.cloned.1.call-done), kind=kOutput, calls=%fused_computation.147 | convolution fusion | flops 1610612736 | bytes 6815744 | tf_op jit(solution)/shard_map/dot_general | solution.py:92
  180.9 4.8 %bitcast_convert_fusion = bf16[32,49,1024]{2,1,0:T(8,128)(2,1)} fusion(bf16[3,256,32,49]{1,3,2,0:T(8,128)(2,1)S(1)} %copy-done.13, f32[3,256,1024]{2,1,0:T(8,128)S(1)} %bitcast.336, f32[3,256]{1,0:T(4,128)S(1)} %add_rsqrt_fusion), kind=kOutput, calls=%fused_computation | convolution fusion | flops 2469429248 | bytes 8768512 | tf_op jit(solution)/shard_map/dot_general | solution.py:144
  185.6 4.9 %all-to-all-start.1 = ((bf16[32,49,1024]{2,1,0:T(8,128)(2,1)}), bf16[32,49,1024]{2,1,0:T(8,128)(2,1)}, u32[]{:S(2)}, u32[]{:S(2)}) async-start(bf16[32,49,1024]{2,1,0:T(8,128)(2,1)} %bitcast_convert_fusion), calls=%async_computation.1 | async-start | bytes 7340032 | tf_op jit(solution)/shard_map/all_to_all | solution.py:23
  190.5 3.2 %convolution_bitcast_fusion.1 = f32[1,16,2,32,1024]{4,3,2,1,0:T(8,128)S(1)} fusion(bf16[16,2,32,768]{3,2,1,0:T(8,128)(2,1)S(1)} %bitcast.332, bf16[768,1024,1,1]{1,0,3,2:T(8,128)(2,1)} %bitcast.338), kind=kOutput, calls=%fused_computation.31 | convolution fusion | flops 1610612736 | bytes 7340032 | tf_op jit(solution)/shard_map/dot_general | solution.py:100
  193.8 1.8 select_bitcast_fusion.1
  197.8 1.8 convolution_bitcast_fusion
  201.8 3.7 %fusion.29 = f32[1,16,32,1024]{3,2,1,0:T(8,128)S(1)} fusion(f32[1,16,32,1024]{3,2,1,0:T(8,128)} %collective-permute-done, f32[1,16,2,32,1024]{4,3,2,1,0:T(8,128)} %copy-done.4, pred[]{:T(512)S(6)} %eq.157), kind=kLoop, calls=%fused_computation.36 | loop fusion | flops 1048576 | bytes 8388609 | tf_op jit(solution)/shard_map/add | solution.py:119
  205.6 1.7 collective-permute-start.1
  207.3 2.3 bitcast_add_fusion
  210.1 26.8 %collective-permute-done.1 = bf16[1,8,32,1024]{3,2,1,0:T(8,128)(2,1)S(1)} collective-permute-done((bf16[1,8,32,1024]{3,2,1,0:T(8,128)(2,1)S(1)}, bf16[1,8,32,1024]{3,2,1,0:T(8,128)(2,1)S(1)}, u32[]{:S(2)}, u32[]{:S(2)}) %collective-permute-start.1) | collective-permute-done | bytes 524320 | tf_op jit(solution)/shard_map/ppermute | solution.py:118
  237.3 2.2 collective-permute-start.2
  239.5 9.9 %collective-permute-done.6 = bf16[1,8,32,1024]{3,2,1,0:T(8,128)(2,1)S(1)} collective-permute-done((bf16[1,8,32,1024]{3,2,1,0:T(8,128)(2,1)S(1)}, bf16[1,8,32,1024]{3,2,1,0:T(8,128)(2,1)S(1)}, u32[]{:S(2)}, u32[]{:S(2)}) %collective-permute-start.6) | collective-permute-done | bytes 524320 | tf_op jit(solution)/shard_map/ppermute | solution.py:118
  249.7 2.7 collective-permute-start.7
  253.7 7.4 %collective-permute-done.7 = bf16[1,4,32,1024]{3,2,1,0:T(8,128)(2,1)S(1)} collective-permute-done((bf16[1,4,32,1024]{3,2,1,0:T(8,128)(2,1)S(1)}, bf16[1,4,32,1024]{3,2,1,0:T(8,128)(2,1)S(1)}, u32[]{:S(2)}, u32[]{:S(2)}) %collective-permute-start.7) | collective-permute-done | bytes 262176 | tf_op jit(solution)/shard_map/ppermute | solution.py:118
  261.3 1.9 collective-permute-start.8
  263.3 2.8 collective-permute-start.4
  267.7 3.5 %collective-permute-start.9 = (bf16[1,1,32,1024]{3,2,1,0:T(8,128)(2,1)S(1)}, bf16[1,1,32,1024]{3,2,1,0:T(8,128)(2,1)S(1)}, u32[]{:S(2)}, u32[]{:S(2)}) collective-permute-start(bf16[1,1,32,1024]{3,2,1,0:T(8,128)(2,1)S(1)} %fusion.66), channel_id=1, source_target_pairs={{0,16},{1,17},{2,18},{3,19},{4,20},{5,21},{6,22},{7,23},{8,24},{9,... | collective-permute-start | bytes 196616 | tf_op jit(solution)/shard_map/ppermute | solution.py:118
  271.2 7.0 %collective-permute-done.4 = bf16[1,1,32,1024]{3,2,1,0:T(8,128)(2,1)S(1)} collective-permute-done((bf16[1,1,32,1024]{3,2,1,0:T(8,128)(2,1)S(1)}, bf16[1,1,32,1024]{3,2,1,0:T(8,128)(2,1)S(1)}, u32[]{:S(2)}, u32[]{:S(2)}) %collective-permute-start.4) | collective-permute-done | bytes 65568 | tf_op jit(solution)/shard_map/ppermute | solution.py:118
  279.7 8.7 %fusion.22 = f32[1024,1024]{1,0:T(8,128)} fusion(bf16[32,49,1024]{2,1,0:T(8,128)(2,1)} %all-to-all-done.1, s32[32,49]{1,0:T(8,128)S(1)} %add_maximum_fusion, pred[32,49]{1,0:T(8,128)(4,1)S(1)} %add_compare_fusion), kind=kOutput, calls=%fused_computation.32 | convolution fusion | flops 3291545600 | bytes 7413408 | tf_op jit(solution)/shard_map/dot_general | solution.py:151
  (90 shorter events, 18.6 us)
Async XLA Ops:
  7.2 47.9 %copy-start = (bf16[1024,1024]{1,0:T(8,128)(2,1)S(1)}, bf16[1024,1024]{1,0:T(8,128)(2,1)}, u32[]{:S(2)}) copy-start(bf16[1024,1024]{1,0:T(8,128)(2,1)} %param.6) | copy-start | bytes 6291460
  60.5 5.2 %copy-start.11 = (s32[3,256]{1,0:T(4,128)S(1)}, s32[3,256]{1,0:T(4,128)}, u32[]{:S(2)}) copy-start(s32[3,256]{1,0:T(4,128)} %param.7) | copy-start | bytes 9220
  60.5 86.8 %all-to-all-start = ((bf16[32,49,1024]{2,1,0:T(8,128)(2,1)}), bf16[32,49,1024]{2,1,0:T(8,128)(2,1)}, u32[]{:S(2)}, u32[]{:S(2)}) async-start(bf16[32,49,1024]{2,1,0:T(8,128)(2,1)} %fusion.19), calls=%async_computation | async-start | bytes 7340032 | tf_op jit(solution)/shard_map/all_to_all | solution.py:23
  64.2 3.8 %copy-start.10 = (s32[3,256,256]{2,1,0:T(8,128)S(1)}, s32[3,256,256]{2,1,0:T(8,128)}, u32[]{:S(2)}) copy-start(s32[3,256,256]{2,1,0:T(8,128)} %param.8) | copy-start | bytes 2359300
  64.2 89.0 %all-gather.4.cloned.1.call-start = ((), (), s32[]{:S(2)}) async-start(), calls=%async_computation.2 | async-start | bytes 2621440 | tf_op jit(solution)/shard_map/all_gather | solution.py:86
  65.0 94.8 %all-gather.6.cloned.1.call-start = ((), (), s32[]{:S(2)}) async-start(), calls=%async_computation.3 | async-start | bytes 2621440 | tf_op jit(solution)/shard_map/all_gather | solution.py:86
  153.2 5.9 %copy-start.12 = (bf16[3,256,1024]{2,1,0:T(8,128)(2,1)}, bf16[3,256,1024]{2,1,0:T(8,128)(2,1)S(1)}, u32[]{:S(2)}) copy-start(bf16[3,256,1024]{2,1,0:T(8,128)(2,1)S(1)} %fusion.16) | copy-start | bytes 4718596
  159.7 6.4 %copy-start.6 = (bf16[3,256,1024]{2,1,0:T(8,128)(2,1)}, bf16[3,256,1024]{2,1,0:T(8,128)(2,1)S(1)}, u32[]{:S(2)}) copy-start(bf16[3,256,1024]{2,1,0:T(8,128)(2,1)S(1)} %multiply_convert_fusion.2) | copy-start | bytes 4718596
  172.6 1.9 copy-start.5
  177.3 3.6 %copy-start.13 = (bf16[3,256,32,49]{1,3,2,0:T(8,128)(2,1)S(1)}, bf16[3,256,32,49]{1,3,2,0:T(8,128)(2,1)}, u32[]{:S(2)}) copy-start(bf16[3,256,32,49]{1,3,2,0:T(8,128)(2,1)} %fusion.25) | copy-start | bytes 7225348
  185.6 4.9 %copy-start.9 = (bf16[768,1024]{0,1:T(8,128)(2,1)S(1)}, bf16[768,1024]{0,1:T(8,128)(2,1)}, u32[]{:S(2)}) copy-start(bf16[768,1024]{0,1:T(8,128)(2,1)} %copy.140) | copy-start | bytes 4718596
  185.6 94.1 %all-to-all-start.1 = ((bf16[32,49,1024]{2,1,0:T(8,128)(2,1)}), bf16[32,49,1024]{2,1,0:T(8,128)(2,1)}, u32[]{:S(2)}, u32[]{:S(2)}) async-start(bf16[32,49,1024]{2,1,0:T(8,128)(2,1)} %bitcast_convert_fusion), calls=%async_computation.1 | async-start | bytes 7340032 | tf_op jit(solution)/shard_map/all_to_all | solution.py:23
  193.7 3.1 %copy-start.4 = (f32[1,16,2,32,1024]{4,3,2,1,0:T(8,128)}, f32[1,16,2,32,1024]{4,3,2,1,0:T(8,128)S(1)}, u32[]{:S(2)}) copy-start(f32[1,16,2,32,1024]{4,3,2,1,0:T(8,128)S(1)} %convolution_bitcast_fusion.1) | copy-start | bytes 12582916
  193.7 3.3 %copy-start.7 = (bf16[3,256,1024]{2,1,0:T(8,128)(2,1)S(1)}, bf16[3,256,1024]{2,1,0:T(8,128)(2,1)}, u32[]{:S(2)}) copy-start(bf16[3,256,1024]{2,1,0:T(8,128)(2,1)} %copy-done.6) | copy-start | bytes 4718596
  193.7 4.1 %copy-start.8 = (bf16[768,1024]{0,1:T(8,128)(2,1)S(1)}, bf16[768,1024]{0,1:T(8,128)(2,1)}, u32[]{:S(2)}) copy-start(bf16[768,1024]{0,1:T(8,128)(2,1)} %copy.155) | copy-start | bytes 4718596
  196.9 4.9 %collective-permute-start = (f32[1,16,32,1024]{3,2,1,0:T(8,128)}, f32[1,16,32,1024]{3,2,1,0:T(8,128)}, u32[]{:S(2)}, u32[]{:S(2)}) collective-permute-start(f32[1,16,32,1024]{3,2,1,0:T(8,128)} %select_bitcast_fusion.1), channel_id=1, source_target_pairs={{0,1},{1,0},{2,3},{3,2},{4,5},{5,4},{6,7},{7,6},{8,9},{9,8},{10,11... | collective-permute-start | bytes 6291464 | tf_op jit(solution)/shard_map/ppermute | solution.py:118
  199.6 2.0 copy-start.2
  201.6 5.7 %collective-permute-start.5 = (f32[1,16,32,1024]{3,2,1,0:T(8,128)S(1)}, f32[1,16,32,1024]{3,2,1,0:T(8,128)}, u32[]{:S(2)}, u32[]{:S(2)}) collective-permute-start(f32[1,16,32,1024]{3,2,1,0:T(8,128)S(1)} %select_bitcast_fusion), channel_id=1, source_target_pairs={{0,1},{1,0},{2,3},{3,2},{4,5},{5,4},{6,7},{7,6},{8,9},{9,8},{10,11... | collective-permute-start | bytes 6291464 | tf_op jit(solution)/shard_map/ppermute | solution.py:118
  201.8 5.5 %copy-start.3 = (f32[1,16,2,32,1024]{4,3,1,2,0:T(8,128)S(1)}, f32[1,16,2,32,1024]{4,3,1,2,0:T(8,128)}, u32[]{:S(2)}) copy-start(f32[1,16,2,32,1024]{4,3,1,2,0:T(8,128)} %copy-done.2) | copy-start | bytes 12582916
  205.6 31.4 %collective-permute-start.1 = (bf16[1,8,32,1024]{3,2,1,0:T(8,128)(2,1)S(1)}, bf16[1,8,32,1024]{3,2,1,0:T(8,128)(2,1)S(1)}, u32[]{:S(2)}, u32[]{:S(2)}) collective-permute-start(bf16[1,8,32,1024]{3,2,1,0:T(8,128)(2,1)S(1)} %fusion.39), channel_id=1, source_target_pairs={{0,2},{1,3},{2,0},{3,1},{4,6},{5,7},{6,4},{7,5},{8,10},{9,11},{10,... | collective-permute-start | bytes 1572872 | tf_op jit(solution)/shard_map/ppermute | solution.py:118
  209.7 39.7 %collective-permute-start.6 = (bf16[1,8,32,1024]{3,2,1,0:T(8,128)(2,1)S(1)}, bf16[1,8,32,1024]{3,2,1,0:T(8,128)(2,1)S(1)}, u32[]{:S(2)}, u32[]{:S(2)}) collective-permute-start(bf16[1,8,32,1024]{3,2,1,0:T(8,128)(2,1)S(1)} %fusion.40), channel_id=1, source_target_pairs={{0,2},{1,3},{2,0},{3,1},{4,6},{5,7},{6,4},{7,5},{8,10},{9,11},{10,... | collective-permute-start | bytes 1572872 | tf_op jit(solution)/shard_map/ppermute | solution.py:118
  237.3 15.1 %collective-permute-start.2 = (bf16[1,4,32,1024]{3,2,1,0:T(8,128)(2,1)S(1)}, bf16[1,4,32,1024]{3,2,1,0:T(8,128)(2,1)S(1)}, u32[]{:S(2)}, u32[]{:S(2)}) collective-permute-start(bf16[1,4,32,1024]{3,2,1,0:T(8,128)(2,1)S(1)} %fusion.44), channel_id=1, source_target_pairs={{0,4},{1,5},{2,6},{3,7},{4,0},{5,1},{6,2},{7,3},{8,12},{9,13},{10,... | collective-permute-start | bytes 786440 | tf_op jit(solution)/shard_map/ppermute | solution.py:118
  249.7 11.5 %collective-permute-start.7 = (bf16[1,4,32,1024]{3,2,1,0:T(8,128)(2,1)S(1)}, bf16[1,4,32,1024]{3,2,1,0:T(8,128)(2,1)S(1)}, u32[]{:S(2)}, u32[]{:S(2)}) collective-permute-start(bf16[1,4,32,1024]{3,2,1,0:T(8,128)(2,1)S(1)} %fusion.45), channel_id=1, source_target_pairs={{0,4},{1,5},{2,6},{3,7},{4,0},{5,1},{6,2},{7,3},{8,12},{9,13},{10,... | collective-permute-start | bytes 786440 | tf_op jit(solution)/shard_map/ppermute | solution.py:118
  252.5 10.7 %collective-permute-start.3 = (bf16[1,2,32,1024]{3,2,1,0:T(8,128)(2,1)S(1)}, bf16[1,2,32,1024]{3,2,1,0:T(8,128)(2,1)S(1)}, u32[]{:S(2)}, u32[]{:S(2)}) collective-permute-start(bf16[1,2,32,1024]{3,2,1,0:T(8,128)(2,1)S(1)} %fusion.51), channel_id=1, source_target_pairs={{0,8},{1,9},{2,10},{3,11},{4,12},{5,13},{6,14},{7,15},{8,0},{9,1},... | collective-permute-start | bytes 393224 | tf_op jit(solution)/shard_map/ppermute | solution.py:118
  261.3 6.4 %collective-permute-start.8 = (bf16[1,2,32,1024]{3,2,1,0:T(8,128)(2,1)S(1)}, bf16[1,2,32,1024]{3,2,1,0:T(8,128)(2,1)S(1)}, u32[]{:S(2)}, u32[]{:S(2)}) collective-permute-start(bf16[1,2,32,1024]{3,2,1,0:T(8,128)(2,1)S(1)} %fusion.52), channel_id=1, source_target_pairs={{0,8},{1,9},{2,10},{3,11},{4,12},{5,13},{6,14},{7,15},{8,0},{9,1},... | collective-permute-start | bytes 393224 | tf_op jit(solution)/shard_map/ppermute | solution.py:118
  263.3 14.9 %collective-permute-start.4 = (bf16[1,1,32,1024]{3,2,1,0:T(8,128)(2,1)S(1)}, bf16[1,1,32,1024]{3,2,1,0:T(8,128)(2,1)S(1)}, u32[]{:S(2)}, u32[]{:S(2)}) collective-permute-start(bf16[1,1,32,1024]{3,2,1,0:T(8,128)(2,1)S(1)} %fusion.65), channel_id=1, source_target_pairs={{0,16},{1,17},{2,18},{3,19},{4,20},{5,21},{6,22},{7,23},{8,24},{9,... | collective-permute-start | bytes 196616 | tf_op jit(solution)/shard_map/ppermute | solution.py:118
  267.7 11.3 %collective-permute-start.9 = (bf16[1,1,32,1024]{3,2,1,0:T(8,128)(2,1)S(1)}, bf16[1,1,32,1024]{3,2,1,0:T(8,128)(2,1)S(1)}, u32[]{:S(2)}, u32[]{:S(2)}) collective-permute-start(bf16[1,1,32,1024]{3,2,1,0:T(8,128)(2,1)S(1)} %fusion.66), channel_id=1, source_target_pairs={{0,16},{1,17},{2,18},{3,19},{4,20},{5,21},{6,22},{7,23},{8,24},{9,... | collective-permute-start | bytes 196616 | tf_op jit(solution)/shard_map/ppermute | solution.py:118
  279.7 8.7 %copy-start.1 = (bf16[1024,1024]{1,0:T(8,128)(2,1)S(1)}, bf16[1024,1024]{1,0:T(8,128)(2,1)}, u32[]{:S(2)}) copy-start(bf16[1024,1024]{1,0:T(8,128)(2,1)} %param.6) | copy-start | bytes 6291460
Sparse Core Ops, SparseCore 0:
  66.6 45.6 all-gather.3
  113.8 26.6 all-gather.5

commit v10 on v8

--- a/solution.py
+++ b/solution.py
@@ -23,7 +23,7 @@
     return lax.all_to_all(values, AXES, 0, 0, tiled=True)
 
 
-def on_device(
+def step_body(
     feature_table, vertex_labels, incidence_mask, weight_one, weight_two, final_layer_sensitivity
 ):
     groups, width = vertex_labels.shape
@@ -111,18 +111,17 @@
             upper = (me // step) % 2 == 1
             keep = jnp.where(upper, pair[:, :, 1], pair[:, :, 0])
             send = jnp.where(upper, pair[:, :, 0], pair[:, :, 1])
-            if step > 1:
-                send = send.astype(jnp.bfloat16)
+            send = send.astype(jnp.bfloat16)
             moved = lax.ppermute(send, AXES, [(i, i ^ step) for i in range(shards)])
             parts = keep + moved.astype(jnp.float32)
             step *= 2
         return parts[:, 0] / (groups * shards)
 
-    mixed_one, first_matmul_result, whole_one = forward_layer(None, weight_one, spread_in)
+    mixed_one, first_matmul_result, _ = forward_layer(None, weight_one, spread_in)
     latent_state = (
         jax.nn.silu(first_matmul_result).astype(jnp.bfloat16).reshape(groups, width, depth)
     )
-    mixed_two, product_two, whole_two = forward_layer(latent_state, weight_two)
+    mixed_two, product_two, _ = forward_layer(latent_state, weight_two)
     delta_two = (
         final_layer_sensitivity.reshape(count, depth).astype(jnp.float32) * swish_slope(product_two)
     ).astype(jnp.bfloat16)
@@ -164,7 +163,7 @@
         P(AXES, None, None),
     )
     return jax.shard_map(
-        on_device,
+        step_body,
         mesh=mesh,
         in_specs=placed,
         out_specs=(P(AXES, None), P(None, AXES), P(None, AXES)),

time: 270 us -> 265 us (0.981)
  waiting for transfers between devices: 133 us -> 128 us
    ppermute x10, waiting for transfers between devices: 53.3 us -> 48.4 us  [reduce_blocks(): moved = lax.ppermute(send, AXES, [(i, i ^ step) for i in range(shards)])]
    convert_element_type x8 -> x10, other arithmetic: 0.38 us -> 3.12 us  [reduce_blocks(): send = send.astype(jnp.bfloat16)]
    unnamed x29 -> x31, local copies, waits for them, and re-layouts: 5.69 us -> 4.32 us
  transfers between devices with their start and end apart: 14 -> 14, of which waited for: 7 -> 7; matrix products, arithmetic and copies ran while one was open for 11% -> 13% of each run, Pallas kernels for 0% -> 0%
where the time goes in v10:
time: 265 us; the launch traced here: 264 us
  waiting for transfers between devices  128 us (48%)
  matrix products  52.8 us (20%)
  starting transfers between devices  27.5 us (10%)
  between operations  14.5 us (5%)
  blocking collectives  14.3 us (5%)
  other arithmetic  13.6 us (5%)
  local copies, waits for them, and re-layouts  13.1 us (5%)
    all_to_all x2, waiting for transfers between devices, exchange(): return lax.all_to_all(values, AXES, 0, 0, tiled=True)  78.8 us
    ppermute x10, waiting for transfers between devices, reduce_blocks(): moved = lax.ppermute(send, AXES, [(i, i ^ step) for i in range(shards)])  48.4 us
    ppermute x10, starting transfers between devices, reduce_blocks(): moved = lax.ppermute(send, AXES, [(i, i ^ step) for i in range(shards)])  18.7 us
    all_to_all x1, blocking collectives, exchange(): return lax.all_to_all(values, AXES, 0, 0, tiled=True)  14.3 us
    dot_general x2, matrix products, forward_layer(): jnp.dot(mixed, lax.all_gather(weight, 'fsdp', axis=1, tiled=True), prefer...  11 us
    dot_general x1, matrix products, step_body(): lax.dot_general(picks, returned, (((0, 1), (0, 1)), ((), ())), preferred_...  8.74 us
    all_to_all x2, starting transfers between devices, exchange(): return lax.all_to_all(values, AXES, 0, 0, tiled=True)  8.55 us
    dot_general x2, matrix products, grad_parts(): lax.dot_general(delta.reshape(count, shards, depth // shards), mixed, (((...  7.61 us
  transfers between devices with their start and end apart: 14, of which 7 were waited for; matrix products, arithmetic and copies ran while one was open for 13% of the time, Pallas kernels for 0%

profile of v10, /device:TPU:0, one launch (start us, length us, event | category | flops | bytes accessed | tf_op | source)
XLA Modules:
  0.0 264.2 jit_solution(16177312815735720257)
XLA Ops:
  8.8 1.7 reduce-window.6
  11.6 3.4 %scatter_custom_fusion = s32[1568]{0:T(1024)S(1)} fusion(s32[768]{0:T(1024)S(1)} %fusion.71, s32[768]{0:T(1024)S(1)} %get-tuple-element.5, s32[]{:T(128)} %constant.137.clone.1), kind=kCustom, calls=%fused_computation.129 | custom fusion | bytes 6276 | tf_op jit(solution)/shard_map/scatter | solution.py:44
  15.1 14.3 %all_to_all.19 = s32[32,1,49]{2,1,0:T(1,128)S(1)} all-to-all(s32[32,1,49]{2,1,0:T(1,128)S(1)} %all_to_all.12), channel_id=1, replica_groups=mesh['node'=8,'fsdp'=4] {'node','fsdp'}, dimensions={0} | all-to-all | bytes 12544 | tf_op jit(solution)/shard_map/all_to_all | solution.py:23
  29.5 5.5 %fusion.18 = bf16[32,49,1024]{2,1,0:T(8,128)(2,1)} fusion(s32[32,49]{1,0:T(8,128)S(1)} %maximum_bitcast_fusion, pred[32,49]{1,0:T(8,128)(4,1)S(1)} %compare_bitcast_fusion, bf16[1024,1024]{1,0:T(8,128)(2,1)S(1)} %copy-done), kind=kOutput, calls=%fused_computation.27 | convolution fusion | flops 3293151232 | bytes 5316256 | tf_op jit(solution)/shard_map/dot_general | solution.py:51
  35.0 3.7 %all-to-all-start.1 = ((bf16[32,49,1024]{2,1,0:T(8,128)(2,1)}), bf16[32,49,1024]{2,1,0:T(8,128)(2,1)}, u32[]{:S(2)}, u32[]{:S(2)}) async-start(bf16[32,49,1024]{2,1,0:T(8,128)(2,1)} %fusion.18), calls=%async_computation.1 | async-start | bytes 7340032 | tf_op jit(solution)/shard_map/all_to_all | solution.py:23
  40.5 2.5 fusion.24
  43.0 78.8 %all-to-all-done.1 = bf16[32,49,1024]{2,1,0:T(8,128)(2,1)} async-done(((bf16[32,49,1024]{2,1,0:T(8,128)(2,1)}), bf16[32,49,1024]{2,1,0:T(8,128)(2,1)}, u32[]{:S(2)}, u32[]{:S(2)}) %all-to-all-start.1) | async-done | bytes 3211296 | tf_op jit(solution)/shard_map/all_to_all | solution.py:23
  121.8 5.9 %fusion.15 = bf16[3,256,1024]{2,1,0:T(8,128)(2,1)S(1)} fusion(bf16[3,256,32,49]{1,3,2,0:T(8,128)(2,1)} %fusion.24, bf16[32,49,1024]{2,1,0:T(8,128)(2,1)} %all-to-all-done.1, f32[3,256]{1,0:T(4,128)S(1)} %add_rsqrt_fusion), kind=kOutput, calls=%fused_computation.19 | convolution fusion | flops 2467823616 | bytes 7195648 | tf_op jit(solution)/shard_map/dot_general | solution.py:70
  127.7 5.9 %multiply_convert_fusion.3 = (bf16[768,1024]{1,0:T(8,128)(2,1)S(1)}, f32[768,1024]{1,0:T(8,128)}) fusion(bf16[768,1024]{1,0:T(8,128)(2,1)S(1)} %bitcast.314, bf16[1024,1024]{1,0:T(8,128)(2,1)} %all-gather.3.cloned.1.call-done), kind=kOutput, calls=%fused_computation.23 | convolution fusion | flops 1614544896 | bytes 8388608 | tf_op jit(solution)/shard_map/dot_general | solution.py:82
  134.2 5.2 %fusion.13 = bf16[768,1024]{1,0:T(8,128)(2,1)S(1)} fusion(bf16[3,256,1024]{2,1,0:T(8,128)(2,1)} %param.11, bf16[768,1024]{1,0:T(8,128)(2,1)S(1)} %bitcast.303, bf16[1024,1024]{1,0:T(8,128)(2,1)} %all-gather.5.cloned.1.call-done), kind=kOutput, calls=%fused_computation.15 | convolution fusion | flops 1618477056 | bytes 6815744 | tf_op jit(solution)/shard_map/dot_general | solution.py:82
  139.4 1.8 fusion.74
  144.2 1.9 copy.104
  146.1 3.6 %fusion.75 = f32[768,1024]{1,0:T(8,128)S(1)} fusion(bf16[768,1024]{1,0:T(8,128)(2,1)S(1)} %fusion.14, bf16[1024,1024]{1,0:T(8,128)(2,1)} %all-gather.3.cloned.1.call-done), kind=kOutput, calls=%fused_computation.138 | convolution fusion | flops 1610612736 | bytes 6815744 | tf_op jit(solution)/shard_map/dot_general | solution.py:90
  149.7 4.8 %bitcast_convert_fusion = bf16[32,49,1024]{2,1,0:T(8,128)(2,1)} fusion(bf16[3,256,32,49]{1,3,2,0:T(8,128)(2,1)S(1)} %copy-done.14, f32[3,256,1024]{2,1,0:T(8,128)S(1)} %bitcast.313, f32[3,256]{1,0:T(4,128)S(1)} %add_rsqrt_fusion), kind=kOutput, calls=%fused_computation.1 | convolution fusion | flops 2469429248 | bytes 8768512 | tf_op jit(solution)/shard_map/dot_general | solution.py:141
  154.5 4.9 %all-to-all-start.2 = ((bf16[32,49,1024]{2,1,0:T(8,128)(2,1)}), bf16[32,49,1024]{2,1,0:T(8,128)(2,1)}, u32[]{:S(2)}, u32[]{:S(2)}) async-start(bf16[32,49,1024]{2,1,0:T(8,128)(2,1)} %bitcast_convert_fusion), calls=%async_computation.2 | async-start | bytes 7340032 | tf_op jit(solution)/shard_map/all_to_all | solution.py:23
  159.4 5.8 %convolution_bitcast_fusion.1 = f32[1,16,2,32,1024]{4,3,2,1,0:T(8,128)} fusion(bf16[16,2,32,768]{3,2,1,0:T(8,128)(2,1)} %bitcast.305, bf16[768,1024,1,1]{1,0,3,2:T(8,128)(2,1)} %bitcast.315), kind=kOutput, calls=%fused_computation.29 | convolution fusion | flops 1610612736 | bytes 7340032 | tf_op jit(solution)/shard_map/dot_general | solution.py:98
  166.8 2.6 fusion.38
  169.9 1.8 convolution_bitcast_fusion
  171.7 2.1 copy-done.2
  174.3 3.3 %fusion.28 = f32[1,16,32,1024]{3,2,1,0:T(8,128)S(1)} fusion(bf16[1,16,32,1024]{3,2,1,0:T(8,128)(2,1)} %collective-permute-done, f32[1,16,2,32,1024]{4,3,2,1,0:T(8,128)} %convolution_bitcast_fusion.1, pred[]{:T(512)S(6)} %eq.133), kind=kLoop, calls=%fused_computation.34 | loop fusion | flops 1572864 | bytes 7340033 | tf_op jit(solution)/shard_map/add | solution.py:116
  179.4 1.8 bitcast_add_fusion
  181.8 24.2 %collective-permute-done.1 = bf16[1,8,32,1024]{3,2,1,0:T(8,128)(2,1)S(1)} collective-permute-done((bf16[1,8,32,1024]{3,2,1,0:T(8,128)(2,1)S(1)}, bf16[1,8,32,1024]{3,2,1,0:T(8,128)(2,1)S(1)}, u32[]{:S(2)}, u32[]{:S(2)}) %collective-permute-start.1) | collective-permute-done | bytes 524320 | tf_op jit(solution)/shard_map/ppermute | solution.py:115
  206.3 2.2 collective-permute-start.2
  208.5 9.7 %collective-permute-done.6 = bf16[1,8,32,1024]{3,2,1,0:T(8,128)(2,1)S(1)} collective-permute-done((bf16[1,8,32,1024]{3,2,1,0:T(8,128)(2,1)S(1)}, bf16[1,8,32,1024]{3,2,1,0:T(8,128)(2,1)S(1)}, u32[]{:S(2)}, u32[]{:S(2)}) %collective-permute-start.6) | collective-permute-done | bytes 524320 | tf_op jit(solution)/shard_map/ppermute | solution.py:115
  218.5 2.7 %collective-permute-start.7 = (bf16[1,4,32,1024]{3,2,1,0:T(8,128)(2,1)S(1)}, bf16[1,4,32,1024]{3,2,1,0:T(8,128)(2,1)S(1)}, u32[]{:S(2)}, u32[]{:S(2)}) collective-permute-start(bf16[1,4,32,1024]{3,2,1,0:T(8,128)(2,1)S(1)} %fusion.46), channel_id=1, source_target_pairs={{0,4},{1,5},{2,6},{3,7},{4,0},{5,1},{6,2},{7,3},{8,12},{9,13},{10,... | collective-permute-start | bytes 786440 | tf_op jit(solution)/shard_map/ppermute | solution.py:115
  221.4 2.4 collective-permute-start.3
  223.8 6.1 %collective-permute-done.7 = bf16[1,4,32,1024]{3,2,1,0:T(8,128)(2,1)S(1)} collective-permute-done((bf16[1,4,32,1024]{3,2,1,0:T(8,128)(2,1)S(1)}, bf16[1,4,32,1024]{3,2,1,0:T(8,128)(2,1)S(1)}, u32[]{:S(2)}, u32[]{:S(2)}) %collective-permute-start.7) | collective-permute-done | bytes 262176 | tf_op jit(solution)/shard_map/ppermute | solution.py:115
  230.1 3.1 %collective-permute-start.8 = (bf16[1,2,32,1024]{3,2,1,0:T(8,128)(2,1)S(1)}, bf16[1,2,32,1024]{3,2,1,0:T(8,128)(2,1)S(1)}, u32[]{:S(2)}, u32[]{:S(2)}) collective-permute-start(bf16[1,2,32,1024]{3,2,1,0:T(8,128)(2,1)S(1)} %fusion.53), channel_id=1, source_target_pairs={{0,8},{1,9},{2,10},{3,11},{4,12},{5,13},{6,14},{7,15},{8,0},{9,1},... | collective-permute-start | bytes 393224 | tf_op jit(solution)/shard_map/ppermute | solution.py:115
  233.2 2.5 collective-permute-start.4
  237.0 3.1 %collective-permute-start.9 = (bf16[1,1,32,1024]{3,2,1,0:T(8,128)(2,1)S(1)}, bf16[1,1,32,1024]{3,2,1,0:T(8,128)(2,1)S(1)}, u32[]{:S(2)}, u32[]{:S(2)}) collective-permute-start(bf16[1,1,32,1024]{3,2,1,0:T(8,128)(2,1)S(1)} %fusion.63), channel_id=1, source_target_pairs={{0,16},{1,17},{2,18},{3,19},{4,20},{5,21},{6,22},{7,23},{8,24},{9,... | collective-permute-start | bytes 196616 | tf_op jit(solution)/shard_map/ppermute | solution.py:115
  240.1 6.9 %collective-permute-done.4 = bf16[1,1,32,1024]{3,2,1,0:T(8,128)(2,1)S(1)} collective-permute-done((bf16[1,1,32,1024]{3,2,1,0:T(8,128)(2,1)S(1)}, bf16[1,1,32,1024]{3,2,1,0:T(8,128)(2,1)S(1)}, u32[]{:S(2)}, u32[]{:S(2)}) %collective-permute-start.4) | collective-permute-done | bytes 65568 | tf_op jit(solution)/shard_map/ppermute | solution.py:115
  248.6 8.7 %fusion.21 = f32[1024,1024]{1,0:T(8,128)} fusion(bf16[32,49,1024]{2,1,0:T(8,128)(2,1)} %all-to-all-done.2, s32[32,49]{1,0:T(8,128)S(1)} %maximum_bitcast_fusion, pred[32,49]{1,0:T(8,128)(4,1)S(1)} %compare_bitcast_fusion), kind=kOutput, calls=%fused_computation.30 | convolution fusion | flops 3291545600 | bytes 7413408 | tf_op jit(solution)/shard_map/dot_general | solution.py:148
  (87 shorter events, 16.8 us)
Async XLA Ops:
  7.2 22.3 %copy-start = (bf16[1024,1024]{1,0:T(8,128)(2,1)S(1)}, bf16[1024,1024]{1,0:T(8,128)(2,1)}, u32[]{:S(2)}) copy-start(bf16[1024,1024]{1,0:T(8,128)(2,1)} %param.6) | copy-start | bytes 6291460
  35.0 5.2 %copy-start.11 = (s32[3,256]{1,0:T(4,128)S(1)}, s32[3,256]{1,0:T(4,128)}, u32[]{:S(2)}) copy-start(s32[3,256]{1,0:T(4,128)} %param.7) | copy-start | bytes 9220
  35.0 5.3 %copy-start.10 = (s32[3,256,256]{2,1,0:T(8,128)S(1)}, s32[3,256,256]{2,1,0:T(8,128)}, u32[]{:S(2)}) copy-start(s32[3,256,256]{2,1,0:T(8,128)} %param.8) | copy-start | bytes 2359300
  35.0 86.8 %all-to-all-start.1 = ((bf16[32,49,1024]{2,1,0:T(8,128)(2,1)}), bf16[32,49,1024]{2,1,0:T(8,128)(2,1)}, u32[]{:S(2)}, u32[]{:S(2)}) async-start(bf16[32,49,1024]{2,1,0:T(8,128)(2,1)} %fusion.18), calls=%async_computation.1 | async-start | bytes 7340032 | tf_op jit(solution)/shard_map/all_to_all | solution.py:23
  38.7 89.1 %all-gather.3.cloned.1.call-start = ((), (), s32[]{:S(2)}) async-start(), calls=%async_computation.3 | async-start | bytes 2621440 | tf_op jit(solution)/shard_map/all_gather | solution.py:84
  39.4 94.8 %all-gather.5.cloned.1.call-start = ((), (), s32[]{:S(2)}) async-start(), calls=%async_computation.4 | async-start | bytes 2621440 | tf_op jit(solution)/shard_map/all_gather | solution.py:84
  127.7 5.9 %copy-start.13 = (bf16[3,256,1024]{2,1,0:T(8,128)(2,1)}, bf16[3,256,1024]{2,1,0:T(8,128)(2,1)S(1)}, u32[]{:S(2)}) copy-start(bf16[3,256,1024]{2,1,0:T(8,128)(2,1)S(1)} %fusion.15) | copy-start | bytes 4718596
  134.2 5.2 %copy-start.5 = (bf16[3,256,1024]{2,1,0:T(8,128)(2,1)}, bf16[3,256,1024]{2,1,0:T(8,128)(2,1)S(1)}, u32[]{:S(2)}) copy-start(bf16[3,256,1024]{2,1,0:T(8,128)(2,1)S(1)} %multiply_convert_fusion.2) | copy-start | bytes 4718596
  134.2 5.2 %copy-start.12 = (bf16[1024,1024]{1,0:T(8,128)(2,1)S(1)}, bf16[1024,1024]{1,0:T(8,128)(2,1)}, u32[]{:S(2)}) copy-start(bf16[1024,1024]{1,0:T(8,128)(2,1)} %all-gather.5.cloned.1.call-done) | copy-start | bytes 6291460
  139.4 1.8 copy-start.7
  141.3 1.9 copy-start.4
  146.1 3.6 %copy-start.14 = (bf16[3,256,32,49]{1,3,2,0:T(8,128)(2,1)S(1)}, bf16[3,256,32,49]{1,3,2,0:T(8,128)(2,1)}, u32[]{:S(2)}) copy-start(bf16[3,256,32,49]{1,3,2,0:T(8,128)(2,1)} %fusion.24) | copy-start | bytes 7225348
  154.5 94.1 %all-to-all-start.2 = ((bf16[32,49,1024]{2,1,0:T(8,128)(2,1)}), bf16[32,49,1024]{2,1,0:T(8,128)(2,1)}, u32[]{:S(2)}, u32[]{:S(2)}) async-start(bf16[32,49,1024]{2,1,0:T(8,128)(2,1)} %bitcast_convert_fusion), calls=%async_computation.2 | async-start | bytes 7340032 | tf_op jit(solution)/shard_map/all_to_all | solution.py:23
  159.4 5.8 %copy-start.8 = (bf16[768,1024]{1,0:T(8,128)(2,1)S(1)}, bf16[768,1024]{1,0:T(8,128)(2,1)}, u32[]{:S(2)}) copy-start(bf16[768,1024]{1,0:T(8,128)(2,1)} %copy-done.7) | copy-start | bytes 4718596
  166.8 2.8 %copy-start.6 = (bf16[3,256,1024]{2,1,0:T(8,128)(2,1)S(1)}, bf16[3,256,1024]{2,1,0:T(8,128)(2,1)}, u32[]{:S(2)}) copy-start(bf16[3,256,1024]{2,1,0:T(8,128)(2,1)} %copy-done.5) | copy-start | bytes 4718596
  166.8 3.1 %copy-start.9 = (bf16[768,1024]{0,1:T(8,128)(2,1)S(1)}, bf16[768,1024]{0,1:T(8,128)(2,1)}, u32[]{:S(2)}) copy-start(bf16[768,1024]{0,1:T(8,128)(2,1)} %copy.119) | copy-start | bytes 4718596
  169.3 4.9 %collective-permute-start = (bf16[1,16,32,1024]{3,2,1,0:T(8,128)(2,1)S(1)}, bf16[1,16,32,1024]{3,2,1,0:T(8,128)(2,1)}, u32[]{:S(2)}, u32[]{:S(2)}) collective-permute-start(bf16[1,16,32,1024]{3,2,1,0:T(8,128)(2,1)S(1)} %fusion.38), channel_id=1, source_target_pairs={{0,1},{1,0},{2,3},{3,2},{4,5},{5,4},{6,7},{7,6},{8,9},{9,8},{10,11... | collective-permute-start | bytes 3145736 | tf_op jit(solution)/shard_map/ppermute | solution.py:115
  171.7 2.1 copy-start.2
  174.0 5.4 %collective-permute-start.5 = (bf16[1,16,32,1024]{3,2,1,0:T(8,128)(2,1)S(1)}, bf16[1,16,32,1024]{3,2,1,0:T(8,128)(2,1)}, u32[]{:S(2)}, u32[]{:S(2)}) collective-permute-start(bf16[1,16,32,1024]{3,2,1,0:T(8,128)(2,1)S(1)} %fusion.39), channel_id=1, source_target_pairs={{0,1},{1,0},{2,3},{3,2},{4,5},{5,4},{6,7},{7,6},{8,9},{9,8},{10,11... | collective-permute-start | bytes 3145736 | tf_op jit(solution)/shard_map/ppermute | solution.py:115
  174.3 5.1 %copy-start.3 = (f32[1,16,2,32,1024]{4,3,1,2,0:T(8,128)S(1)}, f32[1,16,2,32,1024]{4,3,1,2,0:T(8,128)}, u32[]{:S(2)}) copy-start(f32[1,16,2,32,1024]{4,3,1,2,0:T(8,128)} %copy-done.2) | copy-start | bytes 12582916
  177.7 28.4 %collective-permute-start.1 = (bf16[1,8,32,1024]{3,2,1,0:T(8,128)(2,1)S(1)}, bf16[1,8,32,1024]{3,2,1,0:T(8,128)(2,1)S(1)}, u32[]{:S(2)}, u32[]{:S(2)}) collective-permute-start(bf16[1,8,32,1024]{3,2,1,0:T(8,128)(2,1)S(1)} %fusion.40), channel_id=1, source_target_pairs={{0,2},{1,3},{2,0},{3,1},{4,6},{5,7},{6,4},{7,5},{8,10},{9,11},{10,... | collective-permute-start | bytes 1572872 | tf_op jit(solution)/shard_map/ppermute | solution.py:115
  181.3 36.9 %collective-permute-start.6 = (bf16[1,8,32,1024]{3,2,1,0:T(8,128)(2,1)S(1)}, bf16[1,8,32,1024]{3,2,1,0:T(8,128)(2,1)S(1)}, u32[]{:S(2)}, u32[]{:S(2)}) collective-permute-start(bf16[1,8,32,1024]{3,2,1,0:T(8,128)(2,1)S(1)} %fusion.41), channel_id=1, source_target_pairs={{0,2},{1,3},{2,0},{3,1},{4,6},{5,7},{6,4},{7,5},{8,10},{9,11},{10,... | collective-permute-start | bytes 1572872 | tf_op jit(solution)/shard_map/ppermute | solution.py:115
  206.3 14.9 %collective-permute-start.2 = (bf16[1,4,32,1024]{3,2,1,0:T(8,128)(2,1)S(1)}, bf16[1,4,32,1024]{3,2,1,0:T(8,128)(2,1)S(1)}, u32[]{:S(2)}, u32[]{:S(2)}) collective-permute-start(bf16[1,4,32,1024]{3,2,1,0:T(8,128)(2,1)S(1)} %fusion.45), channel_id=1, source_target_pairs={{0,4},{1,5},{2,6},{3,7},{4,0},{5,1},{6,2},{7,3},{8,12},{9,13},{10,... | collective-permute-start | bytes 786440 | tf_op jit(solution)/shard_map/ppermute | solution.py:115
  218.5 11.4 %collective-permute-start.7 = (bf16[1,4,32,1024]{3,2,1,0:T(8,128)(2,1)S(1)}, bf16[1,4,32,1024]{3,2,1,0:T(8,128)(2,1)S(1)}, u32[]{:S(2)}, u32[]{:S(2)}) collective-permute-start(bf16[1,4,32,1024]{3,2,1,0:T(8,128)(2,1)S(1)} %fusion.46), channel_id=1, source_target_pairs={{0,4},{1,5},{2,6},{3,7},{4,0},{5,1},{6,2},{7,3},{8,12},{9,13},{10,... | collective-permute-start | bytes 786440 | tf_op jit(solution)/shard_map/ppermute | solution.py:115
  221.4 11.8 %collective-permute-start.3 = (bf16[1,2,32,1024]{3,2,1,0:T(8,128)(2,1)S(1)}, bf16[1,2,32,1024]{3,2,1,0:T(8,128)(2,1)S(1)}, u32[]{:S(2)}, u32[]{:S(2)}) collective-permute-start(bf16[1,2,32,1024]{3,2,1,0:T(8,128)(2,1)S(1)} %fusion.52), channel_id=1, source_target_pairs={{0,8},{1,9},{2,10},{3,11},{4,12},{5,13},{6,14},{7,15},{8,0},{9,1},... | collective-permute-start | bytes 393224 | tf_op jit(solution)/shard_map/ppermute | solution.py:115
  230.1 6.9 %collective-permute-start.8 = (bf16[1,2,32,1024]{3,2,1,0:T(8,128)(2,1)S(1)}, bf16[1,2,32,1024]{3,2,1,0:T(8,128)(2,1)S(1)}, u32[]{:S(2)}, u32[]{:S(2)}) collective-permute-start(bf16[1,2,32,1024]{3,2,1,0:T(8,128)(2,1)S(1)} %fusion.53), channel_id=1, source_target_pairs={{0,8},{1,9},{2,10},{3,11},{4,12},{5,13},{6,14},{7,15},{8,0},{9,1},... | collective-permute-start | bytes 393224 | tf_op jit(solution)/shard_map/ppermute | solution.py:115
  233.2 13.9 %collective-permute-start.4 = (bf16[1,1,32,1024]{3,2,1,0:T(8,128)(2,1)S(1)}, bf16[1,1,32,1024]{3,2,1,0:T(8,128)(2,1)S(1)}, u32[]{:S(2)}, u32[]{:S(2)}) collective-permute-start(bf16[1,1,32,1024]{3,2,1,0:T(8,128)(2,1)S(1)} %fusion.62), channel_id=1, source_target_pairs={{0,16},{1,17},{2,18},{3,19},{4,20},{5,21},{6,22},{7,23},{8,24},{9,... | collective-permute-start | bytes 196616 | tf_op jit(solution)/shard_map/ppermute | solution.py:115
  237.0 10.9 %collective-permute-start.9 = (bf16[1,1,32,1024]{3,2,1,0:T(8,128)(2,1)S(1)}, bf16[1,1,32,1024]{3,2,1,0:T(8,128)(2,1)S(1)}, u32[]{:S(2)}, u32[]{:S(2)}) collective-permute-start(bf16[1,1,32,1024]{3,2,1,0:T(8,128)(2,1)S(1)} %fusion.63), channel_id=1, source_target_pairs={{0,16},{1,17},{2,18},{3,19},{4,20},{5,21},{6,22},{7,23},{8,24},{9,... | collective-permute-start | bytes 196616 | tf_op jit(solution)/shard_map/ppermute | solution.py:115
  248.6 8.7 %copy-start.1 = (bf16[1024,1024]{1,0:T(8,128)(2,1)S(1)}, bf16[1024,1024]{1,0:T(8,128)(2,1)}, u32[]{:S(2)}) copy-start(bf16[1024,1024]{1,0:T(8,128)(2,1)} %param.6) | copy-start | bytes 6291460
Sparse Core Ops, SparseCore 0:
  41.0 45.6 all-gather.2
  88.3 26.6 all-gather.4

commit v11 on v10

--- a/solution.py
+++ b/solution.py
@@ -79,20 +79,34 @@
             .astype(jnp.bfloat16)
             .reshape(count, depth)
         )
-        product = jnp.dot(
-            mixed,
-            lax.all_gather(weight, "fsdp", axis=1, tiled=True),
-            preferred_element_type=jnp.float32,
-        )
+        product = lax.dot_general(
+            mixed, weight, (((1,), (1,)), ((), ())), preferred_element_type=jnp.float32
+        ).reshape(count, depth)
         return (mixed, product, weight)
 
     def back_weight(delta, weight):
         return lax.dot_general(
-            delta,
-            lax.all_gather(weight, "fsdp", axis=1, tiled=True),
-            (((1,), (1,)), ((), ())),
+            delta.reshape(count, n_fsdp, weight.shape[2]),
+            weight,
+            (((1, 2), (0, 2)), ((), ())),
             preferred_element_type=jnp.float32,
         )
+
+    def gather_columns(weight):
+        column = lax.axis_index("fsdp")
+        blocks = weight[None]
+        step = 1
+        while step < n_fsdp:
+            other = lax.ppermute(blocks, "fsdp", [(i, i ^ step) for i in range(n_fsdp)])
+            upper = (column // step) % 2 == 1
+            blocks = jnp.concatenate(
+                [jnp.where(upper, other, blocks), jnp.where(upper, blocks, other)], axis=0
+            )
+            step *= 2
+        return blocks
+
+    whole_weight_one = gather_columns(weight_one)
+    whole_weight_two = gather_columns(weight_two)
 
     def grad_parts(mixed, delta):
         return lax.dot_general(
@@ -111,22 +125,23 @@
             upper = (me // step) % 2 == 1
             keep = jnp.where(upper, pair[:, :, 1], pair[:, :, 0])
             send = jnp.where(upper, pair[:, :, 0], pair[:, :, 1])
-            send = send.astype(jnp.bfloat16)
+            if step > 1:
+                send = send.astype(jnp.bfloat16)
             moved = lax.ppermute(send, AXES, [(i, i ^ step) for i in range(shards)])
             parts = keep + moved.astype(jnp.float32)
             step *= 2
         return parts[:, 0] / (groups * shards)
 
-    mixed_one, first_matmul_result, _ = forward_layer(None, weight_one, spread_in)
+    mixed_one, first_matmul_result, _ = forward_layer(None, whole_weight_one, spread_in)
     latent_state = (
         jax.nn.silu(first_matmul_result).astype(jnp.bfloat16).reshape(groups, width, depth)
     )
-    mixed_two, product_two, _ = forward_layer(latent_state, weight_two)
+    mixed_two, product_two, _ = forward_layer(latent_state, whole_weight_two)
     delta_two = (
         final_layer_sensitivity.reshape(count, depth).astype(jnp.float32) * swish_slope(product_two)
     ).astype(jnp.bfloat16)
     parts_two = grad_parts(mixed_two, delta_two)
-    upstream_second = back_weight(delta_two, weight_two)
+    upstream_second = back_weight(delta_two, whole_weight_two)
     fetched_second = (normalizer_factor * upstream_second.reshape(groups, width, depth)).astype(
         jnp.bfloat16
     )
@@ -134,7 +149,7 @@
         spread_back(link, fetched_second).reshape(count, depth) * swish_slope(first_matmul_result)
     ).astype(jnp.bfloat16)
     parts_one = grad_parts(mixed_one, delta_one)
-    upstream_first = back_weight(delta_one, weight_one)
+    upstream_first = back_weight(delta_one, whole_weight_one)
     fetched_first = (normalizer_factor * upstream_first.reshape(groups, width, depth)).astype(
         jnp.bfloat16
     )

time: 265 us -> 273 us (1.030)
  local copies, waits for them, and re-layouts: 13.1 us -> 30.1 us
  between operations: 14.5 us -> 1.14 us
  other arithmetic: 13.6 us -> 24.8 us
  matrix products: 52.8 us -> 49.8 us
  waiting for transfers between devices: 128 us -> 125 us
    all_to_all x2, waiting for transfers between devices: 78.8 us -> 0.01 us  [exchange(): return lax.all_to_all(values, AXES, 0, 0, tiled=True)]
    ppermute x0 -> x4, waiting for transfers between devices: none -> 71.6 us  [gather_columns(): other = lax.ppermute(blocks, 'fsdp', [(i, i ^ step) for i in range(n_fsdp)])]
    dot_general x4 -> x2, matrix products: 16.4 us -> 6.44 us  [forward_layer(): lax.dot_general(mixed, weight, (((1,), (1,)), ((), ())), preferred_elemen...]
    dot_general x0 -> x4, local copies, waits for them, and re-layouts: none -> 9.66 us  [the longest x2 4.9 us: forward_layer(): lax.dot_general(mixed, weight, (((1,), (1,)), ((), ())), preferred_elemen...]
    unnamed x31 -> x55, local copies, waits for them, and re-layouts: 4.32 us -> 10.8 us
    select_n x0 -> x5, other arithmetic: none -> 5.93 us  [the longest x3 3.83 us: gather_columns(): jnp.where(upper, other, blocks)]
    ppermute x10, waiting for transfers between devices: 48.4 us -> 53.3 us  [reduce_blocks(): moved = lax.ppermute(send, AXES, [(i, i ^ step) for i in range(shards)])]
    dot_general x1, matrix products: 0.72 us -> 5.56 us  [spread_back(): jnp.einsum('gji,gjd->gid', link, values, preferred_element_type=jnp.float32)]
  transfers between devices with their start and end apart: 14 -> 16, of which waited for: 7 -> 10; matrix products, arithmetic and copies ran while one was open for 13% -> 12% of each run, Pallas kernels for 0% -> 0%
where the time goes in v11:
time: 273 us
  waiting for transfers between devices  125 us (46%)
  matrix products  49.8 us (18%)
  local copies, waits for them, and re-layouts  30.1 us (11%)
  starting transfers between devices  27.7 us (10%)
  other arithmetic  24.8 us (9%)
  blocking collectives  14.3 us (5%)
    ppermute x4, waiting for transfers between devices, gather_columns(): other = lax.ppermute(blocks, 'fsdp', [(i, i ^ step) for i in range(n_fsdp)])  71.6 us
    ppermute x10, waiting for transfers between devices, reduce_blocks(): moved = lax.ppermute(send, AXES, [(i, i ^ step) for i in range(shards)])  53.3 us
    ppermute x10, starting transfers between devices, reduce_blocks(): moved = lax.ppermute(send, AXES, [(i, i ^ step) for i in range(shards)])  16.1 us
    all_to_all x1, blocking collectives, exchange(): return lax.all_to_all(values, AXES, 0, 0, tiled=True)  14.3 us
    unnamed x55, local copies, waits for them, and re-layouts  10.8 us
    all_to_all x2, starting transfers between devices, exchange(): return lax.all_to_all(values, AXES, 0, 0, tiled=True)  8.94 us
    dot_general x1, matrix products, step_body(): lax.dot_general(linked_slots, fetched_first.reshape(count, depth), (((0,)...  8.77 us
    dot_general x1, matrix products, step_body(): lax.dot_general(picks, returned, (((0, 1), (0, 1)), ((), ())), preferred_...  8.74 us
  transfers between devices with their start and end apart: 16, of which 10 were waited for; matrix products, arithmetic and copies ran while one was open for 12% of the time, Pallas kernels for 0%

profile of v11, /device:TPU:0, one launch (start us, length us, event | category | flops | bytes accessed | tf_op | source)
XLA Modules:
  0.0 272.7 jit_solution(17629764375963317477)
XLA Ops:
  5.1 3.4 %scatter_custom_fusion = s32[1568]{0:T(1024)S(1)} fusion(s32[768]{0:T(1024)S(1)} %fusion.92, s32[768]{0:T(1024)S(1)} %get-tuple-element.13, s32[]{:T(128)} %constant.167.clone.1), kind=kCustom, calls=%fused_computation.147 | custom fusion | bytes 6276 | tf_op jit(solution)/shard_map/scatter | solution.py:44
  8.6 14.3 %all_to_all.19 = s32[32,1,49]{2,1,0:T(1,128)S(1)} all-to-all(s32[32,1,49]{2,1,0:T(1,128)S(1)} %all_to_all.12), channel_id=1, replica_groups=mesh['node'=8,'fsdp'=4] {'node','fsdp'}, dimensions={0} | all-to-all | bytes 12544 | tf_op jit(solution)/shard_map/all_to_all | solution.py:23
  23.5 5.5 %fusion.20 = bf16[32,49,1024]{2,1,0:T(8,128)(2,1)} fusion(s32[32,49]{1,0:T(8,128)S(1)} %maximum_bitcast_fusion, pred[32,49]{1,0:T(8,128)(4,1)S(1)} %compare_bitcast_fusion, bf16[1024,1024]{1,0:T(8,128)(2,1)S(1)} %copy-done), kind=kOutput, calls=%fused_computation.29 | convolution fusion | flops 3293151232 | bytes 5316256 | tf_op jit(solution)/shard_map/dot_general | solution.py:51
  29.0 3.9 %all-to-all-start.1 = ((bf16[32,49,1024]{2,1,0:T(8,128)(2,1)}), bf16[32,49,1024]{2,1,0:T(8,128)(2,1)}, u32[]{:S(2)}, u32[]{:S(2)}) async-start(bf16[32,49,1024]{2,1,0:T(8,128)(2,1)} %fusion.20), calls=%async_computation.1 | async-start | bytes 7340032 | tf_op jit(solution)/shard_map/all_to_all | solution.py:23
  42.0 3.2 %fusion.26 = bf16[3,256,32,49]{1,3,2,0:T(8,128)(2,1)} fusion(pred[3,256,49]{1,2,0:T(8,128)(4,1)S(1)} %iota_compare_fusion.2, pred[3,256,32]{1,2,0:T(8,128)(4,1)} %iota_compare_fusion.3, bf16[3,256,256]{2,1,0:T(8,128)(2,1)S(1)} %get-tuple-element.12), kind=kOutput, calls=%fused_computation.33 | convolution fusion | flops 618971136 | bytes 2863872 | tf_op jit(solution)/shard_map/gij,gjsc->gisc/dot_general | solution.py:61
  45.2 46.0 %collective-permute-done.1 = bf16[2,1024,256]{2,1,0:T(8,128)(2,1)S(1)} collective-permute-done((bf16[2,1024,256]{2,1,0:T(8,128)(2,1)}, bf16[2,1024,256]{2,1,0:T(8,128)(2,1)S(1)}, u32[]{:S(2)}, u32[]{:S(2)}) %collective-permute-start.1) | collective-permute-done | bytes 1048608 | tf_op jit(solution)/shard_map/ppermute | solution.py:100
  92.9 2.5 copy.113
  95.3 24.4 %collective-permute-done.3 = bf16[2,1024,256]{2,1,0:T(8,128)(2,1)} collective-permute-done((bf16[2,1024,256]{2,1,0:T(8,128)(2,1)}, bf16[2,1024,256]{2,1,0:T(8,128)(2,1)}, u32[]{:S(2)}, u32[]{:S(2)}) %collective-permute-start.3) | collective-permute-done | bytes 1048608 | tf_op jit(solution)/shard_map/ppermute | solution.py:100
  119.7 2.4 broadcast_select_fusion.1
  124.5 2.4 copy.114
  126.9 6.1 %fusion.17 = bf16[3,256,1024]{2,1,0:T(8,128)(2,1)S(1)} fusion(bf16[3,256,32,49]{1,3,2,0:T(8,128)(2,1)} %fusion.26, bf16[32,49,1024]{2,1,0:T(8,128)(2,1)} %all-to-all-done.1, f32[3,256]{1,0:T(4,128)S(1)} %add_rsqrt_fusion), kind=kOutput, calls=%fused_computation.23 | convolution fusion | flops 2467823616 | bytes 7195648 | tf_op jit(solution)/shard_map/dot_general | solution.py:70
  134.1 3.8 %multiply_convert_fusion.1 = (bf16[768,1024]{1,0:T(8,128)(2,1)S(1)}, f32[768,1024]{1,0:T(8,128)}) fusion(bf16[768,1024]{1,0:T(8,128)(2,1)S(1)} %bitcast.352, bf16[1024,1024]{1,0:T(8,128)(2,1)S(1)} %bitcast.338), kind=kOutput, calls=%fused_computation.25 | convolution fusion | flops 1614544896 | bytes 8388608 | tf_op jit(solution)/shard_map/dot_general | solution.py:82
  139.8 2.6 fusion.13
  142.4 2.4 dot_general.69
  144.8 5.6 %fusion.48 = f32[3,256,1024]{2,1,0:T(8,128)} fusion(bf16[3,256,256]{2,1,0:T(8,128)(2,1)S(1)} %get-tuple-element.12, bf16[3,256,4,256]{3,2,1,0:T(4,128)(2,1)} %dot_general.69, f32[3,256]{1,0:T(4,128)S(1)} %add_rsqrt_fusion, bf16[2,1024,256]{2,1,0:T(8,128)(2,1)} %get-tuple-element.4, bf16[2,1024,256]{2,1,0:T(8,128)(2,1)S(1)} %copy-done.11), kind=kOutput, calls=%fused_computation.51 | convolution fusion | flops 2015887360 | bytes 7212032 | tf_op jit(solution)/shard_map/gji,gjd->gid/dot_general | solution.py:19
  150.4 3.9 %fusion.15 = bf16[768,1024]{1,0:T(8,128)(2,1)S(1)} fusion(f32[3,256,1024]{2,1,0:T(8,128)} %fusion.48, f32[768,1024]{1,0:T(8,128)} %get-tuple-element.16), kind=kLoop, calls=%fused_computation.19 | loop fusion | flops 7077888 | bytes 7864320 | tf_op jit(solution)/shard_map/convert_element_type | solution.py:150
  154.3 2.4 dot_general.72
  158.3 2.8 %copy.133 = bf16[768,1024]{0,1:T(8,128)(2,1)} copy(bf16[768,1024]{1,0:T(8,128)(2,1)} %copy-done.5) | data formatting | bytes 3145728 | tf_op jit(solution)/shard_map/convert_element_type | solution.py:142
  161.1 8.8 %bitcast_convert_fusion = bf16[32,49,1024]{2,1,0:T(8,128)(2,1)} fusion(bf16[3,256,32,49]{1,3,2,0:T(8,128)(2,1)} %fusion.26, bf16[3,256,4,256]{3,2,1,0:T(4,128)(2,1)} %dot_general.72, f32[3,256]{1,0:T(4,128)S(1)} %add_rsqrt_fusion, bf16[2,1024,256]{2,1,0:T(8,128)(2,1)S(1)} %copy-done.9, bf16[2,1024,256]{2,1,0:T(8,128)(2,1)S(1)} %copy-done.7), kind=kOutput, calls=%fused_computation.1 | convolution fusion | flops 4081090560 | bytes 9292800 | tf_op jit(solution)/shard_map/dot_general | solution.py:156
  169.8 5.1 %all-to-all-start.2 = ((bf16[32,49,1024]{2,1,0:T(8,128)(2,1)}), bf16[32,49,1024]{2,1,0:T(8,128)(2,1)}, u32[]{:S(2)}, u32[]{:S(2)}) async-start(bf16[32,49,1024]{2,1,0:T(8,128)(2,1)} %bitcast_convert_fusion), calls=%async_computation.2 | async-start | bytes 7340032 | tf_op jit(solution)/shard_map/all_to_all | solution.py:23
  174.9 3.2 %convolution_bitcast_fusion.1 = f32[1,16,2,32,1024]{4,3,2,1,0:T(8,128)S(1)} fusion(bf16[16,2,32,768]{3,2,1,0:T(8,128)(2,1)S(1)} %bitcast.343, bf16[768,1024,1,1]{1,0,3,2:T(8,128)(2,1)} %bitcast.353), kind=kOutput, calls=%fused_computation.31 | convolution fusion | flops 1610612736 | bytes 7340032 | tf_op jit(solution)/shard_map/dot_general | solution.py:112
  186.0 3.7 %fusion.30 = f32[1,16,32,1024]{3,2,1,0:T(8,128)S(1)} fusion(f32[1,16,32,1024]{3,2,1,0:T(8,128)} %collective-permute-done.4, f32[1,16,2,32,1024]{4,3,2,1,0:T(8,128)} %copy-done.4, pred[]{:T(512)S(6)} %eq.147), kind=kLoop, calls=%fused_computation.38 | loop fusion | flops 1048576 | bytes 8388609 | tf_op jit(solution)/shard_map/add | solution.py:131
  191.4 2.3 bitcast_add_fusion
  194.3 26.9 %collective-permute-done.5 = bf16[1,8,32,1024]{3,2,1,0:T(8,128)(2,1)S(1)} collective-permute-done((bf16[1,8,32,1024]{3,2,1,0:T(8,128)(2,1)S(1)}, bf16[1,8,32,1024]{3,2,1,0:T(8,128)(2,1)S(1)}, u32[]{:S(2)}, u32[]{:S(2)}) %collective-permute-start.5) | collective-permute-done | bytes 524320 | tf_op jit(solution)/shard_map/ppermute | solution.py:130
  221.6 2.0 collective-permute-start.6
  223.6 9.9 %collective-permute-done.10 = bf16[1,8,32,1024]{3,2,1,0:T(8,128)(2,1)S(1)} collective-permute-done((bf16[1,8,32,1024]{3,2,1,0:T(8,128)(2,1)S(1)}, bf16[1,8,32,1024]{3,2,1,0:T(8,128)(2,1)S(1)}, u32[]{:S(2)}, u32[]{:S(2)}) %collective-permute-start.10) | collective-permute-done | bytes 524320 | tf_op jit(solution)/shard_map/ppermute | solution.py:130
  233.8 2.7 collective-permute-start.11
  237.8 7.5 %collective-permute-done.11 = bf16[1,4,32,1024]{3,2,1,0:T(8,128)(2,1)S(1)} collective-permute-done((bf16[1,4,32,1024]{3,2,1,0:T(8,128)(2,1)S(1)}, bf16[1,4,32,1024]{3,2,1,0:T(8,128)(2,1)S(1)}, u32[]{:S(2)}, u32[]{:S(2)}) %collective-permute-start.11) | collective-permute-done | bytes 262176 | tf_op jit(solution)/shard_map/ppermute | solution.py:130
  247.4 2.7 collective-permute-start.8
  251.9 3.4 %collective-permute-start.13 = (bf16[1,1,32,1024]{3,2,1,0:T(8,128)(2,1)S(1)}, bf16[1,1,32,1024]{3,2,1,0:T(8,128)(2,1)S(1)}, u32[]{:S(2)}, u32[]{:S(2)}) collective-permute-start(bf16[1,1,32,1024]{3,2,1,0:T(8,128)(2,1)S(1)} %fusion.84), channel_id=1, source_target_pairs={{0,16},{1,17},{2,18},{3,19},{4,20},{5,21},{6,22},{7,23},{8,24},{9,... | collective-permute-start | bytes 196616 | tf_op jit(solution)/shard_map/ppermute | solution.py:130
  255.4 7.1 %collective-permute-done.8 = bf16[1,1,32,1024]{3,2,1,0:T(8,128)(2,1)S(1)} collective-permute-done((bf16[1,1,32,1024]{3,2,1,0:T(8,128)(2,1)S(1)}, bf16[1,1,32,1024]{3,2,1,0:T(8,128)(2,1)S(1)}, u32[]{:S(2)}, u32[]{:S(2)}) %collective-permute-start.8) | collective-permute-done | bytes 65568 | tf_op jit(solution)/shard_map/ppermute | solution.py:130
  264.0 8.7 %fusion.23 = f32[1024,1024]{1,0:T(8,128)} fusion(bf16[32,49,1024]{2,1,0:T(8,128)(2,1)} %all-to-all-done.2, s32[32,49]{1,0:T(8,128)S(1)} %copy-done.24, pred[32,49]{1,0:T(8,128)(4,1)S(1)} %compare_bitcast_fusion), kind=kOutput, calls=%fused_computation.32 | convolution fusion | flops 3291545600 | bytes 7413408 | tf_op jit(solution)/shard_map/dot_general | solution.py:163
  (122 shorter events, 40.2 us)
Async XLA Ops:
  0.6 22.9 %copy-start = (bf16[1024,1024]{1,0:T(8,128)(2,1)S(1)}, bf16[1024,1024]{1,0:T(8,128)(2,1)}, u32[]{:S(2)}) copy-start(bf16[1024,1024]{1,0:T(8,128)(2,1)} %param.6) | copy-start | bytes 6291460
  29.0 3.9 %copy-start.19 = (bf16[1024,256]{1,0:T(8,128)(2,1)S(1)}, bf16[1024,256]{1,0:T(8,128)(2,1)}, u32[]{:S(2)}) copy-start(bf16[1024,256]{1,0:T(8,128)(2,1)} %param.10) | copy-start | bytes 1572868
  29.0 4.0 %copy-start.20 = (bf16[1024,256]{1,0:T(8,128)(2,1)S(1)}, bf16[1024,256]{1,0:T(8,128)(2,1)}, u32[]{:S(2)}) copy-start(bf16[1024,256]{1,0:T(8,128)(2,1)} %param.9) | copy-start | bytes 1572868
  29.0 4.5 %copy-start.22 = (s32[3,256]{1,0:T(4,128)S(1)}, s32[3,256]{1,0:T(4,128)}, u32[]{:S(2)}) copy-start(s32[3,256]{1,0:T(4,128)} %param.7) | copy-start | bytes 9220
  29.0 4.6 %copy-start.18 = (s32[3,256,256]{2,1,0:T(8,128)S(1)}, s32[3,256,256]{2,1,0:T(8,128)}, u32[]{:S(2)}) copy-start(s32[3,256,256]{2,1,0:T(8,128)} %param.8) | copy-start | bytes 2359300
  29.0 97.9 %all-to-all-start.1 = ((bf16[32,49,1024]{2,1,0:T(8,128)(2,1)}), bf16[32,49,1024]{2,1,0:T(8,128)(2,1)}, u32[]{:S(2)}, u32[]{:S(2)}) async-start(bf16[32,49,1024]{2,1,0:T(8,128)(2,1)} %fusion.20), calls=%async_computation.1 | async-start | bytes 7340032 | tf_op jit(solution)/shard_map/all_to_all | solution.py:23
  32.9 2.0 collective-permute-start.2
  33.0 2.8 %collective-permute-start = (bf16[1,1024,256]{2,1,0:T(8,128)(2,1)S(1)}, bf16[1,1024,256]{2,1,0:T(8,128)(2,1)}, u32[]{:S(2)}, u32[]{:S(2)}) collective-permute-start(bf16[1,1024,256]{2,1,0:T(8,128)(2,1)S(1)} %bitcast.346), channel_id=1, source_target_pairs={{0,1},{1,0},{2,3},{3,2},{4,5},{5,4},{6,7},{7,6},{8,9},{9,8},{10,11... | collective-permute-start | bytes 1572872 | tf_op jit(solution)/shard_map/ppermute | solution.py:100
  38.2 53.0 %collective-permute-start.1 = (bf16[2,1024,256]{2,1,0:T(8,128)(2,1)}, bf16[2,1024,256]{2,1,0:T(8,128)(2,1)S(1)}, u32[]{:S(2)}, u32[]{:S(2)}) collective-permute-start(bf16[2,1024,256]{2,1,0:T(8,128)(2,1)} %pad_maximum_fusion.5), channel_id=1, source_target_pairs={{0,2},{1,3},{2,0},{3,1},{4,6},{5,7},{6,4},{7,5},{8,10},{9,11},{10,... | collective-permute-start | bytes 3145736 | tf_op jit(solution)/shard_map/ppermute | solution.py:100
  41.3 78.4 %collective-permute-start.3 = (bf16[2,1024,256]{2,1,0:T(8,128)(2,1)}, bf16[2,1024,256]{2,1,0:T(8,128)(2,1)}, u32[]{:S(2)}, u32[]{:S(2)}) collective-permute-start(bf16[2,1024,256]{2,1,0:T(8,128)(2,1)} %pad_maximum_fusion.6), channel_id=1, source_target_pairs={{0,2},{1,3},{2,0},{3,1},{4,6},{5,7},{6,4},{7,5},{8,10},{9,11},{10,... | collective-permute-start | bytes 3145736 | tf_op jit(solution)/shard_map/ppermute | solution.py:100
  126.9 7.3 %copy-start.12 = (bf16[4,256,1024]{2,1,0:T(8,128)(2,1)S(1)}, bf16[4,256,1024]{2,1,0:T(8,128)(2,1)}, u32[]{:S(2)}) copy-start(bf16[4,256,1024]{2,1,0:T(8,128)(2,1)} %copy.113) | copy-start | bytes 6291460
  134.1 5.6 %copy-start.25 = (bf16[3,256,1024]{2,1,0:T(8,128)(2,1)S(1)}, bf16[3,256,1024]{2,1,0:T(8,128)(2,1)}, u32[]{:S(2)}) copy-start(bf16[3,256,1024]{2,1,0:T(8,128)(2,1)} %param.11) | copy-start | bytes 4718596
  142.4 8.0 %copy-start.5 = (bf16[768,1024]{1,0:T(8,128)(2,1)}, bf16[768,1024]{1,0:T(8,128)(2,1)S(1)}, u32[]{:S(2)}) copy-start(bf16[768,1024]{1,0:T(8,128)(2,1)S(1)} %fusion.13) | copy-start | bytes 4718596
  158.3 2.8 %copy-start.9 = (bf16[2,1024,256]{2,1,0:T(8,128)(2,1)S(1)}, bf16[2,1024,256]{2,1,0:T(8,128)(2,1)}, u32[]{:S(2)}) copy-start(bf16[2,1024,256]{2,1,0:T(8,128)(2,1)} %copy-done.8) | copy-start | bytes 3145732
  169.8 5.1 %copy-start.17 = (bf16[768,1024]{0,1:T(8,128)(2,1)S(1)}, bf16[768,1024]{0,1:T(8,128)(2,1)}, u32[]{:S(2)}) copy-start(bf16[768,1024]{0,1:T(8,128)(2,1)} %copy.118) | copy-start | bytes 4718596
  169.8 94.1 %all-to-all-start.2 = ((bf16[32,49,1024]{2,1,0:T(8,128)(2,1)}), bf16[32,49,1024]{2,1,0:T(8,128)(2,1)}, u32[]{:S(2)}, u32[]{:S(2)}) async-start(bf16[32,49,1024]{2,1,0:T(8,128)(2,1)} %bitcast_convert_fusion), calls=%async_computation.2 | async-start | bytes 7340032 | tf_op jit(solution)/shard_map/all_to_all | solution.py:23
  178.1 3.1 %copy-start.4 = (f32[1,16,2,32,1024]{4,3,2,1,0:T(8,128)}, f32[1,16,2,32,1024]{4,3,2,1,0:T(8,128)S(1)}, u32[]{:S(2)}) copy-start(f32[1,16,2,32,1024]{4,3,2,1,0:T(8,128)S(1)} %convolution_bitcast_fusion.1) | copy-start | bytes 12582916
  178.1 3.1 %copy-start.15 = (bf16[3,256,1024]{2,1,0:T(8,128)(2,1)S(1)}, bf16[3,256,1024]{2,1,0:T(8,128)(2,1)}, u32[]{:S(2)}) copy-start(bf16[3,256,1024]{2,1,0:T(8,128)(2,1)} %copy-done.14) | copy-start | bytes 4718596
  178.1 4.1 %copy-start.16 = (bf16[768,1024]{0,1:T(8,128)(2,1)S(1)}, bf16[768,1024]{0,1:T(8,128)(2,1)}, u32[]{:S(2)}) copy-start(bf16[768,1024]{0,1:T(8,128)(2,1)} %copy.133) | copy-start | bytes 4718596
  181.2 4.7 %collective-permute-start.4 = (f32[1,16,32,1024]{3,2,1,0:T(8,128)}, f32[1,16,32,1024]{3,2,1,0:T(8,128)}, u32[]{:S(2)}, u32[]{:S(2)}) collective-permute-start(f32[1,16,32,1024]{3,2,1,0:T(8,128)} %select_bitcast_fusion.1), channel_id=1, source_target_pairs={{0,1},{1,0},{2,3},{3,2},{4,5},{5,4},{6,7},{7,6},{8,9},{9,8},{10,11... | collective-permute-start | bytes 6291464 | tf_op jit(solution)/shard_map/ppermute | solution.py:130
  186.0 5.5 %collective-permute-start.9 = (f32[1,16,32,1024]{3,2,1,0:T(8,128)S(1)}, f32[1,16,32,1024]{3,2,1,0:T(8,128)}, u32[]{:S(2)}, u32[]{:S(2)}) collective-permute-start(f32[1,16,32,1024]{3,2,1,0:T(8,128)S(1)} %select_bitcast_fusion), channel_id=1, source_target_pairs={{0,1},{1,0},{2,3},{3,2},{4,5},{5,4},{6,7},{7,6},{8,9},{9,8},{10,11... | collective-permute-start | bytes 6291464 | tf_op jit(solution)/shard_map/ppermute | solution.py:130
  186.0 5.4 %copy-start.3 = (f32[1,16,2,32,1024]{4,3,1,2,0:T(8,128)S(1)}, f32[1,16,2,32,1024]{4,3,1,2,0:T(8,128)}, u32[]{:S(2)}) copy-start(f32[1,16,2,32,1024]{4,3,1,2,0:T(8,128)} %copy-done.2) | copy-start | bytes 12582916
  189.8 31.5 %collective-permute-start.5 = (bf16[1,8,32,1024]{3,2,1,0:T(8,128)(2,1)S(1)}, bf16[1,8,32,1024]{3,2,1,0:T(8,128)(2,1)S(1)}, u32[]{:S(2)}, u32[]{:S(2)}) collective-permute-start(bf16[1,8,32,1024]{3,2,1,0:T(8,128)(2,1)S(1)} %fusion.61), channel_id=1, source_target_pairs={{0,2},{1,3},{2,0},{3,1},{4,6},{5,7},{6,4},{7,5},{8,10},{9,11},{10,... | collective-permute-start | bytes 1572872 | tf_op jit(solution)/shard_map/ppermute | solution.py:130
  193.8 39.7 %collective-permute-start.10 = (bf16[1,8,32,1024]{3,2,1,0:T(8,128)(2,1)S(1)}, bf16[1,8,32,1024]{3,2,1,0:T(8,128)(2,1)S(1)}, u32[]{:S(2)}, u32[]{:S(2)}) collective-permute-start(bf16[1,8,32,1024]{3,2,1,0:T(8,128)(2,1)S(1)} %fusion.62), channel_id=1, source_target_pairs={{0,2},{1,3},{2,0},{3,1},{4,6},{5,7},{6,4},{7,5},{8,10},{9,11},{10,... | collective-permute-start | bytes 1572872 | tf_op jit(solution)/shard_map/ppermute | solution.py:130
  221.6 14.9 %collective-permute-start.6 = (bf16[1,4,32,1024]{3,2,1,0:T(8,128)(2,1)S(1)}, bf16[1,4,32,1024]{3,2,1,0:T(8,128)(2,1)S(1)}, u32[]{:S(2)}, u32[]{:S(2)}) collective-permute-start(bf16[1,4,32,1024]{3,2,1,0:T(8,128)(2,1)S(1)} %fusion.66), channel_id=1, source_target_pairs={{0,4},{1,5},{2,6},{3,7},{4,0},{5,1},{6,2},{7,3},{8,12},{9,13},{10,... | collective-permute-start | bytes 786440 | tf_op jit(solution)/shard_map/ppermute | solution.py:130
  233.8 11.6 %collective-permute-start.11 = (bf16[1,4,32,1024]{3,2,1,0:T(8,128)(2,1)S(1)}, bf16[1,4,32,1024]{3,2,1,0:T(8,128)(2,1)S(1)}, u32[]{:S(2)}, u32[]{:S(2)}) collective-permute-start(bf16[1,4,32,1024]{3,2,1,0:T(8,128)(2,1)S(1)} %fusion.67), channel_id=1, source_target_pairs={{0,4},{1,5},{2,6},{3,7},{4,0},{5,1},{6,2},{7,3},{8,12},{9,13},{10,... | collective-permute-start | bytes 786440 | tf_op jit(solution)/shard_map/ppermute | solution.py:130
  236.6 10.7 %collective-permute-start.7 = (bf16[1,2,32,1024]{3,2,1,0:T(8,128)(2,1)S(1)}, bf16[1,2,32,1024]{3,2,1,0:T(8,128)(2,1)S(1)}, u32[]{:S(2)}, u32[]{:S(2)}) collective-permute-start(bf16[1,2,32,1024]{3,2,1,0:T(8,128)(2,1)S(1)} %fusion.73), channel_id=1, source_target_pairs={{0,8},{1,9},{2,10},{3,11},{4,12},{5,13},{6,14},{7,15},{8,0},{9,1},... | collective-permute-start | bytes 393224 | tf_op jit(solution)/shard_map/ppermute | solution.py:130
  245.5 18.5 %copy-start.24 = (s32[32,49]{1,0:T(8,128)S(1)}, s32[32,49]{1,0:T(8,128)}, u32[]{:S(2)}) copy-start(s32[32,49]{1,0:T(8,128)} %copy-done.23) | copy-start | bytes 18820
  245.5 6.4 %collective-permute-start.12 = (bf16[1,2,32,1024]{3,2,1,0:T(8,128)(2,1)S(1)}, bf16[1,2,32,1024]{3,2,1,0:T(8,128)(2,1)S(1)}, u32[]{:S(2)}, u32[]{:S(2)}) collective-permute-start(bf16[1,2,32,1024]{3,2,1,0:T(8,128)(2,1)S(1)} %fusion.74), channel_id=1, source_target_pairs={{0,8},{1,9},{2,10},{3,11},{4,12},{5,13},{6,14},{7,15},{8,0},{9,1},... | collective-permute-start | bytes 393224 | tf_op jit(solution)/shard_map/ppermute | solution.py:130
  247.4 15.0 %collective-permute-start.8 = (bf16[1,1,32,1024]{3,2,1,0:T(8,128)(2,1)S(1)}, bf16[1,1,32,1024]{3,2,1,0:T(8,128)(2,1)S(1)}, u32[]{:S(2)}, u32[]{:S(2)}) collective-permute-start(bf16[1,1,32,1024]{3,2,1,0:T(8,128)(2,1)S(1)} %fusion.83), channel_id=1, source_target_pairs={{0,16},{1,17},{2,18},{3,19},{4,20},{5,21},{6,22},{7,23},{8,24},{9,... | collective-permute-start | bytes 196616 | tf_op jit(solution)/shard_map/ppermute | solution.py:130
  251.9 11.3 %collective-permute-start.13 = (bf16[1,1,32,1024]{3,2,1,0:T(8,128)(2,1)S(1)}, bf16[1,1,32,1024]{3,2,1,0:T(8,128)(2,1)S(1)}, u32[]{:S(2)}, u32[]{:S(2)}) collective-permute-start(bf16[1,1,32,1024]{3,2,1,0:T(8,128)(2,1)S(1)} %fusion.84), channel_id=1, source_target_pairs={{0,16},{1,17},{2,18},{3,19},{4,20},{5,21},{6,22},{7,23},{8,24},{9,... | collective-permute-start | bytes 196616 | tf_op jit(solution)/shard_map/ppermute | solution.py:130
  264.0 8.7 %copy-start.1 = (bf16[1024,1024]{1,0:T(8,128)(2,1)S(1)}, bf16[1024,1024]{1,0:T(8,128)(2,1)}, u32[]{:S(2)}) copy-start(bf16[1024,1024]{1,0:T(8,128)(2,1)} %param.6) | copy-start | bytes 6291460
  (11 other events, 16.0 us)

commit v12 on v11

--- a/solution.py
+++ b/solution.py
@@ -95,15 +95,18 @@
     def gather_columns(weight):
         column = lax.axis_index("fsdp")
         blocks = weight[None]
-        step = 1
-        while step < n_fsdp:
+        step = n_fsdp // 2
+        while step >= 1:
             other = lax.ppermute(blocks, "fsdp", [(i, i ^ step) for i in range(n_fsdp)])
             upper = (column // step) % 2 == 1
             blocks = jnp.concatenate(
                 [jnp.where(upper, other, blocks), jnp.where(upper, blocks, other)], axis=0
             )
-            step *= 2
-        return blocks
+            step //= 2
+        bits = n_fsdp.bit_length() - 1
+        blocks = blocks.reshape((2,) * bits + weight.shape)
+        blocks = blocks.transpose(tuple(range(bits))[::-1] + (bits, bits + 1))
+        return blocks.reshape((n_fsdp,) + weight.shape)
 
     whole_weight_one = gather_columns(weight_one)
     whole_weight_two = gather_columns(weight_two)

time: 273 us -> 265 us (0.971)
  waiting for transfers between devices: 125 us -> 115 us
    ppermute x4, waiting for transfers between devices: 71.6 us -> 55 us  [gather_columns(): other = lax.ppermute(blocks, 'fsdp', [(i, i ^ step) for i in range(n_fsdp)])]
    all_to_all x2, waiting for transfers between devices: 0.01 us -> 6.65 us  [exchange(): return lax.all_to_all(values, AXES, 0, 0, tiled=True)]
    unnamed x55 -> x45, local copies, waits for them, and re-layouts: 10.8 us -> 8.17 us
  transfers between devices with their start and end apart: 16 -> 16, of which waited for: 10 -> 9; matrix products, arithmetic and copies ran while one was open for 12% -> 13% of each run, Pallas kernels for 0% -> 0%
where the time goes in v12:
time: 265 us; the launch traced here: 264 us
  waiting for transfers between devices  115 us (43%)
  matrix products  50.8 us (19%)
  local copies, waits for them, and re-layouts  31.3 us (12%)
  starting transfers between devices  27.7 us (10%)
  other arithmetic  23.8 us (9%)
  blocking collectives  14.3 us (5%)
    ppermute x4, waiting for transfers between devices, gather_columns(): other = lax.ppermute(blocks, 'fsdp', [(i, i ^ step) for i in range(n_fsdp)])  55 us
    ppermute x10, waiting for transfers between devices, reduce_blocks(): moved = lax.ppermute(send, AXES, [(i, i ^ step) for i in range(shards)])  53.3 us
    ppermute x10, starting transfers between devices, reduce_blocks(): moved = lax.ppermute(send, AXES, [(i, i ^ step) for i in range(shards)])  16.1 us
    all_to_all x1, blocking collectives, exchange(): return lax.all_to_all(values, AXES, 0, 0, tiled=True)  14.3 us
    all_to_all x2, starting transfers between devices, exchange(): return lax.all_to_all(values, AXES, 0, 0, tiled=True)  8.95 us
    dot_general x1, matrix products, step_body(): lax.dot_general(linked_slots, fetched_first.reshape(count, depth), (((0,)...  8.83 us
    dot_general x1, matrix products, step_body(): lax.dot_general(picks, returned, (((0, 1), (0, 1)), ((), ())), preferred_...  8.74 us
    unnamed x45, local copies, waits for them, and re-layouts  8.17 us
  transfers between devices with their start and end apart: 16, of which 9 were waited for; matrix products, arithmetic and copies ran while one was open for 13% of the time, Pallas kernels for 0%

profile of v12, /device:TPU:0, one launch (start us, length us, event | category | flops | bytes accessed | tf_op | source)
XLA Modules:
  0.0 264.0 jit_solution(16969457639953046117)
XLA Ops:
  5.1 3.4 %scatter_custom_fusion = s32[1568]{0:T(1024)S(1)} fusion(s32[768]{0:T(1024)S(1)} %fusion.76, s32[768]{0:T(1024)S(1)} %get-tuple-element.13, s32[]{:T(128)} %constant.167.clone.1), kind=kCustom, calls=%fused_computation.141 | custom fusion | bytes 6276 | tf_op jit(solution)/shard_map/scatter | solution.py:44
  8.6 14.3 %all_to_all.19 = s32[32,1,49]{2,1,0:T(1,128)S(1)} all-to-all(s32[32,1,49]{2,1,0:T(1,128)S(1)} %all_to_all.12), channel_id=1, replica_groups=mesh['node'=8,'fsdp'=4] {'node','fsdp'}, dimensions={0} | all-to-all | bytes 12544 | tf_op jit(solution)/shard_map/all_to_all | solution.py:23
  23.5 5.5 %fusion.20 = bf16[32,49,1024]{2,1,0:T(8,128)(2,1)} fusion(s32[32,49]{1,0:T(8,128)S(1)} %maximum_bitcast_fusion, pred[32,49]{1,0:T(8,128)(4,1)S(1)} %compare_bitcast_fusion, bf16[1024,1024]{1,0:T(8,128)(2,1)S(1)} %copy-done), kind=kOutput, calls=%fused_computation.29 | convolution fusion | flops 3293151232 | bytes 5316256 | tf_op jit(solution)/shard_map/dot_general | solution.py:51
  29.0 3.9 %all-to-all-start.1 = ((bf16[32,49,1024]{2,1,0:T(8,128)(2,1)}), bf16[32,49,1024]{2,1,0:T(8,128)(2,1)}, u32[]{:S(2)}, u32[]{:S(2)}) async-start(bf16[32,49,1024]{2,1,0:T(8,128)(2,1)} %fusion.20), calls=%async_computation.1 | async-start | bytes 7340032 | tf_op jit(solution)/shard_map/all_to_all | solution.py:23
  35.3 44.4 %collective-permute-done.2 = bf16[1,1024,256]{2,1,0:T(8,128)(2,1)S(1)} collective-permute-done((bf16[1,1024,256]{2,1,0:T(8,128)(2,1)S(1)}, bf16[1,1024,256]{2,1,0:T(8,128)(2,1)S(1)}, u32[]{:S(2)}, u32[]{:S(2)}) %collective-permute-start.2) | collective-permute-done | bytes 524320 | tf_op jit(solution)/shard_map/ppermute | solution.py:100
  80.4 10.6 %collective-permute-done = bf16[1,1024,256]{2,1,0:T(8,128)(2,1)} collective-permute-done((bf16[1,1024,256]{2,1,0:T(8,128)(2,1)S(1)}, bf16[1,1024,256]{2,1,0:T(8,128)(2,1)}, u32[]{:S(2)}, u32[]{:S(2)}) %collective-permute-start) | collective-permute-done | bytes 524320 | tf_op jit(solution)/shard_map/ppermute | solution.py:100
  94.9 3.2 %fusion.26 = bf16[3,256,32,49]{1,3,2,0:T(8,128)(2,1)} fusion(pred[3,256,49]{1,2,0:T(8,128)(4,1)S(1)} %iota_compare_fusion.2, pred[3,256,32]{1,2,0:T(8,128)(4,1)} %iota_compare_fusion.3, bf16[3,256,256]{2,1,0:T(8,128)(2,1)S(1)} %get-tuple-element.12), kind=kOutput, calls=%fused_computation.33 | convolution fusion | flops 618971136 | bytes 2863872 | tf_op jit(solution)/shard_map/gij,gjsc->gisc/dot_general | solution.py:61
  99.9 2.1 broadcast_select_fusion.1
  103.7 2.5 copy.118
  106.2 3.0 %copy.120 = bf16[4,256,1024]{2,1,0:T(8,128)(2,1)S(1)} copy(bf16[4,256,1024]{1,2,0:T(8,128)(2,1)} %bitcast.330) | data formatting | bytes 4194304 | tf_op jit(solution)/shard_map/dot_general | solution.py:82
  109.2 6.7 %all-to-all-done.1 = bf16[32,49,1024]{2,1,0:T(8,128)(2,1)} async-done(((bf16[32,49,1024]{2,1,0:T(8,128)(2,1)}), bf16[32,49,1024]{2,1,0:T(8,128)(2,1)}, u32[]{:S(2)}, u32[]{:S(2)}) %all-to-all-start.1) | async-done | bytes 3211296 | tf_op jit(solution)/shard_map/all_to_all | solution.py:23
  115.8 6.1 %fusion.17 = bf16[3,256,1024]{2,1,0:T(8,128)(2,1)S(1)} fusion(bf16[3,256,32,49]{1,3,2,0:T(8,128)(2,1)} %fusion.26, bf16[32,49,1024]{2,1,0:T(8,128)(2,1)} %all-to-all-done.1, f32[3,256]{1,0:T(4,128)S(1)} %add_rsqrt_fusion), kind=kOutput, calls=%fused_computation.23 | convolution fusion | flops 2467823616 | bytes 7195648 | tf_op jit(solution)/shard_map/dot_general | solution.py:70
  123.1 3.8 %multiply_convert_fusion.1 = (bf16[768,1024]{1,0:T(8,128)(2,1)S(1)}, f32[768,1024]{1,0:T(8,128)}) fusion(bf16[768,1024]{1,0:T(8,128)(2,1)S(1)} %bitcast.356, bf16[1024,1024]{1,0:T(8,128)(2,1)S(1)} %bitcast.343), kind=kOutput, calls=%fused_computation.25 | convolution fusion | flops 1614544896 | bytes 8388608 | tf_op jit(solution)/shard_map/dot_general | solution.py:82
  128.6 3.8 %fusion.13 = bf16[768,1024]{1,0:T(8,128)(2,1)} fusion(bf16[3,256,1024]{2,1,0:T(8,128)(2,1)S(1)} %copy-done.20, bf16[768,1024]{1,0:T(8,128)(2,1)S(1)} %bitcast.344, bf16[1024,1024]{1,0:T(8,128)(2,1)S(1)} %bitcast.342), kind=kOutput, calls=%fused_computation.15 | convolution fusion | flops 1618477056 | bytes 6815744 | tf_op jit(solution)/shard_map/dot_general | solution.py:82
  132.4 4.0 %dot_general.69 = bf16[3,256,4,256]{3,2,1,0:T(4,128)(2,1)} reshape(bf16[768,1024]{1,0:T(8,128)(2,1)} %fusion.13) | data formatting | bytes 3145728 | tf_op jit(solution)/shard_map/dot_general | solution.py:88
  136.4 5.3 %fusion.39 = f32[3,256,1024]{2,1,0:T(8,128)} fusion(bf16[3,256,256]{2,1,0:T(8,128)(2,1)S(1)} %get-tuple-element.12, bf16[4,1024,256,1]{2,1,0,3:T(8,128)(2,1)S(1)} %bitcast.331, bf16[3,256,4,256]{3,2,1,0:T(4,128)(2,1)} %dot_general.69, f32[3,256]{1,0:T(4,128)S(1)} %add_rsqrt_fusion), kind=kOutput, calls=%fused_computation.47 | convolution fusion | flops 2014838784 | bytes 7212032 | tf_op jit(solution)/shard_map/gji,gjd->gid/dot_general | solution.py:19
  141.7 3.9 %fusion.15 = bf16[768,1024]{1,0:T(8,128)(2,1)S(1)} fusion(f32[3,256,1024]{2,1,0:T(8,128)} %fusion.39, f32[768,1024]{1,0:T(8,128)} %get-tuple-element.16), kind=kLoop, calls=%fused_computation.19 | loop fusion | flops 7077888 | bytes 7864320 | tf_op jit(solution)/shard_map/convert_element_type | solution.py:153
  145.6 2.4 dot_general.72
  149.5 2.8 %copy.139 = bf16[768,1024]{0,1:T(8,128)(2,1)} copy(bf16[768,1024]{1,0:T(8,128)(2,1)} %fusion.13) | data formatting | bytes 3145728 | tf_op jit(solution)/shard_map/convert_element_type | solution.py:145
  152.3 8.8 %bitcast_convert_fusion = bf16[32,49,1024]{2,1,0:T(8,128)(2,1)} fusion(bf16[3,256,32,49]{1,3,2,0:T(8,128)(2,1)} %fusion.26, bf16[4,1024,256,1]{2,1,0,3:T(8,128)(2,1)S(1)} %bitcast.329, bf16[3,256,4,256]{3,2,1,0:T(4,128)(2,1)} %dot_general.72, f32[3,256]{1,0:T(4,128)S(1)} %add_rsqrt_fusion), kind=kOutput, calls=%fused_computation.1 | convolution fusion | flops 4080041984 | bytes 9292800 | tf_op jit(solution)/shard_map/dot_general | solution.py:159
  161.1 5.1 %all-to-all-start.2 = ((bf16[32,49,1024]{2,1,0:T(8,128)(2,1)}), bf16[32,49,1024]{2,1,0:T(8,128)(2,1)}, u32[]{:S(2)}, u32[]{:S(2)}) async-start(bf16[32,49,1024]{2,1,0:T(8,128)(2,1)} %bitcast_convert_fusion), calls=%async_computation.2 | async-start | bytes 7340032 | tf_op jit(solution)/shard_map/all_to_all | solution.py:23
  166.2 3.2 %convolution_bitcast_fusion.1 = f32[1,16,2,32,1024]{4,3,2,1,0:T(8,128)S(1)} fusion(bf16[16,2,32,768]{3,2,1,0:T(8,128)(2,1)S(1)} %bitcast.347, bf16[768,1024,1,1]{1,0,3,2:T(8,128)(2,1)} %bitcast.357), kind=kOutput, calls=%fused_computation.31 | convolution fusion | flops 1610612736 | bytes 7340032 | tf_op jit(solution)/shard_map/dot_general | solution.py:115
  177.3 3.7 %fusion.30 = f32[1,16,32,1024]{3,2,1,0:T(8,128)S(1)} fusion(f32[1,16,32,1024]{3,2,1,0:T(8,128)} %collective-permute-done.4, f32[1,16,2,32,1024]{4,3,2,1,0:T(8,128)} %copy-done.4, pred[]{:T(512)S(6)} %eq.147), kind=kLoop, calls=%fused_computation.38 | loop fusion | flops 1048576 | bytes 8388609 | tf_op jit(solution)/shard_map/add | solution.py:134
  182.7 2.3 bitcast_add_fusion
  185.6 26.9 %collective-permute-done.5 = bf16[1,8,32,1024]{3,2,1,0:T(8,128)(2,1)S(1)} collective-permute-done((bf16[1,8,32,1024]{3,2,1,0:T(8,128)(2,1)S(1)}, bf16[1,8,32,1024]{3,2,1,0:T(8,128)(2,1)S(1)}, u32[]{:S(2)}, u32[]{:S(2)}) %collective-permute-start.5) | collective-permute-done | bytes 524320 | tf_op jit(solution)/shard_map/ppermute | solution.py:133
  214.9 9.9 %collective-permute-done.10 = bf16[1,8,32,1024]{3,2,1,0:T(8,128)(2,1)S(1)} collective-permute-done((bf16[1,8,32,1024]{3,2,1,0:T(8,128)(2,1)S(1)}, bf16[1,8,32,1024]{3,2,1,0:T(8,128)(2,1)S(1)}, u32[]{:S(2)}, u32[]{:S(2)}) %collective-permute-start.10) | collective-permute-done | bytes 524320 | tf_op jit(solution)/shard_map/ppermute | solution.py:133
  225.1 2.7 %collective-permute-start.11 = (bf16[1,4,32,1024]{3,2,1,0:T(8,128)(2,1)S(1)}, bf16[1,4,32,1024]{3,2,1,0:T(8,128)(2,1)S(1)}, u32[]{:S(2)}, u32[]{:S(2)}) collective-permute-start(bf16[1,4,32,1024]{3,2,1,0:T(8,128)(2,1)S(1)} %fusion.51), channel_id=1, source_target_pairs={{0,4},{1,5},{2,6},{3,7},{4,0},{5,1},{6,2},{7,3},{8,12},{9,13},{10,... | collective-permute-start | bytes 786440 | tf_op jit(solution)/shard_map/ppermute | solution.py:133
  229.2 7.5 %collective-permute-done.11 = bf16[1,4,32,1024]{3,2,1,0:T(8,128)(2,1)S(1)} collective-permute-done((bf16[1,4,32,1024]{3,2,1,0:T(8,128)(2,1)S(1)}, bf16[1,4,32,1024]{3,2,1,0:T(8,128)(2,1)S(1)}, u32[]{:S(2)}, u32[]{:S(2)}) %collective-permute-start.11) | collective-permute-done | bytes 262176 | tf_op jit(solution)/shard_map/ppermute | solution.py:133
  238.8 2.7 %collective-permute-start.8 = (bf16[1,1,32,1024]{3,2,1,0:T(8,128)(2,1)S(1)}, bf16[1,1,32,1024]{3,2,1,0:T(8,128)(2,1)S(1)}, u32[]{:S(2)}, u32[]{:S(2)}) collective-permute-start(bf16[1,1,32,1024]{3,2,1,0:T(8,128)(2,1)S(1)} %fusion.67), channel_id=1, source_target_pairs={{0,16},{1,17},{2,18},{3,19},{4,20},{5,21},{6,22},{7,23},{8,24},{9,... | collective-permute-start | bytes 196616 | tf_op jit(solution)/shard_map/ppermute | solution.py:133
  243.3 3.4 %collective-permute-start.13 = (bf16[1,1,32,1024]{3,2,1,0:T(8,128)(2,1)S(1)}, bf16[1,1,32,1024]{3,2,1,0:T(8,128)(2,1)S(1)}, u32[]{:S(2)}, u32[]{:S(2)}) collective-permute-start(bf16[1,1,32,1024]{3,2,1,0:T(8,128)(2,1)S(1)} %fusion.68), channel_id=1, source_target_pairs={{0,16},{1,17},{2,18},{3,19},{4,20},{5,21},{6,22},{7,23},{8,24},{9,... | collective-permute-start | bytes 196616 | tf_op jit(solution)/shard_map/ppermute | solution.py:133
  246.7 7.1 %collective-permute-done.8 = bf16[1,1,32,1024]{3,2,1,0:T(8,128)(2,1)S(1)} collective-permute-done((bf16[1,1,32,1024]{3,2,1,0:T(8,128)(2,1)S(1)}, bf16[1,1,32,1024]{3,2,1,0:T(8,128)(2,1)S(1)}, u32[]{:S(2)}, u32[]{:S(2)}) %collective-permute-start.8) | collective-permute-done | bytes 65568 | tf_op jit(solution)/shard_map/ppermute | solution.py:133
  255.3 8.7 %fusion.23 = f32[1024,1024]{1,0:T(8,128)} fusion(bf16[32,49,1024]{2,1,0:T(8,128)(2,1)} %all-to-all-done.2, s32[32,49]{1,0:T(8,128)S(1)} %copy-done.19, pred[32,49]{1,0:T(8,128)(4,1)S(1)} %compare_bitcast_fusion), kind=kOutput, calls=%fused_computation.32 | convolution fusion | flops 3291545600 | bytes 7413408 | tf_op jit(solution)/shard_map/dot_general | solution.py:166
  (114 shorter events, 39.3 us)
Async XLA Ops:
  0.6 22.9 %copy-start = (bf16[1024,1024]{1,0:T(8,128)(2,1)S(1)}, bf16[1024,1024]{1,0:T(8,128)(2,1)}, u32[]{:S(2)}) copy-start(bf16[1024,1024]{1,0:T(8,128)(2,1)} %param.6) | copy-start | bytes 6291460
  29.0 3.9 %copy-start.14 = (bf16[1024,256]{1,0:T(8,128)(2,1)S(1)}, bf16[1024,256]{1,0:T(8,128)(2,1)}, u32[]{:S(2)}) copy-start(bf16[1024,256]{1,0:T(8,128)(2,1)} %param.10) | copy-start | bytes 1572868
  29.0 5.4 %copy-start.15 = (bf16[1024,256]{1,0:T(8,128)(2,1)S(1)}, bf16[1024,256]{1,0:T(8,128)(2,1)}, u32[]{:S(2)}) copy-start(bf16[1024,256]{1,0:T(8,128)(2,1)} %param.9) | copy-start | bytes 1572868
  29.0 6.0 %copy-start.17 = (s32[3,256]{1,0:T(4,128)S(1)}, s32[3,256]{1,0:T(4,128)}, u32[]{:S(2)}) copy-start(s32[3,256]{1,0:T(4,128)} %param.7) | copy-start | bytes 9220
  29.0 6.1 %copy-start.13 = (s32[3,256,256]{2,1,0:T(8,128)S(1)}, s32[3,256,256]{2,1,0:T(8,128)}, u32[]{:S(2)}) copy-start(s32[3,256,256]{2,1,0:T(8,128)} %param.8) | copy-start | bytes 2359300
  29.0 86.8 %all-to-all-start.1 = ((bf16[32,49,1024]{2,1,0:T(8,128)(2,1)}), bf16[32,49,1024]{2,1,0:T(8,128)(2,1)}, u32[]{:S(2)}, u32[]{:S(2)}) async-start(bf16[32,49,1024]{2,1,0:T(8,128)(2,1)} %fusion.20), calls=%async_computation.1 | async-start | bytes 7340032 | tf_op jit(solution)/shard_map/all_to_all | solution.py:23
  32.9 46.8 %collective-permute-start.2 = (bf16[1,1024,256]{2,1,0:T(8,128)(2,1)S(1)}, bf16[1,1024,256]{2,1,0:T(8,128)(2,1)S(1)}, u32[]{:S(2)}, u32[]{:S(2)}) collective-permute-start(bf16[1,1024,256]{2,1,0:T(8,128)(2,1)S(1)} %bitcast.349), channel_id=1, source_target_pairs={{0,2},{1,3},{2,0},{3,1},{4,6},{5,7},{6,4},{7,5},{8,10},{9,11},{10,... | collective-permute-start | bytes 1572872 | tf_op jit(solution)/shard_map/ppermute | solution.py:100
  34.4 56.7 %collective-permute-start = (bf16[1,1024,256]{2,1,0:T(8,128)(2,1)S(1)}, bf16[1,1024,256]{2,1,0:T(8,128)(2,1)}, u32[]{:S(2)}, u32[]{:S(2)}) collective-permute-start(bf16[1,1024,256]{2,1,0:T(8,128)(2,1)S(1)} %bitcast.350), channel_id=1, source_target_pairs={{0,2},{1,3},{2,0},{3,1},{4,6},{5,7},{6,4},{7,5},{8,10},{9,11},{10,... | collective-permute-start | bytes 1572872 | tf_op jit(solution)/shard_map/ppermute | solution.py:100
  92.5 5.6 %collective-permute-start.1 = (bf16[2,1024,256]{2,1,0:T(8,128)(2,1)S(1)}, bf16[2,1024,256]{2,1,0:T(8,128)(2,1)}, u32[]{:S(2)}, u32[]{:S(2)}) collective-permute-start(bf16[2,1024,256]{2,1,0:T(8,128)(2,1)S(1)} %pad_maximum_fusion.2), channel_id=1, source_target_pairs={{0,1},{1,0},{2,3},{3,2},{4,5},{5,4},{6,7},{7,6},{8,9},{9,8},{10,11... | collective-permute-start | bytes 3145736 | tf_op jit(solution)/shard_map/ppermute | solution.py:100
  94.3 5.5 %collective-permute-start.3 = (bf16[2,1024,256]{2,1,0:T(8,128)(2,1)}, bf16[2,1024,256]{2,1,0:T(8,128)(2,1)}, u32[]{:S(2)}, u32[]{:S(2)}) collective-permute-start(bf16[2,1024,256]{2,1,0:T(8,128)(2,1)} %pad_maximum_fusion.3), channel_id=1, source_target_pairs={{0,1},{1,0},{2,3},{3,2},{4,5},{5,4},{6,7},{7,6},{8,9},{9,8},{10,11... | collective-permute-start | bytes 3145736 | tf_op jit(solution)/shard_map/ppermute | solution.py:100
  99.9 3.8 %copy-start.5 = (bf16[2,2,1024,256]{3,2,1,0:T(8,128)(2,1)}, bf16[2,2,1024,256]{3,2,1,0:T(8,128)(2,1)S(1)}, u32[]{:S(2)}) copy-start(bf16[2,2,1024,256]{3,2,1,0:T(8,128)(2,1)S(1)} %copy.117) | copy-start | bytes 6291460
  115.8 7.2 %copy-start.8 = (bf16[4,256,1024]{2,1,0:T(8,128)(2,1)S(1)}, bf16[4,256,1024]{2,1,0:T(8,128)(2,1)}, u32[]{:S(2)}) copy-start(bf16[4,256,1024]{2,1,0:T(8,128)(2,1)} %copy.118) | copy-start | bytes 6291460
  132.4 4.0 %copy-start.7 = (bf16[2,2,1024,256]{3,2,1,0:T(8,128)(2,1)S(1)}, bf16[2,2,1024,256]{3,2,1,0:T(8,128)(2,1)}, u32[]{:S(2)}) copy-start(bf16[2,2,1024,256]{3,2,1,0:T(8,128)(2,1)} %copy.119) | copy-start | bytes 6291460
  149.5 2.8 %copy-start.6 = (bf16[2,2,1024,256]{3,2,1,0:T(8,128)(2,1)S(1)}, bf16[2,2,1024,256]{3,2,1,0:T(8,128)(2,1)}, u32[]{:S(2)}) copy-start(bf16[2,2,1024,256]{3,2,1,0:T(8,128)(2,1)} %copy-done.5) | copy-start | bytes 6291460
  161.1 5.1 %copy-start.12 = (bf16[768,1024]{0,1:T(8,128)(2,1)S(1)}, bf16[768,1024]{0,1:T(8,128)(2,1)}, u32[]{:S(2)}) copy-start(bf16[768,1024]{0,1:T(8,128)(2,1)} %copy.124) | copy-start | bytes 4718596
  161.1 94.2 %all-to-all-start.2 = ((bf16[32,49,1024]{2,1,0:T(8,128)(2,1)}), bf16[32,49,1024]{2,1,0:T(8,128)(2,1)}, u32[]{:S(2)}, u32[]{:S(2)}) async-start(bf16[32,49,1024]{2,1,0:T(8,128)(2,1)} %bitcast_convert_fusion), calls=%async_computation.2 | async-start | bytes 7340032 | tf_op jit(solution)/shard_map/all_to_all | solution.py:23
  169.4 3.1 %copy-start.4 = (f32[1,16,2,32,1024]{4,3,2,1,0:T(8,128)}, f32[1,16,2,32,1024]{4,3,2,1,0:T(8,128)S(1)}, u32[]{:S(2)}) copy-start(f32[1,16,2,32,1024]{4,3,2,1,0:T(8,128)S(1)} %convolution_bitcast_fusion.1) | copy-start | bytes 12582916
  169.4 3.1 %copy-start.10 = (bf16[3,256,1024]{2,1,0:T(8,128)(2,1)S(1)}, bf16[3,256,1024]{2,1,0:T(8,128)(2,1)}, u32[]{:S(2)}) copy-start(bf16[3,256,1024]{2,1,0:T(8,128)(2,1)} %copy-done.9) | copy-start | bytes 4718596
  169.5 4.1 %copy-start.11 = (bf16[768,1024]{0,1:T(8,128)(2,1)S(1)}, bf16[768,1024]{0,1:T(8,128)(2,1)}, u32[]{:S(2)}) copy-start(bf16[768,1024]{0,1:T(8,128)(2,1)} %copy.139) | copy-start | bytes 4718596
  172.6 4.7 %collective-permute-start.4 = (f32[1,16,32,1024]{3,2,1,0:T(8,128)}, f32[1,16,32,1024]{3,2,1,0:T(8,128)}, u32[]{:S(2)}, u32[]{:S(2)}) collective-permute-start(f32[1,16,32,1024]{3,2,1,0:T(8,128)} %select_bitcast_fusion.1), channel_id=1, source_target_pairs={{0,1},{1,0},{2,3},{3,2},{4,5},{5,4},{6,7},{7,6},{8,9},{9,8},{10,11... | collective-permute-start | bytes 6291464 | tf_op jit(solution)/shard_map/ppermute | solution.py:133
  177.3 5.5 %collective-permute-start.9 = (f32[1,16,32,1024]{3,2,1,0:T(8,128)S(1)}, f32[1,16,32,1024]{3,2,1,0:T(8,128)}, u32[]{:S(2)}, u32[]{:S(2)}) collective-permute-start(f32[1,16,32,1024]{3,2,1,0:T(8,128)S(1)} %select_bitcast_fusion), channel_id=1, source_target_pairs={{0,1},{1,0},{2,3},{3,2},{4,5},{5,4},{6,7},{7,6},{8,9},{9,8},{10,11... | collective-permute-start | bytes 6291464 | tf_op jit(solution)/shard_map/ppermute | solution.py:133
  177.3 5.4 %copy-start.3 = (f32[1,16,2,32,1024]{4,3,1,2,0:T(8,128)S(1)}, f32[1,16,2,32,1024]{4,3,1,2,0:T(8,128)}, u32[]{:S(2)}) copy-start(f32[1,16,2,32,1024]{4,3,1,2,0:T(8,128)} %copy-done.2) | copy-start | bytes 12582916
  181.1 31.5 %collective-permute-start.5 = (bf16[1,8,32,1024]{3,2,1,0:T(8,128)(2,1)S(1)}, bf16[1,8,32,1024]{3,2,1,0:T(8,128)(2,1)S(1)}, u32[]{:S(2)}, u32[]{:S(2)}) collective-permute-start(bf16[1,8,32,1024]{3,2,1,0:T(8,128)(2,1)S(1)} %fusion.45), channel_id=1, source_target_pairs={{0,2},{1,3},{2,0},{3,1},{4,6},{5,7},{6,4},{7,5},{8,10},{9,11},{10,... | collective-permute-start | bytes 1572872 | tf_op jit(solution)/shard_map/ppermute | solution.py:133
  185.1 39.7 %collective-permute-start.10 = (bf16[1,8,32,1024]{3,2,1,0:T(8,128)(2,1)S(1)}, bf16[1,8,32,1024]{3,2,1,0:T(8,128)(2,1)S(1)}, u32[]{:S(2)}, u32[]{:S(2)}) collective-permute-start(bf16[1,8,32,1024]{3,2,1,0:T(8,128)(2,1)S(1)} %fusion.46), channel_id=1, source_target_pairs={{0,2},{1,3},{2,0},{3,1},{4,6},{5,7},{6,4},{7,5},{8,10},{9,11},{10,... | collective-permute-start | bytes 1572872 | tf_op jit(solution)/shard_map/ppermute | solution.py:133
  212.9 14.9 %collective-permute-start.6 = (bf16[1,4,32,1024]{3,2,1,0:T(8,128)(2,1)S(1)}, bf16[1,4,32,1024]{3,2,1,0:T(8,128)(2,1)S(1)}, u32[]{:S(2)}, u32[]{:S(2)}) collective-permute-start(bf16[1,4,32,1024]{3,2,1,0:T(8,128)(2,1)S(1)} %fusion.50), channel_id=1, source_target_pairs={{0,4},{1,5},{2,6},{3,7},{4,0},{5,1},{6,2},{7,3},{8,12},{9,13},{10,... | collective-permute-start | bytes 786440 | tf_op jit(solution)/shard_map/ppermute | solution.py:133
  225.1 11.6 %collective-permute-start.11 = (bf16[1,4,32,1024]{3,2,1,0:T(8,128)(2,1)S(1)}, bf16[1,4,32,1024]{3,2,1,0:T(8,128)(2,1)S(1)}, u32[]{:S(2)}, u32[]{:S(2)}) collective-permute-start(bf16[1,4,32,1024]{3,2,1,0:T(8,128)(2,1)S(1)} %fusion.51), channel_id=1, source_target_pairs={{0,4},{1,5},{2,6},{3,7},{4,0},{5,1},{6,2},{7,3},{8,12},{9,13},{10,... | collective-permute-start | bytes 786440 | tf_op jit(solution)/shard_map/ppermute | solution.py:133
  228.0 10.7 %collective-permute-start.7 = (bf16[1,2,32,1024]{3,2,1,0:T(8,128)(2,1)S(1)}, bf16[1,2,32,1024]{3,2,1,0:T(8,128)(2,1)S(1)}, u32[]{:S(2)}, u32[]{:S(2)}) collective-permute-start(bf16[1,2,32,1024]{3,2,1,0:T(8,128)(2,1)S(1)} %fusion.57), channel_id=1, source_target_pairs={{0,8},{1,9},{2,10},{3,11},{4,12},{5,13},{6,14},{7,15},{8,0},{9,1},... | collective-permute-start | bytes 393224 | tf_op jit(solution)/shard_map/ppermute | solution.py:133
  236.8 18.5 %copy-start.19 = (s32[32,49]{1,0:T(8,128)S(1)}, s32[32,49]{1,0:T(8,128)}, u32[]{:S(2)}) copy-start(s32[32,49]{1,0:T(8,128)} %copy-done.18) | copy-start | bytes 18820
  236.8 6.4 %collective-permute-start.12 = (bf16[1,2,32,1024]{3,2,1,0:T(8,128)(2,1)S(1)}, bf16[1,2,32,1024]{3,2,1,0:T(8,128)(2,1)S(1)}, u32[]{:S(2)}, u32[]{:S(2)}) collective-permute-start(bf16[1,2,32,1024]{3,2,1,0:T(8,128)(2,1)S(1)} %fusion.58), channel_id=1, source_target_pairs={{0,8},{1,9},{2,10},{3,11},{4,12},{5,13},{6,14},{7,15},{8,0},{9,1},... | collective-permute-start | bytes 393224 | tf_op jit(solution)/shard_map/ppermute | solution.py:133
  238.8 15.0 %collective-permute-start.8 = (bf16[1,1,32,1024]{3,2,1,0:T(8,128)(2,1)S(1)}, bf16[1,1,32,1024]{3,2,1,0:T(8,128)(2,1)S(1)}, u32[]{:S(2)}, u32[]{:S(2)}) collective-permute-start(bf16[1,1,32,1024]{3,2,1,0:T(8,128)(2,1)S(1)} %fusion.67), channel_id=1, source_target_pairs={{0,16},{1,17},{2,18},{3,19},{4,20},{5,21},{6,22},{7,23},{8,24},{9,... | collective-permute-start | bytes 196616 | tf_op jit(solution)/shard_map/ppermute | solution.py:133
  243.3 11.3 %collective-permute-start.13 = (bf16[1,1,32,1024]{3,2,1,0:T(8,128)(2,1)S(1)}, bf16[1,1,32,1024]{3,2,1,0:T(8,128)(2,1)S(1)}, u32[]{:S(2)}, u32[]{:S(2)}) collective-permute-start(bf16[1,1,32,1024]{3,2,1,0:T(8,128)(2,1)S(1)} %fusion.68), channel_id=1, source_target_pairs={{0,16},{1,17},{2,18},{3,19},{4,20},{5,21},{6,22},{7,23},{8,24},{9,... | collective-permute-start | bytes 196616 | tf_op jit(solution)/shard_map/ppermute | solution.py:133
  255.3 8.7 %copy-start.1 = (bf16[1024,1024]{1,0:T(8,128)(2,1)S(1)}, bf16[1024,1024]{1,0:T(8,128)(2,1)}, u32[]{:S(2)}) copy-start(bf16[1024,1024]{1,0:T(8,128)(2,1)} %param.6) | copy-start | bytes 6291460
  (6 other events, 7.3 us)

commit v13 on v12

--- a/solution.py
+++ b/solution.py
@@ -119,20 +119,24 @@
             preferred_element_type=jnp.float32,
         )
 
-    def reduce_blocks(parts):
+    def reduce_blocks(parts, order):
         me = lax.axis_index(AXES)
-        step = 1
-        while step < shards:
+        bits = len(order)
+        axes = [1 + (bits - 1 - order[t]) for t in reversed(range(bits))]
+        parts = parts.reshape((parts.shape[0],) + (2,) * bits + parts.shape[2:])
+        parts = parts.transpose([0] + axes + [bits + 1, bits + 2])
+        parts = parts.reshape((parts.shape[0], shards) + parts.shape[bits + 1 :])
+        for t, bit in enumerate(order):
+            step = 1 << bit
             held = parts.shape[1]
             pair = parts.reshape(parts.shape[0], held // 2, 2, *parts.shape[2:])
             upper = (me // step) % 2 == 1
             keep = jnp.where(upper, pair[:, :, 1], pair[:, :, 0])
             send = jnp.where(upper, pair[:, :, 0], pair[:, :, 1])
-            if step > 1:
+            if t > 0:
                 send = send.astype(jnp.bfloat16)
             moved = lax.ppermute(send, AXES, [(i, i ^ step) for i in range(shards)])
             parts = keep + moved.astype(jnp.float32)
-            step *= 2
         return parts[:, 0] / (groups * shards)
 
     mixed_one, first_matmul_result, _ = forward_layer(None, whole_weight_one, spread_in)
@@ -166,8 +170,13 @@
     table_grad = lax.dot_general(
         picks, returned, (((0, 1), (0, 1)), ((), ())), preferred_element_type=jnp.float32
     )
-    grad_one = reduce_blocks(parts_one[None])[0].T
-    grad_two = reduce_blocks(parts_two[None])[0].T
+    bit_order = list(range(shards.bit_length() - 1))
+    swapped = list(bit_order)
+    cross = n_fsdp.bit_length() - 1
+    if 1 < cross < len(swapped):
+        swapped[1], swapped[cross] = swapped[cross], swapped[1]
+    grad_one = reduce_blocks(parts_one[None], bit_order)[0].T
+    grad_two = reduce_blocks(parts_two[None], swapped)[0].T
     return (table_grad, grad_one, grad_two)
 
 

time: 265 us -> 265 us (level)
  starting transfers between devices: 27.7 us -> 23.9 us
  waiting for transfers between devices: 115 us -> 118 us
    ppermute x10, starting transfers between devices: 16.1 us -> 12.3 us  [reduce_blocks(): moved = lax.ppermute(send, AXES, [(i, i ^ step) for i in range(shards)])]
    ppermute x10, waiting for transfers between devices: 53.3 us -> 56.2 us  [reduce_blocks(): moved = lax.ppermute(send, AXES, [(i, i ^ step) for i in range(shards)])]
where the time goes in v13:
time: 265 us; the launch traced here: 264 us
  waiting for transfers between devices  118 us (45%)
  matrix products  50.8 us (19%)
  local copies, waits for them, and re-layouts  31.7 us (12%)
  other arithmetic  24.2 us (9%)
  starting transfers between devices  23.9 us (9%)
  blocking collectives  14.3 us (5%)
    ppermute x10, waiting for transfers between devices, reduce_blocks(): moved = lax.ppermute(send, AXES, [(i, i ^ step) for i in range(shards)])  56.2 us
    ppermute x4, waiting for transfers between devices, gather_columns(): other = lax.ppermute(blocks, 'fsdp', [(i, i ^ step) for i in range(n_fsdp)])  55 us
    all_to_all x1, blocking collectives, exchange(): return lax.all_to_all(values, AXES, 0, 0, tiled=True)  14.3 us
    ppermute x10, starting transfers between devices, reduce_blocks(): moved = lax.ppermute(send, AXES, [(i, i ^ step) for i in range(shards)])  12.3 us
    all_to_all x2, starting transfers between devices, exchange(): return lax.all_to_all(values, AXES, 0, 0, tiled=True)  8.94 us
    dot_general x1, matrix products, step_body(): lax.dot_general(linked_slots, fetched_first.reshape(count, depth), (((0,)...  8.82 us
    dot_general x1, matrix products, step_body(): lax.dot_general(picks, returned, (((0, 1), (0, 1)), ((), ())), preferred_...  8.74 us
    unnamed x45, local copies, waits for them, and re-layouts  8.02 us
  transfers between devices with their start and end apart: 16, of which 9 were waited for; matrix products, arithmetic and copies ran while one was open for 13% of the time, Pallas kernels for 0%

profile of v13, /device:TPU:0, one launch (start us, length us, event | category | flops | bytes accessed | tf_op | source)
XLA Modules:
  0.0 264.0 jit_solution(1541981837402834755)
XLA Ops:
  5.1 3.4 %scatter_custom_fusion = s32[1568]{0:T(1024)S(1)} fusion(s32[768]{0:T(1024)S(1)} %fusion.77, s32[768]{0:T(1024)S(1)} %get-tuple-element.13, s32[]{:T(128)} %constant.167.clone.1), kind=kCustom, calls=%fused_computation.140 | custom fusion | bytes 6276 | tf_op jit(solution)/shard_map/scatter | solution.py:44
  8.6 14.3 %all_to_all.19 = s32[32,1,49]{2,1,0:T(1,128)S(1)} all-to-all(s32[32,1,49]{2,1,0:T(1,128)S(1)} %all_to_all.12), channel_id=1, replica_groups=mesh['node'=8,'fsdp'=4] {'node','fsdp'}, dimensions={0} | all-to-all | bytes 12544 | tf_op jit(solution)/shard_map/all_to_all | solution.py:23
  23.5 5.5 %fusion.20 = bf16[32,49,1024]{2,1,0:T(8,128)(2,1)} fusion(s32[32,49]{1,0:T(8,128)S(1)} %maximum_bitcast_fusion, pred[32,49]{1,0:T(8,128)(4,1)S(1)} %compare_bitcast_fusion, bf16[1024,1024]{1,0:T(8,128)(2,1)S(1)} %copy-done), kind=kOutput, calls=%fused_computation.29 | convolution fusion | flops 3293151232 | bytes 5316256 | tf_op jit(solution)/shard_map/dot_general | solution.py:51
  29.0 3.9 %all-to-all-start.1 = ((bf16[32,49,1024]{2,1,0:T(8,128)(2,1)}), bf16[32,49,1024]{2,1,0:T(8,128)(2,1)}, u32[]{:S(2)}, u32[]{:S(2)}) async-start(bf16[32,49,1024]{2,1,0:T(8,128)(2,1)} %fusion.20), calls=%async_computation.1 | async-start | bytes 7340032 | tf_op jit(solution)/shard_map/all_to_all | solution.py:23
  35.3 44.4 %collective-permute-done.2 = bf16[1,1024,256]{2,1,0:T(8,128)(2,1)S(1)} collective-permute-done((bf16[1,1024,256]{2,1,0:T(8,128)(2,1)S(1)}, bf16[1,1024,256]{2,1,0:T(8,128)(2,1)S(1)}, u32[]{:S(2)}, u32[]{:S(2)}) %collective-permute-start.2) | collective-permute-done | bytes 524320 | tf_op jit(solution)/shard_map/ppermute | solution.py:100
  80.4 10.6 %collective-permute-done = bf16[1,1024,256]{2,1,0:T(8,128)(2,1)} collective-permute-done((bf16[1,1024,256]{2,1,0:T(8,128)(2,1)S(1)}, bf16[1,1024,256]{2,1,0:T(8,128)(2,1)}, u32[]{:S(2)}, u32[]{:S(2)}) %collective-permute-start) | collective-permute-done | bytes 524320 | tf_op jit(solution)/shard_map/ppermute | solution.py:100
  94.9 3.2 %fusion.26 = bf16[3,256,32,49]{1,3,2,0:T(8,128)(2,1)} fusion(pred[3,256,49]{1,2,0:T(8,128)(4,1)S(1)} %iota_compare_fusion.2, pred[3,256,32]{1,2,0:T(8,128)(4,1)} %iota_compare_fusion.3, bf16[3,256,256]{2,1,0:T(8,128)(2,1)S(1)} %get-tuple-element.12), kind=kOutput, calls=%fused_computation.33 | convolution fusion | flops 618971136 | bytes 2863872 | tf_op jit(solution)/shard_map/gij,gjsc->gisc/dot_general | solution.py:61
  99.9 2.1 broadcast_select_fusion.1
  103.7 2.5 copy.128
  106.2 3.0 %copy.130 = bf16[4,256,1024]{2,1,0:T(8,128)(2,1)S(1)} copy(bf16[4,256,1024]{1,2,0:T(8,128)(2,1)} %bitcast.338) | data formatting | bytes 4194304 | tf_op jit(solution)/shard_map/dot_general | solution.py:82
  109.2 6.7 %all-to-all-done.1 = bf16[32,49,1024]{2,1,0:T(8,128)(2,1)} async-done(((bf16[32,49,1024]{2,1,0:T(8,128)(2,1)}), bf16[32,49,1024]{2,1,0:T(8,128)(2,1)}, u32[]{:S(2)}, u32[]{:S(2)}) %all-to-all-start.1) | async-done | bytes 3211296 | tf_op jit(solution)/shard_map/all_to_all | solution.py:23
  115.8 6.1 %fusion.17 = bf16[3,256,1024]{2,1,0:T(8,128)(2,1)S(1)} fusion(bf16[3,256,32,49]{1,3,2,0:T(8,128)(2,1)} %fusion.26, bf16[32,49,1024]{2,1,0:T(8,128)(2,1)} %all-to-all-done.1, f32[3,256]{1,0:T(4,128)S(1)} %add_rsqrt_fusion), kind=kOutput, calls=%fused_computation.23 | convolution fusion | flops 2467823616 | bytes 7195648 | tf_op jit(solution)/shard_map/dot_general | solution.py:70
  123.1 3.8 %multiply_convert_fusion.1 = (bf16[768,1024]{1,0:T(8,128)(2,1)S(1)}, f32[768,1024]{1,0:T(8,128)}) fusion(bf16[768,1024]{1,0:T(8,128)(2,1)S(1)} %bitcast.364, bf16[1024,1024]{1,0:T(8,128)(2,1)S(1)} %bitcast.351), kind=kOutput, calls=%fused_computation.25 | convolution fusion | flops 1614544896 | bytes 8388608 | tf_op jit(solution)/shard_map/dot_general | solution.py:82
  128.6 3.8 %fusion.13 = bf16[768,1024]{1,0:T(8,128)(2,1)} fusion(bf16[3,256,1024]{2,1,0:T(8,128)(2,1)S(1)} %copy-done.20, bf16[768,1024]{1,0:T(8,128)(2,1)S(1)} %bitcast.352, bf16[1024,1024]{1,0:T(8,128)(2,1)S(1)} %bitcast.350), kind=kOutput, calls=%fused_computation.15 | convolution fusion | flops 1618477056 | bytes 6815744 | tf_op jit(solution)/shard_map/dot_general | solution.py:82
  132.4 4.0 %dot_general.69 = bf16[3,256,4,256]{3,2,1,0:T(4,128)(2,1)} reshape(bf16[768,1024]{1,0:T(8,128)(2,1)} %fusion.13) | data formatting | bytes 3145728 | tf_op jit(solution)/shard_map/dot_general | solution.py:88
  136.4 5.3 %fusion.38 = f32[3,256,1024]{2,1,0:T(8,128)} fusion(bf16[3,256,256]{2,1,0:T(8,128)(2,1)S(1)} %get-tuple-element.12, bf16[4,1024,256,1]{2,1,0,3:T(8,128)(2,1)S(1)} %bitcast.339, bf16[3,256,4,256]{3,2,1,0:T(4,128)(2,1)} %dot_general.69, f32[3,256]{1,0:T(4,128)S(1)} %add_rsqrt_fusion), kind=kOutput, calls=%fused_computation.46 | convolution fusion | flops 2014838784 | bytes 7212032 | tf_op jit(solution)/shard_map/gji,gjd->gid/dot_general | solution.py:19
  141.7 3.9 %fusion.15 = bf16[768,1024]{1,0:T(8,128)(2,1)S(1)} fusion(f32[3,256,1024]{2,1,0:T(8,128)} %fusion.38, f32[768,1024]{1,0:T(8,128)} %get-tuple-element.16), kind=kLoop, calls=%fused_computation.19 | loop fusion | flops 7077888 | bytes 7864320 | tf_op jit(solution)/shard_map/convert_element_type | solution.py:157
  145.6 2.4 dot_general.72
  149.6 2.8 %copy.149 = bf16[768,1024]{0,1:T(8,128)(2,1)} copy(bf16[768,1024]{1,0:T(8,128)(2,1)} %fusion.13) | data formatting | bytes 3145728 | tf_op jit(solution)/shard_map/convert_element_type | solution.py:149
  152.3 8.8 %bitcast_convert_fusion = bf16[32,49,1024]{2,1,0:T(8,128)(2,1)} fusion(bf16[3,256,32,49]{1,3,2,0:T(8,128)(2,1)} %fusion.26, bf16[4,1024,256,1]{2,1,0,3:T(8,128)(2,1)S(1)} %bitcast.337, bf16[3,256,4,256]{3,2,1,0:T(4,128)(2,1)} %dot_general.72, f32[3,256]{1,0:T(4,128)S(1)} %add_rsqrt_fusion), kind=kOutput, calls=%fused_computation.1 | convolution fusion | flops 4080041984 | bytes 9292800 | tf_op jit(solution)/shard_map/dot_general | solution.py:163
  161.2 5.1 %all-to-all-start.2 = ((bf16[32,49,1024]{2,1,0:T(8,128)(2,1)}), bf16[32,49,1024]{2,1,0:T(8,128)(2,1)}, u32[]{:S(2)}, u32[]{:S(2)}) async-start(bf16[32,49,1024]{2,1,0:T(8,128)(2,1)} %bitcast_convert_fusion), calls=%async_computation.2 | async-start | bytes 7340032 | tf_op jit(solution)/shard_map/all_to_all | solution.py:23
  166.3 3.2 %convolution_bitcast_fusion.1 = f32[1,16,2,32,1024]{4,3,2,1,0:T(8,128)S(1)} fusion(bf16[16,2,32,768]{3,2,1,0:T(8,128)(2,1)S(1)} %bitcast.355, bf16[768,1024,1,1]{1,0,3,2:T(8,128)(2,1)} %bitcast.365), kind=kOutput, calls=%fused_computation.31 | convolution fusion | flops 1610612736 | bytes 7340032 | tf_op jit(solution)/shard_map/dot_general | solution.py:115
  177.9 3.9 %fusion.30 = f32[1,16,32,1024]{3,2,1,0:T(8,128)S(1)} fusion(f32[1,16,32,1024]{3,2,1,0:T(8,128)} %collective-permute-done.4, f32[1,16,2,32,1024]{4,3,2,1,0:T(8,128)} %copy-done.4, pred[]{:T(512)S(6)} %eq.147), kind=kLoop, calls=%fused_computation.38 | loop fusion | flops 1048576 | bytes 8388609 | tf_op jit(solution)/shard_map/add | solution.py:139
  183.6 2.3 bitcast_add_fusion
  187.5 25.0 %collective-permute-done.5 = bf16[1,8,32,1024]{3,2,1,0:T(8,128)(2,1)S(1)} collective-permute-done((bf16[1,8,32,1024]{3,2,1,0:T(8,128)(2,1)S(1)}, bf16[1,8,32,1024]{3,2,1,0:T(8,128)(2,1)S(1)}, u32[]{:S(2)}, u32[]{:S(2)}) %collective-permute-start.5) | collective-permute-done | bytes 524320 | tf_op jit(solution)/shard_map/ppermute | solution.py:138
  212.8 2.1 collective-permute-start.6
  215.9 8.3 %collective-permute-done.6 = bf16[1,4,32,1024]{3,2,1,0:T(8,128)(2,1)S(1)} collective-permute-done((bf16[1,4,32,1024]{3,2,1,0:T(8,128)(2,1)S(1)}, bf16[1,4,32,1024]{3,2,1,0:T(8,128)(2,1)S(1)}, u32[]{:S(2)}, u32[]{:S(2)}) %collective-permute-start.6) | collective-permute-done | bytes 262176 | tf_op jit(solution)/shard_map/ppermute | solution.py:138
  224.5 2.1 collective-permute-start.12
  226.6 5.9 %collective-permute-done.7 = bf16[1,2,32,1024]{3,2,1,0:T(8,128)(2,1)S(1)} collective-permute-done((bf16[1,2,32,1024]{3,2,1,0:T(8,128)(2,1)S(1)}, bf16[1,2,32,1024]{3,2,1,0:T(8,128)(2,1)S(1)}, u32[]{:S(2)}, u32[]{:S(2)}) %collective-permute-start.7) | collective-permute-done | bytes 131104 | tf_op jit(solution)/shard_map/ppermute | solution.py:138
  234.5 2.5 collective-permute-start.13
  237.1 16.7 %collective-permute-done.8 = bf16[1,1,32,1024]{3,2,1,0:T(8,128)(2,1)S(1)} collective-permute-done((bf16[1,1,32,1024]{3,2,1,0:T(8,128)(2,1)S(1)}, bf16[1,1,32,1024]{3,2,1,0:T(8,128)(2,1)S(1)}, u32[]{:S(2)}, u32[]{:S(2)}) %collective-permute-start.8) | collective-permute-done | bytes 65568 | tf_op jit(solution)/shard_map/ppermute | solution.py:138
  255.3 8.7 %fusion.23 = f32[1024,1024]{1,0:T(8,128)} fusion(bf16[32,49,1024]{2,1,0:T(8,128)(2,1)} %all-to-all-done.2, s32[32,49]{1,0:T(8,128)S(1)} %copy-done.19, pred[32,49]{1,0:T(8,128)(4,1)S(1)} %compare_bitcast_fusion), kind=kOutput, calls=%fused_computation.32 | convolution fusion | flops 3291545600 | bytes 7413408 | tf_op jit(solution)/shard_map/dot_general | solution.py:170
  (115 shorter events, 36.8 us)
Async XLA Ops:
  0.6 22.9 %copy-start = (bf16[1024,1024]{1,0:T(8,128)(2,1)S(1)}, bf16[1024,1024]{1,0:T(8,128)(2,1)}, u32[]{:S(2)}) copy-start(bf16[1024,1024]{1,0:T(8,128)(2,1)} %param.6) | copy-start | bytes 6291460
  29.0 3.9 %copy-start.14 = (bf16[1024,256]{1,0:T(8,128)(2,1)S(1)}, bf16[1024,256]{1,0:T(8,128)(2,1)}, u32[]{:S(2)}) copy-start(bf16[1024,256]{1,0:T(8,128)(2,1)} %param.10) | copy-start | bytes 1572868
  29.0 5.4 %copy-start.15 = (bf16[1024,256]{1,0:T(8,128)(2,1)S(1)}, bf16[1024,256]{1,0:T(8,128)(2,1)}, u32[]{:S(2)}) copy-start(bf16[1024,256]{1,0:T(8,128)(2,1)} %param.9) | copy-start | bytes 1572868
  29.0 6.0 %copy-start.17 = (s32[3,256]{1,0:T(4,128)S(1)}, s32[3,256]{1,0:T(4,128)}, u32[]{:S(2)}) copy-start(s32[3,256]{1,0:T(4,128)} %param.7) | copy-start | bytes 9220
  29.0 6.1 %copy-start.13 = (s32[3,256,256]{2,1,0:T(8,128)S(1)}, s32[3,256,256]{2,1,0:T(8,128)}, u32[]{:S(2)}) copy-start(s32[3,256,256]{2,1,0:T(8,128)} %param.8) | copy-start | bytes 2359300
  29.0 86.8 %all-to-all-start.1 = ((bf16[32,49,1024]{2,1,0:T(8,128)(2,1)}), bf16[32,49,1024]{2,1,0:T(8,128)(2,1)}, u32[]{:S(2)}, u32[]{:S(2)}) async-start(bf16[32,49,1024]{2,1,0:T(8,128)(2,1)} %fusion.20), calls=%async_computation.1 | async-start | bytes 7340032 | tf_op jit(solution)/shard_map/all_to_all | solution.py:23
  32.9 46.8 %collective-permute-start.2 = (bf16[1,1024,256]{2,1,0:T(8,128)(2,1)S(1)}, bf16[1,1024,256]{2,1,0:T(8,128)(2,1)S(1)}, u32[]{:S(2)}, u32[]{:S(2)}) collective-permute-start(bf16[1,1024,256]{2,1,0:T(8,128)(2,1)S(1)} %bitcast.357), channel_id=1, source_target_pairs={{0,2},{1,3},{2,0},{3,1},{4,6},{5,7},{6,4},{7,5},{8,10},{9,11},{10,... | collective-permute-start | bytes 1572872 | tf_op jit(solution)/shard_map/ppermute | solution.py:100
  34.4 56.7 %collective-permute-start = (bf16[1,1024,256]{2,1,0:T(8,128)(2,1)S(1)}, bf16[1,1024,256]{2,1,0:T(8,128)(2,1)}, u32[]{:S(2)}, u32[]{:S(2)}) collective-permute-start(bf16[1,1024,256]{2,1,0:T(8,128)(2,1)S(1)} %bitcast.358), channel_id=1, source_target_pairs={{0,2},{1,3},{2,0},{3,1},{4,6},{5,7},{6,4},{7,5},{8,10},{9,11},{10,... | collective-permute-start | bytes 1572872 | tf_op jit(solution)/shard_map/ppermute | solution.py:100
  92.5 5.6 %collective-permute-start.1 = (bf16[2,1024,256]{2,1,0:T(8,128)(2,1)S(1)}, bf16[2,1024,256]{2,1,0:T(8,128)(2,1)}, u32[]{:S(2)}, u32[]{:S(2)}) collective-permute-start(bf16[2,1024,256]{2,1,0:T(8,128)(2,1)S(1)} %pad_maximum_fusion.2), channel_id=1, source_target_pairs={{0,1},{1,0},{2,3},{3,2},{4,5},{5,4},{6,7},{7,6},{8,9},{9,8},{10,11... | collective-permute-start | bytes 3145736 | tf_op jit(solution)/shard_map/ppermute | solution.py:100
  94.4 5.5 %collective-permute-start.3 = (bf16[2,1024,256]{2,1,0:T(8,128)(2,1)}, bf16[2,1024,256]{2,1,0:T(8,128)(2,1)}, u32[]{:S(2)}, u32[]{:S(2)}) collective-permute-start(bf16[2,1024,256]{2,1,0:T(8,128)(2,1)} %pad_maximum_fusion.3), channel_id=1, source_target_pairs={{0,1},{1,0},{2,3},{3,2},{4,5},{5,4},{6,7},{7,6},{8,9},{9,8},{10,11... | collective-permute-start | bytes 3145736 | tf_op jit(solution)/shard_map/ppermute | solution.py:100
  99.9 3.8 %copy-start.5 = (bf16[2,2,1024,256]{3,2,1,0:T(8,128)(2,1)}, bf16[2,2,1024,256]{3,2,1,0:T(8,128)(2,1)S(1)}, u32[]{:S(2)}) copy-start(bf16[2,2,1024,256]{3,2,1,0:T(8,128)(2,1)S(1)} %copy.127) | copy-start | bytes 6291460
  115.8 7.2 %copy-start.8 = (bf16[4,256,1024]{2,1,0:T(8,128)(2,1)S(1)}, bf16[4,256,1024]{2,1,0:T(8,128)(2,1)}, u32[]{:S(2)}) copy-start(bf16[4,256,1024]{2,1,0:T(8,128)(2,1)} %copy.128) | copy-start | bytes 6291460
  132.4 4.0 %copy-start.7 = (bf16[2,2,1024,256]{3,2,1,0:T(8,128)(2,1)S(1)}, bf16[2,2,1024,256]{3,2,1,0:T(8,128)(2,1)}, u32[]{:S(2)}) copy-start(bf16[2,2,1024,256]{3,2,1,0:T(8,128)(2,1)} %copy.129) | copy-start | bytes 6291460
  149.6 2.8 %copy-start.6 = (bf16[2,2,1024,256]{3,2,1,0:T(8,128)(2,1)S(1)}, bf16[2,2,1024,256]{3,2,1,0:T(8,128)(2,1)}, u32[]{:S(2)}) copy-start(bf16[2,2,1024,256]{3,2,1,0:T(8,128)(2,1)} %copy-done.5) | copy-start | bytes 6291460
  161.2 5.1 %copy-start.12 = (bf16[768,1024]{0,1:T(8,128)(2,1)S(1)}, bf16[768,1024]{0,1:T(8,128)(2,1)}, u32[]{:S(2)}) copy-start(bf16[768,1024]{0,1:T(8,128)(2,1)} %copy.134) | copy-start | bytes 4718596
  161.2 94.1 %all-to-all-start.2 = ((bf16[32,49,1024]{2,1,0:T(8,128)(2,1)}), bf16[32,49,1024]{2,1,0:T(8,128)(2,1)}, u32[]{:S(2)}, u32[]{:S(2)}) async-start(bf16[32,49,1024]{2,1,0:T(8,128)(2,1)} %bitcast_convert_fusion), calls=%async_computation.2 | async-start | bytes 7340032 | tf_op jit(solution)/shard_map/all_to_all | solution.py:23
  169.5 2.6 copy-start.10
  169.5 3.4 %copy-start.11 = (bf16[768,1024]{0,1:T(8,128)(2,1)S(1)}, bf16[768,1024]{0,1:T(8,128)(2,1)}, u32[]{:S(2)}) copy-start(bf16[768,1024]{0,1:T(8,128)(2,1)} %copy.149) | copy-start | bytes 4718596
  171.6 6.3 %collective-permute-start.4 = (f32[1,16,32,1024]{3,2,1,0:T(8,128)S(1)}, f32[1,16,32,1024]{3,2,1,0:T(8,128)}, u32[]{:S(2)}, u32[]{:S(2)}) collective-permute-start(f32[1,16,32,1024]{3,2,1,0:T(8,128)S(1)} %select_bitcast_fusion.1), channel_id=1, source_target_pairs={{0,1},{1,0},{2,3},{3,2},{4,5},{5,4},{6,7},{7,6},{8,9},{9,8},{10,11... | collective-permute-start | bytes 6291464 | tf_op jit(solution)/shard_map/ppermute | solution.py:138
  175.2 2.7 %copy-start.2 = (f32[1,2,2,2,2,2,32,1024]{7,6,4,3,2,1,5,0:T(8,128)}, f32[1,2,2,2,2,2,32,1024]{7,6,4,3,2,1,5,0:T(8,128)S(1)}, u32[]{:S(2)}) copy-start(f32[1,2,2,2,2,2,32,1024]{7,6,4,3,2,1,5,0:T(8,128)S(1)} %copy.150) | copy-start | bytes 12582916
  177.9 5.6 %collective-permute-start.9 = (f32[1,16,32,1024]{3,2,1,0:T(8,128)}, f32[1,16,32,1024]{3,2,1,0:T(8,128)}, u32[]{:S(2)}, u32[]{:S(2)}) collective-permute-start(f32[1,16,32,1024]{3,2,1,0:T(8,128)} %select_bitcast_fusion), channel_id=1, source_target_pairs={{0,1},{1,0},{2,3},{3,2},{4,5},{5,4},{6,7},{7,6},{8,9},{9,8},{10,11... | collective-permute-start | bytes 6291464 | tf_op jit(solution)/shard_map/ppermute | solution.py:138
  177.9 5.6 %copy-start.3 = (f32[1,2,2,2,2,2,32,1024]{7,6,4,3,2,1,5,0:T(8,128)S(1)}, f32[1,2,2,2,2,2,32,1024]{7,6,4,3,2,1,5,0:T(8,128)}, u32[]{:S(2)}) copy-start(f32[1,2,2,2,2,2,32,1024]{7,6,4,3,2,1,5,0:T(8,128)} %copy-done.2) | copy-start | bytes 12582916
  181.9 30.6 %collective-permute-start.5 = (bf16[1,8,32,1024]{3,2,1,0:T(8,128)(2,1)S(1)}, bf16[1,8,32,1024]{3,2,1,0:T(8,128)(2,1)S(1)}, u32[]{:S(2)}, u32[]{:S(2)}) collective-permute-start(bf16[1,8,32,1024]{3,2,1,0:T(8,128)(2,1)S(1)} %fusion.44), channel_id=1, source_target_pairs={{0,2},{1,3},{2,0},{3,1},{4,6},{5,7},{6,4},{7,5},{8,10},{9,11},{10,... | collective-permute-start | bytes 1572872 | tf_op jit(solution)/shard_map/ppermute | solution.py:138
  185.9 28.9 %collective-permute-start.10 = (bf16[1,8,32,1024]{3,2,1,0:T(8,128)(2,1)S(1)}, bf16[1,8,32,1024]{3,2,1,0:T(8,128)(2,1)S(1)}, u32[]{:S(2)}, u32[]{:S(2)}) collective-permute-start(bf16[1,8,32,1024]{3,2,1,0:T(8,128)(2,1)S(1)} %fusion.45), channel_id=1, source_target_pairs={{0,4},{1,5},{2,6},{3,7},{4,0},{5,1},{6,2},{7,3},{8,12},{9,13},{10,... | collective-permute-start | bytes 1572872 | tf_op jit(solution)/shard_map/ppermute | solution.py:138
  212.8 11.3 %collective-permute-start.6 = (bf16[1,4,32,1024]{3,2,1,0:T(8,128)(2,1)S(1)}, bf16[1,4,32,1024]{3,2,1,0:T(8,128)(2,1)S(1)}, u32[]{:S(2)}, u32[]{:S(2)}) collective-permute-start(bf16[1,4,32,1024]{3,2,1,0:T(8,128)(2,1)S(1)} %fusion.51), channel_id=1, source_target_pairs={{0,4},{1,5},{2,6},{3,7},{4,0},{5,1},{6,2},{7,3},{8,12},{9,13},{10,... | collective-permute-start | bytes 786440 | tf_op jit(solution)/shard_map/ppermute | solution.py:138
  215.2 9.2 %collective-permute-start.11 = (bf16[1,4,32,1024]{3,2,1,0:T(8,128)(2,1)S(1)}, bf16[1,4,32,1024]{3,2,1,0:T(8,128)(2,1)S(1)}, u32[]{:S(2)}, u32[]{:S(2)}) collective-permute-start(bf16[1,4,32,1024]{3,2,1,0:T(8,128)(2,1)S(1)} %fusion.52), channel_id=1, source_target_pairs={{0,2},{1,3},{2,0},{3,1},{4,6},{5,7},{6,4},{7,5},{8,10},{9,11},{10,... | collective-permute-start | bytes 786440 | tf_op jit(solution)/shard_map/ppermute | solution.py:138
  224.3 8.2 %collective-permute-start.7 = (bf16[1,2,32,1024]{3,2,1,0:T(8,128)(2,1)S(1)}, bf16[1,2,32,1024]{3,2,1,0:T(8,128)(2,1)S(1)}, u32[]{:S(2)}, u32[]{:S(2)}) collective-permute-start(bf16[1,2,32,1024]{3,2,1,0:T(8,128)(2,1)S(1)} %fusion.58), channel_id=1, source_target_pairs={{0,8},{1,9},{2,10},{3,11},{4,12},{5,13},{6,14},{7,15},{8,0},{9,1},... | collective-permute-start | bytes 393224 | tf_op jit(solution)/shard_map/ppermute | solution.py:138
  224.5 30.8 %copy-start.19 = (s32[32,49]{1,0:T(8,128)S(1)}, s32[32,49]{1,0:T(8,128)}, u32[]{:S(2)}) copy-start(s32[32,49]{1,0:T(8,128)} %copy-done.18) | copy-start | bytes 18820
  224.5 9.9 %collective-permute-start.12 = (bf16[1,2,32,1024]{3,2,1,0:T(8,128)(2,1)S(1)}, bf16[1,2,32,1024]{3,2,1,0:T(8,128)(2,1)S(1)}, u32[]{:S(2)}, u32[]{:S(2)}) collective-permute-start(bf16[1,2,32,1024]{3,2,1,0:T(8,128)(2,1)S(1)} %fusion.59), channel_id=1, source_target_pairs={{0,8},{1,9},{2,10},{3,11},{4,12},{5,13},{6,14},{7,15},{8,0},{9,1},... | collective-permute-start | bytes 393224 | tf_op jit(solution)/shard_map/ppermute | solution.py:138
  232.5 21.2 %collective-permute-start.8 = (bf16[1,1,32,1024]{3,2,1,0:T(8,128)(2,1)S(1)}, bf16[1,1,32,1024]{3,2,1,0:T(8,128)(2,1)S(1)}, u32[]{:S(2)}, u32[]{:S(2)}) collective-permute-start(bf16[1,1,32,1024]{3,2,1,0:T(8,128)(2,1)S(1)} %fusion.68), channel_id=1, source_target_pairs={{0,16},{1,17},{2,18},{3,19},{4,20},{5,21},{6,22},{7,23},{8,24},{9,... | collective-permute-start | bytes 196616 | tf_op jit(solution)/shard_map/ppermute | solution.py:138
  234.5 20.0 %collective-permute-start.13 = (bf16[1,1,32,1024]{3,2,1,0:T(8,128)(2,1)S(1)}, bf16[1,1,32,1024]{3,2,1,0:T(8,128)(2,1)S(1)}, u32[]{:S(2)}, u32[]{:S(2)}) collective-permute-start(bf16[1,1,32,1024]{3,2,1,0:T(8,128)(2,1)S(1)} %fusion.69), channel_id=1, source_target_pairs={{0,16},{1,17},{2,18},{3,19},{4,20},{5,21},{6,22},{7,23},{8,24},{9,... | collective-permute-start | bytes 196616 | tf_op jit(solution)/shard_map/ppermute | solution.py:138
  255.3 8.7 %copy-start.1 = (bf16[1024,1024]{1,0:T(8,128)(2,1)S(1)}, bf16[1024,1024]{1,0:T(8,128)(2,1)}, u32[]{:S(2)}) copy-start(bf16[1024,1024]{1,0:T(8,128)(2,1)} %param.6) | copy-start | bytes 6291460
  (6 other events, 7.6 us)

commit v14 on v12

--- a/solution.py
+++ b/solution.py
@@ -79,17 +79,12 @@
             .astype(jnp.bfloat16)
             .reshape(count, depth)
         )
-        product = lax.dot_general(
-            mixed, weight, (((1,), (1,)), ((), ())), preferred_element_type=jnp.float32
-        ).reshape(count, depth)
+        product = jnp.dot(mixed, weight, preferred_element_type=jnp.float32)
         return (mixed, product, weight)
 
     def back_weight(delta, weight):
         return lax.dot_general(
-            delta.reshape(count, n_fsdp, weight.shape[2]),
-            weight,
-            (((1, 2), (0, 2)), ((), ())),
-            preferred_element_type=jnp.float32,
+            delta, weight, (((1,), (1,)), ((), ())), preferred_element_type=jnp.float32
         )
 
     def gather_columns(weight):
@@ -106,7 +101,8 @@
         bits = n_fsdp.bit_length() - 1
         blocks = blocks.reshape((2,) * bits + weight.shape)
         blocks = blocks.transpose(tuple(range(bits))[::-1] + (bits, bits + 1))
-        return blocks.reshape((n_fsdp,) + weight.shape)
+        blocks = blocks.reshape((n_fsdp,) + weight.shape)
+        return blocks.transpose(1, 0, 2).reshape(weight.shape[0], n_fsdp * weight.shape[1])
 
     whole_weight_one = gather_columns(weight_one)
     whole_weight_two = gather_columns(weight_two)

time: 265 us -> 256 us (0.966)
  local copies, waits for them, and re-layouts: 31.3 us -> 27.2 us
  waiting for transfers between devices: 115 us -> 112 us
    dot_general x4 -> x0, local copies, waits for them, and re-layouts: 11.8 us -> none  [the longest x2 6.37 us: back_weight(): lax.dot_general(delta.reshape(count, n_fsdp, weight.shape[2]), weight, ((...]
    transpose x0 -> x2, local copies, waits for them, and re-layouts: none -> 7.97 us  [gather_columns(): blocks.transpose(1, 0, 2).reshape(weight.shape[0], n_fsdp * weight.shape[1])]
    all_to_all x2, waiting for transfers between devices: 6.65 us -> 3.98 us  [exchange(): return lax.all_to_all(values, AXES, 0, 0, tiled=True)]
    unnamed x45 -> x41, local copies, waits for them, and re-layouts: 8.17 us -> 6.86 us
  transfers between devices with their start and end apart: 16 -> 16, of which waited for: 9 -> 9; matrix products, arithmetic and copies ran while one was open for 13% -> 14% of each run, Pallas kernels for 0% -> 0%
where the time goes in v14:
time: 256 us
  waiting for transfers between devices  112 us (44%)
  matrix products  50.2 us (20%)
  starting transfers between devices  28.2 us (11%)
  local copies, waits for them, and re-layouts  27.2 us (11%)
  other arithmetic  22.8 us (9%)
  blocking collectives  14.3 us (6%)
    ppermute x4, waiting for transfers between devices, gather_columns(): other = lax.ppermute(blocks, 'fsdp', [(i, i ^ step) for i in range(n_fsdp)])  55 us
    ppermute x10, waiting for transfers between devices, reduce_blocks(): moved = lax.ppermute(send, AXES, [(i, i ^ step) for i in range(shards)])  52.9 us
    ppermute x10, starting transfers between devices, reduce_blocks(): moved = lax.ppermute(send, AXES, [(i, i ^ step) for i in range(shards)])  16.9 us
    all_to_all x1, blocking collectives, exchange(): return lax.all_to_all(values, AXES, 0, 0, tiled=True)  14.3 us
    dot_general x1, matrix products, step_body(): lax.dot_general(picks, returned, (((0, 1), (0, 1)), ((), ())), preferred_...  8.74 us
    all_to_all x2, starting transfers between devices, exchange(): return lax.all_to_all(values, AXES, 0, 0, tiled=True)  8.67 us
    dot_general x1, matrix products, step_body(): lax.dot_general(linked_slots, fetched_first.reshape(count, depth), (((0,)...  8.29 us
    transpose x2, local copies, waits for them, and re-layouts, gather_columns(): blocks.transpose(1, 0, 2).reshape(weight.shape[0], n_fsdp * weight.shape[1])  7.97 us
  transfers between devices with their start and end apart: 16, of which 9 were waited for; matrix products, arithmetic and copies ran while one was open for 14% of the time, Pallas kernels for 0%

profile of v14, /device:TPU:0, one launch (start us, length us, event | category | flops | bytes accessed | tf_op | source)
XLA Modules:
  0.0 255.6 jit_solution(17378755105752291792)
XLA Ops:
  5.1 3.4 %scatter_custom_fusion = s32[1568]{0:T(1024)S(1)} fusion(s32[768]{0:T(1024)S(1)} %fusion.66, s32[768]{0:T(1024)S(1)} %get-tuple-element.13, s32[]{:T(128)} %constant.167.clone.1), kind=kCustom, calls=%fused_computation.137 | custom fusion | bytes 6276 | tf_op jit(solution)/shard_map/scatter | solution.py:44
  8.6 14.3 %all_to_all.19 = s32[32,1,49]{2,1,0:T(1,128)S(1)} all-to-all(s32[32,1,49]{2,1,0:T(1,128)S(1)} %all_to_all.12), channel_id=1, replica_groups=mesh['node'=8,'fsdp'=4] {'node','fsdp'}, dimensions={0} | all-to-all | bytes 12544 | tf_op jit(solution)/shard_map/all_to_all | solution.py:23
  23.5 5.5 %fusion.18 = bf16[32,49,1024]{2,1,0:T(8,128)(2,1)} fusion(s32[32,49]{1,0:T(8,128)S(1)} %maximum_bitcast_fusion, pred[32,49]{1,0:T(8,128)(4,1)S(1)} %compare_bitcast_fusion, bf16[1024,1024]{1,0:T(8,128)(2,1)S(1)} %copy-done), kind=kOutput, calls=%fused_computation.27 | convolution fusion | flops 3293151232 | bytes 5316256 | tf_op jit(solution)/shard_map/dot_general | solution.py:51
  29.0 3.9 %all-to-all-start.1 = ((bf16[32,49,1024]{2,1,0:T(8,128)(2,1)}), bf16[32,49,1024]{2,1,0:T(8,128)(2,1)}, u32[]{:S(2)}, u32[]{:S(2)}) async-start(bf16[32,49,1024]{2,1,0:T(8,128)(2,1)} %fusion.18), calls=%async_computation.1 | async-start | bytes 7340032 | tf_op jit(solution)/shard_map/all_to_all | solution.py:23
  35.3 44.4 %collective-permute-done.2 = bf16[1,1024,256]{2,1,0:T(8,128)(2,1)S(1)} collective-permute-done((bf16[1,1024,256]{2,1,0:T(8,128)(2,1)S(1)}, bf16[1,1024,256]{2,1,0:T(8,128)(2,1)S(1)}, u32[]{:S(2)}, u32[]{:S(2)}) %collective-permute-start.2) | collective-permute-done | bytes 524320 | tf_op jit(solution)/shard_map/ppermute | solution.py:95
  80.5 10.6 %collective-permute-done = bf16[1,1024,256]{2,1,0:T(8,128)(2,1)} collective-permute-done((bf16[1,1024,256]{2,1,0:T(8,128)(2,1)S(1)}, bf16[1,1024,256]{2,1,0:T(8,128)(2,1)}, u32[]{:S(2)}, u32[]{:S(2)}) %collective-permute-start) | collective-permute-done | bytes 524320 | tf_op jit(solution)/shard_map/ppermute | solution.py:95
  95.8 3.3 %fusion.24 = bf16[3,256,32,49]{1,3,2,0:T(8,128)(2,1)} fusion(pred[3,256,49]{1,2,0:T(8,128)(4,1)S(1)} %iota_compare_fusion.2, pred[3,256,32]{1,2,0:T(8,128)(4,1)} %iota_compare_fusion.3, bf16[3,256,256]{2,1,0:T(8,128)(2,1)S(1)} %get-tuple-element.12), kind=kOutput, calls=%fused_computation.31 | convolution fusion | flops 618971136 | bytes 2863872 | tf_op jit(solution)/shard_map/gij,gjsc->gisc/dot_general | solution.py:61
  102.1 4.0 %copy.118 = bf16[1024,4,256]{0,2,1:T(8,128)(2,1)} copy(bf16[1024,4,256]{2,0,1:T(8,128)(2,1)} %bitcast.318) | data formatting | bytes 4194304 | tf_op jit(solution)/shard_map/transpose | solution.py:105
  107.9 4.0 %copy.120 = bf16[1024,4,256]{0,2,1:T(8,128)(2,1)} copy(bf16[1024,4,256]{2,0,1:T(8,128)(2,1)} %bitcast.319) | data formatting | bytes 4194304 | tf_op jit(solution)/shard_map/transpose | solution.py:105
  111.9 4.0 %all-to-all-done.1 = bf16[32,49,1024]{2,1,0:T(8,128)(2,1)} async-done(((bf16[32,49,1024]{2,1,0:T(8,128)(2,1)}), bf16[32,49,1024]{2,1,0:T(8,128)(2,1)}, u32[]{:S(2)}, u32[]{:S(2)}) %all-to-all-start.1) | async-done | bytes 3211296 | tf_op jit(solution)/shard_map/all_to_all | solution.py:23
  115.8 5.9 %fusion.15 = bf16[3,256,1024]{2,1,0:T(8,128)(2,1)S(1)} fusion(bf16[3,256,32,49]{1,3,2,0:T(8,128)(2,1)} %fusion.24, bf16[32,49,1024]{2,1,0:T(8,128)(2,1)} %all-to-all-done.1, f32[3,256]{1,0:T(4,128)S(1)} %add_rsqrt_fusion), kind=kOutput, calls=%fused_computation.19 | convolution fusion | flops 2467823616 | bytes 7195648 | tf_op jit(solution)/shard_map/dot_general | solution.py:70
  121.8 3.8 %multiply_convert_fusion.3 = (bf16[768,1024]{1,0:T(8,128)(2,1)S(1)}, f32[768,1024]{1,0:T(8,128)}) fusion(bf16[768,1024]{1,0:T(8,128)(2,1)S(1)} %bitcast.346, bf16[1024,1024]{0,1:T(8,128)(2,1)S(1)} %bitcast.330), kind=kOutput, calls=%fused_computation.23 | convolution fusion | flops 1614544896 | bytes 8388608 | tf_op jit(solution)/shard_map/dot_general | solution.py:82
  127.4 3.9 %fusion.13 = bf16[768,1024]{1,0:T(8,128)(2,1)} fusion(bf16[3,256,1024]{2,1,0:T(8,128)(2,1)S(1)} %copy-done.18, bf16[768,1024]{1,0:T(8,128)(2,1)S(1)} %bitcast.333, bf16[1024,1024]{0,1:T(8,128)(2,1)S(1)} %bitcast.331), kind=kOutput, calls=%fused_computation.15 | convolution fusion | flops 1618477056 | bytes 6815744 | tf_op jit(solution)/shard_map/dot_general | solution.py:82
  131.2 2.6 %copy.139 = bf16[768,1024]{0,1:T(8,128)(2,1)} copy(bf16[768,1024]{1,0:T(8,128)(2,1)} %fusion.13) | data formatting | bytes 3145728 | tf_op jit(solution)/shard_map/convert_element_type | solution.py:141
  133.8 5.2 %fusion.34 = f32[3,256,1024]{2,1,0:T(8,128)} fusion(bf16[3,256,256]{2,1,0:T(8,128)(2,1)S(1)} %get-tuple-element.12, bf16[3,256,1024]{2,1,0:T(8,128)(2,1)} %bitcast.337, bf16[1024,1024,1]{0,1,2:T(8,128)(2,1)S(1)} %bitcast.332, f32[3,256]{1,0:T(4,128)S(1)} %add_rsqrt_fusion), kind=kOutput, calls=%fused_computation.43 | convolution fusion | flops 2014838784 | bytes 7212032 | tf_op jit(solution)/shard_map/gji,gjd->gid/dot_general | solution.py:19
  139.0 3.9 %fusion.14 = bf16[768,1024]{1,0:T(8,128)(2,1)S(1)} fusion(f32[3,256,1024]{2,1,0:T(8,128)} %fusion.34, f32[768,1024]{1,0:T(8,128)} %get-tuple-element.16), kind=kLoop, calls=%fused_computation.17 | loop fusion | flops 7077888 | bytes 7864320 | tf_op jit(solution)/shard_map/convert_element_type | solution.py:149
  144.5 8.3 %bitcast_convert_fusion = bf16[32,49,1024]{2,1,0:T(8,128)(2,1)} fusion(bf16[3,256,32,49]{1,3,2,0:T(8,128)(2,1)} %fusion.24, bf16[3,256,1024]{2,1,0:T(8,128)(2,1)S(1)} %bitcast.324, bf16[1024,1024,1]{0,1,2:T(8,128)(2,1)} %bitcast.329, f32[3,256]{1,0:T(4,128)S(1)} %add_rsqrt_fusion), kind=kOutput, calls=%fused_computation.1 | convolution fusion | flops 4080041984 | bytes 9292800 | tf_op jit(solution)/shard_map/dot_general | solution.py:155
  152.8 4.8 %all-to-all-start.2 = ((bf16[32,49,1024]{2,1,0:T(8,128)(2,1)}), bf16[32,49,1024]{2,1,0:T(8,128)(2,1)}, u32[]{:S(2)}, u32[]{:S(2)}) async-start(bf16[32,49,1024]{2,1,0:T(8,128)(2,1)} %bitcast_convert_fusion), calls=%async_computation.2 | async-start | bytes 7340032 | tf_op jit(solution)/shard_map/all_to_all | solution.py:23
  157.6 3.2 %convolution_bitcast_fusion.1 = f32[1,16,2,32,1024]{4,3,2,1,0:T(8,128)S(1)} fusion(bf16[16,2,32,768]{3,2,1,0:T(8,128)(2,1)S(1)} %bitcast.336, bf16[768,1024,1,1]{1,0,3,2:T(8,128)(2,1)} %bitcast.347), kind=kOutput, calls=%fused_computation.29 | convolution fusion | flops 1610612736 | bytes 7340032 | tf_op jit(solution)/shard_map/dot_general | solution.py:111
  160.9 1.8 select_bitcast_fusion.1
  168.9 3.7 %fusion.28 = f32[1,16,32,1024]{3,2,1,0:T(8,128)S(1)} fusion(f32[1,16,32,1024]{3,2,1,0:T(8,128)} %collective-permute-done.4, f32[1,16,2,32,1024]{4,3,2,1,0:T(8,128)} %copy-done.4, pred[]{:T(512)S(6)} %eq.147), kind=kLoop, calls=%fused_computation.36 | loop fusion | flops 1048576 | bytes 8388609 | tf_op jit(solution)/shard_map/add | solution.py:130
  174.4 2.3 bitcast_add_fusion
  177.2 26.8 %collective-permute-done.5 = bf16[1,8,32,1024]{3,2,1,0:T(8,128)(2,1)S(1)} collective-permute-done((bf16[1,8,32,1024]{3,2,1,0:T(8,128)(2,1)S(1)}, bf16[1,8,32,1024]{3,2,1,0:T(8,128)(2,1)S(1)}, u32[]{:S(2)}, u32[]{:S(2)}) %collective-permute-start.5) | collective-permute-done | bytes 524320 | tf_op jit(solution)/shard_map/ppermute | solution.py:129
  204.4 2.2 collective-permute-start.6
  206.6 9.9 %collective-permute-done.10 = bf16[1,8,32,1024]{3,2,1,0:T(8,128)(2,1)S(1)} collective-permute-done((bf16[1,8,32,1024]{3,2,1,0:T(8,128)(2,1)S(1)}, bf16[1,8,32,1024]{3,2,1,0:T(8,128)(2,1)S(1)}, u32[]{:S(2)}, u32[]{:S(2)}) %collective-permute-start.10) | collective-permute-done | bytes 524320 | tf_op jit(solution)/shard_map/ppermute | solution.py:129
  216.8 2.7 %collective-permute-start.11 = (bf16[1,4,32,1024]{3,2,1,0:T(8,128)(2,1)S(1)}, bf16[1,4,32,1024]{3,2,1,0:T(8,128)(2,1)S(1)}, u32[]{:S(2)}, u32[]{:S(2)}) collective-permute-start(bf16[1,4,32,1024]{3,2,1,0:T(8,128)(2,1)S(1)} %fusion.41), channel_id=1, source_target_pairs={{0,4},{1,5},{2,6},{3,7},{4,0},{5,1},{6,2},{7,3},{8,12},{9,13},{10,... | collective-permute-start | bytes 786440 | tf_op jit(solution)/shard_map/ppermute | solution.py:129
  220.8 7.4 %collective-permute-done.11 = bf16[1,4,32,1024]{3,2,1,0:T(8,128)(2,1)S(1)} collective-permute-done((bf16[1,4,32,1024]{3,2,1,0:T(8,128)(2,1)S(1)}, bf16[1,4,32,1024]{3,2,1,0:T(8,128)(2,1)S(1)}, u32[]{:S(2)}, u32[]{:S(2)}) %collective-permute-start.11) | collective-permute-done | bytes 262176 | tf_op jit(solution)/shard_map/ppermute | solution.py:129
  228.4 1.9 collective-permute-start.12
  230.4 2.8 %collective-permute-start.8 = (bf16[1,1,32,1024]{3,2,1,0:T(8,128)(2,1)S(1)}, bf16[1,1,32,1024]{3,2,1,0:T(8,128)(2,1)S(1)}, u32[]{:S(2)}, u32[]{:S(2)}) collective-permute-start(bf16[1,1,32,1024]{3,2,1,0:T(8,128)(2,1)S(1)} %fusion.57), channel_id=1, source_target_pairs={{0,16},{1,17},{2,18},{3,19},{4,20},{5,21},{6,22},{7,23},{8,24},{9,... | collective-permute-start | bytes 196616 | tf_op jit(solution)/shard_map/ppermute | solution.py:129
  234.8 3.5 %collective-permute-start.13 = (bf16[1,1,32,1024]{3,2,1,0:T(8,128)(2,1)S(1)}, bf16[1,1,32,1024]{3,2,1,0:T(8,128)(2,1)S(1)}, u32[]{:S(2)}, u32[]{:S(2)}) collective-permute-start(bf16[1,1,32,1024]{3,2,1,0:T(8,128)(2,1)S(1)} %fusion.58), channel_id=1, source_target_pairs={{0,16},{1,17},{2,18},{3,19},{4,20},{5,21},{6,22},{7,23},{8,24},{9,... | collective-permute-start | bytes 196616 | tf_op jit(solution)/shard_map/ppermute | solution.py:129
  238.3 7.0 %collective-permute-done.8 = bf16[1,1,32,1024]{3,2,1,0:T(8,128)(2,1)S(1)} collective-permute-done((bf16[1,1,32,1024]{3,2,1,0:T(8,128)(2,1)S(1)}, bf16[1,1,32,1024]{3,2,1,0:T(8,128)(2,1)S(1)}, u32[]{:S(2)}, u32[]{:S(2)}) %collective-permute-start.8) | collective-permute-done | bytes 65568 | tf_op jit(solution)/shard_map/ppermute | solution.py:129
  246.9 8.7 %fusion.21 = f32[1024,1024]{1,0:T(8,128)} fusion(bf16[32,49,1024]{2,1,0:T(8,128)(2,1)} %all-to-all-done.2, s32[32,49]{1,0:T(8,128)S(1)} %copy-done.17, pred[32,49]{1,0:T(8,128)(4,1)S(1)} %compare_bitcast_fusion), kind=kOutput, calls=%fused_computation.30 | convolution fusion | flops 3291545600 | bytes 7413408 | tf_op jit(solution)/shard_map/dot_general | solution.py:162
  (108 shorter events, 34.8 us)
Async XLA Ops:
  0.6 22.9 %copy-start = (bf16[1024,1024]{1,0:T(8,128)(2,1)S(1)}, bf16[1024,1024]{1,0:T(8,128)(2,1)}, u32[]{:S(2)}) copy-start(bf16[1024,1024]{1,0:T(8,128)(2,1)} %param.6) | copy-start | bytes 6291460
  29.0 3.9 %copy-start.12 = (bf16[1024,256]{1,0:T(8,128)(2,1)S(1)}, bf16[1024,256]{1,0:T(8,128)(2,1)}, u32[]{:S(2)}) copy-start(bf16[1024,256]{1,0:T(8,128)(2,1)} %param.10) | copy-start | bytes 1572868
  29.0 5.4 %copy-start.13 = (bf16[1024,256]{1,0:T(8,128)(2,1)S(1)}, bf16[1024,256]{1,0:T(8,128)(2,1)}, u32[]{:S(2)}) copy-start(bf16[1024,256]{1,0:T(8,128)(2,1)} %param.9) | copy-start | bytes 1572868
  29.0 6.1 %copy-start.15 = (s32[3,256]{1,0:T(4,128)S(1)}, s32[3,256]{1,0:T(4,128)}, u32[]{:S(2)}) copy-start(s32[3,256]{1,0:T(4,128)} %param.7) | copy-start | bytes 9220
  29.0 6.1 %copy-start.11 = (s32[3,256,256]{2,1,0:T(8,128)S(1)}, s32[3,256,256]{2,1,0:T(8,128)}, u32[]{:S(2)}) copy-start(s32[3,256,256]{2,1,0:T(8,128)} %param.8) | copy-start | bytes 2359300
  29.0 86.8 %all-to-all-start.1 = ((bf16[32,49,1024]{2,1,0:T(8,128)(2,1)}), bf16[32,49,1024]{2,1,0:T(8,128)(2,1)}, u32[]{:S(2)}, u32[]{:S(2)}) async-start(bf16[32,49,1024]{2,1,0:T(8,128)(2,1)} %fusion.18), calls=%async_computation.1 | async-start | bytes 7340032 | tf_op jit(solution)/shard_map/all_to_all | solution.py:23
  32.9 46.8 %collective-permute-start.2 = (bf16[1,1024,256]{2,1,0:T(8,128)(2,1)S(1)}, bf16[1,1024,256]{2,1,0:T(8,128)(2,1)S(1)}, u32[]{:S(2)}, u32[]{:S(2)}) collective-permute-start(bf16[1,1024,256]{2,1,0:T(8,128)(2,1)S(1)} %bitcast.339), channel_id=1, source_target_pairs={{0,2},{1,3},{2,0},{3,1},{4,6},{5,7},{6,4},{7,5},{8,10},{9,11},{10,... | collective-permute-start | bytes 1572872 | tf_op jit(solution)/shard_map/ppermute | solution.py:95
  34.4 56.7 %collective-permute-start = (bf16[1,1024,256]{2,1,0:T(8,128)(2,1)S(1)}, bf16[1,1024,256]{2,1,0:T(8,128)(2,1)}, u32[]{:S(2)}, u32[]{:S(2)}) collective-permute-start(bf16[1,1024,256]{2,1,0:T(8,128)(2,1)S(1)} %bitcast.340), channel_id=1, source_target_pairs={{0,2},{1,3},{2,0},{3,1},{4,6},{5,7},{6,4},{7,5},{8,10},{9,11},{10,... | collective-permute-start | bytes 1572872 | tf_op jit(solution)/shard_map/ppermute | solution.py:95
  93.5 5.6 %collective-permute-start.1 = (bf16[2,1024,256]{2,1,0:T(8,128)(2,1)}, bf16[2,1024,256]{2,1,0:T(8,128)(2,1)}, u32[]{:S(2)}, u32[]{:S(2)}) collective-permute-start(bf16[2,1024,256]{2,1,0:T(8,128)(2,1)} %pad_maximum_fusion.2), channel_id=1, source_target_pairs={{0,1},{1,0},{2,3},{3,2},{4,5},{5,4},{6,7},{7,6},{8,9},{9,8},{10,11... | collective-permute-start | bytes 3145736 | tf_op jit(solution)/shard_map/ppermute | solution.py:95
  95.2 10.9 %collective-permute-start.3 = (bf16[2,1024,256]{2,1,0:T(8,128)(2,1)}, bf16[2,1024,256]{2,1,0:T(8,128)(2,1)S(1)}, u32[]{:S(2)}, u32[]{:S(2)}) collective-permute-start(bf16[2,1024,256]{2,1,0:T(8,128)(2,1)} %pad_maximum_fusion.3), channel_id=1, source_target_pairs={{0,1},{1,0},{2,3},{3,2},{4,5},{5,4},{6,7},{7,6},{8,9},{9,8},{10,11... | collective-permute-start | bytes 3145736 | tf_op jit(solution)/shard_map/ppermute | solution.py:95
  111.9 9.9 %copy-start.5 = (bf16[1024,4,256]{0,2,1:T(8,128)(2,1)S(1)}, bf16[1024,4,256]{0,2,1:T(8,128)(2,1)}, u32[]{:S(2)}) copy-start(bf16[1024,4,256]{0,2,1:T(8,128)(2,1)} %copy.118) | copy-start | bytes 6291460
  121.8 3.8 %copy-start.19 = (bf16[3,256,1024]{2,1,0:T(8,128)(2,1)}, bf16[3,256,1024]{2,1,0:T(8,128)(2,1)S(1)}, u32[]{:S(2)}) copy-start(bf16[3,256,1024]{2,1,0:T(8,128)(2,1)S(1)} %fusion.15) | copy-start | bytes 4718596
  121.8 5.6 %copy-start.18 = (bf16[3,256,1024]{2,1,0:T(8,128)(2,1)S(1)}, bf16[3,256,1024]{2,1,0:T(8,128)(2,1)}, u32[]{:S(2)}) copy-start(bf16[3,256,1024]{2,1,0:T(8,128)(2,1)} %param.11) | copy-start | bytes 4718596
  152.8 4.8 %copy-start.10 = (bf16[768,1024]{0,1:T(8,128)(2,1)S(1)}, bf16[768,1024]{0,1:T(8,128)(2,1)}, u32[]{:S(2)}) copy-start(bf16[768,1024]{0,1:T(8,128)(2,1)} %copy.124) | copy-start | bytes 4718596
  152.8 94.0 %all-to-all-start.2 = ((bf16[32,49,1024]{2,1,0:T(8,128)(2,1)}), bf16[32,49,1024]{2,1,0:T(8,128)(2,1)}, u32[]{:S(2)}, u32[]{:S(2)}) async-start(bf16[32,49,1024]{2,1,0:T(8,128)(2,1)} %bitcast_convert_fusion), calls=%async_computation.2 | async-start | bytes 7340032 | tf_op jit(solution)/shard_map/all_to_all | solution.py:23
  160.8 3.1 %copy-start.4 = (f32[1,16,2,32,1024]{4,3,2,1,0:T(8,128)}, f32[1,16,2,32,1024]{4,3,2,1,0:T(8,128)S(1)}, u32[]{:S(2)}) copy-start(f32[1,16,2,32,1024]{4,3,2,1,0:T(8,128)S(1)} %convolution_bitcast_fusion.1) | copy-start | bytes 12582916
  160.8 3.3 %copy-start.8 = (bf16[3,256,1024]{2,1,0:T(8,128)(2,1)S(1)}, bf16[3,256,1024]{2,1,0:T(8,128)(2,1)}, u32[]{:S(2)}) copy-start(bf16[3,256,1024]{2,1,0:T(8,128)(2,1)} %copy-done.7) | copy-start | bytes 4718596
  160.9 4.1 %copy-start.9 = (bf16[768,1024]{0,1:T(8,128)(2,1)S(1)}, bf16[768,1024]{0,1:T(8,128)(2,1)}, u32[]{:S(2)}) copy-start(bf16[768,1024]{0,1:T(8,128)(2,1)} %copy.139) | copy-start | bytes 4718596
  164.0 4.9 %collective-permute-start.4 = (f32[1,16,32,1024]{3,2,1,0:T(8,128)}, f32[1,16,32,1024]{3,2,1,0:T(8,128)}, u32[]{:S(2)}, u32[]{:S(2)}) collective-permute-start(f32[1,16,32,1024]{3,2,1,0:T(8,128)} %select_bitcast_fusion.1), channel_id=1, source_target_pairs={{0,1},{1,0},{2,3},{3,2},{4,5},{5,4},{6,7},{7,6},{8,9},{9,8},{10,11... | collective-permute-start | bytes 6291464 | tf_op jit(solution)/shard_map/ppermute | solution.py:129
  166.8 1.9 copy-start.2
  168.7 5.7 %collective-permute-start.9 = (f32[1,16,32,1024]{3,2,1,0:T(8,128)S(1)}, f32[1,16,32,1024]{3,2,1,0:T(8,128)}, u32[]{:S(2)}, u32[]{:S(2)}) collective-permute-start(f32[1,16,32,1024]{3,2,1,0:T(8,128)S(1)} %select_bitcast_fusion), channel_id=1, source_target_pairs={{0,1},{1,0},{2,3},{3,2},{4,5},{5,4},{6,7},{7,6},{8,9},{9,8},{10,11... | collective-permute-start | bytes 6291464 | tf_op jit(solution)/shard_map/ppermute | solution.py:129
  168.9 5.5 %copy-start.3 = (f32[1,16,2,32,1024]{4,3,1,2,0:T(8,128)S(1)}, f32[1,16,2,32,1024]{4,3,1,2,0:T(8,128)}, u32[]{:S(2)}) copy-start(f32[1,16,2,32,1024]{4,3,1,2,0:T(8,128)} %copy-done.2) | copy-start | bytes 12582916
  172.7 31.4 %collective-permute-start.5 = (bf16[1,8,32,1024]{3,2,1,0:T(8,128)(2,1)S(1)}, bf16[1,8,32,1024]{3,2,1,0:T(8,128)(2,1)S(1)}, u32[]{:S(2)}, u32[]{:S(2)}) collective-permute-start(bf16[1,8,32,1024]{3,2,1,0:T(8,128)(2,1)S(1)} %fusion.35), channel_id=1, source_target_pairs={{0,2},{1,3},{2,0},{3,1},{4,6},{5,7},{6,4},{7,5},{8,10},{9,11},{10,... | collective-permute-start | bytes 1572872 | tf_op jit(solution)/shard_map/ppermute | solution.py:129
  176.8 39.7 %collective-permute-start.10 = (bf16[1,8,32,1024]{3,2,1,0:T(8,128)(2,1)S(1)}, bf16[1,8,32,1024]{3,2,1,0:T(8,128)(2,1)S(1)}, u32[]{:S(2)}, u32[]{:S(2)}) collective-permute-start(bf16[1,8,32,1024]{3,2,1,0:T(8,128)(2,1)S(1)} %fusion.36), channel_id=1, source_target_pairs={{0,2},{1,3},{2,0},{3,1},{4,6},{5,7},{6,4},{7,5},{8,10},{9,11},{10,... | collective-permute-start | bytes 1572872 | tf_op jit(solution)/shard_map/ppermute | solution.py:129
  204.4 15.1 %collective-permute-start.6 = (bf16[1,4,32,1024]{3,2,1,0:T(8,128)(2,1)S(1)}, bf16[1,4,32,1024]{3,2,1,0:T(8,128)(2,1)S(1)}, u32[]{:S(2)}, u32[]{:S(2)}) collective-permute-start(bf16[1,4,32,1024]{3,2,1,0:T(8,128)(2,1)S(1)} %fusion.40), channel_id=1, source_target_pairs={{0,4},{1,5},{2,6},{3,7},{4,0},{5,1},{6,2},{7,3},{8,12},{9,13},{10,... | collective-permute-start | bytes 786440 | tf_op jit(solution)/shard_map/ppermute | solution.py:129
  216.8 11.5 %collective-permute-start.11 = (bf16[1,4,32,1024]{3,2,1,0:T(8,128)(2,1)S(1)}, bf16[1,4,32,1024]{3,2,1,0:T(8,128)(2,1)S(1)}, u32[]{:S(2)}, u32[]{:S(2)}) collective-permute-start(bf16[1,4,32,1024]{3,2,1,0:T(8,128)(2,1)S(1)} %fusion.41), channel_id=1, source_target_pairs={{0,4},{1,5},{2,6},{3,7},{4,0},{5,1},{6,2},{7,3},{8,12},{9,13},{10,... | collective-permute-start | bytes 786440 | tf_op jit(solution)/shard_map/ppermute | solution.py:129
  219.6 10.7 %collective-permute-start.7 = (bf16[1,2,32,1024]{3,2,1,0:T(8,128)(2,1)S(1)}, bf16[1,2,32,1024]{3,2,1,0:T(8,128)(2,1)S(1)}, u32[]{:S(2)}, u32[]{:S(2)}) collective-permute-start(bf16[1,2,32,1024]{3,2,1,0:T(8,128)(2,1)S(1)} %fusion.47), channel_id=1, source_target_pairs={{0,8},{1,9},{2,10},{3,11},{4,12},{5,13},{6,14},{7,15},{8,0},{9,1},... | collective-permute-start | bytes 393224 | tf_op jit(solution)/shard_map/ppermute | solution.py:129
  228.3 18.5 %copy-start.17 = (s32[32,49]{1,0:T(8,128)S(1)}, s32[32,49]{1,0:T(8,128)}, u32[]{:S(2)}) copy-start(s32[32,49]{1,0:T(8,128)} %copy-done.16) | copy-start | bytes 18820
  228.4 6.4 %collective-permute-start.12 = (bf16[1,2,32,1024]{3,2,1,0:T(8,128)(2,1)S(1)}, bf16[1,2,32,1024]{3,2,1,0:T(8,128)(2,1)S(1)}, u32[]{:S(2)}, u32[]{:S(2)}) collective-permute-start(bf16[1,2,32,1024]{3,2,1,0:T(8,128)(2,1)S(1)} %fusion.48), channel_id=1, source_target_pairs={{0,8},{1,9},{2,10},{3,11},{4,12},{5,13},{6,14},{7,15},{8,0},{9,1},... | collective-permute-start | bytes 393224 | tf_op jit(solution)/shard_map/ppermute | solution.py:129
  230.4 14.9 %collective-permute-start.8 = (bf16[1,1,32,1024]{3,2,1,0:T(8,128)(2,1)S(1)}, bf16[1,1,32,1024]{3,2,1,0:T(8,128)(2,1)S(1)}, u32[]{:S(2)}, u32[]{:S(2)}) collective-permute-start(bf16[1,1,32,1024]{3,2,1,0:T(8,128)(2,1)S(1)} %fusion.57), channel_id=1, source_target_pairs={{0,16},{1,17},{2,18},{3,19},{4,20},{5,21},{6,22},{7,23},{8,24},{9,... | collective-permute-start | bytes 196616 | tf_op jit(solution)/shard_map/ppermute | solution.py:129
  234.8 11.3 %collective-permute-start.13 = (bf16[1,1,32,1024]{3,2,1,0:T(8,128)(2,1)S(1)}, bf16[1,1,32,1024]{3,2,1,0:T(8,128)(2,1)S(1)}, u32[]{:S(2)}, u32[]{:S(2)}) collective-permute-start(bf16[1,1,32,1024]{3,2,1,0:T(8,128)(2,1)S(1)} %fusion.58), channel_id=1, source_target_pairs={{0,16},{1,17},{2,18},{3,19},{4,20},{5,21},{6,22},{7,23},{8,24},{9,... | collective-permute-start | bytes 196616 | tf_op jit(solution)/shard_map/ppermute | solution.py:129
  246.9 8.7 %copy-start.1 = (bf16[1024,1024]{1,0:T(8,128)(2,1)S(1)}, bf16[1024,1024]{1,0:T(8,128)(2,1)}, u32[]{:S(2)}) copy-start(bf16[1024,1024]{1,0:T(8,128)(2,1)} %param.6) | copy-start | bytes 6291460
  (4 other events, 4.3 us)

commit v15 on v14

--- a/solution.py
+++ b/solution.py
@@ -108,12 +108,10 @@
     whole_weight_two = gather_columns(weight_two)
 
     def grad_parts(mixed, delta):
-        return lax.dot_general(
-            delta.reshape(count, shards, depth // shards),
-            mixed,
-            (((0,), (0,)), ((), ())),
-            preferred_element_type=jnp.float32,
+        whole = lax.dot_general(
+            mixed, delta, (((0,), (0,)), ((), ())), preferred_element_type=jnp.float32
         )
+        return whole.reshape(depth, shards, depth // shards).transpose(1, 2, 0)
 
     def reduce_blocks(parts):
         me = lax.axis_index(AXES)

time: 256 us -> 252 us (0.984)
  waiting for transfers between devices: 112 us -> 105 us
    ppermute x10, waiting for transfers between devices: 52.9 us -> 45.8 us  [reduce_blocks(): moved = lax.ppermute(send, AXES, [(i, i ^ step) for i in range(shards)])]
    dot_general x0 -> x2, local copies, waits for them, and re-layouts: none -> 4.27 us  [grad_parts(): lax.dot_general(mixed, delta, (((0,), (0,)), ((), ())), preferred_element...]
    convert_element_type x2 -> x0, local copies, waits for them, and re-layouts: 4.16 us -> none  [the longest x1 2.59 us: step_body(): delta_two = (final_layer_sensitivity.reshape(count, depth).astype(jnp.flo...]
    unnamed x41 -> x37, local copies, waits for them, and re-layouts: 6.86 us -> 5.35 us
  transfers between devices with their start and end apart: 16 -> 16, of which waited for: 9 -> 9; matrix products, arithmetic and copies ran while one was open for 14% -> 17% of each run, Pallas kernels for 0% -> 0%
where the time goes in v15:
time: 252 us; the launch traced here: 251 us
  waiting for transfers between devices  105 us (42%)
  matrix products  52 us (21%)
  starting transfers between devices  30.1 us (12%)
  local copies, waits for them, and re-layouts  25.9 us (10%)
  other arithmetic  23.1 us (9%)
  blocking collectives  14.3 us (6%)
    ppermute x4, waiting for transfers between devices, gather_columns(): other = lax.ppermute(blocks, 'fsdp', [(i, i ^ step) for i in range(n_fsdp)])  55.2 us
    ppermute x10, waiting for transfers between devices, reduce_blocks(): moved = lax.ppermute(send, AXES, [(i, i ^ step) for i in range(shards)])  45.8 us
    ppermute x10, starting transfers between devices, reduce_blocks(): moved = lax.ppermute(send, AXES, [(i, i ^ step) for i in range(shards)])  18.9 us
    all_to_all x1, blocking collectives, exchange(): return lax.all_to_all(values, AXES, 0, 0, tiled=True)  14.3 us
    dot_general x1, matrix products, step_body(): lax.dot_general(picks, returned, (((0, 1), (0, 1)), ((), ())), preferred_...  8.74 us
    all_to_all x2, starting transfers between devices, exchange(): return lax.all_to_all(values, AXES, 0, 0, tiled=True)  8.53 us
    dot_general x1, matrix products, step_body(): lax.dot_general(linked_slots, fetched_first.reshape(count, depth), (((0,)...  8.32 us
    transpose x2, local copies, waits for them, and re-layouts, gather_columns(): blocks.transpose(1, 0, 2).reshape(weight.shape[0], n_fsdp * weight.shape[1])  7.99 us
  transfers between devices with their start and end apart: 16, of which 9 were waited for; matrix products, arithmetic and copies ran while one was open for 17% of the time, Pallas kernels for 0%

profile of v15, /device:TPU:0, one launch (start us, length us, event | category | flops | bytes accessed | tf_op | source)
XLA Modules:
  0.0 251.3 jit_solution(9615341922842333647)
XLA Ops:
  5.1 3.4 %scatter_custom_fusion = s32[1568]{0:T(1024)S(1)} fusion(s32[768]{0:T(1024)S(1)} %fusion.66, s32[768]{0:T(1024)S(1)} %get-tuple-element.13, s32[]{:T(128)} %constant.167.clone.1), kind=kCustom, calls=%fused_computation.137 | custom fusion | bytes 6276 | tf_op jit(solution)/shard_map/scatter | solution.py:44
  8.6 14.3 %all_to_all.19 = s32[32,1,49]{2,1,0:T(1,128)S(1)} all-to-all(s32[32,1,49]{2,1,0:T(1,128)S(1)} %all_to_all.12), channel_id=1, replica_groups=mesh['node'=8,'fsdp'=4] {'node','fsdp'}, dimensions={0} | all-to-all | bytes 12544 | tf_op jit(solution)/shard_map/all_to_all | solution.py:23
  23.5 5.5 %fusion.18 = bf16[32,49,1024]{2,1,0:T(8,128)(2,1)} fusion(s32[32,49]{1,0:T(8,128)S(1)} %maximum_bitcast_fusion, pred[32,49]{1,0:T(8,128)(4,1)S(1)} %compare_bitcast_fusion, bf16[1024,1024]{1,0:T(8,128)(2,1)S(1)} %copy-done), kind=kOutput, calls=%fused_computation.27 | convolution fusion | flops 3293151232 | bytes 5316256 | tf_op jit(solution)/shard_map/dot_general | solution.py:51
  29.0 3.7 %all-to-all-start.1 = ((bf16[32,49,1024]{2,1,0:T(8,128)(2,1)}), bf16[32,49,1024]{2,1,0:T(8,128)(2,1)}, u32[]{:S(2)}, u32[]{:S(2)}) async-start(bf16[32,49,1024]{2,1,0:T(8,128)(2,1)} %fusion.18), calls=%async_computation.1 | async-start | bytes 7340032 | tf_op jit(solution)/shard_map/all_to_all | solution.py:23
  35.1 44.4 %collective-permute-done.2 = bf16[1,1024,256]{2,1,0:T(8,128)(2,1)S(1)} collective-permute-done((bf16[1,1024,256]{2,1,0:T(8,128)(2,1)S(1)}, bf16[1,1024,256]{2,1,0:T(8,128)(2,1)S(1)}, u32[]{:S(2)}, u32[]{:S(2)}) %collective-permute-start.2) | collective-permute-done | bytes 524320 | tf_op jit(solution)/shard_map/ppermute | solution.py:95
  80.3 10.8 %collective-permute-done = bf16[1,1024,256]{2,1,0:T(8,128)(2,1)} collective-permute-done((bf16[1,1024,256]{2,1,0:T(8,128)(2,1)S(1)}, bf16[1,1024,256]{2,1,0:T(8,128)(2,1)}, u32[]{:S(2)}, u32[]{:S(2)}) %collective-permute-start) | collective-permute-done | bytes 524320 | tf_op jit(solution)/shard_map/ppermute | solution.py:95
  95.8 3.2 %fusion.24 = bf16[3,256,32,49]{1,3,2,0:T(8,128)(2,1)} fusion(pred[3,256,49]{1,2,0:T(8,128)(4,1)S(1)} %iota_compare_fusion.2, pred[3,256,32]{1,2,0:T(8,128)(4,1)} %iota_compare_fusion.3, bf16[3,256,256]{2,1,0:T(8,128)(2,1)S(1)} %get-tuple-element.12), kind=kOutput, calls=%fused_computation.31 | convolution fusion | flops 618971136 | bytes 2863872 | tf_op jit(solution)/shard_map/gij,gjsc->gisc/dot_general | solution.py:61
  102.1 4.0 %copy.118 = bf16[1024,4,256]{0,2,1:T(8,128)(2,1)} copy(bf16[1024,4,256]{2,0,1:T(8,128)(2,1)} %bitcast.312) | data formatting | bytes 4194304 | tf_op jit(solution)/shard_map/transpose | solution.py:105
  107.9 4.0 %copy.120 = bf16[1024,4,256]{0,2,1:T(8,128)(2,1)} copy(bf16[1024,4,256]{2,0,1:T(8,128)(2,1)} %bitcast.313) | data formatting | bytes 4194304 | tf_op jit(solution)/shard_map/transpose | solution.py:105
  111.9 3.9 %all-to-all-done.1 = bf16[32,49,1024]{2,1,0:T(8,128)(2,1)} async-done(((bf16[32,49,1024]{2,1,0:T(8,128)(2,1)}), bf16[32,49,1024]{2,1,0:T(8,128)(2,1)}, u32[]{:S(2)}, u32[]{:S(2)}) %all-to-all-start.1) | async-done | bytes 3211296 | tf_op jit(solution)/shard_map/all_to_all | solution.py:23
  115.8 5.9 %fusion.15 = bf16[3,256,1024]{2,1,0:T(8,128)(2,1)S(1)} fusion(bf16[3,256,32,49]{1,3,2,0:T(8,128)(2,1)} %fusion.24, bf16[32,49,1024]{2,1,0:T(8,128)(2,1)} %all-to-all-done.1, f32[3,256]{1,0:T(4,128)S(1)} %add_rsqrt_fusion), kind=kOutput, calls=%fused_computation.19 | convolution fusion | flops 2467823616 | bytes 7195648 | tf_op jit(solution)/shard_map/dot_general | solution.py:70
  121.8 3.8 %multiply_convert_fusion.3 = (bf16[768,1024]{1,0:T(8,128)(2,1)S(1)}, f32[768,1024]{1,0:T(8,128)}) fusion(bf16[768,1024]{1,0:T(8,128)(2,1)S(1)} %bitcast.342, bf16[1024,1024]{0,1:T(8,128)(2,1)S(1)} %bitcast.325), kind=kOutput, calls=%fused_computation.23 | convolution fusion | flops 1614544896 | bytes 8388608 | tf_op jit(solution)/shard_map/dot_general | solution.py:82
  127.2 3.8 %fusion.13 = bf16[768,1024]{1,0:T(8,128)(2,1)} fusion(bf16[3,256,1024]{2,1,0:T(8,128)(2,1)S(1)} %copy-done.16, bf16[768,1024]{1,0:T(8,128)(2,1)S(1)} %bitcast.328, bf16[1024,1024]{0,1:T(8,128)(2,1)S(1)} %bitcast.326), kind=kOutput, calls=%fused_computation.15 | convolution fusion | flops 1618477056 | bytes 6815744 | tf_op jit(solution)/shard_map/dot_general | solution.py:82
  131.1 5.3 %fusion.34 = f32[3,256,1024]{2,1,0:T(8,128)} fusion(bf16[3,256,256]{2,1,0:T(8,128)(2,1)S(1)} %get-tuple-element.12, bf16[3,256,1024]{2,1,0:T(8,128)(2,1)} %bitcast.330, bf16[1024,1024,1]{0,1,2:T(8,128)(2,1)S(1)} %bitcast.327, f32[3,256]{1,0:T(4,128)S(1)} %add_rsqrt_fusion), kind=kOutput, calls=%fused_computation.43 | convolution fusion | flops 2014838784 | bytes 7212032 | tf_op jit(solution)/shard_map/gji,gjd->gid/dot_general | solution.py:19
  136.3 3.9 %fusion.14 = bf16[768,1024]{1,0:T(8,128)(2,1)S(1)} fusion(f32[3,256,1024]{2,1,0:T(8,128)} %fusion.34, f32[768,1024]{1,0:T(8,128)} %get-tuple-element.16), kind=kLoop, calls=%fused_computation.17 | loop fusion | flops 7077888 | bytes 7864320 | tf_op jit(solution)/shard_map/convert_element_type | solution.py:147
  140.2 8.3 %bitcast_convert_fusion = bf16[32,49,1024]{2,1,0:T(8,128)(2,1)} fusion(bf16[3,256,32,49]{1,3,2,0:T(8,128)(2,1)} %fusion.24, bf16[3,256,1024]{2,1,0:T(8,128)(2,1)S(1)} %bitcast.318, bf16[1024,1024,1]{0,1,2:T(8,128)(2,1)} %bitcast.324, f32[3,256]{1,0:T(4,128)S(1)} %add_rsqrt_fusion), kind=kOutput, calls=%fused_computation.1 | convolution fusion | flops 4080041984 | bytes 9292800 | tf_op jit(solution)/shard_map/dot_general | solution.py:153
  148.5 4.8 %all-to-all-start.2 = ((bf16[32,49,1024]{2,1,0:T(8,128)(2,1)}), bf16[32,49,1024]{2,1,0:T(8,128)(2,1)}, u32[]{:S(2)}, u32[]{:S(2)}) async-start(bf16[32,49,1024]{2,1,0:T(8,128)(2,1)} %bitcast_convert_fusion), calls=%async_computation.2 | async-start | bytes 7340032 | tf_op jit(solution)/shard_map/all_to_all | solution.py:23
  154.9 3.7 %convolution_bitcast_fusion.1 = f32[1,16,2,32,1024]{4,3,2,1,0:T(8,128)S(1)} fusion(bf16[16,2,32,768]{3,2,1,0:T(8,128)(2,1)} %bitcast.333, bf16[768,1024,1,1]{1,0,3,2:T(8,128)(2,1)} %bitcast.343), kind=kOutput, calls=%fused_computation.29 | convolution fusion | flops 1610612736 | bytes 7340032 | tf_op jit(solution)/shard_map/dot_general | solution.py:111
  161.4 2.7 %copy.139 = bf16[1024,768]{1,0:T(8,128)(2,1)} copy(bf16[1024,768]{0,1:T(8,128)(2,1)} %bitcast.331) | data formatting | bytes 3145728 | tf_op jit(solution)/shard_map/dot_general | solution.py:111
  164.1 3.2 %convolution_bitcast_fusion = f32[1,16,2,32,1024]{4,3,1,2,0:T(8,128)S(1)} fusion(bf16[768,1024,1,1]{1,0,2,3:T(8,128)(2,1)S(1)} %bitcast.329, bf16[16,2,32,768]{3,2,1,0:T(8,128)(2,1)} %bitcast.334), kind=kOutput, calls=%fused_computation.28 | convolution fusion | flops 1610612736 | bytes 7340032 | tf_op jit(solution)/shard_map/dot_general | solution.py:111
  169.8 3.7 %fusion.28 = f32[1,16,32,1024]{3,2,1,0:T(8,128)S(1)} fusion(f32[1,16,32,1024]{3,2,1,0:T(8,128)} %collective-permute-done.4, f32[1,16,2,32,1024]{4,3,2,1,0:T(8,128)} %copy-done.4, pred[]{:T(512)S(6)} %eq.147), kind=kLoop, calls=%fused_computation.36 | loop fusion | flops 1048576 | bytes 8388609 | tf_op jit(solution)/shard_map/add | solution.py:128
  175.3 2.3 bitcast_add_fusion
  178.1 22.3 %collective-permute-done.5 = bf16[1,8,32,1024]{3,2,1,0:T(8,128)(2,1)S(1)} collective-permute-done((bf16[1,8,32,1024]{3,2,1,0:T(8,128)(2,1)S(1)}, bf16[1,8,32,1024]{3,2,1,0:T(8,128)(2,1)S(1)}, u32[]{:S(2)}, u32[]{:S(2)}) %collective-permute-start.5) | collective-permute-done | bytes 524320 | tf_op jit(solution)/shard_map/ppermute | solution.py:127
  202.9 9.3 %collective-permute-done.10 = bf16[1,8,32,1024]{3,2,1,0:T(8,128)(2,1)S(1)} collective-permute-done((bf16[1,8,32,1024]{3,2,1,0:T(8,128)(2,1)S(1)}, bf16[1,8,32,1024]{3,2,1,0:T(8,128)(2,1)S(1)}, u32[]{:S(2)}, u32[]{:S(2)}) %collective-permute-start.10) | collective-permute-done | bytes 524320 | tf_op jit(solution)/shard_map/ppermute | solution.py:127
  212.5 2.9 %collective-permute-start.11 = (bf16[1,4,32,1024]{3,2,1,0:T(8,128)(2,1)S(1)}, bf16[1,4,32,1024]{3,2,1,0:T(8,128)(2,1)S(1)}, u32[]{:S(2)}, u32[]{:S(2)}) collective-permute-start(bf16[1,4,32,1024]{3,2,1,0:T(8,128)(2,1)S(1)} %fusion.41), channel_id=1, source_target_pairs={{0,4},{1,5},{2,6},{3,7},{4,0},{5,1},{6,2},{7,3},{8,12},{9,13},{10,... | collective-permute-start | bytes 786440 | tf_op jit(solution)/shard_map/ppermute | solution.py:127
  215.6 3.0 %collective-permute-start.7 = (bf16[1,2,32,1024]{3,2,1,0:T(8,128)(2,1)S(1)}, bf16[1,2,32,1024]{3,2,1,0:T(8,128)(2,1)S(1)}, u32[]{:S(2)}, u32[]{:S(2)}) collective-permute-start(bf16[1,2,32,1024]{3,2,1,0:T(8,128)(2,1)S(1)} %fusion.47), channel_id=1, source_target_pairs={{0,8},{1,9},{2,10},{3,11},{4,12},{5,13},{6,14},{7,15},{8,0},{9,1},... | collective-permute-start | bytes 393224 | tf_op jit(solution)/shard_map/ppermute | solution.py:127
  218.5 5.6 %collective-permute-done.11 = bf16[1,4,32,1024]{3,2,1,0:T(8,128)(2,1)S(1)} collective-permute-done((bf16[1,4,32,1024]{3,2,1,0:T(8,128)(2,1)S(1)}, bf16[1,4,32,1024]{3,2,1,0:T(8,128)(2,1)S(1)}, u32[]{:S(2)}, u32[]{:S(2)}) %collective-permute-start.11) | collective-permute-done | bytes 262176 | tf_op jit(solution)/shard_map/ppermute | solution.py:127
  224.3 3.1 %collective-permute-start.12 = (bf16[1,2,32,1024]{3,2,1,0:T(8,128)(2,1)S(1)}, bf16[1,2,32,1024]{3,2,1,0:T(8,128)(2,1)S(1)}, u32[]{:S(2)}, u32[]{:S(2)}) collective-permute-start(bf16[1,2,32,1024]{3,2,1,0:T(8,128)(2,1)S(1)} %fusion.48), channel_id=1, source_target_pairs={{0,8},{1,9},{2,10},{3,11},{4,12},{5,13},{6,14},{7,15},{8,0},{9,1},... | collective-permute-start | bytes 393224 | tf_op jit(solution)/shard_map/ppermute | solution.py:127
  227.4 2.3 collective-permute-start.8
  231.4 2.8 %collective-permute-start.13 = (bf16[1,1,32,1024]{3,2,1,0:T(8,128)(2,1)S(1)}, bf16[1,1,32,1024]{3,2,1,0:T(8,128)(2,1)S(1)}, u32[]{:S(2)}, u32[]{:S(2)}) collective-permute-start(bf16[1,1,32,1024]{3,2,1,0:T(8,128)(2,1)S(1)} %fusion.58), channel_id=1, source_target_pairs={{0,16},{1,17},{2,18},{3,19},{4,20},{5,21},{6,22},{7,23},{8,24},{9,... | collective-permute-start | bytes 196616 | tf_op jit(solution)/shard_map/ppermute | solution.py:127
  234.3 6.8 %collective-permute-done.8 = bf16[1,1,32,1024]{3,2,1,0:T(8,128)(2,1)S(1)} collective-permute-done((bf16[1,1,32,1024]{3,2,1,0:T(8,128)(2,1)S(1)}, bf16[1,1,32,1024]{3,2,1,0:T(8,128)(2,1)S(1)}, u32[]{:S(2)}, u32[]{:S(2)}) %collective-permute-start.8) | collective-permute-done | bytes 65568 | tf_op jit(solution)/shard_map/ppermute | solution.py:127
  242.6 8.7 %fusion.21 = f32[1024,1024]{1,0:T(8,128)} fusion(bf16[32,49,1024]{2,1,0:T(8,128)(2,1)} %all-to-all-done.2, s32[32,49]{1,0:T(8,128)S(1)} %copy-done.15, pred[32,49]{1,0:T(8,128)(4,1)S(1)} %compare_bitcast_fusion), kind=kOutput, calls=%fused_computation.30 | convolution fusion | flops 3291545600 | bytes 7413408 | tf_op jit(solution)/shard_map/dot_general | solution.py:160
  (104 shorter events, 34.8 us)
Async XLA Ops:
  0.6 22.9 %copy-start = (bf16[1024,1024]{1,0:T(8,128)(2,1)S(1)}, bf16[1024,1024]{1,0:T(8,128)(2,1)}, u32[]{:S(2)}) copy-start(bf16[1024,1024]{1,0:T(8,128)(2,1)} %param.6) | copy-start | bytes 6291460
  29.0 3.7 %copy-start.10 = (bf16[1024,256]{1,0:T(8,128)(2,1)S(1)}, bf16[1024,256]{1,0:T(8,128)(2,1)}, u32[]{:S(2)}) copy-start(bf16[1024,256]{1,0:T(8,128)(2,1)} %param.10) | copy-start | bytes 1572868
  29.0 5.4 %copy-start.11 = (bf16[1024,256]{1,0:T(8,128)(2,1)S(1)}, bf16[1024,256]{1,0:T(8,128)(2,1)}, u32[]{:S(2)}) copy-start(bf16[1024,256]{1,0:T(8,128)(2,1)} %param.9) | copy-start | bytes 1572868
  29.0 5.9 %copy-start.13 = (s32[3,256]{1,0:T(4,128)S(1)}, s32[3,256]{1,0:T(4,128)}, u32[]{:S(2)}) copy-start(s32[3,256]{1,0:T(4,128)} %param.7) | copy-start | bytes 9220
  29.0 5.9 %copy-start.9 = (s32[3,256,256]{2,1,0:T(8,128)S(1)}, s32[3,256,256]{2,1,0:T(8,128)}, u32[]{:S(2)}) copy-start(s32[3,256,256]{2,1,0:T(8,128)} %param.8) | copy-start | bytes 2359300
  29.0 86.8 %all-to-all-start.1 = ((bf16[32,49,1024]{2,1,0:T(8,128)(2,1)}), bf16[32,49,1024]{2,1,0:T(8,128)(2,1)}, u32[]{:S(2)}, u32[]{:S(2)}) async-start(bf16[32,49,1024]{2,1,0:T(8,128)(2,1)} %fusion.18), calls=%async_computation.1 | async-start | bytes 7340032 | tf_op jit(solution)/shard_map/all_to_all | solution.py:23
  32.7 46.8 %collective-permute-start.2 = (bf16[1,1024,256]{2,1,0:T(8,128)(2,1)S(1)}, bf16[1,1024,256]{2,1,0:T(8,128)(2,1)S(1)}, u32[]{:S(2)}, u32[]{:S(2)}) collective-permute-start(bf16[1,1024,256]{2,1,0:T(8,128)(2,1)S(1)} %bitcast.335), channel_id=1, source_target_pairs={{0,2},{1,3},{2,0},{3,1},{4,6},{5,7},{6,4},{7,5},{8,10},{9,11},{10,... | collective-permute-start | bytes 1572872 | tf_op jit(solution)/shard_map/ppermute | solution.py:95
  34.4 56.7 %collective-permute-start = (bf16[1,1024,256]{2,1,0:T(8,128)(2,1)S(1)}, bf16[1,1024,256]{2,1,0:T(8,128)(2,1)}, u32[]{:S(2)}, u32[]{:S(2)}) collective-permute-start(bf16[1,1024,256]{2,1,0:T(8,128)(2,1)S(1)} %bitcast.336), channel_id=1, source_target_pairs={{0,2},{1,3},{2,0},{3,1},{4,6},{5,7},{6,4},{7,5},{8,10},{9,11},{10,... | collective-permute-start | bytes 1572872 | tf_op jit(solution)/shard_map/ppermute | solution.py:95
  93.5 5.6 %collective-permute-start.1 = (bf16[2,1024,256]{2,1,0:T(8,128)(2,1)}, bf16[2,1024,256]{2,1,0:T(8,128)(2,1)}, u32[]{:S(2)}, u32[]{:S(2)}) collective-permute-start(bf16[2,1024,256]{2,1,0:T(8,128)(2,1)} %pad_maximum_fusion.2), channel_id=1, source_target_pairs={{0,1},{1,0},{2,3},{3,2},{4,5},{5,4},{6,7},{7,6},{8,9},{9,8},{10,11... | collective-permute-start | bytes 3145736 | tf_op jit(solution)/shard_map/ppermute | solution.py:95
  95.2 10.8 %collective-permute-start.3 = (bf16[2,1024,256]{2,1,0:T(8,128)(2,1)}, bf16[2,1024,256]{2,1,0:T(8,128)(2,1)S(1)}, u32[]{:S(2)}, u32[]{:S(2)}) collective-permute-start(bf16[2,1024,256]{2,1,0:T(8,128)(2,1)} %pad_maximum_fusion.3), channel_id=1, source_target_pairs={{0,1},{1,0},{2,3},{3,2},{4,5},{5,4},{6,7},{7,6},{8,9},{9,8},{10,11... | collective-permute-start | bytes 3145736 | tf_op jit(solution)/shard_map/ppermute | solution.py:95
  111.9 9.9 %copy-start.5 = (bf16[1024,4,256]{0,2,1:T(8,128)(2,1)S(1)}, bf16[1024,4,256]{0,2,1:T(8,128)(2,1)}, u32[]{:S(2)}) copy-start(bf16[1024,4,256]{0,2,1:T(8,128)(2,1)} %copy.118) | copy-start | bytes 6291460
  121.7 3.8 %copy-start.17 = (bf16[3,256,1024]{2,1,0:T(8,128)(2,1)}, bf16[3,256,1024]{2,1,0:T(8,128)(2,1)S(1)}, u32[]{:S(2)}) copy-start(bf16[3,256,1024]{2,1,0:T(8,128)(2,1)S(1)} %fusion.15) | copy-start | bytes 4718596
  121.8 4.4 %copy-start.16 = (bf16[3,256,1024]{2,1,0:T(8,128)(2,1)S(1)}, bf16[3,256,1024]{2,1,0:T(8,128)(2,1)}, u32[]{:S(2)}) copy-start(bf16[3,256,1024]{2,1,0:T(8,128)(2,1)} %param.11) | copy-start | bytes 4718596
  125.6 1.6 copy-start.6
  126.2 4.9 %copy-start.7 = (bf16[3,256,1024]{2,1,0:T(8,128)(2,1)}, bf16[3,256,1024]{2,1,0:T(8,128)(2,1)S(1)}, u32[]{:S(2)}) copy-start(bf16[3,256,1024]{2,1,0:T(8,128)(2,1)S(1)} %multiply_convert_fusion.2) | copy-start | bytes 4718596
  148.5 94.0 %all-to-all-start.2 = ((bf16[32,49,1024]{2,1,0:T(8,128)(2,1)}), bf16[32,49,1024]{2,1,0:T(8,128)(2,1)}, u32[]{:S(2)}, u32[]{:S(2)}) async-start(bf16[32,49,1024]{2,1,0:T(8,128)(2,1)} %bitcast_convert_fusion), calls=%async_computation.2 | async-start | bytes 7340032 | tf_op jit(solution)/shard_map/all_to_all | solution.py:23
  158.6 2.6 %copy-start.4 = (f32[1,16,2,32,1024]{4,3,2,1,0:T(8,128)}, f32[1,16,2,32,1024]{4,3,2,1,0:T(8,128)S(1)}, u32[]{:S(2)}) copy-start(f32[1,16,2,32,1024]{4,3,2,1,0:T(8,128)S(1)} %convolution_bitcast_fusion.1) | copy-start | bytes 12582916
  161.3 2.9 %copy-start.8 = (bf16[3,256,1024]{2,1,0:T(8,128)(2,1)S(1)}, bf16[3,256,1024]{2,1,0:T(8,128)(2,1)}, u32[]{:S(2)}) copy-start(bf16[3,256,1024]{2,1,0:T(8,128)(2,1)} %copy-done.7) | copy-start | bytes 4718596
  161.3 8.5 %collective-permute-start.4 = (f32[1,16,32,1024]{3,2,1,0:T(8,128)}, f32[1,16,32,1024]{3,2,1,0:T(8,128)}, u32[]{:S(2)}, u32[]{:S(2)}) collective-permute-start(f32[1,16,32,1024]{3,2,1,0:T(8,128)} %select_bitcast_fusion.1), channel_id=1, source_target_pairs={{0,1},{1,0},{2,3},{3,2},{4,5},{5,4},{6,7},{7,6},{8,9},{9,8},{10,11... | collective-permute-start | bytes 6291464 | tf_op jit(solution)/shard_map/ppermute | solution.py:127
  167.3 2.1 copy-start.2
  169.4 5.9 %collective-permute-start.9 = (f32[1,16,32,1024]{3,2,1,0:T(8,128)S(1)}, f32[1,16,32,1024]{3,2,1,0:T(8,128)}, u32[]{:S(2)}, u32[]{:S(2)}) collective-permute-start(f32[1,16,32,1024]{3,2,1,0:T(8,128)S(1)} %select_bitcast_fusion), channel_id=1, source_target_pairs={{0,1},{1,0},{2,3},{3,2},{4,5},{5,4},{6,7},{7,6},{8,9},{9,8},{10,11... | collective-permute-start | bytes 6291464 | tf_op jit(solution)/shard_map/ppermute | solution.py:127
  169.8 5.5 %copy-start.3 = (f32[1,16,2,32,1024]{4,3,1,2,0:T(8,128)S(1)}, f32[1,16,2,32,1024]{4,3,1,2,0:T(8,128)}, u32[]{:S(2)}) copy-start(f32[1,16,2,32,1024]{4,3,1,2,0:T(8,128)} %copy-done.2) | copy-start | bytes 12582916
  173.6 26.9 %collective-permute-start.5 = (bf16[1,8,32,1024]{3,2,1,0:T(8,128)(2,1)S(1)}, bf16[1,8,32,1024]{3,2,1,0:T(8,128)(2,1)S(1)}, u32[]{:S(2)}, u32[]{:S(2)}) collective-permute-start(bf16[1,8,32,1024]{3,2,1,0:T(8,128)(2,1)S(1)} %fusion.35), channel_id=1, source_target_pairs={{0,2},{1,3},{2,0},{3,1},{4,6},{5,7},{6,4},{7,5},{8,10},{9,11},{10,... | collective-permute-start | bytes 1572872 | tf_op jit(solution)/shard_map/ppermute | solution.py:127
  177.7 34.5 %collective-permute-start.10 = (bf16[1,8,32,1024]{3,2,1,0:T(8,128)(2,1)S(1)}, bf16[1,8,32,1024]{3,2,1,0:T(8,128)(2,1)S(1)}, u32[]{:S(2)}, u32[]{:S(2)}) collective-permute-start(bf16[1,8,32,1024]{3,2,1,0:T(8,128)(2,1)S(1)} %fusion.36), channel_id=1, source_target_pairs={{0,2},{1,3},{2,0},{3,1},{4,6},{5,7},{6,4},{7,5},{8,10},{9,11},{10,... | collective-permute-start | bytes 1572872 | tf_op jit(solution)/shard_map/ppermute | solution.py:127
  200.8 14.6 %collective-permute-start.6 = (bf16[1,4,32,1024]{3,2,1,0:T(8,128)(2,1)S(1)}, bf16[1,4,32,1024]{3,2,1,0:T(8,128)(2,1)S(1)}, u32[]{:S(2)}, u32[]{:S(2)}) collective-permute-start(bf16[1,4,32,1024]{3,2,1,0:T(8,128)(2,1)S(1)} %fusion.40), channel_id=1, source_target_pairs={{0,4},{1,5},{2,6},{3,7},{4,0},{5,1},{6,2},{7,3},{8,12},{9,13},{10,... | collective-permute-start | bytes 786440 | tf_op jit(solution)/shard_map/ppermute | solution.py:127
  212.5 11.6 %collective-permute-start.11 = (bf16[1,4,32,1024]{3,2,1,0:T(8,128)(2,1)S(1)}, bf16[1,4,32,1024]{3,2,1,0:T(8,128)(2,1)S(1)}, u32[]{:S(2)}, u32[]{:S(2)}) collective-permute-start(bf16[1,4,32,1024]{3,2,1,0:T(8,128)(2,1)S(1)} %fusion.41), channel_id=1, source_target_pairs={{0,4},{1,5},{2,6},{3,7},{4,0},{5,1},{6,2},{7,3},{8,12},{9,13},{10,... | collective-permute-start | bytes 786440 | tf_op jit(solution)/shard_map/ppermute | solution.py:127
  215.6 11.8 %collective-permute-start.7 = (bf16[1,2,32,1024]{3,2,1,0:T(8,128)(2,1)S(1)}, bf16[1,2,32,1024]{3,2,1,0:T(8,128)(2,1)S(1)}, u32[]{:S(2)}, u32[]{:S(2)}) collective-permute-start(bf16[1,2,32,1024]{3,2,1,0:T(8,128)(2,1)S(1)} %fusion.47), channel_id=1, source_target_pairs={{0,8},{1,9},{2,10},{3,11},{4,12},{5,13},{6,14},{7,15},{8,0},{9,1},... | collective-permute-start | bytes 393224 | tf_op jit(solution)/shard_map/ppermute | solution.py:127
  224.2 18.4 %copy-start.15 = (s32[32,49]{1,0:T(8,128)S(1)}, s32[32,49]{1,0:T(8,128)}, u32[]{:S(2)}) copy-start(s32[32,49]{1,0:T(8,128)} %copy-done.14) | copy-start | bytes 18820
  224.3 7.1 %collective-permute-start.12 = (bf16[1,2,32,1024]{3,2,1,0:T(8,128)(2,1)S(1)}, bf16[1,2,32,1024]{3,2,1,0:T(8,128)(2,1)S(1)}, u32[]{:S(2)}, u32[]{:S(2)}) collective-permute-start(bf16[1,2,32,1024]{3,2,1,0:T(8,128)(2,1)S(1)} %fusion.48), channel_id=1, source_target_pairs={{0,8},{1,9},{2,10},{3,11},{4,12},{5,13},{6,14},{7,15},{8,0},{9,1},... | collective-permute-start | bytes 393224 | tf_op jit(solution)/shard_map/ppermute | solution.py:127
  227.4 13.6 %collective-permute-start.8 = (bf16[1,1,32,1024]{3,2,1,0:T(8,128)(2,1)S(1)}, bf16[1,1,32,1024]{3,2,1,0:T(8,128)(2,1)S(1)}, u32[]{:S(2)}, u32[]{:S(2)}) collective-permute-start(bf16[1,1,32,1024]{3,2,1,0:T(8,128)(2,1)S(1)} %fusion.57), channel_id=1, source_target_pairs={{0,16},{1,17},{2,18},{3,19},{4,20},{5,21},{6,22},{7,23},{8,24},{9,... | collective-permute-start | bytes 196616 | tf_op jit(solution)/shard_map/ppermute | solution.py:127
  231.4 10.4 %collective-permute-start.13 = (bf16[1,1,32,1024]{3,2,1,0:T(8,128)(2,1)S(1)}, bf16[1,1,32,1024]{3,2,1,0:T(8,128)(2,1)S(1)}, u32[]{:S(2)}, u32[]{:S(2)}) collective-permute-start(bf16[1,1,32,1024]{3,2,1,0:T(8,128)(2,1)S(1)} %fusion.58), channel_id=1, source_target_pairs={{0,16},{1,17},{2,18},{3,19},{4,20},{5,21},{6,22},{7,23},{8,24},{9,... | collective-permute-start | bytes 196616 | tf_op jit(solution)/shard_map/ppermute | solution.py:127
  242.6 8.7 %copy-start.1 = (bf16[1024,1024]{1,0:T(8,128)(2,1)S(1)}, bf16[1024,1024]{1,0:T(8,128)(2,1)}, u32[]{:S(2)}) copy-start(bf16[1024,1024]{1,0:T(8,128)(2,1)} %param.6) | copy-start | bytes 6291460
  (2 other events, 1.4 us)

commit v16 on v15

--- a/solution.py
+++ b/solution.py
@@ -150,10 +150,16 @@
     fetched_first = (normalizer_factor * upstream_first.reshape(groups, width, depth)).astype(
         jnp.bfloat16
     )
+    slots_linked = jnp.einsum(
+        "gij,gjsc->scgi",
+        link,
+        slot_of.reshape(groups, width, shards, capacity),
+        preferred_element_type=jnp.float32,
+    ).astype(jnp.bfloat16)
     outgoing = lax.dot_general(
-        linked_slots,
+        slots_linked.reshape(shards, capacity, count),
         fetched_first.reshape(count, depth),
-        (((0,), (0,)), ((), ())),
+        (((2,), (0,)), ((), ())),
         preferred_element_type=jnp.float32,
     ).astype(jnp.bfloat16)
     returned = exchange(outgoing)

time: 252 us -> 258 us (1.024)
  waiting for transfers between devices: 105 us -> 108 us
    unnamed x37 -> x45, local copies, waits for them, and re-layouts: 5.35 us -> 6.24 us
  transfers between devices with their start and end apart: 16 -> 16, of which waited for: 9 -> 9; matrix products, arithmetic and copies ran while one was open for 17% -> 15% of each run, Pallas kernels for 0% -> 0%
where the time goes in v16:
time: 258 us; the launch traced here: 257 us
  waiting for transfers between devices  108 us (42%)
  matrix products  54 us (21%)
  starting transfers between devices  29.7 us (12%)
  local copies, waits for them, and re-layouts  26.8 us (10%)
  other arithmetic  24 us (9%)
  blocking collectives  14.3 us (6%)
    ppermute x4, waiting for transfers between devices, gather_columns(): other = lax.ppermute(blocks, 'fsdp', [(i, i ^ step) for i in range(n_fsdp)])  55.5 us
    ppermute x10, waiting for transfers between devices, reduce_blocks(): moved = lax.ppermute(send, AXES, [(i, i ^ step) for i in range(shards)])  45.9 us
    ppermute x10, starting transfers between devices, reduce_blocks(): moved = lax.ppermute(send, AXES, [(i, i ^ step) for i in range(shards)])  18.9 us
    all_to_all x1, blocking collectives, exchange(): return lax.all_to_all(values, AXES, 0, 0, tiled=True)  14.3 us
    dot_general x2, matrix products, forward_layer(): product = jnp.dot(mixed, weight, preferred_element_type=jnp.float32)  9.1 us
    dot_general x1, matrix products, step_body(): lax.dot_general(picks, returned, (((0, 1), (0, 1)), ((), ())), preferred_...  8.74 us
    all_to_all x2, starting transfers between devices, exchange(): return lax.all_to_all(values, AXES, 0, 0, tiled=True)  8.51 us
    dot_general x1, matrix products, step_body(): lax.dot_general(linked_slots, answered, (((1, 2), (0, 1)), ((), ())), pre...  8.39 us
  transfers between devices with their start and end apart: 16, of which 9 were waited for; matrix products, arithmetic and copies ran while one was open for 15% of the time, Pallas kernels for 0%

profile of v16, /device:TPU:0, one launch (start us, length us, event | category | flops | bytes accessed | tf_op | source)
XLA Modules:
  0.0 257.5 jit_solution(2740477085835798609)
XLA Ops:
  5.1 3.4 %scatter_custom_fusion = s32[1568]{0:T(1024)S(1)} fusion(s32[768]{0:T(1024)S(1)} %fusion.87, s32[768]{0:T(1024)S(1)} %get-tuple-element.13, s32[]{:T(128)} %constant.167.clone.1), kind=kCustom, calls=%fused_computation.144 | custom fusion | bytes 6276 | tf_op jit(solution)/shard_map/scatter | solution.py:44
  8.6 14.3 %all_to_all.19 = s32[32,1,49]{2,1,0:T(1,128)S(1)} all-to-all(s32[32,1,49]{2,1,0:T(1,128)S(1)} %all_to_all.12), channel_id=1, replica_groups=mesh['node'=8,'fsdp'=4] {'node','fsdp'}, dimensions={0} | all-to-all | bytes 12544 | tf_op jit(solution)/shard_map/all_to_all | solution.py:23
  24.1 5.5 %fusion.31 = bf16[32,49,1024]{2,1,0:T(8,128)(2,1)} fusion(s32[32,49]{1,0:T(8,128)S(1)} %maximum_bitcast_fusion, pred[32,49]{1,0:T(8,128)(4,1)S(1)} %compare_bitcast_fusion, bf16[1024,1024]{1,0:T(8,128)(2,1)S(1)} %copy-done), kind=kOutput, calls=%fused_computation.34 | convolution fusion | flops 3293151232 | bytes 5316256 | tf_op jit(solution)/shard_map/dot_general | solution.py:51
  29.6 3.7 %all-to-all-start.1 = ((bf16[32,49,1024]{2,1,0:T(8,128)(2,1)}), bf16[32,49,1024]{2,1,0:T(8,128)(2,1)}, u32[]{:S(2)}, u32[]{:S(2)}) async-start(bf16[32,49,1024]{2,1,0:T(8,128)(2,1)} %fusion.31), calls=%async_computation.1 | async-start | bytes 7340032 | tf_op jit(solution)/shard_map/all_to_all | solution.py:23
  35.4 44.6 %collective-permute-done.2 = bf16[1,1024,256]{2,1,0:T(8,128)(2,1)S(1)} collective-permute-done((bf16[1,1024,256]{2,1,0:T(8,128)(2,1)S(1)}, bf16[1,1024,256]{2,1,0:T(8,128)(2,1)S(1)}, u32[]{:S(2)}, u32[]{:S(2)}) %collective-permute-start.2) | collective-permute-done | bytes 524320 | tf_op jit(solution)/shard_map/ppermute | solution.py:95
  80.8 10.8 %collective-permute-done = bf16[1,1024,256]{2,1,0:T(8,128)(2,1)} collective-permute-done((bf16[1,1024,256]{2,1,0:T(8,128)(2,1)S(1)}, bf16[1,1024,256]{2,1,0:T(8,128)(2,1)}, u32[]{:S(2)}, u32[]{:S(2)}) %collective-permute-start) | collective-permute-done | bytes 524320 | tf_op jit(solution)/shard_map/ppermute | solution.py:95
  99.1 4.0 %copy.118 = bf16[1024,4,256]{0,2,1:T(8,128)(2,1)} copy(bf16[1024,4,256]{2,0,1:T(8,128)(2,1)} %bitcast.317) | data formatting | bytes 4194304 | tf_op jit(solution)/shard_map/transpose | solution.py:105
  106.1 4.0 %copy.120 = bf16[1024,4,256]{0,2,1:T(8,128)(2,1)} copy(bf16[1024,4,256]{2,0,1:T(8,128)(2,1)} %bitcast.318) | data formatting | bytes 4194304 | tf_op jit(solution)/shard_map/transpose | solution.py:105
  110.1 6.3 %all-to-all-done.1 = bf16[32,49,1024]{2,1,0:T(8,128)(2,1)} async-done(((bf16[32,49,1024]{2,1,0:T(8,128)(2,1)}), bf16[32,49,1024]{2,1,0:T(8,128)(2,1)}, u32[]{:S(2)}, u32[]{:S(2)}) %all-to-all-start.1) | async-done | bytes 3211296 | tf_op jit(solution)/shard_map/all_to_all | solution.py:23
  116.4 8.4 %fusion.17 = bf16[3,256,1024]{2,1,0:T(8,128)(2,1)} fusion(bf16[32,49,1024]{2,1,0:T(8,128)(2,1)} %all-to-all-done.1, pred[3,256,49]{1,2,0:T(8,128)(4,1)S(1)} %copy-done.15, pred[3,256,32]{1,2,0:T(8,128)(4,1)S(1)} %copy-done.16, f32[3,256]{1,0:T(4,128)S(1)} %add_rsqrt_fusion, bf16[3,256,256]{2,1,0:T(8,128)(2,1)S(1)} %get-tuple-element.12), kind=kOutput, calls=%fused_computation.21 | convolution fusion | flops 3086794752 | bytes 5242624 | tf_op jit(solution)/shard_map/dot_general | solution.py:70
  124.8 5.3 %multiply_convert_fusion.3 = (bf16[768,1024]{1,0:T(8,128)(2,1)S(1)}, f32[768,1024]{1,0:T(8,128)}) fusion(bf16[768,1024]{1,0:T(8,128)(2,1)} %bitcast.347, bf16[1024,1024]{0,1:T(8,128)(2,1)S(1)} %bitcast.329), kind=kOutput, calls=%fused_computation.25 | convolution fusion | flops 1614544896 | bytes 8388608 | tf_op jit(solution)/shard_map/dot_general | solution.py:82
  131.7 3.8 %fusion.15 = bf16[768,1024]{1,0:T(8,128)(2,1)} fusion(bf16[3,256,1024]{2,1,0:T(8,128)(2,1)S(1)} %copy-done.21, bf16[768,1024]{1,0:T(8,128)(2,1)S(1)} %bitcast.333, bf16[1024,1024]{0,1:T(8,128)(2,1)S(1)} %bitcast.331), kind=kOutput, calls=%fused_computation.17 | convolution fusion | flops 1618477056 | bytes 6815744 | tf_op jit(solution)/shard_map/dot_general | solution.py:82
  135.5 5.2 %fusion.52 = f32[3,256,1024]{2,1,0:T(8,128)} fusion(bf16[3,256,256]{2,1,0:T(8,128)(2,1)S(1)} %get-tuple-element.12, bf16[3,256,1024]{2,1,0:T(8,128)(2,1)} %bitcast.335, bf16[1024,1024,1]{0,1,2:T(8,128)(2,1)S(1)} %bitcast.332, f32[3,256]{1,0:T(4,128)S(1)} %add_rsqrt_fusion), kind=kOutput, calls=%fused_computation.49 | convolution fusion | flops 2014838784 | bytes 7212032 | tf_op jit(solution)/shard_map/gji,gjd->gid/dot_general | solution.py:19
  140.8 4.3 %fusion.16 = bf16[768,1024]{1,0:T(8,128)(2,1)S(1)} fusion(f32[3,256,1024]{2,1,0:T(8,128)} %fusion.52, f32[768,1024]{1,0:T(8,128)} %get-tuple-element.16), kind=kLoop, calls=%fused_computation.19 | loop fusion | flops 7077888 | bytes 7864320 | tf_op jit(solution)/shard_map/convert_element_type | solution.py:147
  145.0 2.9 %multiply_convert_fusion = bf16[3,256,1024]{2,1,0:T(8,128)(2,1)} fusion(bf16[3,256,1024]{2,1,0:T(8,128)(2,1)S(1)} %bitcast.323, bf16[1024,1024,1]{0,1,2:T(8,128)(2,1)S(1)} %bitcast.330, f32[3,256]{1,0:T(4,128)S(1)} %add_rsqrt_fusion), kind=kOutput, calls=%fused_computation.22 | convolution fusion | flops 1612185600 | bytes 5245952 | tf_op jit(solution)/shard_map/dot_general | solution.py:86
  148.0 6.7 %bitcast_convert_fusion = bf16[32,49,1024]{2,1,0:T(8,128)(2,1)} fusion(pred[3,256,49]{1,2,0:T(8,128)(4,1)S(1)} %copy-done.15, pred[3,256,32]{1,2,0:T(8,128)(4,1)S(1)} %copy-done.16, bf16[3,256,1024]{2,1,0:T(8,128)(2,1)} %multiply_convert_fusion, bf16[3,256,256]{2,1,0:T(8,128)(2,1)S(1)} %get-tuple-element.12), kind=kOutput, calls=%fused_computation.1 | convolution fusion | flops 3086827520 | bytes 5239552 | tf_op jit(solution)/shard_map/dot_general | solution.py:159
  154.7 4.8 %all-to-all-start.2 = ((bf16[32,49,1024]{2,1,0:T(8,128)(2,1)}), bf16[32,49,1024]{2,1,0:T(8,128)(2,1)}, u32[]{:S(2)}, u32[]{:S(2)}) async-start(bf16[32,49,1024]{2,1,0:T(8,128)(2,1)} %bitcast_convert_fusion), calls=%async_computation.2 | async-start | bytes 7340032 | tf_op jit(solution)/shard_map/all_to_all | solution.py:23
  161.1 3.7 %convolution_bitcast_fusion.1 = f32[1,16,2,32,1024]{4,3,2,1,0:T(8,128)S(1)} fusion(bf16[16,2,32,768]{3,2,1,0:T(8,128)(2,1)} %bitcast.338, bf16[768,1024,1,1]{1,0,3,2:T(8,128)(2,1)} %bitcast.348), kind=kOutput, calls=%fused_computation.36 | convolution fusion | flops 1610612736 | bytes 7340032 | tf_op jit(solution)/shard_map/dot_general | solution.py:111
  167.6 2.7 %copy.139 = bf16[1024,768]{1,0:T(8,128)(2,1)} copy(bf16[1024,768]{0,1:T(8,128)(2,1)} %bitcast.336) | data formatting | bytes 3145728 | tf_op jit(solution)/shard_map/dot_general | solution.py:111
  170.3 3.2 %convolution_bitcast_fusion = f32[1,16,2,32,1024]{4,3,1,2,0:T(8,128)S(1)} fusion(bf16[768,1024,1,1]{1,0,2,3:T(8,128)(2,1)S(1)} %bitcast.334, bf16[16,2,32,768]{3,2,1,0:T(8,128)(2,1)} %bitcast.339), kind=kOutput, calls=%fused_computation.35 | convolution fusion | flops 1610612736 | bytes 7340032 | tf_op jit(solution)/shard_map/dot_general | solution.py:111
  175.9 3.7 %fusion.42 = f32[1,16,32,1024]{3,2,1,0:T(8,128)S(1)} fusion(f32[1,16,32,1024]{3,2,1,0:T(8,128)} %collective-permute-done.4, f32[1,16,2,32,1024]{4,3,2,1,0:T(8,128)} %copy-done.4, pred[]{:T(512)S(6)} %eq.147), kind=kLoop, calls=%fused_computation.42 | loop fusion | flops 1048576 | bytes 8388609 | tf_op jit(solution)/shard_map/add | solution.py:128
  181.4 2.3 bitcast_add_fusion
  184.2 22.4 %collective-permute-done.5 = bf16[1,8,32,1024]{3,2,1,0:T(8,128)(2,1)S(1)} collective-permute-done((bf16[1,8,32,1024]{3,2,1,0:T(8,128)(2,1)S(1)}, bf16[1,8,32,1024]{3,2,1,0:T(8,128)(2,1)S(1)}, u32[]{:S(2)}, u32[]{:S(2)}) %collective-permute-start.5) | collective-permute-done | bytes 524320 | tf_op jit(solution)/shard_map/ppermute | solution.py:127
  209.0 9.3 %collective-permute-done.10 = bf16[1,8,32,1024]{3,2,1,0:T(8,128)(2,1)S(1)} collective-permute-done((bf16[1,8,32,1024]{3,2,1,0:T(8,128)(2,1)S(1)}, bf16[1,8,32,1024]{3,2,1,0:T(8,128)(2,1)S(1)}, u32[]{:S(2)}, u32[]{:S(2)}) %collective-permute-start.10) | collective-permute-done | bytes 524320 | tf_op jit(solution)/shard_map/ppermute | solution.py:127
  218.6 2.9 %collective-permute-start.11 = (bf16[1,4,32,1024]{3,2,1,0:T(8,128)(2,1)S(1)}, bf16[1,4,32,1024]{3,2,1,0:T(8,128)(2,1)S(1)}, u32[]{:S(2)}, u32[]{:S(2)}) collective-permute-start(bf16[1,4,32,1024]{3,2,1,0:T(8,128)(2,1)S(1)} %fusion.62), channel_id=1, source_target_pairs={{0,4},{1,5},{2,6},{3,7},{4,0},{5,1},{6,2},{7,3},{8,12},{9,13},{10,... | collective-permute-start | bytes 786440 | tf_op jit(solution)/shard_map/ppermute | solution.py:127
  221.7 2.9 %collective-permute-start.7 = (bf16[1,2,32,1024]{3,2,1,0:T(8,128)(2,1)S(1)}, bf16[1,2,32,1024]{3,2,1,0:T(8,128)(2,1)S(1)}, u32[]{:S(2)}, u32[]{:S(2)}) collective-permute-start(bf16[1,2,32,1024]{3,2,1,0:T(8,128)(2,1)S(1)} %fusion.68), channel_id=1, source_target_pairs={{0,8},{1,9},{2,10},{3,11},{4,12},{5,13},{6,14},{7,15},{8,0},{9,1},... | collective-permute-start | bytes 393224 | tf_op jit(solution)/shard_map/ppermute | solution.py:127
  224.6 5.6 %collective-permute-done.11 = bf16[1,4,32,1024]{3,2,1,0:T(8,128)(2,1)S(1)} collective-permute-done((bf16[1,4,32,1024]{3,2,1,0:T(8,128)(2,1)S(1)}, bf16[1,4,32,1024]{3,2,1,0:T(8,128)(2,1)S(1)}, u32[]{:S(2)}, u32[]{:S(2)}) %collective-permute-start.11) | collective-permute-done | bytes 262176 | tf_op jit(solution)/shard_map/ppermute | solution.py:127
  230.4 3.1 %collective-permute-start.12 = (bf16[1,2,32,1024]{3,2,1,0:T(8,128)(2,1)S(1)}, bf16[1,2,32,1024]{3,2,1,0:T(8,128)(2,1)S(1)}, u32[]{:S(2)}, u32[]{:S(2)}) collective-permute-start(bf16[1,2,32,1024]{3,2,1,0:T(8,128)(2,1)S(1)} %fusion.69), channel_id=1, source_target_pairs={{0,8},{1,9},{2,10},{3,11},{4,12},{5,13},{6,14},{7,15},{8,0},{9,1},... | collective-permute-start | bytes 393224 | tf_op jit(solution)/shard_map/ppermute | solution.py:127
  233.6 2.3 collective-permute-start.8
  237.6 2.9 %collective-permute-start.13 = (bf16[1,1,32,1024]{3,2,1,0:T(8,128)(2,1)S(1)}, bf16[1,1,32,1024]{3,2,1,0:T(8,128)(2,1)S(1)}, u32[]{:S(2)}, u32[]{:S(2)}) collective-permute-start(bf16[1,1,32,1024]{3,2,1,0:T(8,128)(2,1)S(1)} %fusion.79), channel_id=1, source_target_pairs={{0,16},{1,17},{2,18},{3,19},{4,20},{5,21},{6,22},{7,23},{8,24},{9,... | collective-permute-start | bytes 196616 | tf_op jit(solution)/shard_map/ppermute | solution.py:127
  240.4 6.7 %collective-permute-done.8 = bf16[1,1,32,1024]{3,2,1,0:T(8,128)(2,1)S(1)} collective-permute-done((bf16[1,1,32,1024]{3,2,1,0:T(8,128)(2,1)S(1)}, bf16[1,1,32,1024]{3,2,1,0:T(8,128)(2,1)S(1)}, u32[]{:S(2)}, u32[]{:S(2)}) %collective-permute-start.8) | collective-permute-done | bytes 65568 | tf_op jit(solution)/shard_map/ppermute | solution.py:127
  248.7 8.7 %fusion.34 = f32[1024,1024]{1,0:T(8,128)} fusion(bf16[32,49,1024]{2,1,0:T(8,128)(2,1)} %all-to-all-done.2, s32[32,49]{1,0:T(8,128)S(1)} %copy-done.18, pred[32,49]{1,0:T(8,128)(4,1)S(1)} %copy-done.20), kind=kOutput, calls=%fused_computation.37 | convolution fusion | flops 3291545600 | bytes 7413408 | tf_op jit(solution)/shard_map/dot_general | solution.py:166
  (112 shorter events, 36.1 us)
Async XLA Ops:
  0.6 23.5 %copy-start = (bf16[1024,1024]{1,0:T(8,128)(2,1)S(1)}, bf16[1024,1024]{1,0:T(8,128)(2,1)}, u32[]{:S(2)}) copy-start(bf16[1024,1024]{1,0:T(8,128)(2,1)} %param.6) | copy-start | bytes 6291460
  29.6 3.7 %copy-start.11 = (bf16[1024,256]{1,0:T(8,128)(2,1)S(1)}, bf16[1024,256]{1,0:T(8,128)(2,1)}, u32[]{:S(2)}) copy-start(bf16[1024,256]{1,0:T(8,128)(2,1)} %param.10) | copy-start | bytes 1572868
  29.6 5.4 %copy-start.12 = (bf16[1024,256]{1,0:T(8,128)(2,1)S(1)}, bf16[1024,256]{1,0:T(8,128)(2,1)}, u32[]{:S(2)}) copy-start(bf16[1024,256]{1,0:T(8,128)(2,1)} %param.9) | copy-start | bytes 1572868
  29.6 86.8 %all-to-all-start.1 = ((bf16[32,49,1024]{2,1,0:T(8,128)(2,1)}), bf16[32,49,1024]{2,1,0:T(8,128)(2,1)}, u32[]{:S(2)}, u32[]{:S(2)}) async-start(bf16[32,49,1024]{2,1,0:T(8,128)(2,1)} %fusion.31), calls=%async_computation.1 | async-start | bytes 7340032 | tf_op jit(solution)/shard_map/all_to_all | solution.py:23
  33.3 46.8 %collective-permute-start.2 = (bf16[1,1024,256]{2,1,0:T(8,128)(2,1)S(1)}, bf16[1,1024,256]{2,1,0:T(8,128)(2,1)S(1)}, u32[]{:S(2)}, u32[]{:S(2)}) collective-permute-start(bf16[1,1024,256]{2,1,0:T(8,128)(2,1)S(1)} %bitcast.340), channel_id=1, source_target_pairs={{0,2},{1,3},{2,0},{3,1},{4,6},{5,7},{6,4},{7,5},{8,10},{9,11},{10,... | collective-permute-start | bytes 1572872 | tf_op jit(solution)/shard_map/ppermute | solution.py:95
  34.9 56.7 %collective-permute-start = (bf16[1,1024,256]{2,1,0:T(8,128)(2,1)S(1)}, bf16[1,1024,256]{2,1,0:T(8,128)(2,1)}, u32[]{:S(2)}, u32[]{:S(2)}) collective-permute-start(bf16[1,1024,256]{2,1,0:T(8,128)(2,1)S(1)} %bitcast.341), channel_id=1, source_target_pairs={{0,2},{1,3},{2,0},{3,1},{4,6},{5,7},{6,4},{7,5},{8,10},{9,11},{10,... | collective-permute-start | bytes 1572872 | tf_op jit(solution)/shard_map/ppermute | solution.py:95
  94.1 3.2 %collective-permute-start.1 = (bf16[2,1024,256]{2,1,0:T(8,128)(2,1)}, bf16[2,1024,256]{2,1,0:T(8,128)(2,1)S(1)}, u32[]{:S(2)}, u32[]{:S(2)}) collective-permute-start(bf16[2,1024,256]{2,1,0:T(8,128)(2,1)} %pad_maximum_fusion.2), channel_id=1, source_target_pairs={{0,1},{1,0},{2,3},{3,2},{4,5},{5,4},{6,7},{7,6},{8,9},{9,8},{10,11... | collective-permute-start | bytes 3145736 | tf_op jit(solution)/shard_map/ppermute | solution.py:95
  95.7 7.3 %collective-permute-start.3 = (bf16[2,1024,256]{2,1,0:T(8,128)(2,1)}, bf16[2,1024,256]{2,1,0:T(8,128)(2,1)}, u32[]{:S(2)}, u32[]{:S(2)}) collective-permute-start(bf16[2,1024,256]{2,1,0:T(8,128)(2,1)} %pad_maximum_fusion.3), channel_id=1, source_target_pairs={{0,1},{1,0},{2,3},{3,2},{4,5},{5,4},{6,7},{7,6},{8,9},{9,8},{10,11... | collective-permute-start | bytes 3145736 | tf_op jit(solution)/shard_map/ppermute | solution.py:95
  106.1 10.2 %copy-start.15 = (pred[3,256,49]{1,2,0:T(8,128)(4,1)S(1)}, pred[3,256,49]{1,2,0:T(8,128)(4,1)}, u32[]{:S(2)}) copy-start(pred[3,256,49]{1,2,0:T(8,128)(4,1)} %iota_compare_fusion.2) | copy-start | bytes 112900
  106.1 10.2 %copy-start.16 = (pred[3,256,32]{1,2,0:T(8,128)(4,1)S(1)}, pred[3,256,32]{1,2,0:T(8,128)(4,1)}, u32[]{:S(2)}) copy-start(pred[3,256,32]{1,2,0:T(8,128)(4,1)} %iota_compare_fusion.3) | copy-start | bytes 73732
  116.4 8.4 %copy-start.5 = (bf16[1024,4,256]{0,2,1:T(8,128)(2,1)S(1)}, bf16[1024,4,256]{0,2,1:T(8,128)(2,1)}, u32[]{:S(2)}) copy-start(bf16[1024,4,256]{0,2,1:T(8,128)(2,1)} %copy.118) | copy-start | bytes 6291460
  124.8 5.9 %copy-start.21 = (bf16[3,256,1024]{2,1,0:T(8,128)(2,1)S(1)}, bf16[3,256,1024]{2,1,0:T(8,128)(2,1)}, u32[]{:S(2)}) copy-start(bf16[3,256,1024]{2,1,0:T(8,128)(2,1)} %param.11) | copy-start | bytes 4718596
  130.6 4.9 %copy-start.8 = (bf16[3,256,1024]{2,1,0:T(8,128)(2,1)}, bf16[3,256,1024]{2,1,0:T(8,128)(2,1)S(1)}, u32[]{:S(2)}) copy-start(bf16[3,256,1024]{2,1,0:T(8,128)(2,1)S(1)} %multiply_convert_fusion.2) | copy-start | bytes 4718596
  140.8 4.3 %copy-start.6 = (bf16[1024,4,256]{0,2,1:T(8,128)(2,1)S(1)}, bf16[1024,4,256]{0,2,1:T(8,128)(2,1)}, u32[]{:S(2)}) copy-start(bf16[1024,4,256]{0,2,1:T(8,128)(2,1)} %copy.118) | copy-start | bytes 6291460
  154.7 94.0 %all-to-all-start.2 = ((bf16[32,49,1024]{2,1,0:T(8,128)(2,1)}), bf16[32,49,1024]{2,1,0:T(8,128)(2,1)}, u32[]{:S(2)}, u32[]{:S(2)}) async-start(bf16[32,49,1024]{2,1,0:T(8,128)(2,1)} %bitcast_convert_fusion), calls=%async_computation.2 | async-start | bytes 7340032 | tf_op jit(solution)/shard_map/all_to_all | solution.py:23
  164.7 2.6 %copy-start.4 = (f32[1,16,2,32,1024]{4,3,2,1,0:T(8,128)}, f32[1,16,2,32,1024]{4,3,2,1,0:T(8,128)S(1)}, u32[]{:S(2)}) copy-start(f32[1,16,2,32,1024]{4,3,2,1,0:T(8,128)S(1)} %convolution_bitcast_fusion.1) | copy-start | bytes 12582916
  167.4 2.9 %copy-start.9 = (bf16[3,256,1024]{2,1,0:T(8,128)(2,1)S(1)}, bf16[3,256,1024]{2,1,0:T(8,128)(2,1)}, u32[]{:S(2)}) copy-start(bf16[3,256,1024]{2,1,0:T(8,128)(2,1)} %copy-done.8) | copy-start | bytes 4718596
  167.4 8.5 %collective-permute-start.4 = (f32[1,16,32,1024]{3,2,1,0:T(8,128)}, f32[1,16,32,1024]{3,2,1,0:T(8,128)}, u32[]{:S(2)}, u32[]{:S(2)}) collective-permute-start(f32[1,16,32,1024]{3,2,1,0:T(8,128)} %select_bitcast_fusion.1), channel_id=1, source_target_pairs={{0,1},{1,0},{2,3},{3,2},{4,5},{5,4},{6,7},{7,6},{8,9},{9,8},{10,11... | collective-permute-start | bytes 6291464 | tf_op jit(solution)/shard_map/ppermute | solution.py:127
  173.5 2.0 copy-start.2
  175.5 5.9 %collective-permute-start.9 = (f32[1,16,32,1024]{3,2,1,0:T(8,128)S(1)}, f32[1,16,32,1024]{3,2,1,0:T(8,128)}, u32[]{:S(2)}, u32[]{:S(2)}) collective-permute-start(f32[1,16,32,1024]{3,2,1,0:T(8,128)S(1)} %select_bitcast_fusion), channel_id=1, source_target_pairs={{0,1},{1,0},{2,3},{3,2},{4,5},{5,4},{6,7},{7,6},{8,9},{9,8},{10,11... | collective-permute-start | bytes 6291464 | tf_op jit(solution)/shard_map/ppermute | solution.py:127
  175.9 5.5 %copy-start.3 = (f32[1,16,2,32,1024]{4,3,1,2,0:T(8,128)S(1)}, f32[1,16,2,32,1024]{4,3,1,2,0:T(8,128)}, u32[]{:S(2)}) copy-start(f32[1,16,2,32,1024]{4,3,1,2,0:T(8,128)} %copy-done.2) | copy-start | bytes 12582916
  179.7 26.9 %collective-permute-start.5 = (bf16[1,8,32,1024]{3,2,1,0:T(8,128)(2,1)S(1)}, bf16[1,8,32,1024]{3,2,1,0:T(8,128)(2,1)S(1)}, u32[]{:S(2)}, u32[]{:S(2)}) collective-permute-start(bf16[1,8,32,1024]{3,2,1,0:T(8,128)(2,1)S(1)} %fusion.53), channel_id=1, source_target_pairs={{0,2},{1,3},{2,0},{3,1},{4,6},{5,7},{6,4},{7,5},{8,10},{9,11},{10,... | collective-permute-start | bytes 1572872 | tf_op jit(solution)/shard_map/ppermute | solution.py:127
  183.8 34.6 %collective-permute-start.10 = (bf16[1,8,32,1024]{3,2,1,0:T(8,128)(2,1)S(1)}, bf16[1,8,32,1024]{3,2,1,0:T(8,128)(2,1)S(1)}, u32[]{:S(2)}, u32[]{:S(2)}) collective-permute-start(bf16[1,8,32,1024]{3,2,1,0:T(8,128)(2,1)S(1)} %fusion.54), channel_id=1, source_target_pairs={{0,2},{1,3},{2,0},{3,1},{4,6},{5,7},{6,4},{7,5},{8,10},{9,11},{10,... | collective-permute-start | bytes 1572872 | tf_op jit(solution)/shard_map/ppermute | solution.py:127
  206.9 14.6 %collective-permute-start.6 = (bf16[1,4,32,1024]{3,2,1,0:T(8,128)(2,1)S(1)}, bf16[1,4,32,1024]{3,2,1,0:T(8,128)(2,1)S(1)}, u32[]{:S(2)}, u32[]{:S(2)}) collective-permute-start(bf16[1,4,32,1024]{3,2,1,0:T(8,128)(2,1)S(1)} %fusion.61), channel_id=1, source_target_pairs={{0,4},{1,5},{2,6},{3,7},{4,0},{5,1},{6,2},{7,3},{8,12},{9,13},{10,... | collective-permute-start | bytes 786440 | tf_op jit(solution)/shard_map/ppermute | solution.py:127
  218.6 11.6 %collective-permute-start.11 = (bf16[1,4,32,1024]{3,2,1,0:T(8,128)(2,1)S(1)}, bf16[1,4,32,1024]{3,2,1,0:T(8,128)(2,1)S(1)}, u32[]{:S(2)}, u32[]{:S(2)}) collective-permute-start(bf16[1,4,32,1024]{3,2,1,0:T(8,128)(2,1)S(1)} %fusion.62), channel_id=1, source_target_pairs={{0,4},{1,5},{2,6},{3,7},{4,0},{5,1},{6,2},{7,3},{8,12},{9,13},{10,... | collective-permute-start | bytes 786440 | tf_op jit(solution)/shard_map/ppermute | solution.py:127
  221.7 11.8 %collective-permute-start.7 = (bf16[1,2,32,1024]{3,2,1,0:T(8,128)(2,1)S(1)}, bf16[1,2,32,1024]{3,2,1,0:T(8,128)(2,1)S(1)}, u32[]{:S(2)}, u32[]{:S(2)}) collective-permute-start(bf16[1,2,32,1024]{3,2,1,0:T(8,128)(2,1)S(1)} %fusion.68), channel_id=1, source_target_pairs={{0,8},{1,9},{2,10},{3,11},{4,12},{5,13},{6,14},{7,15},{8,0},{9,1},... | collective-permute-start | bytes 393224 | tf_op jit(solution)/shard_map/ppermute | solution.py:127
  230.3 18.4 %copy-start.18 = (s32[32,49]{1,0:T(8,128)S(1)}, s32[32,49]{1,0:T(8,128)}, u32[]{:S(2)}) copy-start(s32[32,49]{1,0:T(8,128)} %copy-done.17) | copy-start | bytes 18820
  230.3 18.4 %copy-start.20 = (pred[32,49]{1,0:T(8,128)(4,1)S(1)}, pred[32,49]{1,0:T(8,128)(4,1)}, u32[]{:S(2)}) copy-start(pred[32,49]{1,0:T(8,128)(4,1)} %copy-done.19) | copy-start | bytes 4708
  230.4 7.1 %collective-permute-start.12 = (bf16[1,2,32,1024]{3,2,1,0:T(8,128)(2,1)S(1)}, bf16[1,2,32,1024]{3,2,1,0:T(8,128)(2,1)S(1)}, u32[]{:S(2)}, u32[]{:S(2)}) collective-permute-start(bf16[1,2,32,1024]{3,2,1,0:T(8,128)(2,1)S(1)} %fusion.69), channel_id=1, source_target_pairs={{0,8},{1,9},{2,10},{3,11},{4,12},{5,13},{6,14},{7,15},{8,0},{9,1},... | collective-permute-start | bytes 393224 | tf_op jit(solution)/shard_map/ppermute | solution.py:127
  233.6 13.6 %collective-permute-start.8 = (bf16[1,1,32,1024]{3,2,1,0:T(8,128)(2,1)S(1)}, bf16[1,1,32,1024]{3,2,1,0:T(8,128)(2,1)S(1)}, u32[]{:S(2)}, u32[]{:S(2)}) collective-permute-start(bf16[1,1,32,1024]{3,2,1,0:T(8,128)(2,1)S(1)} %fusion.78), channel_id=1, source_target_pairs={{0,16},{1,17},{2,18},{3,19},{4,20},{5,21},{6,22},{7,23},{8,24},{9,... | collective-permute-start | bytes 196616 | tf_op jit(solution)/shard_map/ppermute | solution.py:127
  237.6 10.4 %collective-permute-start.13 = (bf16[1,1,32,1024]{3,2,1,0:T(8,128)(2,1)S(1)}, bf16[1,1,32,1024]{3,2,1,0:T(8,128)(2,1)S(1)}, u32[]{:S(2)}, u32[]{:S(2)}) collective-permute-start(bf16[1,1,32,1024]{3,2,1,0:T(8,128)(2,1)S(1)} %fusion.79), channel_id=1, source_target_pairs={{0,16},{1,17},{2,18},{3,19},{4,20},{5,21},{6,22},{7,23},{8,24},{9,... | collective-permute-start | bytes 196616 | tf_op jit(solution)/shard_map/ppermute | solution.py:127
  248.7 8.8 %copy-start.1 = (bf16[1024,1024]{1,0:T(8,128)(2,1)S(1)}, bf16[1024,1024]{1,0:T(8,128)(2,1)}, u32[]{:S(2)}) copy-start(bf16[1024,1024]{1,0:T(8,128)(2,1)} %param.6) | copy-start | bytes 6291460
  (6 other events, 6.6 us)

commit v17 on v15

--- a/solution.py
+++ b/solution.py
@@ -157,8 +157,14 @@
         preferred_element_type=jnp.float32,
     ).astype(jnp.bfloat16)
     returned = exchange(outgoing)
+    picked_rows = (
+        (jnp.arange(rows_here, dtype=jnp.int32)[:, None, None] == safe_rows) & valid
+    ).astype(jnp.bfloat16)
     table_grad = lax.dot_general(
-        picks, returned, (((0, 1), (0, 1)), ((), ())), preferred_element_type=jnp.float32
+        picked_rows,
+        returned,
+        (((1, 2), (0, 1)), ((), ())),
+        preferred_element_type=jnp.float32,
     )
     grad_one = reduce_blocks(parts_one[None])[0].T
     grad_two = reduce_blocks(parts_two[None])[0].T

time: 252 us -> 252 us (level)
  no operation moved by 1% of the time
where the time goes in v17:
time: 252 us; the launch traced here: 251 us
  waiting for transfers between devices  105 us (42%)
  matrix products  52 us (21%)
  starting transfers between devices  30.1 us (12%)
  local copies, waits for them, and re-layouts  25.9 us (10%)
  other arithmetic  23.1 us (9%)
  blocking collectives  14.3 us (6%)
    ppermute x4, waiting for transfers between devices, gather_columns(): other = lax.ppermute(blocks, 'fsdp', [(i, i ^ step) for i in range(n_fsdp)])  55.2 us
    ppermute x10, waiting for transfers between devices, reduce_blocks(): moved = lax.ppermute(send, AXES, [(i, i ^ step) for i in range(shards)])  45.8 us
    ppermute x10, starting transfers between devices, reduce_blocks(): moved = lax.ppermute(send, AXES, [(i, i ^ step) for i in range(shards)])  18.9 us
    all_to_all x1, blocking collectives, exchange(): return lax.all_to_all(values, AXES, 0, 0, tiled=True)  14.3 us
    dot_general x1, matrix products, step_body(): lax.dot_general(picked_rows, returned, (((1, 2), (0, 1)), ((), ())), pref...  8.74 us
    all_to_all x2, starting transfers between devices, exchange(): return lax.all_to_all(values, AXES, 0, 0, tiled=True)  8.53 us
    dot_general x1, matrix products, step_body(): lax.dot_general(linked_slots, fetched_first.reshape(count, depth), (((0,)...  8.32 us
    transpose x2, local copies, waits for them, and re-layouts, gather_columns(): blocks.transpose(1, 0, 2).reshape(weight.shape[0], n_fsdp * weight.shape[1])  7.99 us
  transfers between devices with their start and end apart: 16, of which 9 were waited for; matrix products, arithmetic and copies ran while one was open for 17% of the time, Pallas kernels for 0%

profile of v17, /device:TPU:0, one launch (start us, length us, event | category | flops | bytes accessed | tf_op | source)
XLA Modules:
  0.0 251.3 jit_solution(13344232349441538827)
XLA Ops:
  5.1 3.4 %scatter_custom_fusion = s32[1568]{0:T(1024)S(1)} fusion(s32[768]{0:T(1024)S(1)} %fusion.67, s32[768]{0:T(1024)S(1)} %get-tuple-element.13, s32[]{:T(128)} %constant.167.clone.1), kind=kCustom, calls=%fused_computation.139 | custom fusion | bytes 6276 | tf_op jit(solution)/shard_map/scatter | solution.py:44
  8.6 14.3 %all_to_all.19 = s32[32,1,49]{2,1,0:T(1,128)S(1)} all-to-all(s32[32,1,49]{2,1,0:T(1,128)S(1)} %all_to_all.12), channel_id=1, replica_groups=mesh['node'=8,'fsdp'=4] {'node','fsdp'}, dimensions={0} | all-to-all | bytes 12544 | tf_op jit(solution)/shard_map/all_to_all | solution.py:23
  23.5 5.5 %fusion.19 = bf16[32,49,1024]{2,1,0:T(8,128)(2,1)} fusion(s32[32,49]{1,0:T(8,128)S(1)} %maximum_bitcast_fusion, pred[32,49]{1,0:T(8,128)(4,1)S(1)} %compare_bitcast_fusion, bf16[1024,1024]{1,0:T(8,128)(2,1)S(1)} %copy-done), kind=kOutput, calls=%fused_computation.29 | convolution fusion | flops 3293151232 | bytes 5316256 | tf_op jit(solution)/shard_map/dot_general | solution.py:51
  29.0 3.7 %all-to-all-start.1 = ((bf16[32,49,1024]{2,1,0:T(8,128)(2,1)}), bf16[32,49,1024]{2,1,0:T(8,128)(2,1)}, u32[]{:S(2)}, u32[]{:S(2)}) async-start(bf16[32,49,1024]{2,1,0:T(8,128)(2,1)} %fusion.19), calls=%async_computation.1 | async-start | bytes 7340032 | tf_op jit(solution)/shard_map/all_to_all | solution.py:23
  35.1 44.4 %collective-permute-done.2 = bf16[1,1024,256]{2,1,0:T(8,128)(2,1)S(1)} collective-permute-done((bf16[1,1024,256]{2,1,0:T(8,128)(2,1)S(1)}, bf16[1,1024,256]{2,1,0:T(8,128)(2,1)S(1)}, u32[]{:S(2)}, u32[]{:S(2)}) %collective-permute-start.2) | collective-permute-done | bytes 524320 | tf_op jit(solution)/shard_map/ppermute | solution.py:95
  80.3 10.8 %collective-permute-done = bf16[1,1024,256]{2,1,0:T(8,128)(2,1)} collective-permute-done((bf16[1,1024,256]{2,1,0:T(8,128)(2,1)S(1)}, bf16[1,1024,256]{2,1,0:T(8,128)(2,1)}, u32[]{:S(2)}, u32[]{:S(2)}) %collective-permute-start) | collective-permute-done | bytes 524320 | tf_op jit(solution)/shard_map/ppermute | solution.py:95
  95.8 3.2 %fusion.25 = bf16[3,256,32,49]{1,3,2,0:T(8,128)(2,1)} fusion(pred[3,256,49]{1,2,0:T(8,128)(4,1)S(1)} %iota_compare_fusion.3, pred[3,256,32]{1,2,0:T(8,128)(4,1)} %iota_compare_fusion.4, bf16[3,256,256]{2,1,0:T(8,128)(2,1)S(1)} %get-tuple-element.12), kind=kOutput, calls=%fused_computation.33 | convolution fusion | flops 618971136 | bytes 2863872 | tf_op jit(solution)/shard_map/gij,gjsc->gisc/dot_general | solution.py:61
  102.1 4.0 %copy.118 = bf16[1024,4,256]{0,2,1:T(8,128)(2,1)} copy(bf16[1024,4,256]{2,0,1:T(8,128)(2,1)} %bitcast.312) | data formatting | bytes 4194304 | tf_op jit(solution)/shard_map/transpose | solution.py:105
  107.9 4.0 %copy.120 = bf16[1024,4,256]{0,2,1:T(8,128)(2,1)} copy(bf16[1024,4,256]{2,0,1:T(8,128)(2,1)} %bitcast.313) | data formatting | bytes 4194304 | tf_op jit(solution)/shard_map/transpose | solution.py:105
  111.9 3.9 %all-to-all-done.1 = bf16[32,49,1024]{2,1,0:T(8,128)(2,1)} async-done(((bf16[32,49,1024]{2,1,0:T(8,128)(2,1)}), bf16[32,49,1024]{2,1,0:T(8,128)(2,1)}, u32[]{:S(2)}, u32[]{:S(2)}) %all-to-all-start.1) | async-done | bytes 3211296 | tf_op jit(solution)/shard_map/all_to_all | solution.py:23
  115.8 5.9 %fusion.16 = bf16[3,256,1024]{2,1,0:T(8,128)(2,1)S(1)} fusion(bf16[3,256,32,49]{1,3,2,0:T(8,128)(2,1)} %fusion.25, bf16[32,49,1024]{2,1,0:T(8,128)(2,1)} %all-to-all-done.1, f32[3,256]{1,0:T(4,128)S(1)} %add_rsqrt_fusion), kind=kOutput, calls=%fused_computation.21 | convolution fusion | flops 2467823616 | bytes 7195648 | tf_op jit(solution)/shard_map/dot_general | solution.py:70
  121.8 3.8 %multiply_convert_fusion.3 = (bf16[768,1024]{1,0:T(8,128)(2,1)S(1)}, f32[768,1024]{1,0:T(8,128)}) fusion(bf16[768,1024]{1,0:T(8,128)(2,1)S(1)} %bitcast.342, bf16[1024,1024]{0,1:T(8,128)(2,1)S(1)} %bitcast.325), kind=kOutput, calls=%fused_computation.25 | convolution fusion | flops 1614544896 | bytes 8388608 | tf_op jit(solution)/shard_map/dot_general | solution.py:82
  127.2 3.8 %fusion.14 = bf16[768,1024]{1,0:T(8,128)(2,1)} fusion(bf16[3,256,1024]{2,1,0:T(8,128)(2,1)S(1)} %copy-done.16, bf16[768,1024]{1,0:T(8,128)(2,1)S(1)} %bitcast.328, bf16[1024,1024]{0,1:T(8,128)(2,1)S(1)} %bitcast.326), kind=kOutput, calls=%fused_computation.17 | convolution fusion | flops 1618477056 | bytes 6815744 | tf_op jit(solution)/shard_map/dot_general | solution.py:82
  131.1 5.3 %fusion.35 = f32[3,256,1024]{2,1,0:T(8,128)} fusion(bf16[3,256,256]{2,1,0:T(8,128)(2,1)S(1)} %get-tuple-element.12, bf16[3,256,1024]{2,1,0:T(8,128)(2,1)} %bitcast.330, bf16[1024,1024,1]{0,1,2:T(8,128)(2,1)S(1)} %bitcast.327, f32[3,256]{1,0:T(4,128)S(1)} %add_rsqrt_fusion), kind=kOutput, calls=%fused_computation.45 | convolution fusion | flops 2014838784 | bytes 7212032 | tf_op jit(solution)/shard_map/gji,gjd->gid/dot_general | solution.py:19
  136.3 3.9 %fusion.15 = bf16[768,1024]{1,0:T(8,128)(2,1)S(1)} fusion(f32[3,256,1024]{2,1,0:T(8,128)} %fusion.35, f32[768,1024]{1,0:T(8,128)} %get-tuple-element.16), kind=kLoop, calls=%fused_computation.19 | loop fusion | flops 7077888 | bytes 7864320 | tf_op jit(solution)/shard_map/convert_element_type | solution.py:147
  140.2 8.3 %bitcast_convert_fusion = bf16[32,49,1024]{2,1,0:T(8,128)(2,1)} fusion(bf16[3,256,32,49]{1,3,2,0:T(8,128)(2,1)} %fusion.25, bf16[3,256,1024]{2,1,0:T(8,128)(2,1)S(1)} %bitcast.318, bf16[1024,1024,1]{0,1,2:T(8,128)(2,1)} %bitcast.324, f32[3,256]{1,0:T(4,128)S(1)} %add_rsqrt_fusion), kind=kOutput, calls=%fused_computation.1 | convolution fusion | flops 4080041984 | bytes 9292800 | tf_op jit(solution)/shard_map/dot_general | solution.py:153
  148.5 4.8 %all-to-all-start.2 = ((bf16[32,49,1024]{2,1,0:T(8,128)(2,1)}), bf16[32,49,1024]{2,1,0:T(8,128)(2,1)}, u32[]{:S(2)}, u32[]{:S(2)}) async-start(bf16[32,49,1024]{2,1,0:T(8,128)(2,1)} %bitcast_convert_fusion), calls=%async_computation.2 | async-start | bytes 7340032 | tf_op jit(solution)/shard_map/all_to_all | solution.py:23
  154.9 3.7 %convolution_bitcast_fusion.1 = f32[1,16,2,32,1024]{4,3,2,1,0:T(8,128)S(1)} fusion(bf16[16,2,32,768]{3,2,1,0:T(8,128)(2,1)} %bitcast.333, bf16[768,1024,1,1]{1,0,3,2:T(8,128)(2,1)} %bitcast.343), kind=kOutput, calls=%fused_computation.31 | convolution fusion | flops 1610612736 | bytes 7340032 | tf_op jit(solution)/shard_map/dot_general | solution.py:111
  161.4 2.7 %copy.139 = bf16[1024,768]{1,0:T(8,128)(2,1)} copy(bf16[1024,768]{0,1:T(8,128)(2,1)} %bitcast.331) | data formatting | bytes 3145728 | tf_op jit(solution)/shard_map/dot_general | solution.py:111
  164.1 3.2 %convolution_bitcast_fusion = f32[1,16,2,32,1024]{4,3,1,2,0:T(8,128)S(1)} fusion(bf16[768,1024,1,1]{1,0,2,3:T(8,128)(2,1)S(1)} %bitcast.329, bf16[16,2,32,768]{3,2,1,0:T(8,128)(2,1)} %bitcast.334), kind=kOutput, calls=%fused_computation.30 | convolution fusion | flops 1610612736 | bytes 7340032 | tf_op jit(solution)/shard_map/dot_general | solution.py:111
  169.8 3.7 %fusion.29 = f32[1,16,32,1024]{3,2,1,0:T(8,128)S(1)} fusion(f32[1,16,32,1024]{3,2,1,0:T(8,128)} %collective-permute-done.4, f32[1,16,2,32,1024]{4,3,2,1,0:T(8,128)} %copy-done.4, pred[]{:T(512)S(6)} %eq.163), kind=kLoop, calls=%fused_computation.38 | loop fusion | flops 1048576 | bytes 8388609 | tf_op jit(solution)/shard_map/add | solution.py:128
  175.3 2.3 bitcast_add_fusion
  178.1 22.3 %collective-permute-done.5 = bf16[1,8,32,1024]{3,2,1,0:T(8,128)(2,1)S(1)} collective-permute-done((bf16[1,8,32,1024]{3,2,1,0:T(8,128)(2,1)S(1)}, bf16[1,8,32,1024]{3,2,1,0:T(8,128)(2,1)S(1)}, u32[]{:S(2)}, u32[]{:S(2)}) %collective-permute-start.5) | collective-permute-done | bytes 524320 | tf_op jit(solution)/shard_map/ppermute | solution.py:127
  202.9 9.3 %collective-permute-done.10 = bf16[1,8,32,1024]{3,2,1,0:T(8,128)(2,1)S(1)} collective-permute-done((bf16[1,8,32,1024]{3,2,1,0:T(8,128)(2,1)S(1)}, bf16[1,8,32,1024]{3,2,1,0:T(8,128)(2,1)S(1)}, u32[]{:S(2)}, u32[]{:S(2)}) %collective-permute-start.10) | collective-permute-done | bytes 524320 | tf_op jit(solution)/shard_map/ppermute | solution.py:127
  212.5 2.9 %collective-permute-start.11 = (bf16[1,4,32,1024]{3,2,1,0:T(8,128)(2,1)S(1)}, bf16[1,4,32,1024]{3,2,1,0:T(8,128)(2,1)S(1)}, u32[]{:S(2)}, u32[]{:S(2)}) collective-permute-start(bf16[1,4,32,1024]{3,2,1,0:T(8,128)(2,1)S(1)} %fusion.42), channel_id=1, source_target_pairs={{0,4},{1,5},{2,6},{3,7},{4,0},{5,1},{6,2},{7,3},{8,12},{9,13},{10,... | collective-permute-start | bytes 786440 | tf_op jit(solution)/shard_map/ppermute | solution.py:127
  215.6 3.0 %collective-permute-start.7 = (bf16[1,2,32,1024]{3,2,1,0:T(8,128)(2,1)S(1)}, bf16[1,2,32,1024]{3,2,1,0:T(8,128)(2,1)S(1)}, u32[]{:S(2)}, u32[]{:S(2)}) collective-permute-start(bf16[1,2,32,1024]{3,2,1,0:T(8,128)(2,1)S(1)} %fusion.48), channel_id=1, source_target_pairs={{0,8},{1,9},{2,10},{3,11},{4,12},{5,13},{6,14},{7,15},{8,0},{9,1},... | collective-permute-start | bytes 393224 | tf_op jit(solution)/shard_map/ppermute | solution.py:127
  218.5 5.6 %collective-permute-done.11 = bf16[1,4,32,1024]{3,2,1,0:T(8,128)(2,1)S(1)} collective-permute-done((bf16[1,4,32,1024]{3,2,1,0:T(8,128)(2,1)S(1)}, bf16[1,4,32,1024]{3,2,1,0:T(8,128)(2,1)S(1)}, u32[]{:S(2)}, u32[]{:S(2)}) %collective-permute-start.11) | collective-permute-done | bytes 262176 | tf_op jit(solution)/shard_map/ppermute | solution.py:127
  224.3 3.1 %collective-permute-start.12 = (bf16[1,2,32,1024]{3,2,1,0:T(8,128)(2,1)S(1)}, bf16[1,2,32,1024]{3,2,1,0:T(8,128)(2,1)S(1)}, u32[]{:S(2)}, u32[]{:S(2)}) collective-permute-start(bf16[1,2,32,1024]{3,2,1,0:T(8,128)(2,1)S(1)} %fusion.49), channel_id=1, source_target_pairs={{0,8},{1,9},{2,10},{3,11},{4,12},{5,13},{6,14},{7,15},{8,0},{9,1},... | collective-permute-start | bytes 393224 | tf_op jit(solution)/shard_map/ppermute | solution.py:127
  227.4 2.3 collective-permute-start.8
  231.4 2.8 %collective-permute-start.13 = (bf16[1,1,32,1024]{3,2,1,0:T(8,128)(2,1)S(1)}, bf16[1,1,32,1024]{3,2,1,0:T(8,128)(2,1)S(1)}, u32[]{:S(2)}, u32[]{:S(2)}) collective-permute-start(bf16[1,1,32,1024]{3,2,1,0:T(8,128)(2,1)S(1)} %fusion.59), channel_id=1, source_target_pairs={{0,16},{1,17},{2,18},{3,19},{4,20},{5,21},{6,22},{7,23},{8,24},{9,... | collective-permute-start | bytes 196616 | tf_op jit(solution)/shard_map/ppermute | solution.py:127
  234.3 6.8 %collective-permute-done.8 = bf16[1,1,32,1024]{3,2,1,0:T(8,128)(2,1)S(1)} collective-permute-done((bf16[1,1,32,1024]{3,2,1,0:T(8,128)(2,1)S(1)}, bf16[1,1,32,1024]{3,2,1,0:T(8,128)(2,1)S(1)}, u32[]{:S(2)}, u32[]{:S(2)}) %collective-permute-start.8) | collective-permute-done | bytes 65568 | tf_op jit(solution)/shard_map/ppermute | solution.py:127
  242.6 8.7 %fusion.22 = f32[1024,1024]{1,0:T(8,128)} fusion(bf16[32,49,1024]{2,1,0:T(8,128)(2,1)} %all-to-all-done.2, s32[32,49]{1,0:T(8,128)S(1)} %copy-done.15, pred[32,49]{1,0:T(8,128)(4,1)S(1)} %compare_bitcast_fusion), kind=kOutput, calls=%fused_computation.32 | convolution fusion | flops 3291545600 | bytes 7413408 | tf_op jit(solution)/shard_map/dot_general | solution.py:163
  (104 shorter events, 34.8 us)
Async XLA Ops:
  0.6 22.9 %copy-start = (bf16[1024,1024]{1,0:T(8,128)(2,1)S(1)}, bf16[1024,1024]{1,0:T(8,128)(2,1)}, u32[]{:S(2)}) copy-start(bf16[1024,1024]{1,0:T(8,128)(2,1)} %param.6) | copy-start | bytes 6291460
  29.0 3.7 %copy-start.10 = (bf16[1024,256]{1,0:T(8,128)(2,1)S(1)}, bf16[1024,256]{1,0:T(8,128)(2,1)}, u32[]{:S(2)}) copy-start(bf16[1024,256]{1,0:T(8,128)(2,1)} %param.10) | copy-start | bytes 1572868
  29.0 5.4 %copy-start.11 = (bf16[1024,256]{1,0:T(8,128)(2,1)S(1)}, bf16[1024,256]{1,0:T(8,128)(2,1)}, u32[]{:S(2)}) copy-start(bf16[1024,256]{1,0:T(8,128)(2,1)} %param.9) | copy-start | bytes 1572868
  29.0 5.9 %copy-start.13 = (s32[3,256]{1,0:T(4,128)S(1)}, s32[3,256]{1,0:T(4,128)}, u32[]{:S(2)}) copy-start(s32[3,256]{1,0:T(4,128)} %param.7) | copy-start | bytes 9220
  29.0 5.9 %copy-start.9 = (s32[3,256,256]{2,1,0:T(8,128)S(1)}, s32[3,256,256]{2,1,0:T(8,128)}, u32[]{:S(2)}) copy-start(s32[3,256,256]{2,1,0:T(8,128)} %param.8) | copy-start | bytes 2359300
  29.0 86.8 %all-to-all-start.1 = ((bf16[32,49,1024]{2,1,0:T(8,128)(2,1)}), bf16[32,49,1024]{2,1,0:T(8,128)(2,1)}, u32[]{:S(2)}, u32[]{:S(2)}) async-start(bf16[32,49,1024]{2,1,0:T(8,128)(2,1)} %fusion.19), calls=%async_computation.1 | async-start | bytes 7340032 | tf_op jit(solution)/shard_map/all_to_all | solution.py:23
  32.7 46.8 %collective-permute-start.2 = (bf16[1,1024,256]{2,1,0:T(8,128)(2,1)S(1)}, bf16[1,1024,256]{2,1,0:T(8,128)(2,1)S(1)}, u32[]{:S(2)}, u32[]{:S(2)}) collective-permute-start(bf16[1,1024,256]{2,1,0:T(8,128)(2,1)S(1)} %bitcast.335), channel_id=1, source_target_pairs={{0,2},{1,3},{2,0},{3,1},{4,6},{5,7},{6,4},{7,5},{8,10},{9,11},{10,... | collective-permute-start | bytes 1572872 | tf_op jit(solution)/shard_map/ppermute | solution.py:95
  34.4 56.7 %collective-permute-start = (bf16[1,1024,256]{2,1,0:T(8,128)(2,1)S(1)}, bf16[1,1024,256]{2,1,0:T(8,128)(2,1)}, u32[]{:S(2)}, u32[]{:S(2)}) collective-permute-start(bf16[1,1024,256]{2,1,0:T(8,128)(2,1)S(1)} %bitcast.336), channel_id=1, source_target_pairs={{0,2},{1,3},{2,0},{3,1},{4,6},{5,7},{6,4},{7,5},{8,10},{9,11},{10,... | collective-permute-start | bytes 1572872 | tf_op jit(solution)/shard_map/ppermute | solution.py:95
  93.5 5.6 %collective-permute-start.1 = (bf16[2,1024,256]{2,1,0:T(8,128)(2,1)}, bf16[2,1024,256]{2,1,0:T(8,128)(2,1)}, u32[]{:S(2)}, u32[]{:S(2)}) collective-permute-start(bf16[2,1024,256]{2,1,0:T(8,128)(2,1)} %pad_maximum_fusion.2), channel_id=1, source_target_pairs={{0,1},{1,0},{2,3},{3,2},{4,5},{5,4},{6,7},{7,6},{8,9},{9,8},{10,11... | collective-permute-start | bytes 3145736 | tf_op jit(solution)/shard_map/ppermute | solution.py:95
  95.2 10.8 %collective-permute-start.3 = (bf16[2,1024,256]{2,1,0:T(8,128)(2,1)}, bf16[2,1024,256]{2,1,0:T(8,128)(2,1)S(1)}, u32[]{:S(2)}, u32[]{:S(2)}) collective-permute-start(bf16[2,1024,256]{2,1,0:T(8,128)(2,1)} %pad_maximum_fusion.3), channel_id=1, source_target_pairs={{0,1},{1,0},{2,3},{3,2},{4,5},{5,4},{6,7},{7,6},{8,9},{9,8},{10,11... | collective-permute-start | bytes 3145736 | tf_op jit(solution)/shard_map/ppermute | solution.py:95
  111.9 9.9 %copy-start.5 = (bf16[1024,4,256]{0,2,1:T(8,128)(2,1)S(1)}, bf16[1024,4,256]{0,2,1:T(8,128)(2,1)}, u32[]{:S(2)}) copy-start(bf16[1024,4,256]{0,2,1:T(8,128)(2,1)} %copy.118) | copy-start | bytes 6291460
  121.7 3.8 %copy-start.17 = (bf16[3,256,1024]{2,1,0:T(8,128)(2,1)}, bf16[3,256,1024]{2,1,0:T(8,128)(2,1)S(1)}, u32[]{:S(2)}) copy-start(bf16[3,256,1024]{2,1,0:T(8,128)(2,1)S(1)} %fusion.16) | copy-start | bytes 4718596
  121.8 4.4 %copy-start.16 = (bf16[3,256,1024]{2,1,0:T(8,128)(2,1)S(1)}, bf16[3,256,1024]{2,1,0:T(8,128)(2,1)}, u32[]{:S(2)}) copy-start(bf16[3,256,1024]{2,1,0:T(8,128)(2,1)} %param.11) | copy-start | bytes 4718596
  125.6 1.6 copy-start.6
  126.2 4.9 %copy-start.7 = (bf16[3,256,1024]{2,1,0:T(8,128)(2,1)}, bf16[3,256,1024]{2,1,0:T(8,128)(2,1)S(1)}, u32[]{:S(2)}) copy-start(bf16[3,256,1024]{2,1,0:T(8,128)(2,1)S(1)} %multiply_convert_fusion.2) | copy-start | bytes 4718596
  148.5 94.0 %all-to-all-start.2 = ((bf16[32,49,1024]{2,1,0:T(8,128)(2,1)}), bf16[32,49,1024]{2,1,0:T(8,128)(2,1)}, u32[]{:S(2)}, u32[]{:S(2)}) async-start(bf16[32,49,1024]{2,1,0:T(8,128)(2,1)} %bitcast_convert_fusion), calls=%async_computation.2 | async-start | bytes 7340032 | tf_op jit(solution)/shard_map/all_to_all | solution.py:23
  158.6 2.6 %copy-start.4 = (f32[1,16,2,32,1024]{4,3,2,1,0:T(8,128)}, f32[1,16,2,32,1024]{4,3,2,1,0:T(8,128)S(1)}, u32[]{:S(2)}) copy-start(f32[1,16,2,32,1024]{4,3,2,1,0:T(8,128)S(1)} %convolution_bitcast_fusion.1) | copy-start | bytes 12582916
  161.3 2.9 %copy-start.8 = (bf16[3,256,1024]{2,1,0:T(8,128)(2,1)S(1)}, bf16[3,256,1024]{2,1,0:T(8,128)(2,1)}, u32[]{:S(2)}) copy-start(bf16[3,256,1024]{2,1,0:T(8,128)(2,1)} %copy-done.7) | copy-start | bytes 4718596
  161.3 8.5 %collective-permute-start.4 = (f32[1,16,32,1024]{3,2,1,0:T(8,128)}, f32[1,16,32,1024]{3,2,1,0:T(8,128)}, u32[]{:S(2)}, u32[]{:S(2)}) collective-permute-start(f32[1,16,32,1024]{3,2,1,0:T(8,128)} %select_bitcast_fusion.1), channel_id=1, source_target_pairs={{0,1},{1,0},{2,3},{3,2},{4,5},{5,4},{6,7},{7,6},{8,9},{9,8},{10,11... | collective-permute-start | bytes 6291464 | tf_op jit(solution)/shard_map/ppermute | solution.py:127
  167.3 2.1 copy-start.2
  169.4 5.9 %collective-permute-start.9 = (f32[1,16,32,1024]{3,2,1,0:T(8,128)S(1)}, f32[1,16,32,1024]{3,2,1,0:T(8,128)}, u32[]{:S(2)}, u32[]{:S(2)}) collective-permute-start(f32[1,16,32,1024]{3,2,1,0:T(8,128)S(1)} %select_bitcast_fusion), channel_id=1, source_target_pairs={{0,1},{1,0},{2,3},{3,2},{4,5},{5,4},{6,7},{7,6},{8,9},{9,8},{10,11... | collective-permute-start | bytes 6291464 | tf_op jit(solution)/shard_map/ppermute | solution.py:127
  169.8 5.5 %copy-start.3 = (f32[1,16,2,32,1024]{4,3,1,2,0:T(8,128)S(1)}, f32[1,16,2,32,1024]{4,3,1,2,0:T(8,128)}, u32[]{:S(2)}) copy-start(f32[1,16,2,32,1024]{4,3,1,2,0:T(8,128)} %copy-done.2) | copy-start | bytes 12582916
  173.6 26.9 %collective-permute-start.5 = (bf16[1,8,32,1024]{3,2,1,0:T(8,128)(2,1)S(1)}, bf16[1,8,32,1024]{3,2,1,0:T(8,128)(2,1)S(1)}, u32[]{:S(2)}, u32[]{:S(2)}) collective-permute-start(bf16[1,8,32,1024]{3,2,1,0:T(8,128)(2,1)S(1)} %fusion.36), channel_id=1, source_target_pairs={{0,2},{1,3},{2,0},{3,1},{4,6},{5,7},{6,4},{7,5},{8,10},{9,11},{10,... | collective-permute-start | bytes 1572872 | tf_op jit(solution)/shard_map/ppermute | solution.py:127
  177.7 34.5 %collective-permute-start.10 = (bf16[1,8,32,1024]{3,2,1,0:T(8,128)(2,1)S(1)}, bf16[1,8,32,1024]{3,2,1,0:T(8,128)(2,1)S(1)}, u32[]{:S(2)}, u32[]{:S(2)}) collective-permute-start(bf16[1,8,32,1024]{3,2,1,0:T(8,128)(2,1)S(1)} %fusion.37), channel_id=1, source_target_pairs={{0,2},{1,3},{2,0},{3,1},{4,6},{5,7},{6,4},{7,5},{8,10},{9,11},{10,... | collective-permute-start | bytes 1572872 | tf_op jit(solution)/shard_map/ppermute | solution.py:127
  200.8 14.6 %collective-permute-start.6 = (bf16[1,4,32,1024]{3,2,1,0:T(8,128)(2,1)S(1)}, bf16[1,4,32,1024]{3,2,1,0:T(8,128)(2,1)S(1)}, u32[]{:S(2)}, u32[]{:S(2)}) collective-permute-start(bf16[1,4,32,1024]{3,2,1,0:T(8,128)(2,1)S(1)} %fusion.41), channel_id=1, source_target_pairs={{0,4},{1,5},{2,6},{3,7},{4,0},{5,1},{6,2},{7,3},{8,12},{9,13},{10,... | collective-permute-start | bytes 786440 | tf_op jit(solution)/shard_map/ppermute | solution.py:127
  212.5 11.6 %collective-permute-start.11 = (bf16[1,4,32,1024]{3,2,1,0:T(8,128)(2,1)S(1)}, bf16[1,4,32,1024]{3,2,1,0:T(8,128)(2,1)S(1)}, u32[]{:S(2)}, u32[]{:S(2)}) collective-permute-start(bf16[1,4,32,1024]{3,2,1,0:T(8,128)(2,1)S(1)} %fusion.42), channel_id=1, source_target_pairs={{0,4},{1,5},{2,6},{3,7},{4,0},{5,1},{6,2},{7,3},{8,12},{9,13},{10,... | collective-permute-start | bytes 786440 | tf_op jit(solution)/shard_map/ppermute | solution.py:127
  215.6 11.8 %collective-permute-start.7 = (bf16[1,2,32,1024]{3,2,1,0:T(8,128)(2,1)S(1)}, bf16[1,2,32,1024]{3,2,1,0:T(8,128)(2,1)S(1)}, u32[]{:S(2)}, u32[]{:S(2)}) collective-permute-start(bf16[1,2,32,1024]{3,2,1,0:T(8,128)(2,1)S(1)} %fusion.48), channel_id=1, source_target_pairs={{0,8},{1,9},{2,10},{3,11},{4,12},{5,13},{6,14},{7,15},{8,0},{9,1},... | collective-permute-start | bytes 393224 | tf_op jit(solution)/shard_map/ppermute | solution.py:127
  224.2 18.4 %copy-start.15 = (s32[32,49]{1,0:T(8,128)S(1)}, s32[32,49]{1,0:T(8,128)}, u32[]{:S(2)}) copy-start(s32[32,49]{1,0:T(8,128)} %copy-done.14) | copy-start | bytes 18820
  224.3 7.1 %collective-permute-start.12 = (bf16[1,2,32,1024]{3,2,1,0:T(8,128)(2,1)S(1)}, bf16[1,2,32,1024]{3,2,1,0:T(8,128)(2,1)S(1)}, u32[]{:S(2)}, u32[]{:S(2)}) collective-permute-start(bf16[1,2,32,1024]{3,2,1,0:T(8,128)(2,1)S(1)} %fusion.49), channel_id=1, source_target_pairs={{0,8},{1,9},{2,10},{3,11},{4,12},{5,13},{6,14},{7,15},{8,0},{9,1},... | collective-permute-start | bytes 393224 | tf_op jit(solution)/shard_map/ppermute | solution.py:127
  227.4 13.6 %collective-permute-start.8 = (bf16[1,1,32,1024]{3,2,1,0:T(8,128)(2,1)S(1)}, bf16[1,1,32,1024]{3,2,1,0:T(8,128)(2,1)S(1)}, u32[]{:S(2)}, u32[]{:S(2)}) collective-permute-start(bf16[1,1,32,1024]{3,2,1,0:T(8,128)(2,1)S(1)} %fusion.58), channel_id=1, source_target_pairs={{0,16},{1,17},{2,18},{3,19},{4,20},{5,21},{6,22},{7,23},{8,24},{9,... | collective-permute-start | bytes 196616 | tf_op jit(solution)/shard_map/ppermute | solution.py:127
  231.4 10.4 %collective-permute-start.13 = (bf16[1,1,32,1024]{3,2,1,0:T(8,128)(2,1)S(1)}, bf16[1,1,32,1024]{3,2,1,0:T(8,128)(2,1)S(1)}, u32[]{:S(2)}, u32[]{:S(2)}) collective-permute-start(bf16[1,1,32,1024]{3,2,1,0:T(8,128)(2,1)S(1)} %fusion.59), channel_id=1, source_target_pairs={{0,16},{1,17},{2,18},{3,19},{4,20},{5,21},{6,22},{7,23},{8,24},{9,... | collective-permute-start | bytes 196616 | tf_op jit(solution)/shard_map/ppermute | solution.py:127
  242.6 8.7 %copy-start.1 = (bf16[1024,1024]{1,0:T(8,128)(2,1)S(1)}, bf16[1024,1024]{1,0:T(8,128)(2,1)}, u32[]{:S(2)}) copy-start(bf16[1024,1024]{1,0:T(8,128)(2,1)} %param.6) | copy-start | bytes 6291460
  (2 other events, 1.4 us)
